TPU v7x, 1024 devices: a whole 4x8x16 slice. The times are simulated.
1024 devices in a mesh: rad: 8 (over z_lo), azi: 128 (over x, z_hi, y, core).
Axes of the slice: x: 4, y: 8, z: 16 (z_hi: 2, z_lo: 8; z = z_hi * 8 + z_lo), core: 2. Of those that a mesh axis runs over, the one named last changes fastest.
Arguments:
- fields: float32 [5, 1, 8192, 1024], P(None, None, 'azi', 'rad'), may hold values from -2 to 2, as said below
- shifts: int32 [3, 1024], P(None, 'rad'), may hold values from 0 to 192, as said below
Outputs:
- advanced: float32 [5, 1, 8192, 1024], P(None, None, 'azi', 'rad')
Inputs may be any that keep to these rules, and one draw needn't show every extreme that they name: `fields`: every field component lies within -2 to 2; temperature within 0.5 to 1.5. `shifts`: each step has a row with shift 192 and a row with shift 0.
All inputs are finite; a program needn't handle non-finite values.
Results may differ from a plain program's by a relative error of at most 0.00002.
Values sent between devices are 32-bit elements; how exact they have to be, the bound alone decides.
No kernel may reach another device: no remote copies, remote signals or barrier semaphores. Data moves between devices by JAX's collectives and lax.ppermute only.
A program may use at most 32 MiB of HBM per device.

v0:
```python
import jax
import jax.numpy as jnp
from jax import lax
from jax.sharding import PartitionSpec as P

STEPS = 3
SMAX = 192


courant = 0.2
viscous = 0.1


def passed_along(value, axis, steps):
    count = lax.axis_size(axis)
    pairs = [(source, (source + steps) % count) for source in range(count)]
    return lax.ppermute(value, axis, pairs)


def padded_2(value, sides, width, wrap):
    for axis, dim in sides:
        count, length = (lax.axis_size(axis), value.shape[dim])
        up = [(i, (i + 1) % count) for i in range(count if wrap else count - 1)]
        down = [(j, i) for i, j in up]
        last = lax.slice_in_dim(value, length - width, length, axis=dim)
        initial = lax.slice_in_dim(value, 0, width, axis=dim)
        before = lax.ppermute(last, axis, up)
        after = lax.ppermute(initial, axis, down)
        value = jnp.concatenate([before, value, after], axis=dim)
    return value


def update(padded, inverse):
    centre = padded[:, :, 1:-1, 1:-1]
    inner = padded[:, :, 1:-1, :-2]
    outer = padded[:, :, 1:-1, 2:]
    behind = padded[:, :, :-2, 1:-1]
    ahead = padded[:, :, 2:, 1:-1]
    polar_pad = jnp.concatenate([centre, centre, centre], axis=1)
    polar_sum = polar_pad[:, 2:] + polar_pad[:, :-2]
    radial_vel = centre[1]
    azim_vel = centre[2]
    advect = courant * (
        jnp.maximum(radial_vel, 0.0) * (centre - inner)
        + jnp.minimum(radial_vel, 0.0) * (outer - centre)
        + inverse
        * (
            jnp.maximum(azim_vel, 0.0) * (centre - behind)
            + jnp.minimum(azim_vel, 0.0) * (ahead - centre)
        )
    )
    laplace = (
        outer
        + inner
        - 2.0 * centre
        + inverse * inverse * (ahead + behind - 2.0 * centre)
        + (polar_sum - 2.0 * centre)
    )
    radial_diff = (outer - inner) * 0.5
    azim_diff = (ahead - behind) * 0.5
    diverge = radial_diff[1] + inverse * azim_diff[2]
    log_rho = centre[0]
    temper = centre[4]
    new_log = log_rho - advect[0] - courant * diverge
    new_radial = (
        radial_vel
        - advect[1]
        - courant * (temper * radial_diff[0] + radial_diff[4])
        + 0.5 * courant * inverse * azim_vel * azim_vel
        + viscous * laplace[1]
    )
    new_azim = (
        azim_vel
        - advect[2]
        - courant * inverse * (temper * azim_diff[0] + azim_diff[4])
        - 0.5 * courant * inverse * radial_vel * azim_vel
        + viscous * laplace[2]
    )
    new_polar = centre[3] - advect[3] + viscous * laplace[3]
    new_temper = temper - advect[4] - courant * 0.4 * temper * diverge + viscous * laplace[4]
    return jnp.stack([new_log, new_radial, new_azim, new_polar, new_temper])


def rotate_pieces(fields, offsets):
    width = fields.shape[2]
    count = (SMAX + width - 1) // width
    pieces = [fields]
    for blocks in range(1, count + 1):
        pieces.append(passed_along(fields, "azi", blocks))
    extended = jnp.concatenate(pieces[::-1], axis=2)
    nbits = SMAX.bit_length()
    reach = (1 << nbits) - 1
    anchor = count * width
    front = jnp.zeros(fields.shape[:2] + (reach - anchor,) + fields.shape[3:], fields.dtype)
    window = jnp.concatenate([front, extended], axis=2)
    for bit in range(nbits):
        amount = 1 << bit
        length = window.shape[2] - amount
        chosen = offsets // amount % 2 == 1
        window = jnp.where(
            chosen[None, None, None, :], window[:, :, :length], window[:, :, amount:]
        )
    return window


def local(fields, shifts):
    rows = fields.shape[3]
    total_rows = rows * lax.axis_size("rad")
    row_index = lax.axis_index("rad") * rows + jnp.arange(rows, dtype=jnp.int32)
    radius = 1.0 + (row_index.astype(jnp.float32) + 0.5) / jnp.float32(total_rows)
    inverse = 1.0 / radius
    for step in range(STEPS):
        radial_pad = padded_2(fields, (("rad", 3),), 1, False)
        padded = padded_2(radial_pad, (("azi", 2),), 1, True)
        fields = update(padded, inverse)
        fields = rotate_pieces(fields, shifts[step])
    return fields


def solution(mesh):
    placed = (P(None, None, "azi", "rad"), P(None, "rad"))
    return jax.shard_map(
        local, mesh=mesh, in_specs=placed, out_specs=P(None, None, "azi", "rad"), check_vma=False
    )
```

profile of v0, /device:TPU:192, one launch (start us, length us, event | category | flops | bytes accessed | tf_op | source)
XLA Modules:
  0.0 236.6 jit_solution(8990504700044526449)
XLA Ops:
  0.0 1.2 fusion.105
  1.2 5.5 %collective-permute-start = (f32[5,1,64,1]{3,2,1,0:T(8,128)S(1)}, f32[5,1,64,1]{3,2,1,0:T(8,128)S(1)}, u32[]{:S(2)}, u32[]{:S(2)}) collective-permute-start(f32[5,1,64,1]{3,2,1,0:T(8,128)S(1)} %get-tuple-element.30), channel_id=1, source_target_pairs={{0,128},{128,256},{256,384},{384,512},{512,640},{640,768},{768,896... | collective-permute-start | bytes 3848 | tf_op jit(solution)/shard_map/ppermute | solution.py:27
  6.7 1.9 collective-permute-start.1
  8.6 0.7 copy-done.1
  9.4 0.7 collective-permute-done
  10.1 5.3 %collective-permute-done.1 = f32[5,1,64,1]{3,2,1,0:T(8,128)S(1)} collective-permute-done((f32[5,1,64,1]{3,2,1,0:T(8,128)S(1)}, f32[5,1,64,1]{3,2,1,0:T(8,128)S(1)}, u32[]{:S(2)}, u32[]{:S(2)}) %collective-permute-start.1) | collective-permute-done | bytes 1312 | tf_op jit(solution)/shard_map/ppermute | solution.py:28
  15.4 0.1 pad_maximum_fusion.30
  15.5 1.9 collective-permute-start.2
  17.5 17.9 %collective-permute-start.3 = (f32[5,1,1,130]{3,2,1,0:T(1,128)S(1)}, f32[5,1,1,130]{3,2,1,0:T(1,128)S(1)}, u32[]{:S(2)}, u32[]{:S(2)}) collective-permute-start(f32[5,1,1,130]{3,2,1,0:T(1,128)S(1)} %get-tuple-element.15), channel_id=1, source_target_pairs={{1,0},{2,1},{3,2},{4,3},{5,4},{6,5},{7,6},{8,7},{9,8},{10,9},{11,1... | collective-permute-start | bytes 7808 | tf_op jit(solution)/shard_map/ppermute | solution.py:28
  35.4 1.3 collective-permute-done.3
  36.7 0.2 subtract_multiply_fusion.4
  36.9 0.3 subtract_add_fusion.2
  37.2 0.3 add_multiply_fusion.2
  37.6 1.9 collective-permute-start.4
  39.5 1.9 collective-permute-start.5
  41.4 1.9 collective-permute-start.6
  43.4 15.8 %collective-permute-done.4 = f32[5,1,64,128]{3,2,1,0:T(8,128)S(1)} collective-permute-done((f32[5,1,64,128]{3,2,1,0:T(8,128)S(1)}, f32[5,1,64,128]{3,2,1,0:T(8,128)S(1)}, u32[]{:S(2)}, u32[]{:S(2)}) %collective-permute-start.4) | collective-permute-done | bytes 163872 | tf_op jit(solution)/shard_map/ppermute | solution.py:17
  59.2 24.5 %collective-permute-done.5 = f32[5,1,64,128]{3,2,1,0:T(8,128)S(1)} collective-permute-done((f32[5,1,64,128]{3,2,1,0:T(8,128)S(1)}, f32[5,1,64,128]{3,2,1,0:T(8,128)S(1)}, u32[]{:S(2)}, u32[]{:S(2)}) %collective-permute-start.5) | collective-permute-done | bytes 163872 | tf_op jit(solution)/shard_map/ppermute | solution.py:17
  83.7 1.9 collective-permute-done.6
  85.7 0.8 concatenate.62
  86.5 0.1 slice_select_fusion.5
  86.6 0.1 slice_select_fusion.4
  87.1 0.1 fusion.104
  87.2 1.9 collective-permute-start.7
  89.1 3.9 %collective-permute-start.8 = (f32[5,1,64,1]{3,2,1,0:T(8,128)S(1)}, f32[5,1,64,1]{3,2,1,0:T(8,128)S(1)}, u32[]{:S(2)}, u32[]{:S(2)}) collective-permute-start(f32[5,1,64,1]{3,2,1,0:T(8,128)S(1)} %get-tuple-element.23), channel_id=1, source_target_pairs={{128,0},{256,128},{384,256},{512,384},{640,512},{768,640},{896,768... | collective-permute-start | bytes 3848 | tf_op jit(solution)/shard_map/ppermute | solution.py:28
  93.0 1.4 collective-permute-done.7
  94.4 3.1 %collective-permute-done.8 = f32[5,1,64,1]{3,2,1,0:T(8,128)S(1)} collective-permute-done((f32[5,1,64,1]{3,2,1,0:T(8,128)S(1)}, f32[5,1,64,1]{3,2,1,0:T(8,128)S(1)}, u32[]{:S(2)}, u32[]{:S(2)}) %collective-permute-start.8) | collective-permute-done | bytes 1312 | tf_op jit(solution)/shard_map/ppermute | solution.py:28
  97.5 0.1 pad_maximum_fusion.27
  97.6 1.9 collective-permute-start.10
  99.6 2.4 %collective-permute-start.9 = (f32[5,1,1,130]{3,2,1,0:T(1,128)S(1)}, f32[5,1,1,130]{3,2,1,0:T(1,128)S(1)}, u32[]{:S(2)}, u32[]{:S(2)}) collective-permute-start(f32[5,1,1,130]{3,2,1,0:T(1,128)S(1)} %get-tuple-element.12), channel_id=1, source_target_pairs={{0,1},{1,2},{2,3},{3,4},{4,5},{5,6},{6,7},{7,8},{8,9},{9,10},{10,1... | collective-permute-start | bytes 7808 | tf_op jit(solution)/shard_map/ppermute | solution.py:27
  102.0 15.4 %collective-permute-done.9 = f32[5,1,1,130]{3,2,1,0:T(1,128)S(1)} collective-permute-done((f32[5,1,1,130]{3,2,1,0:T(1,128)S(1)}, f32[5,1,1,130]{3,2,1,0:T(1,128)S(1)}, u32[]{:S(2)}, u32[]{:S(2)}) %collective-permute-start.9) | collective-permute-done | bytes 2632 | tf_op jit(solution)/shard_map/ppermute | solution.py:27
  117.4 0.3 subtract_add_fusion.1
  117.7 0.2 subtract_multiply_fusion.2
  117.9 0.3 add_multiply_fusion.1
  118.3 1.9 collective-permute-start.11
  120.2 1.9 collective-permute-start.12
  122.2 1.9 collective-permute-start.13
  124.1 17.8 %collective-permute-done.11 = f32[5,1,64,128]{3,2,1,0:T(8,128)S(1)} collective-permute-done((f32[5,1,64,128]{3,2,1,0:T(8,128)S(1)}, f32[5,1,64,128]{3,2,1,0:T(8,128)S(1)}, u32[]{:S(2)}, u32[]{:S(2)}) %collective-permute-start.11) | collective-permute-done | bytes 163872 | tf_op jit(solution)/shard_map/ppermute | solution.py:17
  141.9 6.9 %collective-permute-done.12 = f32[5,1,64,128]{3,2,1,0:T(8,128)S(1)} collective-permute-done((f32[5,1,64,128]{3,2,1,0:T(8,128)S(1)}, f32[5,1,64,128]{3,2,1,0:T(8,128)S(1)}, u32[]{:S(2)}, u32[]{:S(2)}) %collective-permute-start.12) | collective-permute-done | bytes 163872 | tf_op jit(solution)/shard_map/ppermute | solution.py:17
  148.7 2.3 collective-permute-done.13
  151.1 0.8 concatenate.68
  151.9 0.1 slice_select_fusion.3
  152.0 0.1 slice_select_fusion.2
  152.5 0.1 fusion.103
  152.6 4.6 %collective-permute-start.14 = (f32[5,1,64,1]{3,2,1,0:T(8,128)S(1)}, f32[5,1,64,1]{3,2,1,0:T(8,128)S(1)}, u32[]{:S(2)}, u32[]{:S(2)}) collective-permute-start(f32[5,1,64,1]{3,2,1,0:T(8,128)S(1)} %get-tuple-element.18), channel_id=1, source_target_pairs={{0,128},{128,256},{256,384},{384,512},{512,640},{640,768},{768,896... | collective-permute-start | bytes 3848 | tf_op jit(solution)/shard_map/ppermute | solution.py:27
  157.1 5.1 %collective-permute-start.15 = (f32[5,1,64,1]{3,2,1,0:T(8,128)S(1)}, f32[5,1,64,1]{3,2,1,0:T(8,128)S(1)}, u32[]{:S(2)}, u32[]{:S(2)}) collective-permute-start(f32[5,1,64,1]{3,2,1,0:T(8,128)S(1)} %get-tuple-element.17), channel_id=1, source_target_pairs={{128,0},{256,128},{384,256},{512,384},{640,512},{768,640},{896,768... | collective-permute-start | bytes 3848 | tf_op jit(solution)/shard_map/ppermute | solution.py:28
  162.2 1.4 collective-permute-done.14
  163.6 2.0 collective-permute-done.15
  165.6 0.1 pad_maximum_fusion.24
  165.7 1.9 collective-permute-start.16
  167.6 16.6 %collective-permute-start.17 = (f32[5,1,1,130]{3,2,1,0:T(1,128)S(1)}, f32[5,1,1,130]{3,2,1,0:T(1,128)S(1)}, u32[]{:S(2)}, u32[]{:S(2)}) collective-permute-start(f32[5,1,1,130]{3,2,1,0:T(1,128)S(1)} %get-tuple-element.7), channel_id=1, source_target_pairs={{1,0},{2,1},{3,2},{4,3},{5,4},{6,5},{7,6},{8,7},{9,8},{10,9},{11,1... | collective-permute-start | bytes 7808 | tf_op jit(solution)/shard_map/ppermute | solution.py:28
  184.2 1.3 collective-permute-done.17
  185.5 0.3 subtract_add_fusion
  185.8 0.2 subtract_multiply_fusion
  186.0 0.3 add_multiply_fusion
  186.4 1.9 collective-permute-start.18
  188.3 1.9 collective-permute-start.19
  190.2 1.9 collective-permute-start.20
  192.2 16.5 %collective-permute-done.18 = f32[5,1,64,128]{3,2,1,0:T(8,128)S(1)} collective-permute-done((f32[5,1,64,128]{3,2,1,0:T(8,128)S(1)}, f32[5,1,64,128]{3,2,1,0:T(8,128)S(1)}, u32[]{:S(2)}, u32[]{:S(2)}) %collective-permute-start.18) | collective-permute-done | bytes 163872 | tf_op jit(solution)/shard_map/ppermute | solution.py:17
  208.7 24.1 %collective-permute-done.19 = f32[5,1,64,128]{3,2,1,0:T(8,128)S(1)} collective-permute-done((f32[5,1,64,128]{3,2,1,0:T(8,128)S(1)}, f32[5,1,64,128]{3,2,1,0:T(8,128)S(1)}, u32[]{:S(2)}, u32[]{:S(2)}) %collective-permute-start.19) | collective-permute-done | bytes 163872 | tf_op jit(solution)/shard_map/ppermute | solution.py:17
  232.8 1.7 collective-permute-done.20
  234.6 0.8 concatenate.74
  235.4 0.1 slice_select_fusion.1
  235.9 0.7 slice_select_fusion.21
  (47 shorter events, 1.4 us)
Async XLA Ops:
  0.0 8.6 %copy-start = (f32[5,1,64,128]{3,2,1,0:T(8,128)S(1)}, f32[5,1,64,128]{3,2,1,0:T(8,128)}, u32[]{:S(2)}) copy-start(f32[5,1,64,128]{3,2,1,0:T(8,128)} %param.2) | copy-start | bytes 491524
  1.2 8.9 %collective-permute-start = (f32[5,1,64,1]{3,2,1,0:T(8,128)S(1)}, f32[5,1,64,1]{3,2,1,0:T(8,128)S(1)}, u32[]{:S(2)}, u32[]{:S(2)}) collective-permute-start(f32[5,1,64,1]{3,2,1,0:T(8,128)S(1)} %get-tuple-element.30), channel_id=1, source_target_pairs={{0,128},{128,256},{256,384},{384,512},{512,640},{640,768},{768,896... | collective-permute-start | bytes 3848 | tf_op jit(solution)/shard_map/ppermute | solution.py:27
  6.7 8.8 %collective-permute-start.1 = (f32[5,1,64,1]{3,2,1,0:T(8,128)S(1)}, f32[5,1,64,1]{3,2,1,0:T(8,128)S(1)}, u32[]{:S(2)}, u32[]{:S(2)}) collective-permute-start(f32[5,1,64,1]{3,2,1,0:T(8,128)S(1)} %get-tuple-element.29), channel_id=1, source_target_pairs={{128,0},{256,128},{384,256},{512,384},{640,512},{768,640},{896,768... | collective-permute-start | bytes 3848 | tf_op jit(solution)/shard_map/ppermute | solution.py:28
  8.6 0.7 copy-start.1
  15.5 19.9 %collective-permute-start.2 = (f32[5,1,1,130]{3,2,1,0:T(1,128)S(1)}, f32[5,1,1,130]{3,2,1,0:T(1,128)S(1)}, u32[]{:S(2)}, u32[]{:S(2)}) collective-permute-start(f32[5,1,1,130]{3,2,1,0:T(1,128)S(1)} %get-tuple-element.16), channel_id=1, source_target_pairs={{0,1},{1,2},{2,3},{3,4},{4,5},{5,6},{6,7},{7,8},{8,9},{9,10},{10,1... | collective-permute-start | bytes 7808 | tf_op jit(solution)/shard_map/ppermute | solution.py:27
  17.5 19.2 %collective-permute-start.3 = (f32[5,1,1,130]{3,2,1,0:T(1,128)S(1)}, f32[5,1,1,130]{3,2,1,0:T(1,128)S(1)}, u32[]{:S(2)}, u32[]{:S(2)}) collective-permute-start(f32[5,1,1,130]{3,2,1,0:T(1,128)S(1)} %get-tuple-element.15), channel_id=1, source_target_pairs={{1,0},{2,1},{3,2},{4,3},{5,4},{6,5},{7,6},{8,7},{9,8},{10,9},{11,1... | collective-permute-start | bytes 7808 | tf_op jit(solution)/shard_map/ppermute | solution.py:28
  37.6 21.7 %collective-permute-start.4 = (f32[5,1,64,128]{3,2,1,0:T(8,128)S(1)}, f32[5,1,64,128]{3,2,1,0:T(8,128)S(1)}, u32[]{:S(2)}, u32[]{:S(2)}) collective-permute-start(f32[5,1,64,128]{3,2,1,0:T(8,128)S(1)} %fusion.40), channel_id=1, source_target_pairs={{0,3},{1,4},{2,5},{3,6},{4,7},{5,8},{6,9},{7,10},{8,11},{9,12},{10... | collective-permute-start | bytes 491528 | tf_op jit(solution)/shard_map/ppermute | solution.py:17
  39.5 44.2 %collective-permute-start.5 = (f32[5,1,64,128]{3,2,1,0:T(8,128)S(1)}, f32[5,1,64,128]{3,2,1,0:T(8,128)S(1)}, u32[]{:S(2)}, u32[]{:S(2)}) collective-permute-start(f32[5,1,64,128]{3,2,1,0:T(8,128)S(1)} %fusion.40), channel_id=1, source_target_pairs={{0,2},{1,3},{2,4},{3,5},{4,6},{5,7},{6,8},{7,9},{8,10},{9,11},{10,... | collective-permute-start | bytes 491528 | tf_op jit(solution)/shard_map/ppermute | solution.py:17
  41.4 44.2 %collective-permute-start.6 = (f32[5,1,64,128]{3,2,1,0:T(8,128)S(1)}, f32[5,1,64,128]{3,2,1,0:T(8,128)S(1)}, u32[]{:S(2)}, u32[]{:S(2)}) collective-permute-start(f32[5,1,64,128]{3,2,1,0:T(8,128)S(1)} %fusion.40), channel_id=1, source_target_pairs={{0,1},{1,2},{2,3},{3,4},{4,5},{5,6},{6,7},{7,8},{8,9},{9,10},{10,1... | collective-permute-start | bytes 491528 | tf_op jit(solution)/shard_map/ppermute | solution.py:17
  87.2 7.2 %collective-permute-start.7 = (f32[5,1,64,1]{3,2,1,0:T(8,128)S(1)}, f32[5,1,64,1]{3,2,1,0:T(8,128)S(1)}, u32[]{:S(2)}, u32[]{:S(2)}) collective-permute-start(f32[5,1,64,1]{3,2,1,0:T(8,128)S(1)} %get-tuple-element.24), channel_id=1, source_target_pairs={{0,128},{128,256},{256,384},{384,512},{512,640},{640,768},{768,896... | collective-permute-start | bytes 3848 | tf_op jit(solution)/shard_map/ppermute | solution.py:27
  89.1 8.4 %collective-permute-start.8 = (f32[5,1,64,1]{3,2,1,0:T(8,128)S(1)}, f32[5,1,64,1]{3,2,1,0:T(8,128)S(1)}, u32[]{:S(2)}, u32[]{:S(2)}) collective-permute-start(f32[5,1,64,1]{3,2,1,0:T(8,128)S(1)} %get-tuple-element.23), channel_id=1, source_target_pairs={{128,0},{256,128},{384,256},{512,384},{640,512},{768,640},{896,768... | collective-permute-start | bytes 3848 | tf_op jit(solution)/shard_map/ppermute | solution.py:28
  97.6 4.4 %collective-permute-start.10 = (f32[5,1,1,130]{3,2,1,0:T(1,128)S(1)}, f32[5,1,1,130]{3,2,1,0:T(1,128)S(1)}, u32[]{:S(2)}, u32[]{:S(2)}) collective-permute-start(f32[5,1,1,130]{3,2,1,0:T(1,128)S(1)} %get-tuple-element.11), channel_id=1, source_target_pairs={{1,0},{2,1},{3,2},{4,3},{5,4},{6,5},{7,6},{8,7},{9,8},{10,9},{11,1... | collective-permute-start | bytes 7808 | tf_op jit(solution)/shard_map/ppermute | solution.py:28
  99.6 17.9 %collective-permute-start.9 = (f32[5,1,1,130]{3,2,1,0:T(1,128)S(1)}, f32[5,1,1,130]{3,2,1,0:T(1,128)S(1)}, u32[]{:S(2)}, u32[]{:S(2)}) collective-permute-start(f32[5,1,1,130]{3,2,1,0:T(1,128)S(1)} %get-tuple-element.12), channel_id=1, source_target_pairs={{0,1},{1,2},{2,3},{3,4},{4,5},{5,6},{6,7},{7,8},{8,9},{9,10},{10,1... | collective-permute-start | bytes 7808 | tf_op jit(solution)/shard_map/ppermute | solution.py:27
  118.3 23.6 %collective-permute-start.11 = (f32[5,1,64,128]{3,2,1,0:T(8,128)S(1)}, f32[5,1,64,128]{3,2,1,0:T(8,128)S(1)}, u32[]{:S(2)}, u32[]{:S(2)}) collective-permute-start(f32[5,1,64,128]{3,2,1,0:T(8,128)S(1)} %fusion.25), channel_id=1, source_target_pairs={{0,3},{1,4},{2,5},{3,6},{4,7},{5,8},{6,9},{7,10},{8,11},{9,12},{10... | collective-permute-start | bytes 491528 | tf_op jit(solution)/shard_map/ppermute | solution.py:17
  120.2 28.5 %collective-permute-start.12 = (f32[5,1,64,128]{3,2,1,0:T(8,128)S(1)}, f32[5,1,64,128]{3,2,1,0:T(8,128)S(1)}, u32[]{:S(2)}, u32[]{:S(2)}) collective-permute-start(f32[5,1,64,128]{3,2,1,0:T(8,128)S(1)} %fusion.25), channel_id=1, source_target_pairs={{0,2},{1,3},{2,4},{3,5},{4,6},{5,7},{6,8},{7,9},{8,10},{9,11},{10,... | collective-permute-start | bytes 491528 | tf_op jit(solution)/shard_map/ppermute | solution.py:17
  122.2 28.9 %collective-permute-start.13 = (f32[5,1,64,128]{3,2,1,0:T(8,128)S(1)}, f32[5,1,64,128]{3,2,1,0:T(8,128)S(1)}, u32[]{:S(2)}, u32[]{:S(2)}) collective-permute-start(f32[5,1,64,128]{3,2,1,0:T(8,128)S(1)} %fusion.25), channel_id=1, source_target_pairs={{0,1},{1,2},{2,3},{3,4},{4,5},{5,6},{6,7},{7,8},{8,9},{9,10},{10,1... | collective-permute-start | bytes 491528 | tf_op jit(solution)/shard_map/ppermute | solution.py:17
  152.6 11.0 %collective-permute-start.14 = (f32[5,1,64,1]{3,2,1,0:T(8,128)S(1)}, f32[5,1,64,1]{3,2,1,0:T(8,128)S(1)}, u32[]{:S(2)}, u32[]{:S(2)}) collective-permute-start(f32[5,1,64,1]{3,2,1,0:T(8,128)S(1)} %get-tuple-element.18), channel_id=1, source_target_pairs={{0,128},{128,256},{256,384},{384,512},{512,640},{640,768},{768,896... | collective-permute-start | bytes 3848 | tf_op jit(solution)/shard_map/ppermute | solution.py:27
  157.1 8.4 %collective-permute-start.15 = (f32[5,1,64,1]{3,2,1,0:T(8,128)S(1)}, f32[5,1,64,1]{3,2,1,0:T(8,128)S(1)}, u32[]{:S(2)}, u32[]{:S(2)}) collective-permute-start(f32[5,1,64,1]{3,2,1,0:T(8,128)S(1)} %get-tuple-element.17), channel_id=1, source_target_pairs={{128,0},{256,128},{384,256},{512,384},{640,512},{768,640},{896,768... | collective-permute-start | bytes 3848 | tf_op jit(solution)/shard_map/ppermute | solution.py:28
  165.7 18.5 %collective-permute-start.16 = (f32[5,1,1,130]{3,2,1,0:T(1,128)S(1)}, f32[5,1,1,130]{3,2,1,0:T(1,128)S(1)}, u32[]{:S(2)}, u32[]{:S(2)}) collective-permute-start(f32[5,1,1,130]{3,2,1,0:T(1,128)S(1)} %get-tuple-element.8), channel_id=1, source_target_pairs={{0,1},{1,2},{2,3},{3,4},{4,5},{5,6},{6,7},{7,8},{8,9},{9,10},{10,1... | collective-permute-start | bytes 7808 | tf_op jit(solution)/shard_map/ppermute | solution.py:27
  167.6 17.9 %collective-permute-start.17 = (f32[5,1,1,130]{3,2,1,0:T(1,128)S(1)}, f32[5,1,1,130]{3,2,1,0:T(1,128)S(1)}, u32[]{:S(2)}, u32[]{:S(2)}) collective-permute-start(f32[5,1,1,130]{3,2,1,0:T(1,128)S(1)} %get-tuple-element.7), channel_id=1, source_target_pairs={{1,0},{2,1},{3,2},{4,3},{5,4},{6,5},{7,6},{8,7},{9,8},{10,9},{11,1... | collective-permute-start | bytes 7808 | tf_op jit(solution)/shard_map/ppermute | solution.py:28
  186.4 22.3 %collective-permute-start.18 = (f32[5,1,64,128]{3,2,1,0:T(8,128)S(1)}, f32[5,1,64,128]{3,2,1,0:T(8,128)S(1)}, u32[]{:S(2)}, u32[]{:S(2)}) collective-permute-start(f32[5,1,64,128]{3,2,1,0:T(8,128)S(1)} %fusion.10), channel_id=1, source_target_pairs={{0,3},{1,4},{2,5},{3,6},{4,7},{5,8},{6,9},{7,10},{8,11},{9,12},{10... | collective-permute-start | bytes 491528 | tf_op jit(solution)/shard_map/ppermute | solution.py:17
  188.3 44.5 %collective-permute-start.19 = (f32[5,1,64,128]{3,2,1,0:T(8,128)S(1)}, f32[5,1,64,128]{3,2,1,0:T(8,128)S(1)}, u32[]{:S(2)}, u32[]{:S(2)}) collective-permute-start(f32[5,1,64,128]{3,2,1,0:T(8,128)S(1)} %fusion.10), channel_id=1, source_target_pairs={{0,2},{1,3},{2,4},{3,5},{4,6},{5,7},{6,8},{7,9},{8,10},{9,11},{10,... | collective-permute-start | bytes 491528 | tf_op jit(solution)/shard_map/ppermute | solution.py:17
  190.2 44.3 %collective-permute-start.20 = (f32[5,1,64,128]{3,2,1,0:T(8,128)S(1)}, f32[5,1,64,128]{3,2,1,0:T(8,128)S(1)}, u32[]{:S(2)}, u32[]{:S(2)}) collective-permute-start(f32[5,1,64,128]{3,2,1,0:T(8,128)S(1)} %fusion.10), channel_id=1, source_target_pairs={{0,1},{1,2},{2,3},{3,4},{4,5},{5,6},{6,7},{7,8},{8,9},{9,10},{10,1... | collective-permute-start | bytes 491528 | tf_op jit(solution)/shard_map/ppermute | solution.py:17
where the time goes:
time: 237 us
  waiting for transfers between devices  144 us (61%)
  starting transfers between devices  82.8 us (35%)
  other arithmetic  5.05 us (2%)
  local copies, waits for them, and re-layouts  4.55 us (2%)
    ppermute x9, waiting for transfers between devices, passed_along(): return lax.ppermute(value, axis, pairs)  112 us
    ppermute x6, starting transfers between devices, padded_2(): after = lax.ppermute(initial, axis, down)  47.3 us
    ppermute x6, waiting for transfers between devices, padded_2(): before = lax.ppermute(last, axis, up)  18.8 us
    ppermute x6, starting transfers between devices, padded_2(): before = lax.ppermute(last, axis, up)  18.2 us
    ppermute x9, starting transfers between devices, passed_along(): return lax.ppermute(value, axis, pairs)  17.3 us
    ppermute x6, waiting for transfers between devices, padded_2(): after = lax.ppermute(initial, axis, down)  13 us
  transfers between devices with their start and end apart: 21, of which 18 were waited for; matrix products, arithmetic and copies ran while one was open for 0% of the time, Pallas kernels for 0%

commit v1 on v0

v1 whole, which is shorter than its diff:
```python
import jax
import jax.numpy as jnp
from jax import lax
from jax.sharding import PartitionSpec as P

STEPS = 3
SMAX = 192


courant = 0.2
viscous = 0.1


def passed_along(value, axis, steps, wrap=True):
    count = lax.axis_size(axis)
    if wrap:
        pairs = [(source, (source + steps) % count) for source in range(count)]
    else:
        pairs = [
            (source, source + steps)
            for source in range(count)
            if 0 <= source + steps < count
        ]
    return lax.ppermute(value, axis, pairs)


def update(padded, inverse):
    centre = padded[:, :, 1:-1, 1:-1]
    inner = padded[:, :, 1:-1, :-2]
    outer = padded[:, :, 1:-1, 2:]
    behind = padded[:, :, :-2, 1:-1]
    ahead = padded[:, :, 2:, 1:-1]
    polar_pad = jnp.concatenate([centre[:, :1], centre, centre[:, -1:]], axis=1)
    polar_sum = polar_pad[:, 2:] + polar_pad[:, :-2]
    radial_vel = centre[1]
    azim_vel = centre[2]
    advect = courant * (
        jnp.maximum(radial_vel, 0.0) * (centre - inner)
        + jnp.minimum(radial_vel, 0.0) * (outer - centre)
        + inverse
        * (
            jnp.maximum(azim_vel, 0.0) * (centre - behind)
            + jnp.minimum(azim_vel, 0.0) * (ahead - centre)
        )
    )
    laplace = (
        outer
        + inner
        - 2.0 * centre
        + inverse * inverse * (ahead + behind - 2.0 * centre)
        + (polar_sum - 2.0 * centre)
    )
    radial_diff = (outer - inner) * 0.5
    azim_diff = (ahead - behind) * 0.5
    diverge = radial_diff[1] + inverse * azim_diff[2]
    log_rho = centre[0]
    temper = centre[4]
    new_log = log_rho - advect[0] - courant * diverge
    new_radial = (
        radial_vel
        - advect[1]
        - courant * (temper * radial_diff[0] + radial_diff[4])
        + 0.5 * courant * inverse * azim_vel * azim_vel
        + viscous * laplace[1]
    )
    new_azim = (
        azim_vel
        - advect[2]
        - courant * inverse * (temper * azim_diff[0] + azim_diff[4])
        - 0.5 * courant * inverse * radial_vel * azim_vel
        + viscous * laplace[2]
    )
    new_polar = centre[3] - advect[3] + viscous * laplace[3]
    new_temper = temper - advect[4] - courant * 0.4 * temper * diverge + viscous * laplace[4]
    return jnp.stack([new_log, new_radial, new_azim, new_polar, new_temper])


def halo_exchange(fields, shifts, width):
    cells = fields.shape[2]
    last = fields[:, :, cells - width :]
    first = fields[:, :, :width]
    before = passed_along(last, "azi", 1)
    after = passed_along(first, "azi", -1)
    wide = jnp.concatenate([before, fields, after], axis=2)

    rows = wide.shape[3]
    shape = wide.shape[:3] + (width,)
    count = shape[0] * shape[1] * shape[2] * shape[3]

    def pack(lo, hi):
        part = wide[:, :, :, lo:hi].reshape(-1)
        rates = shifts[:, lo:hi].astype(jnp.float32).reshape(-1)
        return jnp.concatenate([part, rates])

    def unpack(flat):
        part = flat[:count].reshape(shape)
        rates = flat[count:].reshape(shifts.shape[0], width)
        return part, rates.astype(jnp.int32)

    inner, inner_shift = unpack(passed_along(pack(rows - width, rows), "rad", 1, False))
    outer, outer_shift = unpack(passed_along(pack(0, width), "rad", -1, False))
    wide = jnp.concatenate([inner, wide, outer], axis=3)
    wide_shifts = jnp.concatenate([inner_shift, shifts, outer_shift], axis=1)
    return wide, wide_shifts


def rotate_window(window, offsets, out_len):
    take = SMAX - offsets
    nbits = SMAX.bit_length()
    spare = (1 << nbits) - 1 + out_len - window.shape[2]
    if spare > 0:
        pad = jnp.zeros(window.shape[:2] + (spare,) + window.shape[3:], window.dtype)
        window = jnp.concatenate([window, pad], axis=2)
    for bit in range(nbits):
        amount = 1 << bit
        length = window.shape[2] - amount
        chosen = take // amount % 2 == 1
        window = jnp.where(
            chosen[None, None, None, :], window[:, :, amount:], window[:, :, :length]
        )
    return window[:, :, :out_len]


def local(fields, shifts):
    cells = fields.shape[2]
    rows = fields.shape[3]
    total_rows = rows * lax.axis_size("rad")
    width = STEPS
    wide, wide_shifts = halo_exchange(fields, shifts, width)
    start_row = lax.axis_index("rad") * rows
    blocks = (SMAX + cells - 1) // cells
    for step in range(STEPS):
        w = width - step
        row_index = start_row - w + jnp.arange(rows + 2 * w, dtype=jnp.int32)
        inside = (row_index >= 0) & (row_index < total_rows)
        wide = jnp.where(inside[None, None, None, :], wide, 0.0)
        inner_rows = row_index[1:-1]
        radius = 1.0 + (inner_rows.astype(jnp.float32) + 0.5) / jnp.float32(total_rows)
        inverse = 1.0 / radius
        updated = update(wide, inverse)
        a = w - 1
        head = updated[:, :, :cells]
        pieces = [passed_along(head, "azi", k) for k in range(blocks, 0, -1)]
        window = jnp.concatenate(pieces + [updated], axis=2)
        window = window[:, :, blocks * cells - SMAX :]
        wide_shifts = wide_shifts[:, 1:-1]
        wide = rotate_window(window, wide_shifts[step], cells + 2 * a)
    return wide


def solution(mesh):
    placed = (P(None, None, "azi", "rad"), P(None, "rad"))
    return jax.shard_map(
        local, mesh=mesh, in_specs=placed, out_specs=P(None, None, "azi", "rad"), check_vma=False
    )
```

time: 237 us -> 241 us (1.017)
  the two profiles are of different devices: /device:TPU:192 before, /device:TPU:198 now
where the time goes in v1:
time: 241 us
  waiting for transfers between devices  182 us (76%)
  starting transfers between devices  44.3 us (18%)
  other arithmetic  9.81 us (4%)
  local copies, waits for them, and re-layouts  3.6 us (1%)
    ppermute x13, waiting for transfers between devices, passed_along(): return lax.ppermute(value, axis, pairs)  182 us
    ppermute x13, starting transfers between devices, passed_along(): return lax.ppermute(value, axis, pairs)  44.3 us
  transfers between devices with their start and end apart: 13, of which 11 were waited for; matrix products, arithmetic and copies ran while one was open for 1% of the time, Pallas kernels for 0%

profile of v1, /device:TPU:198, one launch (start us, length us, event | category | flops | bytes accessed | tf_op | source)
XLA Modules:
  0.0 240.6 jit_solution(4357674366787632629)
XLA Ops:
  0.0 0.8 fusion.103
  0.8 1.9 collective-permute-start
  2.7 19.3 %collective-permute-start.1 = (f32[5,1,3,128]{3,2,1,0:T(4,128)S(1)}, f32[5,1,3,128]{3,2,1,0:T(4,128)S(1)}, u32[]{:S(2)}, u32[]{:S(2)}) collective-permute-start(f32[5,1,3,128]{3,2,1,0:T(4,128)S(1)} %get-tuple-element.47), channel_id=1, source_target_pairs={{0,127},{1,0},{2,1},{3,2},{4,3},{5,4},{6,5},{7,6},{8,7},{9,8},{10,... | collective-permute-start | bytes 23048 | tf_op jit(solution)/shard_map/ppermute | solution.py:24
  22.0 0.8 slice_convert_fusion.1
  23.4 0.9 pad_maximum_fusion
  24.3 0.1 fusion.102
  24.4 0.2 reshape.1273
  24.7 3.4 %collective-permute-start.2 = (f32[1059]{0:T(1024)S(1)}, f32[1059]{0:T(1024)S(1)}, u32[]{:S(2)}, u32[]{:S(2)}) collective-permute-start(f32[1059]{0:T(1024)S(1)} %pad_maximum_fusion.1), channel_id=1, source_target_pairs={{0,128},{128,256},{256,384},{384,512},{512,640},{640,768},{768,896... | collective-permute-start | bytes 12716 | tf_op jit(solution)/shard_map/ppermute | solution.py:24
  28.1 0.2 reshape.1275
  28.4 2.5 %collective-permute-start.3 = (f32[1059]{0:T(1024)S(1)}, f32[1059]{0:T(1024)S(1)}, u32[]{:S(2)}, u32[]{:S(2)}) collective-permute-start(f32[1059]{0:T(1024)S(1)} %pad_maximum_fusion.2), channel_id=1, source_target_pairs={{128,0},{256,128},{384,256},{512,384},{640,512},{768,640},{896,768... | collective-permute-start | bytes 12716 | tf_op jit(solution)/shard_map/ppermute | solution.py:24
  30.9 0.2 concatenate.40
  31.1 4.1 %collective-permute-done.3 = f32[1059]{0:T(1024)S(1)} collective-permute-done((f32[1059]{0:T(1024)S(1)}, f32[1059]{0:T(1024)S(1)}, u32[]{:S(2)}, u32[]{:S(2)}) %collective-permute-start.3) | collective-permute-done | bytes 4268 | tf_op jit(solution)/shard_map/ppermute | solution.py:24
  35.1 0.2 concatenate.41
  35.3 0.2 maximum_select_fusion
  35.6 0.1 maximum_bitcast_fusion.3
  35.7 0.2 subtract_multiply_fusion.3
  35.9 0.6 subtract_add_fusion.1
  36.5 0.1 fusion.37
  36.6 0.1 fusion.4
  36.7 0.1 fusion.29
  36.9 0.1 fusion.24
  37.1 1.9 collective-permute-start.4
  39.0 1.9 collective-permute-start.5
  40.9 1.9 collective-permute-start.6
  43.4 26.9 %collective-permute-done.4 = f32[5,1,64,132]{3,2,1,0:T(8,128)S(1)} collective-permute-done((f32[5,1,64,132]{3,2,1,0:T(8,128)S(1)}, f32[5,1,64,132]{3,2,1,0:T(8,128)S(1)}, u32[]{:S(2)}, u32[]{:S(2)}) %collective-permute-start.4) | collective-permute-done | bytes 168992 | tf_op jit(solution)/shard_map/ppermute | solution.py:24
  70.3 65.2 %collective-permute-done.5 = f32[5,1,64,132]{3,2,1,0:T(8,128)S(1)} collective-permute-done((f32[5,1,64,132]{3,2,1,0:T(8,128)S(1)}, f32[5,1,64,132]{3,2,1,0:T(8,128)S(1)}, u32[]{:S(2)}, u32[]{:S(2)}) %collective-permute-start.5) | collective-permute-done | bytes 168992 | tf_op jit(solution)/shard_map/ppermute | solution.py:24
  135.6 7.5 %collective-permute-done.6 = f32[5,1,64,132]{3,2,1,0:T(8,128)S(1)} collective-permute-done((f32[5,1,64,132]{3,2,1,0:T(8,128)S(1)}, f32[5,1,64,132]{3,2,1,0:T(8,128)S(1)}, u32[]{:S(2)}, u32[]{:S(2)}) %collective-permute-start.6) | collective-permute-done | bytes 168992 | tf_op jit(solution)/shard_map/ppermute | solution.py:24
  143.1 0.7 concatenate.43
  143.8 0.2 slice_select_fusion
  144.0 0.2 slice_select_fusion.5
  144.1 0.2 slice_select_fusion.4
  144.3 0.1 slice_select_fusion.7
  144.5 0.1 slice_select_fusion.9
  144.6 0.1 slice_select_fusion.11
  144.8 0.1 maximum_bitcast_fusion.1
  145.0 0.2 subtract_multiply_fusion.1
  145.1 0.6 subtract_add_fusion
  145.8 0.1 fusion.7
  146.0 0.1 fusion.14
  146.2 0.1 fusion.9
  146.3 1.9 collective-permute-start.7
  148.3 1.9 collective-permute-start.8
  150.2 1.9 collective-permute-start.9
  152.2 15.3 %collective-permute-done.7 = f32[5,1,64,130]{3,2,1,0:T(8,128)S(1)} collective-permute-done((f32[5,1,64,130]{3,2,1,0:T(8,128)S(1)}, f32[5,1,64,130]{3,2,1,0:T(8,128)S(1)}, u32[]{:S(2)}, u32[]{:S(2)}) %collective-permute-start.7) | collective-permute-done | bytes 166432 | tf_op jit(solution)/shard_map/ppermute | solution.py:24
  167.5 39.1 %collective-permute-done.8 = f32[5,1,64,130]{3,2,1,0:T(8,128)S(1)} collective-permute-done((f32[5,1,64,130]{3,2,1,0:T(8,128)S(1)}, f32[5,1,64,130]{3,2,1,0:T(8,128)S(1)}, u32[]{:S(2)}, u32[]{:S(2)}) %collective-permute-start.8) | collective-permute-done | bytes 166432 | tf_op jit(solution)/shard_map/ppermute | solution.py:24
  206.6 7.1 %collective-permute-done.9 = f32[5,1,64,130]{3,2,1,0:T(8,128)S(1)} collective-permute-done((f32[5,1,64,130]{3,2,1,0:T(8,128)S(1)}, f32[5,1,64,130]{3,2,1,0:T(8,128)S(1)}, u32[]{:S(2)}, u32[]{:S(2)}) %collective-permute-start.9) | collective-permute-done | bytes 166432 | tf_op jit(solution)/shard_map/ppermute | solution.py:24
  213.7 0.7 concatenate.44
  214.4 0.2 slice_select_fusion.3
  214.6 0.2 slice_select_fusion.2
  214.8 0.2 slice_select_fusion.1
  215.0 0.1 slice_select_fusion.6
  215.1 0.1 slice_select_fusion.8
  215.2 0.1 slice_select_fusion.10
  215.6 0.1 subtract_multiply_fusion.5
  215.7 0.3 subtract_add_fusion.2
  216.1 0.1 constant_dynamic-update-slice_fusion.3
  216.2 0.1 constant_dynamic-update-slice_fusion.2
  216.4 1.9 collective-permute-start.10
  218.4 1.9 collective-permute-start.11
  220.4 1.9 collective-permute-start.12
  222.3 13.6 %collective-permute-done.10 = f32[5,1,64,128]{3,2,1,0:T(8,128)S(1)} collective-permute-done((f32[5,1,64,128]{3,2,1,0:T(8,128)S(1)}, f32[5,1,64,128]{3,2,1,0:T(8,128)S(1)}, u32[]{:S(2)}, u32[]{:S(2)}) %collective-permute-start.10) | collective-permute-done | bytes 163872 | tf_op jit(solution)/shard_map/ppermute | solution.py:24
  235.9 1.9 collective-permute-done.11
  237.8 1.4 collective-permute-done.12
  239.9 0.7 slice_select_fusion.23
  (63 shorter events, 2.9 us)
Async XLA Ops:
  0.0 35.3 %copy-start = (f32[5,1,64,128]{3,2,1,0:T(8,128)S(1)}, f32[5,1,64,128]{3,2,1,0:T(8,128)}, u32[]{:S(2)}) copy-start(f32[5,1,64,128]{3,2,1,0:T(8,128)} %param.2) | copy-start | bytes 491524
  0.8 22.5 %collective-permute-start = (f32[5,1,3,128]{3,2,1,0:T(4,128)S(1)}, f32[5,1,3,128]{3,2,1,0:T(4,128)S(1)}, u32[]{:S(2)}, u32[]{:S(2)}) collective-permute-start(f32[5,1,3,128]{3,2,1,0:T(4,128)S(1)} %get-tuple-element.46), channel_id=1, source_target_pairs={{0,1},{1,2},{2,3},{3,4},{4,5},{5,6},{6,7},{7,8},{8,9},{9,10},{10,1... | collective-permute-start | bytes 23048 | tf_op jit(solution)/shard_map/ppermute | solution.py:24
  2.7 20.6 %collective-permute-start.1 = (f32[5,1,3,128]{3,2,1,0:T(4,128)S(1)}, f32[5,1,3,128]{3,2,1,0:T(4,128)S(1)}, u32[]{:S(2)}, u32[]{:S(2)}) collective-permute-start(f32[5,1,3,128]{3,2,1,0:T(4,128)S(1)} %get-tuple-element.47), channel_id=1, source_target_pairs={{0,127},{1,0},{2,1},{3,2},{4,3},{5,4},{6,5},{7,6},{8,7},{9,8},{10,... | collective-permute-start | bytes 23048 | tf_op jit(solution)/shard_map/ppermute | solution.py:24
  24.7 6.1 %collective-permute-start.2 = (f32[1059]{0:T(1024)S(1)}, f32[1059]{0:T(1024)S(1)}, u32[]{:S(2)}, u32[]{:S(2)}) collective-permute-start(f32[1059]{0:T(1024)S(1)} %pad_maximum_fusion.1), channel_id=1, source_target_pairs={{0,128},{128,256},{256,384},{384,512},{512,640},{640,768},{768,896... | collective-permute-start | bytes 12716 | tf_op jit(solution)/shard_map/ppermute | solution.py:24
  28.4 6.7 %collective-permute-start.3 = (f32[1059]{0:T(1024)S(1)}, f32[1059]{0:T(1024)S(1)}, u32[]{:S(2)}, u32[]{:S(2)}) collective-permute-start(f32[1059]{0:T(1024)S(1)} %pad_maximum_fusion.2), channel_id=1, source_target_pairs={{128,0},{256,128},{384,256},{512,384},{640,512},{768,640},{896,768... | collective-permute-start | bytes 12716 | tf_op jit(solution)/shard_map/ppermute | solution.py:24
  36.5 6.7 %copy-start.1 = (s32[3,128]{1,0:T(4,128)S(1)}, s32[3,128]{1,0:T(4,128)}, u32[]{:S(2)}) copy-start(s32[3,128]{1,0:T(4,128)} %param.3) | copy-start | bytes 4612
  37.1 33.3 %collective-permute-start.4 = (f32[5,1,64,132]{3,2,1,0:T(8,128)S(1)}, f32[5,1,64,132]{3,2,1,0:T(8,128)S(1)}, u32[]{:S(2)}, u32[]{:S(2)}) collective-permute-start(f32[5,1,64,132]{3,2,1,0:T(8,128)S(1)} %slice.635), channel_id=1, source_target_pairs={{0,3},{1,4},{2,5},{3,6},{4,7},{5,8},{6,9},{7,10},{8,11},{9,12},{10... | collective-permute-start | bytes 506888 | tf_op jit(solution)/shard_map/ppermute | solution.py:24
  39.0 96.6 %collective-permute-start.5 = (f32[5,1,64,132]{3,2,1,0:T(8,128)S(1)}, f32[5,1,64,132]{3,2,1,0:T(8,128)S(1)}, u32[]{:S(2)}, u32[]{:S(2)}) collective-permute-start(f32[5,1,64,132]{3,2,1,0:T(8,128)S(1)} %slice.635), channel_id=1, source_target_pairs={{0,2},{1,3},{2,4},{3,5},{4,6},{5,7},{6,8},{7,9},{8,10},{9,11},{10,... | collective-permute-start | bytes 506888 | tf_op jit(solution)/shard_map/ppermute | solution.py:24
  40.9 102.1 %collective-permute-start.6 = (f32[5,1,64,132]{3,2,1,0:T(8,128)S(1)}, f32[5,1,64,132]{3,2,1,0:T(8,128)S(1)}, u32[]{:S(2)}, u32[]{:S(2)}) collective-permute-start(f32[5,1,64,132]{3,2,1,0:T(8,128)S(1)} %slice.635), channel_id=1, source_target_pairs={{0,1},{1,2},{2,3},{3,4},{4,5},{5,6},{6,7},{7,8},{8,9},{9,10},{10,1... | collective-permute-start | bytes 506888 | tf_op jit(solution)/shard_map/ppermute | solution.py:24
  146.3 21.1 %collective-permute-start.7 = (f32[5,1,64,130]{3,2,1,0:T(8,128)S(1)}, f32[5,1,64,130]{3,2,1,0:T(8,128)S(1)}, u32[]{:S(2)}, u32[]{:S(2)}) collective-permute-start(f32[5,1,64,130]{3,2,1,0:T(8,128)S(1)} %slice.677), channel_id=1, source_target_pairs={{0,3},{1,4},{2,5},{3,6},{4,7},{5,8},{6,9},{7,10},{8,11},{9,12},{10... | collective-permute-start | bytes 499208 | tf_op jit(solution)/shard_map/ppermute | solution.py:24
  148.3 58.3 %collective-permute-start.8 = (f32[5,1,64,130]{3,2,1,0:T(8,128)S(1)}, f32[5,1,64,130]{3,2,1,0:T(8,128)S(1)}, u32[]{:S(2)}, u32[]{:S(2)}) collective-permute-start(f32[5,1,64,130]{3,2,1,0:T(8,128)S(1)} %slice.677), channel_id=1, source_target_pairs={{0,2},{1,3},{2,4},{3,5},{4,6},{5,7},{6,8},{7,9},{8,10},{9,11},{10,... | collective-permute-start | bytes 499208 | tf_op jit(solution)/shard_map/ppermute | solution.py:24
  150.2 63.5 %collective-permute-start.9 = (f32[5,1,64,130]{3,2,1,0:T(8,128)S(1)}, f32[5,1,64,130]{3,2,1,0:T(8,128)S(1)}, u32[]{:S(2)}, u32[]{:S(2)}) collective-permute-start(f32[5,1,64,130]{3,2,1,0:T(8,128)S(1)} %slice.677), channel_id=1, source_target_pairs={{0,1},{1,2},{2,3},{3,4},{4,5},{5,6},{6,7},{7,8},{8,9},{9,10},{10,1... | collective-permute-start | bytes 499208 | tf_op jit(solution)/shard_map/ppermute | solution.py:24
  216.4 19.4 %collective-permute-start.10 = (f32[5,1,64,128]{3,2,1,0:T(8,128)S(1)}, f32[5,1,64,128]{3,2,1,0:T(8,128)S(1)}, u32[]{:S(2)}, u32[]{:S(2)}) collective-permute-start(f32[5,1,64,128]{3,2,1,0:T(8,128)S(1)} %get-tuple-element.5), channel_id=1, source_target_pairs={{0,3},{1,4},{2,5},{3,6},{4,7},{5,8},{6,9},{7,10},{8,11},{9,12},{10... | collective-permute-start | bytes 491528 | tf_op jit(solution)/shard_map/ppermute | solution.py:24
  218.4 19.4 %collective-permute-start.11 = (f32[5,1,64,128]{3,2,1,0:T(8,128)S(1)}, f32[5,1,64,128]{3,2,1,0:T(8,128)S(1)}, u32[]{:S(2)}, u32[]{:S(2)}) collective-permute-start(f32[5,1,64,128]{3,2,1,0:T(8,128)S(1)} %get-tuple-element.5), channel_id=1, source_target_pairs={{0,2},{1,3},{2,4},{3,5},{4,6},{5,7},{6,8},{7,9},{8,10},{9,11},{10,... | collective-permute-start | bytes 491528 | tf_op jit(solution)/shard_map/ppermute | solution.py:24
  220.4 18.9 %collective-permute-start.12 = (f32[5,1,64,128]{3,2,1,0:T(8,128)S(1)}, f32[5,1,64,128]{3,2,1,0:T(8,128)S(1)}, u32[]{:S(2)}, u32[]{:S(2)}) collective-permute-start(f32[5,1,64,128]{3,2,1,0:T(8,128)S(1)} %get-tuple-element.5), channel_id=1, source_target_pairs={{0,1},{1,2},{2,3},{3,4},{4,5},{5,6},{6,7},{7,8},{8,9},{9,10},{10,1... | collective-permute-start | bytes 491528 | tf_op jit(solution)/shard_map/ppermute | solution.py:24

commit v2 on v1

--- a/solution.py
+++ b/solution.py
@@ -5,6 +5,7 @@
 
 STEPS = 3
 SMAX = 192
+PLANE = 16
 
 
 courant = 0.2
@@ -121,6 +122,47 @@
     return window[:, :, :out_len]
 
 
+def crossing_relays(groups, count, plane, blocks):
+    half = plane // 2
+    first, second = [], [[] for _ in range(blocks)]
+    for g in range(groups):
+        for block in range(count // plane):
+            base = block * plane
+            after = (base + plane) % count
+            relay = {}
+            for j in range(1, blocks + 1):
+                lane = (3 * g + j - 1) % half
+                relay[j] = base + 2 * lane + (j - 1) // 2
+                first.append((g * count + base + plane - j, g * count + relay[j]))
+            for k in range(1, blocks + 1):
+                for i in range(k):
+                    second[k - 1].append((g * count + relay[k - i], g * count + after + i))
+    return first, second
+
+
+def rotation_pieces(head, plane, blocks):
+    count = lax.axis_size("azi")
+    groups = lax.axis_size("rad")
+    if count % plane or count <= plane or plane < 2 * blocks:
+        return [passed_along(head, "azi", k) for k in range(1, blocks + 1)]
+    near = []
+    for k in range(1, blocks + 1):
+        pairs = [
+            (a, (a + k) % count)
+            for a in range(count)
+            if a // plane == ((a + k) % count) // plane
+        ]
+        near.append(lax.ppermute(head, "azi", pairs))
+    first, second = crossing_relays(groups, count, plane, blocks)
+    relayed = lax.ppermute(head, ("rad", "azi"), first)
+    position = lax.axis_index("azi") % plane
+    pieces = []
+    for k in range(1, blocks + 1):
+        far = lax.ppermute(relayed, ("rad", "azi"), second[k - 1])
+        pieces.append(jnp.where(position < k, far, near[k - 1]))
+    return pieces
+
+
 def local(fields, shifts):
     cells = fields.shape[2]
     rows = fields.shape[3]
@@ -140,8 +182,8 @@
         updated = update(wide, inverse)
         a = w - 1
         head = updated[:, :, :cells]
-        pieces = [passed_along(head, "azi", k) for k in range(blocks, 0, -1)]
-        window = jnp.concatenate(pieces + [updated], axis=2)
+        pieces = rotation_pieces(head, PLANE, blocks)
+        window = jnp.concatenate(pieces[::-1] + [updated], axis=2)
         window = window[:, :, blocks * cells - SMAX :]
         wide_shifts = wide_shifts[:, 1:-1]
         wide = rotate_window(window, wide_shifts[step], cells + 2 * a)

time: 241 us -> 190 us (0.79)
  the two profiles are of different devices: /device:TPU:198 before, /device:TPU:6 now
where the time goes in v2:
time: 190 us; the launch traced here: 189 us
  starting transfers between devices  108 us (57%)
  waiting for transfers between devices  66.8 us (35%)
  other arithmetic  10.1 us (5%)
  local copies, waits for them, and re-layouts  3.57 us (2%)
    ppermute x9, starting transfers between devices, rotation_pieces(): far = lax.ppermute(relayed, ('rad', 'azi'), second[k - 1])  63.2 us
    ppermute x9, waiting for transfers between devices, rotation_pieces(): far = lax.ppermute(relayed, ('rad', 'azi'), second[k - 1])  35.4 us
    ppermute x4, starting transfers between devices, passed_along(): return lax.ppermute(value, axis, pairs)  28.5 us
    ppermute x3, waiting for transfers between devices, rotation_pieces(): relayed = lax.ppermute(head, ('rad', 'azi'), first)  27.2 us
    ppermute x9, starting transfers between devices, rotation_pieces(): near.append(lax.ppermute(head, 'azi', pairs))  11.9 us
    ppermute x4, waiting for transfers between devices, passed_along(): return lax.ppermute(value, axis, pairs)  4.09 us
    ppermute x3, starting transfers between devices, rotation_pieces(): relayed = lax.ppermute(head, ('rad', 'azi'), first)  3.88 us
  transfers between devices with their start and end apart: 25, of which 12 were waited for; matrix products, arithmetic and copies ran while one was open for 1% of the time, Pallas kernels for 0%

profile of v2, /device:TPU:6, one launch (start us, length us, event | category | flops | bytes accessed | tf_op | source)
XLA Modules:
  0.0 188.9 jit_solution(18022376340885605386)
XLA Ops:
  0.0 0.8 fusion.103
  0.8 1.9 %collective-permute-start = (f32[5,1,3,128]{3,2,1,0:T(4,128)S(1)}, f32[5,1,3,128]{3,2,1,0:T(4,128)S(1)}, u32[]{:S(2)}, u32[]{:S(2)}) collective-permute-start(f32[5,1,3,128]{3,2,1,0:T(4,128)S(1)} %get-tuple-element.46), channel_id=1, source_target_pairs={{0,1},{1,2},{2,3},{3,4},{4,5},{5,6},{6,7},{7,8},{8,9},{9,10},{10,1... | collective-permute-start | bytes 23048 | tf_op jit(solution)/shard_map/ppermute | solution.py:25
  2.7 22.0 %collective-permute-start.1 = (f32[5,1,3,128]{3,2,1,0:T(4,128)S(1)}, f32[5,1,3,128]{3,2,1,0:T(4,128)S(1)}, u32[]{:S(2)}, u32[]{:S(2)}) collective-permute-start(f32[5,1,3,128]{3,2,1,0:T(4,128)S(1)} %get-tuple-element.47), channel_id=1, source_target_pairs={{0,127},{1,0},{2,1},{3,2},{4,3},{5,4},{6,5},{7,6},{8,7},{9,8},{10,... | collective-permute-start | bytes 23048 | tf_op jit(solution)/shard_map/ppermute | solution.py:25
  24.7 0.8 slice_convert_fusion.1
  26.1 0.9 pad_maximum_fusion
  27.1 0.2 reshape.1273
  27.4 3.4 %collective-permute-start.2 = (f32[1059]{0:T(1024)S(1)}, f32[1059]{0:T(1024)S(1)}, u32[]{:S(2)}, u32[]{:S(2)}) collective-permute-start(f32[1059]{0:T(1024)S(1)} %pad_maximum_fusion.1), channel_id=1, source_target_pairs={{0,128},{128,256},{256,384},{384,512},{512,640},{640,768},{768,896... | collective-permute-start | bytes 12716 | tf_op jit(solution)/shard_map/ppermute | solution.py:25
  30.8 0.2 reshape.1275
  31.1 1.3 collective-permute-start.3
  32.4 0.2 concatenate.40
  32.6 4.0 %collective-permute-done.3 = f32[1059]{0:T(1024)S(1)} collective-permute-done((f32[1059]{0:T(1024)S(1)}, f32[1059]{0:T(1024)S(1)}, u32[]{:S(2)}, u32[]{:S(2)}) %collective-permute-start.3) | collective-permute-done | bytes 4268 | tf_op jit(solution)/shard_map/ppermute | solution.py:25
  36.6 0.2 concatenate.41
  36.8 0.2 maximum_select_fusion
  37.2 0.2 subtract_multiply_fusion.3
  37.3 0.6 subtract_add_fusion.1
  38.0 0.1 fusion.4
  38.2 0.1 fusion.29
  38.6 1.3 collective-permute-start.4
  39.9 1.3 collective-permute-start.10
  41.2 1.3 collective-permute-start.8
  42.5 1.3 collective-permute-start.6
  44.3 11.6 %collective-permute-done.4 = f32[5,1,64,132]{3,2,1,0:T(8,128)} collective-permute-done((f32[5,1,64,132]{3,2,1,0:T(8,128)S(1)}, f32[5,1,64,132]{3,2,1,0:T(8,128)}, u32[]{:S(2)}, u32[]{:S(2)}) %collective-permute-start.4) | collective-permute-done | bytes 168992 | tf_op jit(solution)/shard_map/ppermute | solution.py:157
  55.9 8.1 %collective-permute-start.9 = (f32[5,1,64,132]{3,2,1,0:T(8,128)}, f32[5,1,64,132]{3,2,1,0:T(8,128)S(1)}, u32[]{:S(2)}, u32[]{:S(2)}) collective-permute-start(f32[5,1,64,132]{3,2,1,0:T(8,128)} %collective-permute-done.4), channel_id=1, source_target_pairs={{0,16},{16,32},{32,48},{48,64},{64,80},{80,96},{96,112},{112,0},{1... | collective-permute-start | bytes 506888 | tf_op jit(solution)/shard_map/ppermute | solution.py:161
  64.0 1.9 %collective-permute-start.7 = (f32[5,1,64,132]{3,2,1,0:T(8,128)}, f32[5,1,64,132]{3,2,1,0:T(8,128)S(1)}, u32[]{:S(2)}, u32[]{:S(2)}) collective-permute-start(f32[5,1,64,132]{3,2,1,0:T(8,128)} %collective-permute-done.4), channel_id=1, source_target_pairs={{2,16},{0,17},{18,32},{16,33},{34,48},{32,49},{50,64},{48,65},{66,... | collective-permute-start | bytes 506888 | tf_op jit(solution)/shard_map/ppermute | solution.py:161
  65.9 9.7 %collective-permute-start.5 = (f32[5,1,64,132]{3,2,1,0:T(8,128)}, f32[5,1,64,132]{3,2,1,0:T(8,128)S(1)}, u32[]{:S(2)}, u32[]{:S(2)}) collective-permute-start(f32[5,1,64,132]{3,2,1,0:T(8,128)} %collective-permute-done.4), channel_id=1, source_target_pairs={{5,16},{2,17},{0,18},{21,32},{18,33},{16,34},{37,48},{34,49},{32,5... | collective-permute-start | bytes 506888 | tf_op jit(solution)/shard_map/ppermute | solution.py:161
  75.6 2.0 %collective-permute-done.9 = f32[5,1,64,132]{3,2,1,0:T(8,128)S(1)} collective-permute-done((f32[5,1,64,132]{3,2,1,0:T(8,128)}, f32[5,1,64,132]{3,2,1,0:T(8,128)S(1)}, u32[]{:S(2)}, u32[]{:S(2)}) %collective-permute-start.9) | collective-permute-done | bytes 168992 | tf_op jit(solution)/shard_map/ppermute | solution.py:161
  77.6 7.8 %collective-permute-done.7 = f32[5,1,64,132]{3,2,1,0:T(8,128)S(1)} collective-permute-done((f32[5,1,64,132]{3,2,1,0:T(8,128)}, f32[5,1,64,132]{3,2,1,0:T(8,128)S(1)}, u32[]{:S(2)}, u32[]{:S(2)}) %collective-permute-start.7) | collective-permute-done | bytes 168992 | tf_op jit(solution)/shard_map/ppermute | solution.py:161
  85.5 6.1 %collective-permute-done.5 = f32[5,1,64,132]{3,2,1,0:T(8,128)S(1)} collective-permute-done((f32[5,1,64,132]{3,2,1,0:T(8,128)}, f32[5,1,64,132]{3,2,1,0:T(8,128)S(1)}, u32[]{:S(2)}, u32[]{:S(2)}) %collective-permute-start.5) | collective-permute-done | bytes 168992 | tf_op jit(solution)/shard_map/ppermute | solution.py:161
  91.7 0.7 concatenate.43
  92.4 0.2 slice_select_fusion
  92.6 0.2 slice_select_fusion.5
  92.7 0.2 slice_select_fusion.4
  92.9 0.1 slice_select_fusion.7
  93.6 0.2 subtract_multiply_fusion.1
  93.7 0.6 subtract_add_fusion
  94.4 0.1 fusion.7
  94.6 0.1 fusion.14
  94.9 1.3 collective-permute-start.11
  96.3 1.3 collective-permute-start.17
  97.6 10.4 %collective-permute-done.11 = f32[5,1,64,130]{3,2,1,0:T(8,128)S(1)} collective-permute-done((f32[5,1,64,130]{3,2,1,0:T(8,128)S(1)}, f32[5,1,64,130]{3,2,1,0:T(8,128)S(1)}, u32[]{:S(2)}, u32[]{:S(2)}) %collective-permute-start.11) | collective-permute-done | bytes 166432 | tf_op jit(solution)/shard_map/ppermute | solution.py:157
  108.0 3.3 %collective-permute-start.16 = (f32[5,1,64,130]{3,2,1,0:T(8,128)S(1)}, f32[5,1,64,130]{3,2,1,0:T(8,128)S(1)}, u32[]{:S(2)}, u32[]{:S(2)}) collective-permute-start(f32[5,1,64,130]{3,2,1,0:T(8,128)S(1)} %collective-permute-done.11), channel_id=1, source_target_pairs={{0,16},{16,32},{32,48},{48,64},{64,80},{80,96},{96,112},{112,0},{1... | collective-permute-start | bytes 499208 | tf_op jit(solution)/shard_map/ppermute | solution.py:161
  111.4 1.3 collective-permute-start.15
  112.7 1.3 collective-permute-start.13
  114.0 1.9 %collective-permute-start.14 = (f32[5,1,64,130]{3,2,1,0:T(8,128)S(1)}, f32[5,1,64,130]{3,2,1,0:T(8,128)S(1)}, u32[]{:S(2)}, u32[]{:S(2)}) collective-permute-start(f32[5,1,64,130]{3,2,1,0:T(8,128)S(1)} %collective-permute-done.11), channel_id=1, source_target_pairs={{2,16},{0,17},{18,32},{16,33},{34,48},{32,49},{50,64},{48,65},{66,... | collective-permute-start | bytes 499208 | tf_op jit(solution)/shard_map/ppermute | solution.py:161
  116.0 14.7 %collective-permute-start.12 = (f32[5,1,64,130]{3,2,1,0:T(8,128)S(1)}, f32[5,1,64,130]{3,2,1,0:T(8,128)S(1)}, u32[]{:S(2)}, u32[]{:S(2)}) collective-permute-start(f32[5,1,64,130]{3,2,1,0:T(8,128)S(1)} %collective-permute-done.11), channel_id=1, source_target_pairs={{5,16},{2,17},{0,18},{21,32},{18,33},{16,34},{37,48},{34,49},{32,5... | collective-permute-start | bytes 499208 | tf_op jit(solution)/shard_map/ppermute | solution.py:161
  130.8 4.9 %collective-permute-done.14 = f32[5,1,64,130]{3,2,1,0:T(8,128)S(1)} collective-permute-done((f32[5,1,64,130]{3,2,1,0:T(8,128)S(1)}, f32[5,1,64,130]{3,2,1,0:T(8,128)S(1)}, u32[]{:S(2)}, u32[]{:S(2)}) %collective-permute-start.14) | collective-permute-done | bytes 166432 | tf_op jit(solution)/shard_map/ppermute | solution.py:161
  135.7 5.5 %collective-permute-done.12 = f32[5,1,64,130]{3,2,1,0:T(8,128)S(1)} collective-permute-done((f32[5,1,64,130]{3,2,1,0:T(8,128)S(1)}, f32[5,1,64,130]{3,2,1,0:T(8,128)S(1)}, u32[]{:S(2)}, u32[]{:S(2)}) %collective-permute-start.12) | collective-permute-done | bytes 166432 | tf_op jit(solution)/shard_map/ppermute | solution.py:161
  141.3 0.7 concatenate.44
  142.1 0.2 slice_select_fusion.3
  142.2 0.2 slice_select_fusion.2
  142.4 0.2 slice_select_fusion.1
  142.6 0.1 slice_select_fusion.6
  143.3 0.3 subtract_add_fusion.2
  144.1 1.3 collective-permute-start.18
  145.4 1.3 collective-permute-start.20
  146.7 5.2 %collective-permute-done.18 = f32[5,1,64,128]{3,2,1,0:T(8,128)S(1)} collective-permute-done((f32[5,1,64,128]{3,2,1,0:T(8,128)S(1)}, f32[5,1,64,128]{3,2,1,0:T(8,128)S(1)}, u32[]{:S(2)}, u32[]{:S(2)}) %collective-permute-start.18) | collective-permute-done | bytes 163872 | tf_op jit(solution)/shard_map/ppermute | solution.py:157
  151.9 12.1 %collective-permute-start.19 = (f32[5,1,64,128]{3,2,1,0:T(8,128)S(1)}, f32[5,1,64,128]{3,2,1,0:T(8,128)S(1)}, u32[]{:S(2)}, u32[]{:S(2)}) collective-permute-start(f32[5,1,64,128]{3,2,1,0:T(8,128)S(1)} %collective-permute-done.18), channel_id=1, source_target_pairs={{5,16},{2,17},{0,18},{21,32},{18,33},{16,34},{37,48},{34,49},{32,5... | collective-permute-start | bytes 491528 | tf_op jit(solution)/shard_map/ppermute | solution.py:161
  164.1 1.5 collective-permute-start.22
  165.6 1.3 collective-permute-start.24
  166.9 3.3 %collective-permute-start.21 = (f32[5,1,64,128]{3,2,1,0:T(8,128)S(1)}, f32[5,1,64,128]{3,2,1,0:T(8,128)S(1)}, u32[]{:S(2)}, u32[]{:S(2)}) collective-permute-start(f32[5,1,64,128]{3,2,1,0:T(8,128)S(1)} %collective-permute-done.18), channel_id=1, source_target_pairs={{2,16},{0,17},{18,32},{16,33},{34,48},{32,49},{50,64},{48,65},{66,... | collective-permute-start | bytes 491528 | tf_op jit(solution)/shard_map/ppermute | solution.py:161
  170.2 8.2 %collective-permute-start.23 = (f32[5,1,64,128]{3,2,1,0:T(8,128)S(1)}, f32[5,1,64,128]{3,2,1,0:T(8,128)S(1)}, u32[]{:S(2)}, u32[]{:S(2)}) collective-permute-start(f32[5,1,64,128]{3,2,1,0:T(8,128)S(1)} %collective-permute-done.18), channel_id=1, source_target_pairs={{0,16},{16,32},{32,48},{48,64},{64,80},{80,96},{96,112},{112,0},{1... | collective-permute-start | bytes 491528 | tf_op jit(solution)/shard_map/ppermute | solution.py:161
  178.4 7.4 %collective-permute-done.21 = f32[5,1,64,128]{3,2,1,0:T(8,128)S(1)} collective-permute-done((f32[5,1,64,128]{3,2,1,0:T(8,128)S(1)}, f32[5,1,64,128]{3,2,1,0:T(8,128)S(1)}, u32[]{:S(2)}, u32[]{:S(2)}) %collective-permute-start.21) | collective-permute-done | bytes 163872 | tf_op jit(solution)/shard_map/ppermute | solution.py:161
  185.8 1.7 collective-permute-done.23
  188.2 0.7 slice_select_fusion.23
  (93 shorter events, 4.6 us)
Async XLA Ops:
  0.0 36.8 %copy-start = (f32[5,1,64,128]{3,2,1,0:T(8,128)S(1)}, f32[5,1,64,128]{3,2,1,0:T(8,128)}, u32[]{:S(2)}) copy-start(f32[5,1,64,128]{3,2,1,0:T(8,128)} %param.2) | copy-start | bytes 491524
  0.8 25.2 %collective-permute-start = (f32[5,1,3,128]{3,2,1,0:T(4,128)S(1)}, f32[5,1,3,128]{3,2,1,0:T(4,128)S(1)}, u32[]{:S(2)}, u32[]{:S(2)}) collective-permute-start(f32[5,1,3,128]{3,2,1,0:T(4,128)S(1)} %get-tuple-element.46), channel_id=1, source_target_pairs={{0,1},{1,2},{2,3},{3,4},{4,5},{5,6},{6,7},{7,8},{8,9},{9,10},{10,1... | collective-permute-start | bytes 23048 | tf_op jit(solution)/shard_map/ppermute | solution.py:25
  2.7 23.3 %collective-permute-start.1 = (f32[5,1,3,128]{3,2,1,0:T(4,128)S(1)}, f32[5,1,3,128]{3,2,1,0:T(4,128)S(1)}, u32[]{:S(2)}, u32[]{:S(2)}) collective-permute-start(f32[5,1,3,128]{3,2,1,0:T(4,128)S(1)} %get-tuple-element.47), channel_id=1, source_target_pairs={{0,127},{1,0},{2,1},{3,2},{4,3},{5,4},{6,5},{7,6},{8,7},{9,8},{10,... | collective-permute-start | bytes 23048 | tf_op jit(solution)/shard_map/ppermute | solution.py:25
  27.4 5.0 %collective-permute-start.2 = (f32[1059]{0:T(1024)S(1)}, f32[1059]{0:T(1024)S(1)}, u32[]{:S(2)}, u32[]{:S(2)}) collective-permute-start(f32[1059]{0:T(1024)S(1)} %pad_maximum_fusion.1), channel_id=1, source_target_pairs={{0,128},{128,256},{256,384},{384,512},{512,640},{640,768},{768,896... | collective-permute-start | bytes 12716 | tf_op jit(solution)/shard_map/ppermute | solution.py:25
  31.1 5.5 %collective-permute-start.3 = (f32[1059]{0:T(1024)S(1)}, f32[1059]{0:T(1024)S(1)}, u32[]{:S(2)}, u32[]{:S(2)}) collective-permute-start(f32[1059]{0:T(1024)S(1)} %pad_maximum_fusion.2), channel_id=1, source_target_pairs={{128,0},{256,128},{384,256},{512,384},{640,512},{768,640},{896,768... | collective-permute-start | bytes 12716 | tf_op jit(solution)/shard_map/ppermute | solution.py:25
  37.9 6.2 %copy-start.1 = (s32[3,128]{1,0:T(4,128)S(1)}, s32[3,128]{1,0:T(4,128)}, u32[]{:S(2)}) copy-start(s32[3,128]{1,0:T(4,128)} %param.3) | copy-start | bytes 4612
  38.6 17.3 %collective-permute-start.4 = (f32[5,1,64,132]{3,2,1,0:T(8,128)S(1)}, f32[5,1,64,132]{3,2,1,0:T(8,128)}, u32[]{:S(2)}, u32[]{:S(2)}) collective-permute-start(f32[5,1,64,132]{3,2,1,0:T(8,128)S(1)} %slice.635), channel_id=1, source_target_pairs={{15,0},{14,2},{13,5},{31,16},{30,18},{29,21},{47,32},{46,34},{45,3... | collective-permute-start | bytes 506888 | tf_op jit(solution)/shard_map/ppermute | solution.py:157
  39.9 26.0 %collective-permute-start.10 = (f32[5,1,64,132]{3,2,1,0:T(8,128)S(1)}, f32[5,1,64,132]{3,2,1,0:T(8,128)S(1)}, u32[]{:S(2)}, u32[]{:S(2)}) collective-permute-start(f32[5,1,64,132]{3,2,1,0:T(8,128)S(1)} %slice.635), channel_id=1, source_target_pairs={{0,1},{1,2},{2,3},{3,4},{4,5},{5,6},{6,7},{7,8},{8,9},{9,10},{10,1... | collective-permute-start | bytes 506888 | tf_op jit(solution)/shard_map/ppermute | solution.py:155
  41.2 36.4 %collective-permute-start.8 = (f32[5,1,64,132]{3,2,1,0:T(8,128)S(1)}, f32[5,1,64,132]{3,2,1,0:T(8,128)S(1)}, u32[]{:S(2)}, u32[]{:S(2)}) collective-permute-start(f32[5,1,64,132]{3,2,1,0:T(8,128)S(1)} %slice.635), channel_id=1, source_target_pairs={{0,2},{1,3},{2,4},{3,5},{4,6},{5,7},{6,8},{7,9},{8,10},{9,11},{10,... | collective-permute-start | bytes 506888 | tf_op jit(solution)/shard_map/ppermute | solution.py:155
  42.5 43.0 %collective-permute-start.6 = (f32[5,1,64,132]{3,2,1,0:T(8,128)S(1)}, f32[5,1,64,132]{3,2,1,0:T(8,128)S(1)}, u32[]{:S(2)}, u32[]{:S(2)}) collective-permute-start(f32[5,1,64,132]{3,2,1,0:T(8,128)S(1)} %slice.635), channel_id=1, source_target_pairs={{0,3},{1,4},{2,5},{3,6},{4,7},{5,8},{6,9},{7,10},{8,11},{9,12},{10... | collective-permute-start | bytes 506888 | tf_op jit(solution)/shard_map/ppermute | solution.py:155
  55.9 21.7 %collective-permute-start.9 = (f32[5,1,64,132]{3,2,1,0:T(8,128)}, f32[5,1,64,132]{3,2,1,0:T(8,128)S(1)}, u32[]{:S(2)}, u32[]{:S(2)}) collective-permute-start(f32[5,1,64,132]{3,2,1,0:T(8,128)} %collective-permute-done.4), channel_id=1, source_target_pairs={{0,16},{16,32},{32,48},{48,64},{64,80},{80,96},{96,112},{112,0},{1... | collective-permute-start | bytes 506888 | tf_op jit(solution)/shard_map/ppermute | solution.py:161
  64.0 21.5 %collective-permute-start.7 = (f32[5,1,64,132]{3,2,1,0:T(8,128)}, f32[5,1,64,132]{3,2,1,0:T(8,128)S(1)}, u32[]{:S(2)}, u32[]{:S(2)}) collective-permute-start(f32[5,1,64,132]{3,2,1,0:T(8,128)} %collective-permute-done.4), channel_id=1, source_target_pairs={{2,16},{0,17},{18,32},{16,33},{34,48},{32,49},{50,64},{48,65},{66,... | collective-permute-start | bytes 506888 | tf_op jit(solution)/shard_map/ppermute | solution.py:161
  65.9 25.7 %collective-permute-start.5 = (f32[5,1,64,132]{3,2,1,0:T(8,128)}, f32[5,1,64,132]{3,2,1,0:T(8,128)S(1)}, u32[]{:S(2)}, u32[]{:S(2)}) collective-permute-start(f32[5,1,64,132]{3,2,1,0:T(8,128)} %collective-permute-done.4), channel_id=1, source_target_pairs={{5,16},{2,17},{0,18},{21,32},{18,33},{16,34},{37,48},{34,49},{32,5... | collective-permute-start | bytes 506888 | tf_op jit(solution)/shard_map/ppermute | solution.py:161
  94.9 13.1 %collective-permute-start.11 = (f32[5,1,64,130]{3,2,1,0:T(8,128)S(1)}, f32[5,1,64,130]{3,2,1,0:T(8,128)S(1)}, u32[]{:S(2)}, u32[]{:S(2)}) collective-permute-start(f32[5,1,64,130]{3,2,1,0:T(8,128)S(1)} %slice.677), channel_id=1, source_target_pairs={{15,0},{14,2},{13,5},{31,16},{30,18},{29,21},{47,32},{46,34},{45,3... | collective-permute-start | bytes 499208 | tf_op jit(solution)/shard_map/ppermute | solution.py:157
  96.3 19.7 %collective-permute-start.17 = (f32[5,1,64,130]{3,2,1,0:T(8,128)S(1)}, f32[5,1,64,130]{3,2,1,0:T(8,128)S(1)}, u32[]{:S(2)}, u32[]{:S(2)}) collective-permute-start(f32[5,1,64,130]{3,2,1,0:T(8,128)S(1)} %slice.677), channel_id=1, source_target_pairs={{0,1},{1,2},{2,3},{3,4},{4,5},{5,6},{6,7},{7,8},{8,9},{9,10},{10,1... | collective-permute-start | bytes 499208 | tf_op jit(solution)/shard_map/ppermute | solution.py:155
  108.0 22.7 %collective-permute-start.16 = (f32[5,1,64,130]{3,2,1,0:T(8,128)S(1)}, f32[5,1,64,130]{3,2,1,0:T(8,128)S(1)}, u32[]{:S(2)}, u32[]{:S(2)}) collective-permute-start(f32[5,1,64,130]{3,2,1,0:T(8,128)S(1)} %collective-permute-done.11), channel_id=1, source_target_pairs={{0,16},{16,32},{32,48},{48,64},{64,80},{80,96},{96,112},{112,0},{1... | collective-permute-start | bytes 499208 | tf_op jit(solution)/shard_map/ppermute | solution.py:161
  111.4 19.4 %collective-permute-start.15 = (f32[5,1,64,130]{3,2,1,0:T(8,128)S(1)}, f32[5,1,64,130]{3,2,1,0:T(8,128)S(1)}, u32[]{:S(2)}, u32[]{:S(2)}) collective-permute-start(f32[5,1,64,130]{3,2,1,0:T(8,128)S(1)} %slice.677), channel_id=1, source_target_pairs={{0,2},{1,3},{2,4},{3,5},{4,6},{5,7},{6,8},{7,9},{8,10},{9,11},{10,... | collective-permute-start | bytes 499208 | tf_op jit(solution)/shard_map/ppermute | solution.py:155
  112.7 23.0 %collective-permute-start.13 = (f32[5,1,64,130]{3,2,1,0:T(8,128)S(1)}, f32[5,1,64,130]{3,2,1,0:T(8,128)S(1)}, u32[]{:S(2)}, u32[]{:S(2)}) collective-permute-start(f32[5,1,64,130]{3,2,1,0:T(8,128)S(1)} %slice.677), channel_id=1, source_target_pairs={{0,3},{1,4},{2,5},{3,6},{4,7},{5,8},{6,9},{7,10},{8,11},{9,12},{10... | collective-permute-start | bytes 499208 | tf_op jit(solution)/shard_map/ppermute | solution.py:155
  114.0 21.6 %collective-permute-start.14 = (f32[5,1,64,130]{3,2,1,0:T(8,128)S(1)}, f32[5,1,64,130]{3,2,1,0:T(8,128)S(1)}, u32[]{:S(2)}, u32[]{:S(2)}) collective-permute-start(f32[5,1,64,130]{3,2,1,0:T(8,128)S(1)} %collective-permute-done.11), channel_id=1, source_target_pairs={{2,16},{0,17},{18,32},{16,33},{34,48},{32,49},{50,64},{48,65},{66,... | collective-permute-start | bytes 499208 | tf_op jit(solution)/shard_map/ppermute | solution.py:161
  116.0 25.3 %collective-permute-start.12 = (f32[5,1,64,130]{3,2,1,0:T(8,128)S(1)}, f32[5,1,64,130]{3,2,1,0:T(8,128)S(1)}, u32[]{:S(2)}, u32[]{:S(2)}) collective-permute-start(f32[5,1,64,130]{3,2,1,0:T(8,128)S(1)} %collective-permute-done.11), channel_id=1, source_target_pairs={{5,16},{2,17},{0,18},{21,32},{18,33},{16,34},{37,48},{34,49},{32,5... | collective-permute-start | bytes 499208 | tf_op jit(solution)/shard_map/ppermute | solution.py:161
  144.1 7.8 %collective-permute-start.18 = (f32[5,1,64,128]{3,2,1,0:T(8,128)S(1)}, f32[5,1,64,128]{3,2,1,0:T(8,128)S(1)}, u32[]{:S(2)}, u32[]{:S(2)}) collective-permute-start(f32[5,1,64,128]{3,2,1,0:T(8,128)S(1)} %get-tuple-element.5), channel_id=1, source_target_pairs={{15,0},{14,2},{13,5},{31,16},{30,18},{29,21},{47,32},{46,34},{45,3... | collective-permute-start | bytes 491528 | tf_op jit(solution)/shard_map/ppermute | solution.py:157
  145.4 24.8 %collective-permute-start.20 = (f32[5,1,64,128]{3,2,1,0:T(8,128)S(1)}, f32[5,1,64,128]{3,2,1,0:T(8,128)S(1)}, u32[]{:S(2)}, u32[]{:S(2)}) collective-permute-start(f32[5,1,64,128]{3,2,1,0:T(8,128)S(1)} %get-tuple-element.5), channel_id=1, source_target_pairs={{0,3},{1,4},{2,5},{3,6},{4,7},{5,8},{6,9},{7,10},{8,11},{9,12},{10... | collective-permute-start | bytes 491528 | tf_op jit(solution)/shard_map/ppermute | solution.py:155
  151.9 26.4 %collective-permute-start.19 = (f32[5,1,64,128]{3,2,1,0:T(8,128)S(1)}, f32[5,1,64,128]{3,2,1,0:T(8,128)S(1)}, u32[]{:S(2)}, u32[]{:S(2)}) collective-permute-start(f32[5,1,64,128]{3,2,1,0:T(8,128)S(1)} %collective-permute-done.18), channel_id=1, source_target_pairs={{5,16},{2,17},{0,18},{21,32},{18,33},{16,34},{37,48},{34,49},{32,5... | collective-permute-start | bytes 491528 | tf_op jit(solution)/shard_map/ppermute | solution.py:161
  164.1 14.3 %collective-permute-start.22 = (f32[5,1,64,128]{3,2,1,0:T(8,128)S(1)}, f32[5,1,64,128]{3,2,1,0:T(8,128)S(1)}, u32[]{:S(2)}, u32[]{:S(2)}) collective-permute-start(f32[5,1,64,128]{3,2,1,0:T(8,128)S(1)} %get-tuple-element.5), channel_id=1, source_target_pairs={{0,2},{1,3},{2,4},{3,5},{4,6},{5,7},{6,8},{7,9},{8,10},{9,11},{10,... | collective-permute-start | bytes 491528 | tf_op jit(solution)/shard_map/ppermute | solution.py:155
  165.6 20.3 %collective-permute-start.24 = (f32[5,1,64,128]{3,2,1,0:T(8,128)S(1)}, f32[5,1,64,128]{3,2,1,0:T(8,128)S(1)}, u32[]{:S(2)}, u32[]{:S(2)}) collective-permute-start(f32[5,1,64,128]{3,2,1,0:T(8,128)S(1)} %get-tuple-element.5), channel_id=1, source_target_pairs={{0,1},{1,2},{2,3},{3,4},{4,5},{5,6},{6,7},{7,8},{8,9},{9,10},{10,1... | collective-permute-start | bytes 491528 | tf_op jit(solution)/shard_map/ppermute | solution.py:155
  166.9 18.9 %collective-permute-start.21 = (f32[5,1,64,128]{3,2,1,0:T(8,128)S(1)}, f32[5,1,64,128]{3,2,1,0:T(8,128)S(1)}, u32[]{:S(2)}, u32[]{:S(2)}) collective-permute-start(f32[5,1,64,128]{3,2,1,0:T(8,128)S(1)} %collective-permute-done.18), channel_id=1, source_target_pairs={{2,16},{0,17},{18,32},{16,33},{34,48},{32,49},{50,64},{48,65},{66,... | collective-permute-start | bytes 491528 | tf_op jit(solution)/shard_map/ppermute | solution.py:161
  170.2 17.4 %collective-permute-start.23 = (f32[5,1,64,128]{3,2,1,0:T(8,128)S(1)}, f32[5,1,64,128]{3,2,1,0:T(8,128)S(1)}, u32[]{:S(2)}, u32[]{:S(2)}) collective-permute-start(f32[5,1,64,128]{3,2,1,0:T(8,128)S(1)} %collective-permute-done.18), channel_id=1, source_target_pairs={{0,16},{16,32},{32,48},{48,64},{64,80},{80,96},{96,112},{112,0},{1... | collective-permute-start | bytes 491528 | tf_op jit(solution)/shard_map/ppermute | solution.py:161

commit v3 on v2

--- a/solution.py
+++ b/solution.py
@@ -122,6 +122,14 @@
     return window[:, :, :out_len]
 
 
+def relay_seat(lane, source, plane, blocks):
+    if source // 2 == lane:
+        return source
+    if 2 * lane + 1 < plane - blocks and 2 * lane < blocks:
+        return 2 * lane + 1
+    return 2 * lane
+
+
 def crossing_relays(groups, count, plane, blocks):
     half = plane // 2
     first, second = [], [[] for _ in range(blocks)]
@@ -132,7 +140,7 @@
             relay = {}
             for j in range(1, blocks + 1):
                 lane = (3 * g + j - 1) % half
-                relay[j] = base + 2 * lane + (j - 1) // 2
+                relay[j] = base + relay_seat(lane, plane - j, plane, blocks)
                 first.append((g * count + base + plane - j, g * count + relay[j]))
             for k in range(1, blocks + 1):
                 for i in range(k):
@@ -155,6 +163,8 @@
         near.append(lax.ppermute(head, "azi", pairs))
     first, second = crossing_relays(groups, count, plane, blocks)
     relayed = lax.ppermute(head, ("rad", "azi"), first)
+    near_and_relayed = lax.optimization_barrier((near, relayed))
+    near, relayed = near_and_relayed
     position = lax.axis_index("azi") % plane
     pieces = []
     for k in range(1, blocks + 1):

time: 190 us -> 208 us (1.095)
  the two profiles are of different devices: /device:TPU:6 before, /device:TPU:128 now
where the time goes in v3:
time: 208 us; the launch traced here: 207 us
  waiting for transfers between devices  112 us (54%)
  starting transfers between devices  81.2 us (39%)
  other arithmetic  10.1 us (5%)
  local copies, waits for them, and re-layouts  3.57 us (2%)
    ppermute x9, waiting for transfers between devices, rotation_pieces(): far = lax.ppermute(relayed, ('rad', 'azi'), second[k - 1])  84.8 us
    ppermute x9, starting transfers between devices, rotation_pieces(): near.append(lax.ppermute(head, 'azi', pairs))  37.7 us
    ppermute x4, starting transfers between devices, passed_along(): return lax.ppermute(value, axis, pairs)  29.8 us
    ppermute x9, waiting for transfers between devices, rotation_pieces(): near.append(lax.ppermute(head, 'azi', pairs))  24 us
    ppermute x9, starting transfers between devices, rotation_pieces(): far = lax.ppermute(relayed, ('rad', 'azi'), second[k - 1])  11.6 us
  transfers between devices with their start and end apart: 25, of which 15 were waited for; matrix products, arithmetic and copies ran while one was open for 1% of the time, Pallas kernels for 0%

profile of v3, /device:TPU:128, one launch (start us, length us, event | category | flops | bytes accessed | tf_op | source)
XLA Modules:
  0.0 207.5 jit_solution(10505452690578080217)
XLA Ops:
  0.0 0.8 fusion.103
  0.8 1.9 collective-permute-start
  2.7 22.1 %collective-permute-start.1 = (f32[5,1,3,128]{3,2,1,0:T(4,128)S(1)}, f32[5,1,3,128]{3,2,1,0:T(4,128)S(1)}, u32[]{:S(2)}, u32[]{:S(2)}) collective-permute-start(f32[5,1,3,128]{3,2,1,0:T(4,128)S(1)} %get-tuple-element.71), channel_id=1, source_target_pairs={{0,127},{1,0},{2,1},{3,2},{4,3},{5,4},{6,5},{7,6},{8,7},{9,8},{10,... | collective-permute-start | bytes 23048 | tf_op jit(solution)/shard_map/ppermute | solution.py:25
  24.8 0.8 slice_convert_fusion.1
  26.2 0.9 pad_maximum_fusion
  27.3 0.2 reshape.1273
  27.5 3.4 %collective-permute-start.2 = (f32[1059]{0:T(1024)S(1)}, f32[1059]{0:T(1024)S(1)}, u32[]{:S(2)}, u32[]{:S(2)}) collective-permute-start(f32[1059]{0:T(1024)S(1)} %pad_maximum_fusion.1), channel_id=1, source_target_pairs={{0,128},{128,256},{256,384},{384,512},{512,640},{640,768},{768,896... | collective-permute-start | bytes 12716 | tf_op jit(solution)/shard_map/ppermute | solution.py:25
  30.9 0.2 reshape.1275
  31.2 2.5 %collective-permute-start.3 = (f32[1059]{0:T(1024)S(1)}, f32[1059]{0:T(1024)S(1)}, u32[]{:S(2)}, u32[]{:S(2)}) collective-permute-start(f32[1059]{0:T(1024)S(1)} %pad_maximum_fusion.2), channel_id=1, source_target_pairs={{128,0},{256,128},{384,256},{512,384},{640,512},{768,640},{896,768... | collective-permute-start | bytes 12716 | tf_op jit(solution)/shard_map/ppermute | solution.py:25
  33.7 0.2 concatenate.40
  33.9 2.8 %collective-permute-done.3 = f32[1059]{0:T(1024)S(1)} collective-permute-done((f32[1059]{0:T(1024)S(1)}, f32[1059]{0:T(1024)S(1)}, u32[]{:S(2)}, u32[]{:S(2)}) %collective-permute-start.3) | collective-permute-done | bytes 4268 | tf_op jit(solution)/shard_map/ppermute | solution.py:25
  36.7 0.2 concatenate.41
  36.9 0.2 maximum_select_fusion
  37.3 0.2 subtract_multiply_fusion.3
  37.5 0.6 subtract_add_fusion.1
  38.7 1.3 collective-permute-start.4
  40.0 1.3 collective-permute-start.5
  41.3 1.3 collective-permute-start.6
  42.6 0.7 collective-permute-start.7
  43.8 2.0 collective-permute-done.5
  45.9 3.5 %collective-permute-done.6 = f32[5,1,64,132]{3,2,1,0:T(8,128)S(1)} collective-permute-done((f32[5,1,64,132]{3,2,1,0:T(8,128)S(1)}, f32[5,1,64,132]{3,2,1,0:T(8,128)S(1)}, u32[]{:S(2)}, u32[]{:S(2)}) %collective-permute-start.6) | collective-permute-done | bytes 168992 | tf_op jit(solution)/shard_map/ppermute | solution.py:163
  49.4 1.3 collective-permute-start.10
  50.7 1.3 collective-permute-start.9
  52.0 1.3 collective-permute-start.8
  53.3 30.8 %collective-permute-done.10 = f32[5,1,64,132]{3,2,1,0:T(8,128)S(1)} collective-permute-done((f32[5,1,64,132]{3,2,1,0:T(8,128)S(1)}, f32[5,1,64,132]{3,2,1,0:T(8,128)S(1)}, u32[]{:S(2)}, u32[]{:S(2)}) %collective-permute-start.10) | collective-permute-done | bytes 168992 | tf_op jit(solution)/shard_map/ppermute | solution.py:171
  84.3 4.3 %collective-permute-done.8 = f32[5,1,64,132]{3,2,1,0:T(8,128)S(1)} collective-permute-done((f32[5,1,64,132]{3,2,1,0:T(8,128)S(1)}, f32[5,1,64,132]{3,2,1,0:T(8,128)S(1)}, u32[]{:S(2)}, u32[]{:S(2)}) %collective-permute-start.8) | collective-permute-done | bytes 168992 | tf_op jit(solution)/shard_map/ppermute | solution.py:171
  88.7 0.7 concatenate.43
  89.4 0.2 slice_select_fusion
  89.6 0.2 slice_select_fusion.5
  89.7 0.2 slice_select_fusion.4
  89.9 0.1 slice_select_fusion.7
  90.6 0.2 subtract_multiply_fusion.1
  90.7 0.6 subtract_add_fusion
  91.6 0.1 fusion.14
  91.9 9.1 %collective-permute-start.11 = (f32[5,1,64,130]{3,2,1,0:T(8,128)S(1)}, f32[5,1,64,130]{3,2,1,0:T(8,128)S(1)}, u32[]{:S(2)}, u32[]{:S(2)}) collective-permute-start(f32[5,1,64,130]{3,2,1,0:T(8,128)S(1)} %slice.677), channel_id=1, source_target_pairs={{0,1},{1,2},{2,3},{3,4},{4,5},{5,6},{6,7},{7,8},{8,9},{9,10},{10,1... | collective-permute-start | bytes 499208 | tf_op jit(solution)/shard_map/ppermute | solution.py:163
  101.1 6.7 %collective-permute-start.12 = (f32[5,1,64,130]{3,2,1,0:T(8,128)S(1)}, f32[5,1,64,130]{3,2,1,0:T(8,128)S(1)}, u32[]{:S(2)}, u32[]{:S(2)}) collective-permute-start(f32[5,1,64,130]{3,2,1,0:T(8,128)S(1)} %slice.677), channel_id=1, source_target_pairs={{0,2},{1,3},{2,4},{3,5},{4,6},{5,7},{6,8},{7,9},{8,10},{9,11},{10,... | collective-permute-start | bytes 499208 | tf_op jit(solution)/shard_map/ppermute | solution.py:163
  107.8 1.3 collective-permute-start.13
  109.1 0.7 collective-permute-start.14
  109.9 6.1 %collective-permute-done.12 = f32[5,1,64,130]{3,2,1,0:T(8,128)S(1)} collective-permute-done((f32[5,1,64,130]{3,2,1,0:T(8,128)S(1)}, f32[5,1,64,130]{3,2,1,0:T(8,128)S(1)}, u32[]{:S(2)}, u32[]{:S(2)}) %collective-permute-start.12) | collective-permute-done | bytes 166432 | tf_op jit(solution)/shard_map/ppermute | solution.py:163
  116.0 7.0 %collective-permute-done.13 = f32[5,1,64,130]{3,2,1,0:T(8,128)S(1)} collective-permute-done((f32[5,1,64,130]{3,2,1,0:T(8,128)S(1)}, f32[5,1,64,130]{3,2,1,0:T(8,128)S(1)}, u32[]{:S(2)}, u32[]{:S(2)}) %collective-permute-start.13) | collective-permute-done | bytes 166432 | tf_op jit(solution)/shard_map/ppermute | solution.py:163
  123.0 1.3 collective-permute-start.17
  124.3 1.3 collective-permute-start.16
  125.6 1.3 collective-permute-start.15
  126.9 24.7 %collective-permute-done.17 = f32[5,1,64,130]{3,2,1,0:T(8,128)S(1)} collective-permute-done((f32[5,1,64,130]{3,2,1,0:T(8,128)S(1)}, f32[5,1,64,130]{3,2,1,0:T(8,128)S(1)}, u32[]{:S(2)}, u32[]{:S(2)}) %collective-permute-start.17) | collective-permute-done | bytes 166432 | tf_op jit(solution)/shard_map/ppermute | solution.py:171
  151.6 0.8 collective-permute-done.16
  152.5 0.7 concatenate.44
  153.3 0.2 slice_select_fusion.3
  153.4 0.2 slice_select_fusion.2
  153.6 0.2 slice_select_fusion.1
  153.8 0.1 slice_select_fusion.6
  154.5 0.3 subtract_add_fusion.2
  155.3 8.6 %collective-permute-start.18 = (f32[5,1,64,128]{3,2,1,0:T(8,128)S(1)}, f32[5,1,64,128]{3,2,1,0:T(8,128)S(1)}, u32[]{:S(2)}, u32[]{:S(2)}) collective-permute-start(f32[5,1,64,128]{3,2,1,0:T(8,128)S(1)} %get-tuple-element.29), channel_id=1, source_target_pairs={{0,1},{1,2},{2,3},{3,4},{4,5},{5,6},{6,7},{7,8},{8,9},{9,10},{10,1... | collective-permute-start | bytes 491528 | tf_op jit(solution)/shard_map/ppermute | solution.py:163
  163.9 6.7 %collective-permute-start.19 = (f32[5,1,64,128]{3,2,1,0:T(8,128)S(1)}, f32[5,1,64,128]{3,2,1,0:T(8,128)S(1)}, u32[]{:S(2)}, u32[]{:S(2)}) collective-permute-start(f32[5,1,64,128]{3,2,1,0:T(8,128)S(1)} %get-tuple-element.29), channel_id=1, source_target_pairs={{0,2},{1,3},{2,4},{3,5},{4,6},{5,7},{6,8},{7,9},{8,10},{9,11},{10,... | collective-permute-start | bytes 491528 | tf_op jit(solution)/shard_map/ppermute | solution.py:163
  170.6 1.3 collective-permute-start.20
  171.9 0.7 collective-permute-start.21
  172.6 2.6 %collective-permute-done.19 = f32[5,1,64,128]{3,2,1,0:T(8,128)S(1)} collective-permute-done((f32[5,1,64,128]{3,2,1,0:T(8,128)S(1)}, f32[5,1,64,128]{3,2,1,0:T(8,128)S(1)}, u32[]{:S(2)}, u32[]{:S(2)}) %collective-permute-start.19) | collective-permute-done | bytes 163872 | tf_op jit(solution)/shard_map/ppermute | solution.py:163
  175.2 2.7 %collective-permute-done.20 = f32[5,1,64,128]{3,2,1,0:T(8,128)S(1)} collective-permute-done((f32[5,1,64,128]{3,2,1,0:T(8,128)S(1)}, f32[5,1,64,128]{3,2,1,0:T(8,128)S(1)}, u32[]{:S(2)}, u32[]{:S(2)}) %collective-permute-start.20) | collective-permute-done | bytes 163872 | tf_op jit(solution)/shard_map/ppermute | solution.py:163
  177.9 1.3 collective-permute-start.22
  179.3 1.3 collective-permute-start.23
  180.6 1.3 collective-permute-start.24
  181.9 18.5 %collective-permute-done.22 = f32[5,1,64,128]{3,2,1,0:T(8,128)S(1)} collective-permute-done((f32[5,1,64,128]{3,2,1,0:T(8,128)S(1)}, f32[5,1,64,128]{3,2,1,0:T(8,128)S(1)}, u32[]{:S(2)}, u32[]{:S(2)}) %collective-permute-start.22) | collective-permute-done | bytes 163872 | tf_op jit(solution)/shard_map/ppermute | solution.py:171
  200.3 3.2 %collective-permute-done.23 = f32[5,1,64,128]{3,2,1,0:T(8,128)S(1)} collective-permute-done((f32[5,1,64,128]{3,2,1,0:T(8,128)S(1)}, f32[5,1,64,128]{3,2,1,0:T(8,128)S(1)}, u32[]{:S(2)}, u32[]{:S(2)}) %collective-permute-start.23) | collective-permute-done | bytes 163872 | tf_op jit(solution)/shard_map/ppermute | solution.py:171
  203.5 2.6 %collective-permute-done.24 = f32[5,1,64,128]{3,2,1,0:T(8,128)S(1)} collective-permute-done((f32[5,1,64,128]{3,2,1,0:T(8,128)S(1)}, f32[5,1,64,128]{3,2,1,0:T(8,128)S(1)}, u32[]{:S(2)}, u32[]{:S(2)}) %collective-permute-start.24) | collective-permute-done | bytes 163872 | tf_op jit(solution)/shard_map/ppermute | solution.py:171
  206.8 0.7 slice_select_fusion.23
  (93 shorter events, 4.9 us)
Async XLA Ops:
  0.0 36.9 %copy-start = (f32[5,1,64,128]{3,2,1,0:T(8,128)S(1)}, f32[5,1,64,128]{3,2,1,0:T(8,128)}, u32[]{:S(2)}) copy-start(f32[5,1,64,128]{3,2,1,0:T(8,128)} %param.2) | copy-start | bytes 491524
  0.8 25.3 %collective-permute-start = (f32[5,1,3,128]{3,2,1,0:T(4,128)S(1)}, f32[5,1,3,128]{3,2,1,0:T(4,128)S(1)}, u32[]{:S(2)}, u32[]{:S(2)}) collective-permute-start(f32[5,1,3,128]{3,2,1,0:T(4,128)S(1)} %get-tuple-element.70), channel_id=1, source_target_pairs={{0,1},{1,2},{2,3},{3,4},{4,5},{5,6},{6,7},{7,8},{8,9},{9,10},{10,1... | collective-permute-start | bytes 23048 | tf_op jit(solution)/shard_map/ppermute | solution.py:25
  2.7 23.5 %collective-permute-start.1 = (f32[5,1,3,128]{3,2,1,0:T(4,128)S(1)}, f32[5,1,3,128]{3,2,1,0:T(4,128)S(1)}, u32[]{:S(2)}, u32[]{:S(2)}) collective-permute-start(f32[5,1,3,128]{3,2,1,0:T(4,128)S(1)} %get-tuple-element.71), channel_id=1, source_target_pairs={{0,127},{1,0},{2,1},{3,2},{4,3},{5,4},{6,5},{7,6},{8,7},{9,8},{10,... | collective-permute-start | bytes 23048 | tf_op jit(solution)/shard_map/ppermute | solution.py:25
  27.5 6.2 %collective-permute-start.2 = (f32[1059]{0:T(1024)S(1)}, f32[1059]{0:T(1024)S(1)}, u32[]{:S(2)}, u32[]{:S(2)}) collective-permute-start(f32[1059]{0:T(1024)S(1)} %pad_maximum_fusion.1), channel_id=1, source_target_pairs={{0,128},{128,256},{256,384},{384,512},{512,640},{640,768},{768,896... | collective-permute-start | bytes 12716 | tf_op jit(solution)/shard_map/ppermute | solution.py:25
  31.2 5.5 %collective-permute-start.3 = (f32[1059]{0:T(1024)S(1)}, f32[1059]{0:T(1024)S(1)}, u32[]{:S(2)}, u32[]{:S(2)}) collective-permute-start(f32[1059]{0:T(1024)S(1)} %pad_maximum_fusion.2), channel_id=1, source_target_pairs={{128,0},{256,128},{384,256},{512,384},{640,512},{768,640},{896,768... | collective-permute-start | bytes 12716 | tf_op jit(solution)/shard_map/ppermute | solution.py:25
  38.1 5.6 %copy-start.1 = (s32[3,128]{1,0:T(4,128)S(1)}, s32[3,128]{1,0:T(4,128)}, u32[]{:S(2)}) copy-start(s32[3,128]{1,0:T(4,128)} %param.3) | copy-start | bytes 4612
  38.7 5.1 %collective-permute-start.4 = (f32[5,1,64,132]{3,2,1,0:T(8,128)S(1)}, f32[5,1,64,132]{3,2,1,0:T(8,128)S(1)}, u32[]{:S(2)}, u32[]{:S(2)}) collective-permute-start(f32[5,1,64,132]{3,2,1,0:T(8,128)S(1)} %slice.635), channel_id=1, source_target_pairs={{0,1},{1,2},{2,3},{3,4},{4,5},{5,6},{6,7},{7,8},{8,9},{9,10},{10,1... | collective-permute-start | bytes 506888 | tf_op jit(solution)/shard_map/ppermute | solution.py:163
  40.0 5.9 %collective-permute-start.5 = (f32[5,1,64,132]{3,2,1,0:T(8,128)S(1)}, f32[5,1,64,132]{3,2,1,0:T(8,128)S(1)}, u32[]{:S(2)}, u32[]{:S(2)}) collective-permute-start(f32[5,1,64,132]{3,2,1,0:T(8,128)S(1)} %slice.635), channel_id=1, source_target_pairs={{0,2},{1,3},{2,4},{3,5},{4,6},{5,7},{6,8},{7,9},{8,10},{9,11},{10,... | collective-permute-start | bytes 506888 | tf_op jit(solution)/shard_map/ppermute | solution.py:163
  41.3 8.1 %collective-permute-start.6 = (f32[5,1,64,132]{3,2,1,0:T(8,128)S(1)}, f32[5,1,64,132]{3,2,1,0:T(8,128)S(1)}, u32[]{:S(2)}, u32[]{:S(2)}) collective-permute-start(f32[5,1,64,132]{3,2,1,0:T(8,128)S(1)} %slice.635), channel_id=1, source_target_pairs={{0,3},{1,4},{2,5},{3,6},{4,7},{5,8},{6,9},{7,10},{8,11},{9,12},{10... | collective-permute-start | bytes 506888 | tf_op jit(solution)/shard_map/ppermute | solution.py:163
  42.6 6.8 %collective-permute-start.7 = (f32[5,1,64,132]{3,2,1,0:T(8,128)S(1)}, f32[5,1,64,132]{3,2,1,0:T(8,128)S(1)}, u32[]{:S(2)}, u32[]{:S(2)}) collective-permute-start(f32[5,1,64,132]{3,2,1,0:T(8,128)S(1)} %slice.635), channel_id=1, source_target_pairs={{15,1},{14,3},{13,4},{31,17},{30,19},{29,20},{47,33},{46,35},{45,3... | collective-permute-start | bytes 506888 | tf_op jit(solution)/shard_map/ppermute | solution.py:165
  49.4 34.8 %collective-permute-start.10 = (f32[5,1,64,132]{3,2,1,0:T(8,128)S(1)}, f32[5,1,64,132]{3,2,1,0:T(8,128)S(1)}, u32[]{:S(2)}, u32[]{:S(2)}) collective-permute-start(f32[5,1,64,132]{3,2,1,0:T(8,128)S(1)} %collective-permute-done.7), channel_id=1, source_target_pairs={{1,16},{17,32},{33,48},{49,64},{65,80},{81,96},{97,112},{113,0},{1... | collective-permute-start | bytes 506888 | tf_op jit(solution)/shard_map/ppermute | solution.py:171
  50.7 33.5 %collective-permute-start.9 = (f32[5,1,64,132]{3,2,1,0:T(8,128)S(1)}, f32[5,1,64,132]{3,2,1,0:T(8,128)S(1)}, u32[]{:S(2)}, u32[]{:S(2)}) collective-permute-start(f32[5,1,64,132]{3,2,1,0:T(8,128)S(1)} %collective-permute-done.7), channel_id=1, source_target_pairs={{3,16},{1,17},{19,32},{17,33},{35,48},{33,49},{51,64},{49,65},{67,... | collective-permute-start | bytes 506888 | tf_op jit(solution)/shard_map/ppermute | solution.py:171
  52.0 36.6 %collective-permute-start.8 = (f32[5,1,64,132]{3,2,1,0:T(8,128)S(1)}, f32[5,1,64,132]{3,2,1,0:T(8,128)S(1)}, u32[]{:S(2)}, u32[]{:S(2)}) collective-permute-start(f32[5,1,64,132]{3,2,1,0:T(8,128)S(1)} %collective-permute-done.7), channel_id=1, source_target_pairs={{4,16},{3,17},{1,18},{20,32},{19,33},{17,34},{36,48},{35,49},{33,5... | collective-permute-start | bytes 506888 | tf_op jit(solution)/shard_map/ppermute | solution.py:171
  91.9 17.9 %collective-permute-start.11 = (f32[5,1,64,130]{3,2,1,0:T(8,128)S(1)}, f32[5,1,64,130]{3,2,1,0:T(8,128)S(1)}, u32[]{:S(2)}, u32[]{:S(2)}) collective-permute-start(f32[5,1,64,130]{3,2,1,0:T(8,128)S(1)} %slice.677), channel_id=1, source_target_pairs={{0,1},{1,2},{2,3},{3,4},{4,5},{5,6},{6,7},{7,8},{8,9},{9,10},{10,1... | collective-permute-start | bytes 499208 | tf_op jit(solution)/shard_map/ppermute | solution.py:163
  101.1 14.9 %collective-permute-start.12 = (f32[5,1,64,130]{3,2,1,0:T(8,128)S(1)}, f32[5,1,64,130]{3,2,1,0:T(8,128)S(1)}, u32[]{:S(2)}, u32[]{:S(2)}) collective-permute-start(f32[5,1,64,130]{3,2,1,0:T(8,128)S(1)} %slice.677), channel_id=1, source_target_pairs={{0,2},{1,3},{2,4},{3,5},{4,6},{5,7},{6,8},{7,9},{8,10},{9,11},{10,... | collective-permute-start | bytes 499208 | tf_op jit(solution)/shard_map/ppermute | solution.py:163
  107.8 15.2 %collective-permute-start.13 = (f32[5,1,64,130]{3,2,1,0:T(8,128)S(1)}, f32[5,1,64,130]{3,2,1,0:T(8,128)S(1)}, u32[]{:S(2)}, u32[]{:S(2)}) collective-permute-start(f32[5,1,64,130]{3,2,1,0:T(8,128)S(1)} %slice.677), channel_id=1, source_target_pairs={{0,3},{1,4},{2,5},{3,6},{4,7},{5,8},{6,9},{7,10},{8,11},{9,12},{10... | collective-permute-start | bytes 499208 | tf_op jit(solution)/shard_map/ppermute | solution.py:163
  109.1 13.8 %collective-permute-start.14 = (f32[5,1,64,130]{3,2,1,0:T(8,128)S(1)}, f32[5,1,64,130]{3,2,1,0:T(8,128)S(1)}, u32[]{:S(2)}, u32[]{:S(2)}) collective-permute-start(f32[5,1,64,130]{3,2,1,0:T(8,128)S(1)} %slice.677), channel_id=1, source_target_pairs={{15,1},{14,3},{13,4},{31,17},{30,19},{29,20},{47,33},{46,35},{45,3... | collective-permute-start | bytes 499208 | tf_op jit(solution)/shard_map/ppermute | solution.py:165
  123.0 28.6 %collective-permute-start.17 = (f32[5,1,64,130]{3,2,1,0:T(8,128)S(1)}, f32[5,1,64,130]{3,2,1,0:T(8,128)S(1)}, u32[]{:S(2)}, u32[]{:S(2)}) collective-permute-start(f32[5,1,64,130]{3,2,1,0:T(8,128)S(1)} %collective-permute-done.14), channel_id=1, source_target_pairs={{1,16},{17,32},{33,48},{49,64},{65,80},{81,96},{97,112},{113,0},{1... | collective-permute-start | bytes 499208 | tf_op jit(solution)/shard_map/ppermute | solution.py:171
  124.3 28.1 %collective-permute-start.16 = (f32[5,1,64,130]{3,2,1,0:T(8,128)S(1)}, f32[5,1,64,130]{3,2,1,0:T(8,128)S(1)}, u32[]{:S(2)}, u32[]{:S(2)}) collective-permute-start(f32[5,1,64,130]{3,2,1,0:T(8,128)S(1)} %collective-permute-done.14), channel_id=1, source_target_pairs={{3,16},{1,17},{19,32},{17,33},{35,48},{33,49},{51,64},{49,65},{67,... | collective-permute-start | bytes 499208 | tf_op jit(solution)/shard_map/ppermute | solution.py:171
  125.6 26.8 %collective-permute-start.15 = (f32[5,1,64,130]{3,2,1,0:T(8,128)S(1)}, f32[5,1,64,130]{3,2,1,0:T(8,128)S(1)}, u32[]{:S(2)}, u32[]{:S(2)}) collective-permute-start(f32[5,1,64,130]{3,2,1,0:T(8,128)S(1)} %collective-permute-done.14), channel_id=1, source_target_pairs={{4,16},{3,17},{1,18},{20,32},{19,33},{17,34},{36,48},{35,49},{33,5... | collective-permute-start | bytes 499208 | tf_op jit(solution)/shard_map/ppermute | solution.py:171
  155.3 17.3 %collective-permute-start.18 = (f32[5,1,64,128]{3,2,1,0:T(8,128)S(1)}, f32[5,1,64,128]{3,2,1,0:T(8,128)S(1)}, u32[]{:S(2)}, u32[]{:S(2)}) collective-permute-start(f32[5,1,64,128]{3,2,1,0:T(8,128)S(1)} %get-tuple-element.29), channel_id=1, source_target_pairs={{0,1},{1,2},{2,3},{3,4},{4,5},{5,6},{6,7},{7,8},{8,9},{9,10},{10,1... | collective-permute-start | bytes 491528 | tf_op jit(solution)/shard_map/ppermute | solution.py:163
  163.9 11.3 %collective-permute-start.19 = (f32[5,1,64,128]{3,2,1,0:T(8,128)S(1)}, f32[5,1,64,128]{3,2,1,0:T(8,128)S(1)}, u32[]{:S(2)}, u32[]{:S(2)}) collective-permute-start(f32[5,1,64,128]{3,2,1,0:T(8,128)S(1)} %get-tuple-element.29), channel_id=1, source_target_pairs={{0,2},{1,3},{2,4},{3,5},{4,6},{5,7},{6,8},{7,9},{8,10},{9,11},{10,... | collective-permute-start | bytes 491528 | tf_op jit(solution)/shard_map/ppermute | solution.py:163
  170.6 7.3 %collective-permute-start.20 = (f32[5,1,64,128]{3,2,1,0:T(8,128)S(1)}, f32[5,1,64,128]{3,2,1,0:T(8,128)S(1)}, u32[]{:S(2)}, u32[]{:S(2)}) collective-permute-start(f32[5,1,64,128]{3,2,1,0:T(8,128)S(1)} %get-tuple-element.29), channel_id=1, source_target_pairs={{0,3},{1,4},{2,5},{3,6},{4,7},{5,8},{6,9},{7,10},{8,11},{9,12},{10... | collective-permute-start | bytes 491528 | tf_op jit(solution)/shard_map/ppermute | solution.py:163
  171.9 6.0 %collective-permute-start.21 = (f32[5,1,64,128]{3,2,1,0:T(8,128)S(1)}, f32[5,1,64,128]{3,2,1,0:T(8,128)S(1)}, u32[]{:S(2)}, u32[]{:S(2)}) collective-permute-start(f32[5,1,64,128]{3,2,1,0:T(8,128)S(1)} %get-tuple-element.29), channel_id=1, source_target_pairs={{15,1},{14,3},{13,4},{31,17},{30,19},{29,20},{47,33},{46,35},{45,3... | collective-permute-start | bytes 491528 | tf_op jit(solution)/shard_map/ppermute | solution.py:165
  177.9 22.4 %collective-permute-start.22 = (f32[5,1,64,128]{3,2,1,0:T(8,128)S(1)}, f32[5,1,64,128]{3,2,1,0:T(8,128)S(1)}, u32[]{:S(2)}, u32[]{:S(2)}) collective-permute-start(f32[5,1,64,128]{3,2,1,0:T(8,128)S(1)} %collective-permute-done.21), channel_id=1, source_target_pairs={{4,16},{3,17},{1,18},{20,32},{19,33},{17,34},{36,48},{35,49},{33,5... | collective-permute-start | bytes 491528 | tf_op jit(solution)/shard_map/ppermute | solution.py:171
  179.3 24.2 %collective-permute-start.23 = (f32[5,1,64,128]{3,2,1,0:T(8,128)S(1)}, f32[5,1,64,128]{3,2,1,0:T(8,128)S(1)}, u32[]{:S(2)}, u32[]{:S(2)}) collective-permute-start(f32[5,1,64,128]{3,2,1,0:T(8,128)S(1)} %collective-permute-done.21), channel_id=1, source_target_pairs={{3,16},{1,17},{19,32},{17,33},{35,48},{33,49},{51,64},{49,65},{67,... | collective-permute-start | bytes 491528 | tf_op jit(solution)/shard_map/ppermute | solution.py:171
  180.6 25.5 %collective-permute-start.24 = (f32[5,1,64,128]{3,2,1,0:T(8,128)S(1)}, f32[5,1,64,128]{3,2,1,0:T(8,128)S(1)}, u32[]{:S(2)}, u32[]{:S(2)}) collective-permute-start(f32[5,1,64,128]{3,2,1,0:T(8,128)S(1)} %collective-permute-done.21), channel_id=1, source_target_pairs={{1,16},{17,32},{33,48},{49,64},{65,80},{81,96},{97,112},{113,0},{1... | collective-permute-start | bytes 491528 | tf_op jit(solution)/shard_map/ppermute | solution.py:171

commit v4 on v3

--- a/solution.py
+++ b/solution.py
@@ -132,19 +132,16 @@
 
 def crossing_relays(groups, count, plane, blocks):
     half = plane // 2
-    first, second = [], [[] for _ in range(blocks)]
+    first, second = [], []
     for g in range(groups):
         for block in range(count // plane):
             base = block * plane
             after = (base + plane) % count
-            relay = {}
             for j in range(1, blocks + 1):
                 lane = (3 * g + j - 1) % half
-                relay[j] = base + relay_seat(lane, plane - j, plane, blocks)
-                first.append((g * count + base + plane - j, g * count + relay[j]))
-            for k in range(1, blocks + 1):
-                for i in range(k):
-                    second[k - 1].append((g * count + relay[k - i], g * count + after + i))
+                relay = base + relay_seat(lane, plane - j, plane, blocks)
+                first.append((g * count + base + plane - j, g * count + relay))
+                second.append((g * count + relay, g * count + after + blocks - j))
     return first, second
 
 
@@ -163,12 +160,20 @@
         near.append(lax.ppermute(head, "azi", pairs))
     first, second = crossing_relays(groups, count, plane, blocks)
     relayed = lax.ppermute(head, ("rad", "azi"), first)
-    near_and_relayed = lax.optimization_barrier((near, relayed))
-    near, relayed = near_and_relayed
+    crossed = lax.ppermute(relayed, ("rad", "azi"), second)
     position = lax.axis_index("azi") % plane
     pieces = []
     for k in range(1, blocks + 1):
-        far = lax.ppermute(relayed, ("rad", "azi"), second[k - 1])
+        if k == blocks:
+            far = crossed
+        else:
+            t = blocks - k
+            pairs = [
+                (base + i + t, base + i)
+                for base in range(0, count, plane)
+                for i in range(blocks - t)
+            ]
+            far = lax.ppermute(crossed, "azi", pairs)
         pieces.append(jnp.where(position < k, far, near[k - 1]))
     return pieces
 

time: 208 us -> 167 us (0.80)
  the two profiles are of different devices: /device:TPU:128 before, /device:TPU:64 now
where the time goes in v4:
time: 167 us
  waiting for transfers between devices  84.7 us (51%)
  starting transfers between devices  67.4 us (40%)
  other arithmetic  10.1 us (6%)
  local copies, waits for them, and re-layouts  3.57 us (2%)
    ppermute x3, waiting for transfers between devices, rotation_pieces(): crossed = lax.ppermute(relayed, ('rad', 'azi'), second)  62.9 us
    ppermute x4, starting transfers between devices, passed_along(): return lax.ppermute(value, axis, pairs)  34 us
    ppermute x6, waiting for transfers between devices, rotation_pieces(): far = lax.ppermute(crossed, 'azi', pairs)  20.5 us
    ppermute x9, starting transfers between devices, rotation_pieces(): near.append(lax.ppermute(head, 'azi', pairs))  19.8 us
    ppermute x6, starting transfers between devices, rotation_pieces(): far = lax.ppermute(crossed, 'azi', pairs)  7.72 us
    ppermute x3, starting transfers between devices, rotation_pieces(): crossed = lax.ppermute(relayed, ('rad', 'azi'), second)  3.88 us
  transfers between devices with their start and end apart: 25, of which 9 were waited for; matrix products, arithmetic and copies ran while one was open for 2% of the time, Pallas kernels for 0%

profile of v4, /device:TPU:64, one launch (start us, length us, event | category | flops | bytes accessed | tf_op | source)
XLA Modules:
  0.0 166.8 jit_solution(9515863729459683614)
XLA Ops:
  0.0 0.8 fusion.103
  0.8 1.9 %collective-permute-start = (f32[5,1,3,128]{3,2,1,0:T(4,128)S(1)}, f32[5,1,3,128]{3,2,1,0:T(4,128)S(1)}, u32[]{:S(2)}, u32[]{:S(2)}) collective-permute-start(f32[5,1,3,128]{3,2,1,0:T(4,128)S(1)} %get-tuple-element.46), channel_id=1, source_target_pairs={{0,1},{1,2},{2,3},{3,4},{4,5},{5,6},{6,7},{7,8},{8,9},{9,10},{10,1... | collective-permute-start | bytes 23048 | tf_op jit(solution)/shard_map/ppermute | solution.py:25
  2.7 23.0 %collective-permute-start.1 = (f32[5,1,3,128]{3,2,1,0:T(4,128)S(1)}, f32[5,1,3,128]{3,2,1,0:T(4,128)S(1)}, u32[]{:S(2)}, u32[]{:S(2)}) collective-permute-start(f32[5,1,3,128]{3,2,1,0:T(4,128)S(1)} %get-tuple-element.47), channel_id=1, source_target_pairs={{0,127},{1,0},{2,1},{3,2},{4,3},{5,4},{6,5},{7,6},{8,7},{9,8},{10,... | collective-permute-start | bytes 23048 | tf_op jit(solution)/shard_map/ppermute | solution.py:25
  25.7 0.8 slice_convert_fusion.1
  27.1 0.9 pad_maximum_fusion
  28.2 0.2 reshape.1273
  28.4 3.4 %collective-permute-start.2 = (f32[1059]{0:T(1024)S(1)}, f32[1059]{0:T(1024)S(1)}, u32[]{:S(2)}, u32[]{:S(2)}) collective-permute-start(f32[1059]{0:T(1024)S(1)} %pad_maximum_fusion.1), channel_id=1, source_target_pairs={{0,128},{128,256},{256,384},{384,512},{512,640},{640,768},{768,896... | collective-permute-start | bytes 12716 | tf_op jit(solution)/shard_map/ppermute | solution.py:25
  31.8 0.2 reshape.1275
  32.1 5.7 %collective-permute-start.3 = (f32[1059]{0:T(1024)S(1)}, f32[1059]{0:T(1024)S(1)}, u32[]{:S(2)}, u32[]{:S(2)}) collective-permute-start(f32[1059]{0:T(1024)S(1)} %pad_maximum_fusion.2), channel_id=1, source_target_pairs={{128,0},{256,128},{384,256},{512,384},{640,512},{768,640},{896,768... | collective-permute-start | bytes 12716 | tf_op jit(solution)/shard_map/ppermute | solution.py:25
  37.8 0.2 concatenate.40
  38.0 1.1 collective-permute-done.3
  39.1 0.2 concatenate.41
  39.3 0.2 maximum_select_fusion
  39.7 0.2 subtract_multiply_fusion.3
  39.9 0.6 subtract_add_fusion.1
  40.6 0.1 fusion.4
  40.7 0.1 fusion.29
  41.1 0.7 collective-permute-start.4
  41.8 1.3 collective-permute-start.10
  43.1 1.3 collective-permute-start.8
  44.4 1.3 collective-permute-start.6
  46.2 1.3 collective-permute-start.5
  47.6 27.3 %collective-permute-done.5 = f32[5,1,64,132]{3,2,1,0:T(8,128)S(1)} collective-permute-done((f32[5,1,64,132]{3,2,1,0:T(8,128)S(1)}, f32[5,1,64,132]{3,2,1,0:T(8,128)S(1)}, u32[]{:S(2)}, u32[]{:S(2)}) %collective-permute-start.5) | collective-permute-done | bytes 168992 | tf_op jit(solution)/shard_map/ppermute | solution.py:163
  74.9 1.3 collective-permute-start.9
  76.2 1.3 collective-permute-start.7
  77.5 6.3 %collective-permute-done.9 = f32[5,1,64,132]{3,2,1,0:T(8,128)S(1)} collective-permute-done((f32[5,1,64,132]{3,2,1,0:T(8,128)S(1)}, f32[5,1,64,132]{3,2,1,0:T(8,128)S(1)}, u32[]{:S(2)}, u32[]{:S(2)}) %collective-permute-start.9) | collective-permute-done | bytes 168992 | tf_op jit(solution)/shard_map/ppermute | solution.py:176
  84.0 0.7 concatenate.43
  84.7 0.2 slice_select_fusion
  84.9 0.2 slice_select_fusion.5
  85.0 0.2 slice_select_fusion.4
  85.2 0.1 slice_select_fusion.7
  85.4 0.1 slice_select_fusion.9
  85.9 0.2 subtract_multiply_fusion.1
  86.0 0.6 subtract_add_fusion
  86.7 0.1 fusion.7
  86.9 0.1 fusion.14
  87.2 0.7 collective-permute-start.11
  88.0 1.3 collective-permute-start.13
  89.3 1.3 collective-permute-start.12
  90.6 5.2 %collective-permute-start.17 = (f32[5,1,64,130]{3,2,1,0:T(8,128)S(1)}, f32[5,1,64,130]{3,2,1,0:T(8,128)S(1)}, u32[]{:S(2)}, u32[]{:S(2)}) collective-permute-start(f32[5,1,64,130]{3,2,1,0:T(8,128)S(1)} %slice.677), channel_id=1, source_target_pairs={{0,1},{1,2},{2,3},{3,4},{4,5},{5,6},{6,7},{7,8},{8,9},{9,10},{10,1... | collective-permute-start | bytes 499208 | tf_op jit(solution)/shard_map/ppermute | solution.py:160
  95.8 1.6 collective-permute-start.15
  97.5 20.0 %collective-permute-done.12 = f32[5,1,64,130]{3,2,1,0:T(8,128)S(1)} collective-permute-done((f32[5,1,64,130]{3,2,1,0:T(8,128)S(1)}, f32[5,1,64,130]{3,2,1,0:T(8,128)S(1)}, u32[]{:S(2)}, u32[]{:S(2)}) %collective-permute-start.12) | collective-permute-done | bytes 166432 | tf_op jit(solution)/shard_map/ppermute | solution.py:163
  117.5 1.3 collective-permute-start.16
  118.8 1.3 collective-permute-start.14
  120.1 6.3 %collective-permute-done.16 = f32[5,1,64,130]{3,2,1,0:T(8,128)S(1)} collective-permute-done((f32[5,1,64,130]{3,2,1,0:T(8,128)S(1)}, f32[5,1,64,130]{3,2,1,0:T(8,128)S(1)}, u32[]{:S(2)}, u32[]{:S(2)}) %collective-permute-start.16) | collective-permute-done | bytes 166432 | tf_op jit(solution)/shard_map/ppermute | solution.py:176
  126.6 0.7 concatenate.44
  127.3 0.2 slice_select_fusion.3
  127.5 0.2 slice_select_fusion.2
  127.7 0.2 slice_select_fusion.1
  127.8 0.1 slice_select_fusion.6
  128.0 0.1 slice_select_fusion.8
  128.5 0.1 subtract_multiply_fusion.5
  128.6 0.3 subtract_add_fusion.2
  129.3 0.7 collective-permute-start.18
  130.0 1.3 collective-permute-start.20
  131.3 1.3 collective-permute-start.19
  132.7 4.9 %collective-permute-start.22 = (f32[5,1,64,128]{3,2,1,0:T(8,128)S(1)}, f32[5,1,64,128]{3,2,1,0:T(8,128)S(1)}, u32[]{:S(2)}, u32[]{:S(2)}) collective-permute-start(f32[5,1,64,128]{3,2,1,0:T(8,128)S(1)} %get-tuple-element.5), channel_id=1, source_target_pairs={{0,2},{1,3},{2,4},{3,5},{4,6},{5,7},{6,8},{7,9},{8,10},{9,11},{10,... | collective-permute-start | bytes 491528 | tf_op jit(solution)/shard_map/ppermute | solution.py:160
  137.6 1.6 collective-permute-start.24
  139.2 15.6 %collective-permute-done.19 = f32[5,1,64,128]{3,2,1,0:T(8,128)S(1)} collective-permute-done((f32[5,1,64,128]{3,2,1,0:T(8,128)S(1)}, f32[5,1,64,128]{3,2,1,0:T(8,128)S(1)}, u32[]{:S(2)}, u32[]{:S(2)}) %collective-permute-start.19) | collective-permute-done | bytes 163872 | tf_op jit(solution)/shard_map/ppermute | solution.py:163
  154.8 1.3 collective-permute-start.21
  156.1 1.3 collective-permute-start.23
  157.4 2.2 %collective-permute-done.21 = f32[5,1,64,128]{3,2,1,0:T(8,128)S(1)} collective-permute-done((f32[5,1,64,128]{3,2,1,0:T(8,128)S(1)}, f32[5,1,64,128]{3,2,1,0:T(8,128)S(1)}, u32[]{:S(2)}, u32[]{:S(2)}) %collective-permute-start.21) | collective-permute-done | bytes 163872 | tf_op jit(solution)/shard_map/ppermute | solution.py:176
  159.7 5.7 %collective-permute-done.23 = f32[5,1,64,128]{3,2,1,0:T(8,128)S(1)} collective-permute-done((f32[5,1,64,128]{3,2,1,0:T(8,128)S(1)}, f32[5,1,64,128]{3,2,1,0:T(8,128)S(1)}, u32[]{:S(2)}, u32[]{:S(2)}) %collective-permute-start.23) | collective-permute-done | bytes 163872 | tf_op jit(solution)/shard_map/ppermute | solution.py:176
  166.1 0.7 slice_select_fusion.23
  (93 shorter events, 4.2 us)
Async XLA Ops:
  0.0 39.3 %copy-start = (f32[5,1,64,128]{3,2,1,0:T(8,128)S(1)}, f32[5,1,64,128]{3,2,1,0:T(8,128)}, u32[]{:S(2)}) copy-start(f32[5,1,64,128]{3,2,1,0:T(8,128)} %param.2) | copy-start | bytes 491524
  0.8 26.2 %collective-permute-start = (f32[5,1,3,128]{3,2,1,0:T(4,128)S(1)}, f32[5,1,3,128]{3,2,1,0:T(4,128)S(1)}, u32[]{:S(2)}, u32[]{:S(2)}) collective-permute-start(f32[5,1,3,128]{3,2,1,0:T(4,128)S(1)} %get-tuple-element.46), channel_id=1, source_target_pairs={{0,1},{1,2},{2,3},{3,4},{4,5},{5,6},{6,7},{7,8},{8,9},{9,10},{10,1... | collective-permute-start | bytes 23048 | tf_op jit(solution)/shard_map/ppermute | solution.py:25
  2.7 24.4 %collective-permute-start.1 = (f32[5,1,3,128]{3,2,1,0:T(4,128)S(1)}, f32[5,1,3,128]{3,2,1,0:T(4,128)S(1)}, u32[]{:S(2)}, u32[]{:S(2)}) collective-permute-start(f32[5,1,3,128]{3,2,1,0:T(4,128)S(1)} %get-tuple-element.47), channel_id=1, source_target_pairs={{0,127},{1,0},{2,1},{3,2},{4,3},{5,4},{6,5},{7,6},{8,7},{9,8},{10,... | collective-permute-start | bytes 23048 | tf_op jit(solution)/shard_map/ppermute | solution.py:25
  28.4 9.4 %collective-permute-start.2 = (f32[1059]{0:T(1024)S(1)}, f32[1059]{0:T(1024)S(1)}, u32[]{:S(2)}, u32[]{:S(2)}) collective-permute-start(f32[1059]{0:T(1024)S(1)} %pad_maximum_fusion.1), channel_id=1, source_target_pairs={{0,128},{128,256},{256,384},{384,512},{512,640},{640,768},{768,896... | collective-permute-start | bytes 12716 | tf_op jit(solution)/shard_map/ppermute | solution.py:25
  32.1 7.0 %collective-permute-start.3 = (f32[1059]{0:T(1024)S(1)}, f32[1059]{0:T(1024)S(1)}, u32[]{:S(2)}, u32[]{:S(2)}) collective-permute-start(f32[1059]{0:T(1024)S(1)} %pad_maximum_fusion.2), channel_id=1, source_target_pairs={{128,0},{256,128},{384,256},{512,384},{640,512},{768,640},{896,768... | collective-permute-start | bytes 12716 | tf_op jit(solution)/shard_map/ppermute | solution.py:25
  40.5 5.6 %copy-start.1 = (s32[3,128]{1,0:T(4,128)S(1)}, s32[3,128]{1,0:T(4,128)}, u32[]{:S(2)}) copy-start(s32[3,128]{1,0:T(4,128)} %param.3) | copy-start | bytes 4612
  41.1 5.1 %collective-permute-start.4 = (f32[5,1,64,132]{3,2,1,0:T(8,128)S(1)}, f32[5,1,64,132]{3,2,1,0:T(8,128)S(1)}, u32[]{:S(2)}, u32[]{:S(2)}) collective-permute-start(f32[5,1,64,132]{3,2,1,0:T(8,128)S(1)} %slice.635), channel_id=1, source_target_pairs={{15,1},{14,3},{13,4},{31,17},{30,19},{29,20},{47,33},{46,35},{45,3... | collective-permute-start | bytes 506888 | tf_op jit(solution)/shard_map/ppermute | solution.py:162
  41.8 35.8 %collective-permute-start.10 = (f32[5,1,64,132]{3,2,1,0:T(8,128)S(1)}, f32[5,1,64,132]{3,2,1,0:T(8,128)S(1)}, u32[]{:S(2)}, u32[]{:S(2)}) collective-permute-start(f32[5,1,64,132]{3,2,1,0:T(8,128)S(1)} %slice.635), channel_id=1, source_target_pairs={{0,1},{1,2},{2,3},{3,4},{4,5},{5,6},{6,7},{7,8},{8,9},{9,10},{10,1... | collective-permute-start | bytes 506888 | tf_op jit(solution)/shard_map/ppermute | solution.py:160
  43.1 40.8 %collective-permute-start.8 = (f32[5,1,64,132]{3,2,1,0:T(8,128)S(1)}, f32[5,1,64,132]{3,2,1,0:T(8,128)S(1)}, u32[]{:S(2)}, u32[]{:S(2)}) collective-permute-start(f32[5,1,64,132]{3,2,1,0:T(8,128)S(1)} %slice.635), channel_id=1, source_target_pairs={{0,2},{1,3},{2,4},{3,5},{4,6},{5,7},{6,8},{7,9},{8,10},{9,11},{10,... | collective-permute-start | bytes 506888 | tf_op jit(solution)/shard_map/ppermute | solution.py:160
  44.4 33.1 %collective-permute-start.6 = (f32[5,1,64,132]{3,2,1,0:T(8,128)S(1)}, f32[5,1,64,132]{3,2,1,0:T(8,128)S(1)}, u32[]{:S(2)}, u32[]{:S(2)}) collective-permute-start(f32[5,1,64,132]{3,2,1,0:T(8,128)S(1)} %slice.635), channel_id=1, source_target_pairs={{0,3},{1,4},{2,5},{3,6},{4,7},{5,8},{6,9},{7,10},{8,11},{9,12},{10... | collective-permute-start | bytes 506888 | tf_op jit(solution)/shard_map/ppermute | solution.py:160
  46.2 28.6 %collective-permute-start.5 = (f32[5,1,64,132]{3,2,1,0:T(8,128)S(1)}, f32[5,1,64,132]{3,2,1,0:T(8,128)S(1)}, u32[]{:S(2)}, u32[]{:S(2)}) collective-permute-start(f32[5,1,64,132]{3,2,1,0:T(8,128)S(1)} %collective-permute-done.4), channel_id=1, source_target_pairs={{1,18},{3,17},{4,16},{17,34},{19,33},{20,32},{33,50},{35,49},{36,4... | collective-permute-start | bytes 506888 | tf_op jit(solution)/shard_map/ppermute | solution.py:163
  74.9 9.0 %collective-permute-start.9 = (f32[5,1,64,132]{3,2,1,0:T(8,128)S(1)}, f32[5,1,64,132]{3,2,1,0:T(8,128)S(1)}, u32[]{:S(2)}, u32[]{:S(2)}) collective-permute-start(f32[5,1,64,132]{3,2,1,0:T(8,128)S(1)} %collective-permute-done.5), channel_id=1, source_target_pairs={{2,0},{18,16},{34,32},{50,48},{66,64},{82,80},{98,96},{114,112},{1... | collective-permute-start | bytes 506888 | tf_op jit(solution)/shard_map/ppermute | solution.py:176
  76.2 7.7 %collective-permute-start.7 = (f32[5,1,64,132]{3,2,1,0:T(8,128)S(1)}, f32[5,1,64,132]{3,2,1,0:T(8,128)S(1)}, u32[]{:S(2)}, u32[]{:S(2)}) collective-permute-start(f32[5,1,64,132]{3,2,1,0:T(8,128)S(1)} %collective-permute-done.5), channel_id=1, source_target_pairs={{1,0},{2,1},{17,16},{18,17},{33,32},{34,33},{49,48},{50,49},{65,64... | collective-permute-start | bytes 506888 | tf_op jit(solution)/shard_map/ppermute | solution.py:176
  87.2 2.0 %collective-permute-start.11 = (f32[5,1,64,130]{3,2,1,0:T(8,128)S(1)}, f32[5,1,64,130]{3,2,1,0:T(8,128)S(1)}, u32[]{:S(2)}, u32[]{:S(2)}) collective-permute-start(f32[5,1,64,130]{3,2,1,0:T(8,128)S(1)} %slice.677), channel_id=1, source_target_pairs={{15,1},{14,3},{13,4},{31,17},{30,19},{29,20},{47,33},{46,35},{45,3... | collective-permute-start | bytes 499208 | tf_op jit(solution)/shard_map/ppermute | solution.py:162
  88.0 32.1 %collective-permute-start.13 = (f32[5,1,64,130]{3,2,1,0:T(8,128)S(1)}, f32[5,1,64,130]{3,2,1,0:T(8,128)S(1)}, u32[]{:S(2)}, u32[]{:S(2)}) collective-permute-start(f32[5,1,64,130]{3,2,1,0:T(8,128)S(1)} %slice.677), channel_id=1, source_target_pairs={{0,3},{1,4},{2,5},{3,6},{4,7},{5,8},{6,9},{7,10},{8,11},{9,12},{10... | collective-permute-start | bytes 499208 | tf_op jit(solution)/shard_map/ppermute | solution.py:160
  89.3 28.2 %collective-permute-start.12 = (f32[5,1,64,130]{3,2,1,0:T(8,128)S(1)}, f32[5,1,64,130]{3,2,1,0:T(8,128)S(1)}, u32[]{:S(2)}, u32[]{:S(2)}) collective-permute-start(f32[5,1,64,130]{3,2,1,0:T(8,128)S(1)} %collective-permute-done.11), channel_id=1, source_target_pairs={{1,18},{3,17},{4,16},{17,34},{19,33},{20,32},{33,50},{35,49},{36,4... | collective-permute-start | bytes 499208 | tf_op jit(solution)/shard_map/ppermute | solution.py:163
  90.6 29.5 %collective-permute-start.17 = (f32[5,1,64,130]{3,2,1,0:T(8,128)S(1)}, f32[5,1,64,130]{3,2,1,0:T(8,128)S(1)}, u32[]{:S(2)}, u32[]{:S(2)}) collective-permute-start(f32[5,1,64,130]{3,2,1,0:T(8,128)S(1)} %slice.677), channel_id=1, source_target_pairs={{0,1},{1,2},{2,3},{3,4},{4,5},{5,6},{6,7},{7,8},{8,9},{9,10},{10,1... | collective-permute-start | bytes 499208 | tf_op jit(solution)/shard_map/ppermute | solution.py:160
  95.8 30.7 %collective-permute-start.15 = (f32[5,1,64,130]{3,2,1,0:T(8,128)S(1)}, f32[5,1,64,130]{3,2,1,0:T(8,128)S(1)}, u32[]{:S(2)}, u32[]{:S(2)}) collective-permute-start(f32[5,1,64,130]{3,2,1,0:T(8,128)S(1)} %slice.677), channel_id=1, source_target_pairs={{0,2},{1,3},{2,4},{3,5},{4,6},{5,7},{6,8},{7,9},{8,10},{9,11},{10,... | collective-permute-start | bytes 499208 | tf_op jit(solution)/shard_map/ppermute | solution.py:160
  117.5 9.0 %collective-permute-start.16 = (f32[5,1,64,130]{3,2,1,0:T(8,128)S(1)}, f32[5,1,64,130]{3,2,1,0:T(8,128)S(1)}, u32[]{:S(2)}, u32[]{:S(2)}) collective-permute-start(f32[5,1,64,130]{3,2,1,0:T(8,128)S(1)} %collective-permute-done.12), channel_id=1, source_target_pairs={{2,0},{18,16},{34,32},{50,48},{66,64},{82,80},{98,96},{114,112},{1... | collective-permute-start | bytes 499208 | tf_op jit(solution)/shard_map/ppermute | solution.py:176
  118.8 7.7 %collective-permute-start.14 = (f32[5,1,64,130]{3,2,1,0:T(8,128)S(1)}, f32[5,1,64,130]{3,2,1,0:T(8,128)S(1)}, u32[]{:S(2)}, u32[]{:S(2)}) collective-permute-start(f32[5,1,64,130]{3,2,1,0:T(8,128)S(1)} %collective-permute-done.12), channel_id=1, source_target_pairs={{1,0},{2,1},{17,16},{18,17},{33,32},{34,33},{49,48},{50,49},{65,64... | collective-permute-start | bytes 499208 | tf_op jit(solution)/shard_map/ppermute | solution.py:176
  129.3 2.0 %collective-permute-start.18 = (f32[5,1,64,128]{3,2,1,0:T(8,128)S(1)}, f32[5,1,64,128]{3,2,1,0:T(8,128)S(1)}, u32[]{:S(2)}, u32[]{:S(2)}) collective-permute-start(f32[5,1,64,128]{3,2,1,0:T(8,128)S(1)} %get-tuple-element.5), channel_id=1, source_target_pairs={{15,1},{14,3},{13,4},{31,17},{30,19},{29,20},{47,33},{46,35},{45,3... | collective-permute-start | bytes 491528 | tf_op jit(solution)/shard_map/ppermute | solution.py:162
  130.0 27.4 %collective-permute-start.20 = (f32[5,1,64,128]{3,2,1,0:T(8,128)S(1)}, f32[5,1,64,128]{3,2,1,0:T(8,128)S(1)}, u32[]{:S(2)}, u32[]{:S(2)}) collective-permute-start(f32[5,1,64,128]{3,2,1,0:T(8,128)S(1)} %get-tuple-element.5), channel_id=1, source_target_pairs={{0,3},{1,4},{2,5},{3,6},{4,7},{5,8},{6,9},{7,10},{8,11},{9,12},{10... | collective-permute-start | bytes 491528 | tf_op jit(solution)/shard_map/ppermute | solution.py:160
  131.3 23.5 %collective-permute-start.19 = (f32[5,1,64,128]{3,2,1,0:T(8,128)S(1)}, f32[5,1,64,128]{3,2,1,0:T(8,128)S(1)}, u32[]{:S(2)}, u32[]{:S(2)}) collective-permute-start(f32[5,1,64,128]{3,2,1,0:T(8,128)S(1)} %collective-permute-done.18), channel_id=1, source_target_pairs={{1,18},{3,17},{4,16},{17,34},{19,33},{20,32},{33,50},{35,49},{36,4... | collective-permute-start | bytes 491528 | tf_op jit(solution)/shard_map/ppermute | solution.py:163
  132.7 24.7 %collective-permute-start.22 = (f32[5,1,64,128]{3,2,1,0:T(8,128)S(1)}, f32[5,1,64,128]{3,2,1,0:T(8,128)S(1)}, u32[]{:S(2)}, u32[]{:S(2)}) collective-permute-start(f32[5,1,64,128]{3,2,1,0:T(8,128)S(1)} %get-tuple-element.5), channel_id=1, source_target_pairs={{0,2},{1,3},{2,4},{3,5},{4,6},{5,7},{6,8},{7,9},{8,10},{9,11},{10,... | collective-permute-start | bytes 491528 | tf_op jit(solution)/shard_map/ppermute | solution.py:160
  137.6 22.1 %collective-permute-start.24 = (f32[5,1,64,128]{3,2,1,0:T(8,128)S(1)}, f32[5,1,64,128]{3,2,1,0:T(8,128)S(1)}, u32[]{:S(2)}, u32[]{:S(2)}) collective-permute-start(f32[5,1,64,128]{3,2,1,0:T(8,128)S(1)} %get-tuple-element.5), channel_id=1, source_target_pairs={{0,1},{1,2},{2,3},{3,4},{4,5},{5,6},{6,7},{7,8},{8,9},{9,10},{10,1... | collective-permute-start | bytes 491528 | tf_op jit(solution)/shard_map/ppermute | solution.py:160
  154.8 4.8 %collective-permute-start.21 = (f32[5,1,64,128]{3,2,1,0:T(8,128)S(1)}, f32[5,1,64,128]{3,2,1,0:T(8,128)S(1)}, u32[]{:S(2)}, u32[]{:S(2)}) collective-permute-start(f32[5,1,64,128]{3,2,1,0:T(8,128)S(1)} %collective-permute-done.19), channel_id=1, source_target_pairs={{1,0},{2,1},{17,16},{18,17},{33,32},{34,33},{49,48},{50,49},{65,64... | collective-permute-start | bytes 491528 | tf_op jit(solution)/shard_map/ppermute | solution.py:176
  156.1 9.3 %collective-permute-start.23 = (f32[5,1,64,128]{3,2,1,0:T(8,128)S(1)}, f32[5,1,64,128]{3,2,1,0:T(8,128)S(1)}, u32[]{:S(2)}, u32[]{:S(2)}) collective-permute-start(f32[5,1,64,128]{3,2,1,0:T(8,128)S(1)} %collective-permute-done.19), channel_id=1, source_target_pairs={{2,0},{18,16},{34,32},{50,48},{66,64},{82,80},{98,96},{114,112},{1... | collective-permute-start | bytes 491528 | tf_op jit(solution)/shard_map/ppermute | solution.py:176

commit v5 on v4

--- a/solution.py
+++ b/solution.py
@@ -6,6 +6,7 @@
 STEPS = 3
 SMAX = 192
 PLANE = 16
+GROUP = 4
 
 
 courant = 0.2
@@ -178,17 +179,68 @@
     return pieces
 
 
+def in_group(value, delta, group):
+    count = lax.axis_size("azi")
+    pairs = [(a, a - a % group + (a % group + delta) % group) for a in range(count)]
+    return lax.ppermute(value, "azi", pairs)
+
+
+def by_source(received, seat, group):
+    stacked = jnp.stack(received)
+    return [
+        lax.dynamic_index_in_dim(stacked, (seat - p) % group, keepdims=False)
+        for p in range(group)
+    ]
+
+
+def regroup(wide, wide_shifts, cells, rows, width, group):
+    seat = lax.axis_index("azi") % group
+    part = rows // group
+    span = part + 2 * width
+    received = []
+    for delta in range(group):
+        target = (seat + delta) % group
+        piece = lax.dynamic_slice_in_dim(wide, target * part, span, axis=3)
+        received.append(piece if delta == 0 else in_group(piece, delta, group))
+    pieces = by_source(received, seat, group)
+    cut = [pieces[0][:, :, : cells + width]]
+    cut += [p[:, :, width : cells + width] for p in pieces[1:-1]]
+    cut.append(pieces[-1][:, :, width:])
+    grouped = jnp.concatenate(cut, axis=2)
+    grouped_shifts = lax.dynamic_slice_in_dim(wide_shifts, seat * part, span, axis=1)
+    return grouped, grouped_shifts
+
+
+def ungroup(out, cells, group):
+    seat = lax.axis_index("azi") % group
+    received = []
+    for delta in range(group):
+        target = (seat + delta) % group
+        piece = lax.dynamic_slice_in_dim(out, target * cells, cells, axis=2)
+        received.append(piece if delta == 0 else in_group(piece, delta, group))
+    return jnp.concatenate(by_source(received, seat, group), axis=3)
+
+
 def local(fields, shifts):
     cells = fields.shape[2]
     rows = fields.shape[3]
+    count = lax.axis_size("azi")
     total_rows = rows * lax.axis_size("rad")
     width = STEPS
     wide, wide_shifts = halo_exchange(fields, shifts, width)
+    group = GROUP
+    if count % group or rows % group or group * cells < SMAX:
+        group = 1
     start_row = lax.axis_index("rad") * rows
-    blocks = (SMAX + cells - 1) // cells
+    if group > 1:
+        wide, wide_shifts = regroup(wide, wide_shifts, cells, rows, width, group)
+        start_row = start_row + lax.axis_index("azi") % group * (rows // group)
+    span = cells * group
+    sub_rows = rows // group
+    blocks = (SMAX + span - 1) // span
     for step in range(STEPS):
         w = width - step
-        row_index = start_row - w + jnp.arange(rows + 2 * w, dtype=jnp.int32)
+        row_index = start_row - w + jnp.arange(sub_rows + 2 * w, dtype=jnp.int32)
         inside = (row_index >= 0) & (row_index < total_rows)
         wide = jnp.where(inside[None, None, None, :], wide, 0.0)
         inner_rows = row_index[1:-1]
@@ -196,12 +248,19 @@
         inverse = 1.0 / radius
         updated = update(wide, inverse)
         a = w - 1
-        head = updated[:, :, :cells]
-        pieces = rotation_pieces(head, PLANE, blocks)
-        window = jnp.concatenate(pieces[::-1] + [updated], axis=2)
-        window = window[:, :, blocks * cells - SMAX :]
+        if group > 1:
+            head = updated[:, :, blocks * span - SMAX : span]
+            pieces = [passed_along(head, "azi", group * k) for k in range(1, blocks + 1)]
+            window = jnp.concatenate(pieces[::-1] + [updated], axis=2)
+        else:
+            head = updated[:, :, :span]
+            pieces = rotation_pieces(head, PLANE, blocks)
+            window = jnp.concatenate(pieces[::-1] + [updated], axis=2)
+            window = window[:, :, blocks * span - SMAX :]
         wide_shifts = wide_shifts[:, 1:-1]
-        wide = rotate_window(window, wide_shifts[step], cells + 2 * a)
+        wide = rotate_window(window, wide_shifts[step], span + 2 * a)
+    if group > 1:
+        wide = ungroup(wide, cells, group)
     return wide
 
 

time: 167 us -> 187 us (1.12)
  the two profiles are of different devices: /device:TPU:64 before, /device:TPU:72 now
where the time goes in v5:
time: 187 us
  waiting for transfers between devices  78.3 us (42%)
  starting transfers between devices  73.7 us (39%)
  other arithmetic  26.2 us (14%)
  local copies, waits for them, and re-layouts  7.62 us (4%)
    ppermute x7, waiting for transfers between devices, passed_along(): return lax.ppermute(value, axis, pairs)  69.6 us
    ppermute x6, starting transfers between devices, in_group(): return lax.ppermute(value, 'azi', pairs)  48.5 us
    ppermute x7, starting transfers between devices, passed_along(): return lax.ppermute(value, axis, pairs)  25.2 us
    ppermute x6, waiting for transfers between devices, in_group(): return lax.ppermute(value, 'azi', pairs)  8.65 us
    select_n x22, other arithmetic, rotate_window(): jnp.where(chosen[None, None, None, :], window[:, :, amount:], window[:, :...  8.56 us
    add x3, other arithmetic, update(): outer + inner - 2.0 * centre  5.48 us
  transfers between devices with their start and end apart: 13, of which 9 were waited for; matrix products, arithmetic and copies ran while one was open for 1% of the time, Pallas kernels for 0%

profile of v5, /device:TPU:72, one launch (start us, length us, event | category | flops | bytes accessed | tf_op | source)
XLA Modules:
  0.0 186.6 jit_solution(5670131505231135944)
XLA Ops:
  0.0 0.7 fusion.105
  0.8 1.9 %collective-permute-start.1 = (f32[5,1,3,128]{3,2,1,0:T(4,128)S(1)}, f32[5,1,3,128]{3,2,1,0:T(4,128)S(1)}, u32[]{:S(2)}, u32[]{:S(2)}) collective-permute-start(f32[5,1,3,128]{3,2,1,0:T(4,128)S(1)} %get-tuple-element.53), channel_id=1, source_target_pairs={{0,127},{1,0},{2,1},{3,2},{4,3},{5,4},{6,5},{7,6},{8,7},{9,8},{10,... | collective-permute-start | bytes 23048 | tf_op jit(solution)/shard_map/ppermute | solution.py:26
  2.7 2.4 %collective-permute-start = (f32[5,1,3,128]{3,2,1,0:T(4,128)S(1)}, f32[5,1,3,128]{3,2,1,0:T(4,128)S(1)}, u32[]{:S(2)}, u32[]{:S(2)}) collective-permute-start(f32[5,1,3,128]{3,2,1,0:T(4,128)S(1)} %get-tuple-element.52), channel_id=1, source_target_pairs={{0,1},{1,2},{2,3},{3,4},{4,5},{5,6},{6,7},{7,8},{8,9},{9,10},{10,1... | collective-permute-start | bytes 23048 | tf_op jit(solution)/shard_map/ppermute | solution.py:26
  5.2 0.6 copy-done.1
  6.7 1.0 collective-permute-done
  7.8 0.2 reshape.1283
  8.1 13.0 %collective-permute-start.3 = (f32[1059]{0:T(1024)S(1)}, f32[1059]{0:T(1024)S(1)}, u32[]{:S(2)}, u32[]{:S(2)}) collective-permute-start(f32[1059]{0:T(1024)S(1)} %pad_maximum_fusion.6), channel_id=1, source_target_pairs={{128,0},{256,128},{384,256},{512,384},{640,512},{768,640},{896,768... | collective-permute-start | bytes 12716 | tf_op jit(solution)/shard_map/ppermute | solution.py:26
  21.1 0.2 reshape.1281
  21.4 1.9 %collective-permute-start.2 = (f32[1059]{0:T(1024)S(1)}, f32[1059]{0:T(1024)S(1)}, u32[]{:S(2)}, u32[]{:S(2)}) collective-permute-start(f32[1059]{0:T(1024)S(1)} %pad_maximum_fusion.5), channel_id=1, source_target_pairs={{0,128},{128,256},{256,384},{384,512},{512,640},{640,768},{768,896... | collective-permute-start | bytes 12716 | tf_op jit(solution)/shard_map/ppermute | solution.py:26
  23.5 3.4 %collective-permute-done.2 = f32[1059]{0:T(1024)S(1)} collective-permute-done((f32[1059]{0:T(1024)S(1)}, f32[1059]{0:T(1024)S(1)}, u32[]{:S(2)}, u32[]{:S(2)}) %collective-permute-start.2) | collective-permute-done | bytes 4268 | tf_op jit(solution)/shard_map/ppermute | solution.py:26
  27.1 0.2 reshape.1286
  27.5 0.2 pad_maximum_fusion.1
  27.9 9.1 %collective-permute-start.6 = (f32[5,1,70,38]{3,2,1,0:T(8,128)S(1)}, f32[5,1,70,38]{3,2,1,0:T(8,128)S(1)}, u32[]{:S(2)}, u32[]{:S(2)}) collective-permute-start(f32[5,1,70,38]{3,2,1,0:T(8,128)S(1)} %get-tuple-element.18), channel_id=1, source_target_pairs={{0,3},{1,0},{2,1},{3,2},{4,7},{5,4},{6,5},{7,6},{8,11},{9,8},{10,9... | collective-permute-start | bytes 159608 | tf_op jit(solution)/shard_map/ppermute | solution.py:185
  37.0 0.2 fusion.106
  37.5 18.6 %collective-permute-start.5 = (f32[5,1,70,38]{3,2,0,1:T(8,128)S(1)}, f32[5,1,70,38]{3,2,0,1:T(8,128)S(1)}, u32[]{:S(2)}, u32[]{:S(2)}) collective-permute-start(f32[5,1,70,38]{3,2,0,1:T(8,128)S(1)} %get-tuple-element.20), channel_id=1, source_target_pairs={{0,2},{1,3},{2,0},{3,1},{4,6},{5,7},{6,4},{7,5},{8,10},{9,11},{10,... | collective-permute-start | bytes 159608 | tf_op jit(solution)/shard_map/ppermute | solution.py:185
  56.1 2.1 %collective-permute-start.4 = (f32[5,1,70,38]{3,2,0,1:T(8,128)S(1)}, f32[5,1,70,38]{3,2,0,1:T(8,128)S(1)}, u32[]{:S(2)}, u32[]{:S(2)}) collective-permute-start(f32[5,1,70,38]{3,2,0,1:T(8,128)S(1)} %get-tuple-element.19), channel_id=1, source_target_pairs={{0,1},{1,2},{2,3},{3,0},{4,5},{5,6},{6,7},{7,4},{8,9},{9,10},{10,1... | collective-permute-start | bytes 159608 | tf_op jit(solution)/shard_map/ppermute | solution.py:185
  58.3 3.3 %collective-permute-done.5 = f32[5,1,70,38]{3,2,0,1:T(8,128)S(1)} collective-permute-done((f32[5,1,70,38]{3,2,0,1:T(8,128)S(1)}, f32[5,1,70,38]{3,2,0,1:T(8,128)S(1)}, u32[]{:S(2)}, u32[]{:S(2)}) %collective-permute-start.5) | collective-permute-done | bytes 53232 | tf_op jit(solution)/shard_map/ppermute | solution.py:185
  61.5 1.8 collective-permute-done.4
  63.6 0.3 slice.632
  64.0 0.3 slice.631
  64.4 0.3 slice.630
  64.8 1.3 broadcast_select_fusion.7
  66.2 0.3 broadcast_maximum_fusion.1
  66.5 1.2 subtract_multiply_fusion.1
  67.7 2.6 %subtract_add_fusion = (f32[5,1,260,36]{2,1,3,0:T(1,128)S(1)}, f32[5,1,260,36]{2,1,3,0:T(1,128)S(1)}, f32[5,1,260,36]{2,1,3,0:T(1,128)S(1)}) fusion(f32[5,1,262,38]{2,1,3,0:T(1,128)S(1)} %broadcast_select_fusion.7, f32[36]{0:T(128)S(1)} %get-tuple-element.85, f32[260,36]{0,1:T(8,128)S(1)} %get-tuple-element.87, f32[260,36]{0,1:T(8,128)S(1)} %get-tuple-element.88, ...), kind=kLoop, calls=%fused_computation.32 | loop fusion | flops 1170000 | bytes 1647648 | tf_op jit(solution)/shard_map/add | solution.py:49
  70.3 0.2 fusion.17
  70.5 0.5 fusion.3
  71.0 0.5 fusion.10
  71.5 0.2 fusion.8
  71.7 0.3 fusion.5
  72.0 0.4 slice.658
  72.4 2.1 %collective-permute-start.7 = (f32[5,1,192,36]{2,1,3,0:T(1,128)S(1)}, f32[5,1,192,36]{2,1,3,0:T(1,128)S(1)}, u32[]{:S(2)}, u32[]{:S(2)}) collective-permute-start(f32[5,1,192,36]{2,1,3,0:T(1,128)S(1)} %slice.658), channel_id=1, source_target_pairs={{0,4},{1,5},{2,6},{3,7},{4,8},{5,9},{6,10},{7,11},{8,12},{9,13},{1... | collective-permute-start | bytes 414728 | tf_op jit(solution)/shard_map/ppermute | solution.py:26
  74.6 26.9 %collective-permute-done.7 = f32[5,1,192,36]{2,1,3,0:T(1,128)S(1)} collective-permute-done((f32[5,1,192,36]{2,1,3,0:T(1,128)S(1)}, f32[5,1,192,36]{2,1,3,0:T(1,128)S(1)}, u32[]{:S(2)}, u32[]{:S(2)}) %collective-permute-start.7) | collective-permute-done | bytes 138272 | tf_op jit(solution)/shard_map/ppermute | solution.py:26
  101.5 0.8 maximum_maximum_fusion
  102.4 1.1 broadcast_select_fusion
  103.4 0.9 broadcast_select_fusion.1
  104.3 0.9 broadcast_select_fusion.2
  105.2 0.9 broadcast_select_fusion.3
  106.0 0.9 broadcast_select_fusion.4
  106.9 0.9 broadcast_select_fusion.5
  107.8 0.9 broadcast_select_fusion.6
  108.6 0.4 broadcast_select_fusion.9
  109.0 0.3 broadcast_maximum_fusion.3
  109.3 1.1 subtract_multiply_fusion.3
  110.5 2.7 %subtract_add_fusion.1 = (f32[5,1,258,34]{2,1,3,0:T(1,128)S(1)}, f32[5,1,258,34]{2,1,3,0:T(1,128)S(1)}, f32[5,1,258,34]{2,1,3,0:T(1,128)S(1)}) fusion(f32[5,1,260,36]{2,1,3,0:T(1,128)S(1)} %broadcast_select_fusion.9, f32[34]{0:T(128)S(1)} %get-tuple-element.83, f32[258,34]{0,1:T(8,128)S(1)} %bitcast.227, f32[258,34]{0,1:T(8,128)S(1)} %bitcast.228, ...), kind=kLoop, calls=%fused_computation.37 | loop fusion | flops 1096500 | bytes 1544144 | tf_op jit(solution)/shard_map/add | solution.py:49
  113.2 0.2 fusion.34
  113.4 0.5 fusion.20
  113.9 0.5 fusion.27
  114.4 0.2 fusion.25
  114.6 0.2 fusion.22
  114.8 0.4 slice.700
  115.2 1.9 %collective-permute-start.8 = (f32[5,1,192,34]{2,1,3,0:T(1,128)S(1)}, f32[5,1,192,34]{2,1,3,0:T(1,128)S(1)}, u32[]{:S(2)}, u32[]{:S(2)}) collective-permute-start(f32[5,1,192,34]{2,1,3,0:T(1,128)S(1)} %slice.700), channel_id=1, source_target_pairs={{0,4},{1,5},{2,6},{3,7},{4,8},{5,9},{6,10},{7,11},{8,12},{9,13},{1... | collective-permute-start | bytes 391688 | tf_op jit(solution)/shard_map/ppermute | solution.py:26
  117.3 19.3 %collective-permute-done.8 = f32[5,1,192,34]{2,1,3,0:T(1,128)S(1)} collective-permute-done((f32[5,1,192,34]{2,1,3,0:T(1,128)S(1)}, f32[5,1,192,34]{2,1,3,0:T(1,128)S(1)}, u32[]{:S(2)}, u32[]{:S(2)}) %collective-permute-start.8) | collective-permute-done | bytes 130592 | tf_op jit(solution)/shard_map/ppermute | solution.py:26
  136.6 0.8 maximum_maximum_fusion.1
  137.4 0.9 fusion.103
  139.9 0.3 subtract_add_fusion.2
  140.8 1.9 %collective-permute-start.9 = (f32[5,1,192,32]{2,3,1,0:T(8,128)S(1)}, f32[5,1,192,32]{2,3,1,0:T(8,128)S(1)}, u32[]{:S(2)}, u32[]{:S(2)}) collective-permute-start(f32[5,1,192,32]{2,3,1,0:T(8,128)S(1)} %slice.742), channel_id=1, source_target_pairs={{0,4},{1,5},{2,6},{3,7},{4,8},{5,9},{6,10},{7,11},{8,12},{9,13},{1... | collective-permute-start | bytes 368648 | tf_op jit(solution)/shard_map/ppermute | solution.py:26
  142.8 19.0 %collective-permute-done.9 = f32[5,1,192,32]{2,3,1,0:T(8,128)S(1)} collective-permute-done((f32[5,1,192,32]{2,3,1,0:T(8,128)S(1)}, f32[5,1,192,32]{2,3,1,0:T(8,128)S(1)}, u32[]{:S(2)}, u32[]{:S(2)}) %collective-permute-start.9) | collective-permute-done | bytes 122912 | tf_op jit(solution)/shard_map/ppermute | solution.py:26
  163.4 1.9 %collective-permute-start.12 = (f32[5,1,64,32]{2,3,0,1:T(8,128)S(1)}, f32[5,1,64,32]{2,3,0,1:T(8,128)S(1)}, u32[]{:S(2)}, u32[]{:S(2)}) collective-permute-start(f32[5,1,64,32]{2,3,0,1:T(8,128)S(1)} %get-tuple-element.49), channel_id=1, source_target_pairs={{0,3},{1,0},{2,1},{3,2},{4,7},{5,4},{6,5},{7,6},{8,11},{9,8},{10,9... | collective-permute-start | bytes 122888 | tf_op jit(solution)/shard_map/ppermute | solution.py:185
  165.3 14.6 %collective-permute-start.11 = (f32[5,1,64,32]{2,3,0,1:T(8,128)S(1)}, f32[5,1,64,32]{2,3,0,1:T(8,128)S(1)}, u32[]{:S(2)}, u32[]{:S(2)}) collective-permute-start(f32[5,1,64,32]{2,3,0,1:T(8,128)S(1)} %get-tuple-element.50), channel_id=1, source_target_pairs={{0,2},{1,3},{2,0},{3,1},{4,6},{5,7},{6,4},{7,5},{8,10},{9,11},{10,... | collective-permute-start | bytes 122888 | tf_op jit(solution)/shard_map/ppermute | solution.py:185
  179.9 2.1 %collective-permute-start.10 = (f32[5,1,64,32]{2,3,0,1:T(8,128)S(1)}, f32[5,1,64,32]{2,3,0,1:T(8,128)S(1)}, u32[]{:S(2)}, u32[]{:S(2)}) collective-permute-start(f32[5,1,64,32]{2,3,0,1:T(8,128)S(1)} %get-tuple-element.51), channel_id=1, source_target_pairs={{0,1},{1,2},{2,3},{3,0},{4,5},{5,6},{6,7},{7,4},{8,9},{9,10},{10,1... | collective-permute-start | bytes 122888 | tf_op jit(solution)/shard_map/ppermute | solution.py:185
  182.1 0.9 collective-permute-done.11
  183.0 2.7 %collective-permute-done.10 = f32[5,1,64,32]{2,3,0,1:T(8,128)S(1)} collective-permute-done((f32[5,1,64,32]{2,3,0,1:T(8,128)S(1)}, f32[5,1,64,32]{2,3,0,1:T(8,128)S(1)}, u32[]{:S(2)}, u32[]{:S(2)}) %collective-permute-start.10) | collective-permute-done | bytes 40992 | tf_op jit(solution)/shard_map/ppermute | solution.py:185
  185.8 0.8 copy.56
  (81 shorter events, 6.6 us)
Async XLA Ops:
  0.8 5.9 %collective-permute-start.1 = (f32[5,1,3,128]{3,2,1,0:T(4,128)S(1)}, f32[5,1,3,128]{3,2,1,0:T(4,128)S(1)}, u32[]{:S(2)}, u32[]{:S(2)}) collective-permute-start(f32[5,1,3,128]{3,2,1,0:T(4,128)S(1)} %get-tuple-element.53), channel_id=1, source_target_pairs={{0,127},{1,0},{2,1},{3,2},{4,3},{5,4},{6,5},{7,6},{8,7},{9,8},{10,... | collective-permute-start | bytes 23048 | tf_op jit(solution)/shard_map/ppermute | solution.py:26
  2.7 5.0 %collective-permute-start = (f32[5,1,3,128]{3,2,1,0:T(4,128)S(1)}, f32[5,1,3,128]{3,2,1,0:T(4,128)S(1)}, u32[]{:S(2)}, u32[]{:S(2)}) collective-permute-start(f32[5,1,3,128]{3,2,1,0:T(4,128)S(1)} %get-tuple-element.52), channel_id=1, source_target_pairs={{0,1},{1,2},{2,3},{3,4},{4,5},{5,6},{6,7},{7,8},{8,9},{9,10},{10,1... | collective-permute-start | bytes 23048 | tf_op jit(solution)/shard_map/ppermute | solution.py:26
  5.1 0.7 copy-start.1
  5.1 2.6 %copy-start = (f32[5,1,64,128]{3,2,1,0:T(8,128)S(1)}, f32[5,1,64,128]{3,2,1,0:T(8,128)}, u32[]{:S(2)}) copy-start(f32[5,1,64,128]{3,2,1,0:T(8,128)} %param.2) | copy-start | bytes 491524
  8.1 15.2 %collective-permute-start.3 = (f32[1059]{0:T(1024)S(1)}, f32[1059]{0:T(1024)S(1)}, u32[]{:S(2)}, u32[]{:S(2)}) collective-permute-start(f32[1059]{0:T(1024)S(1)} %pad_maximum_fusion.6), channel_id=1, source_target_pairs={{128,0},{256,128},{384,256},{512,384},{640,512},{768,640},{896,768... | collective-permute-start | bytes 12716 | tf_op jit(solution)/shard_map/ppermute | solution.py:26
  21.4 5.5 %collective-permute-start.2 = (f32[1059]{0:T(1024)S(1)}, f32[1059]{0:T(1024)S(1)}, u32[]{:S(2)}, u32[]{:S(2)}) collective-permute-start(f32[1059]{0:T(1024)S(1)} %pad_maximum_fusion.5), channel_id=1, source_target_pairs={{0,128},{128,256},{256,384},{384,512},{512,640},{640,768},{768,896... | collective-permute-start | bytes 12716 | tf_op jit(solution)/shard_map/ppermute | solution.py:26
  27.9 30.4 %collective-permute-start.6 = (f32[5,1,70,38]{3,2,1,0:T(8,128)S(1)}, f32[5,1,70,38]{3,2,1,0:T(8,128)S(1)}, u32[]{:S(2)}, u32[]{:S(2)}) collective-permute-start(f32[5,1,70,38]{3,2,1,0:T(8,128)S(1)} %get-tuple-element.18), channel_id=1, source_target_pairs={{0,3},{1,0},{2,1},{3,2},{4,7},{5,4},{6,5},{7,6},{8,11},{9,8},{10,9... | collective-permute-start | bytes 159608 | tf_op jit(solution)/shard_map/ppermute | solution.py:185
  37.5 24.1 %collective-permute-start.5 = (f32[5,1,70,38]{3,2,0,1:T(8,128)S(1)}, f32[5,1,70,38]{3,2,0,1:T(8,128)S(1)}, u32[]{:S(2)}, u32[]{:S(2)}) collective-permute-start(f32[5,1,70,38]{3,2,0,1:T(8,128)S(1)} %get-tuple-element.20), channel_id=1, source_target_pairs={{0,2},{1,3},{2,0},{3,1},{4,6},{5,7},{6,4},{7,5},{8,10},{9,11},{10,... | collective-permute-start | bytes 159608 | tf_op jit(solution)/shard_map/ppermute | solution.py:185
  56.1 7.3 %collective-permute-start.4 = (f32[5,1,70,38]{3,2,0,1:T(8,128)S(1)}, f32[5,1,70,38]{3,2,0,1:T(8,128)S(1)}, u32[]{:S(2)}, u32[]{:S(2)}) collective-permute-start(f32[5,1,70,38]{3,2,0,1:T(8,128)S(1)} %get-tuple-element.19), channel_id=1, source_target_pairs={{0,1},{1,2},{2,3},{3,0},{4,5},{5,6},{6,7},{7,4},{8,9},{9,10},{10,1... | collective-permute-start | bytes 159608 | tf_op jit(solution)/shard_map/ppermute | solution.py:185
  72.4 29.1 %collective-permute-start.7 = (f32[5,1,192,36]{2,1,3,0:T(1,128)S(1)}, f32[5,1,192,36]{2,1,3,0:T(1,128)S(1)}, u32[]{:S(2)}, u32[]{:S(2)}) collective-permute-start(f32[5,1,192,36]{2,1,3,0:T(1,128)S(1)} %slice.658), channel_id=1, source_target_pairs={{0,4},{1,5},{2,6},{3,7},{4,8},{5,9},{6,10},{7,11},{8,12},{9,13},{1... | collective-permute-start | bytes 414728 | tf_op jit(solution)/shard_map/ppermute | solution.py:26
  115.2 21.4 %collective-permute-start.8 = (f32[5,1,192,34]{2,1,3,0:T(1,128)S(1)}, f32[5,1,192,34]{2,1,3,0:T(1,128)S(1)}, u32[]{:S(2)}, u32[]{:S(2)}) collective-permute-start(f32[5,1,192,34]{2,1,3,0:T(1,128)S(1)} %slice.700), channel_id=1, source_target_pairs={{0,4},{1,5},{2,6},{3,7},{4,8},{5,9},{6,10},{7,11},{8,12},{9,13},{1... | collective-permute-start | bytes 391688 | tf_op jit(solution)/shard_map/ppermute | solution.py:26
  140.8 21.0 %collective-permute-start.9 = (f32[5,1,192,32]{2,3,1,0:T(8,128)S(1)}, f32[5,1,192,32]{2,3,1,0:T(8,128)S(1)}, u32[]{:S(2)}, u32[]{:S(2)}) collective-permute-start(f32[5,1,192,32]{2,3,1,0:T(8,128)S(1)} %slice.742), channel_id=1, source_target_pairs={{0,4},{1,5},{2,6},{3,7},{4,8},{5,9},{6,10},{7,11},{8,12},{9,13},{1... | collective-permute-start | bytes 368648 | tf_op jit(solution)/shard_map/ppermute | solution.py:26
  163.4 18.7 %collective-permute-start.12 = (f32[5,1,64,32]{2,3,0,1:T(8,128)S(1)}, f32[5,1,64,32]{2,3,0,1:T(8,128)S(1)}, u32[]{:S(2)}, u32[]{:S(2)}) collective-permute-start(f32[5,1,64,32]{2,3,0,1:T(8,128)S(1)} %get-tuple-element.49), channel_id=1, source_target_pairs={{0,3},{1,0},{2,1},{3,2},{4,7},{5,4},{6,5},{7,6},{8,11},{9,8},{10,9... | collective-permute-start | bytes 122888 | tf_op jit(solution)/shard_map/ppermute | solution.py:185
  165.3 17.7 %collective-permute-start.11 = (f32[5,1,64,32]{2,3,0,1:T(8,128)S(1)}, f32[5,1,64,32]{2,3,0,1:T(8,128)S(1)}, u32[]{:S(2)}, u32[]{:S(2)}) collective-permute-start(f32[5,1,64,32]{2,3,0,1:T(8,128)S(1)} %get-tuple-element.50), channel_id=1, source_target_pairs={{0,2},{1,3},{2,0},{3,1},{4,6},{5,7},{6,4},{7,5},{8,10},{9,11},{10,... | collective-permute-start | bytes 122888 | tf_op jit(solution)/shard_map/ppermute | solution.py:185
  179.9 5.8 %collective-permute-start.10 = (f32[5,1,64,32]{2,3,0,1:T(8,128)S(1)}, f32[5,1,64,32]{2,3,0,1:T(8,128)S(1)}, u32[]{:S(2)}, u32[]{:S(2)}) collective-permute-start(f32[5,1,64,32]{2,3,0,1:T(8,128)S(1)} %get-tuple-element.51), channel_id=1, source_target_pairs={{0,1},{1,2},{2,3},{3,0},{4,5},{5,6},{6,7},{7,4},{8,9},{9,10},{10,1... | collective-permute-start | bytes 122888 | tf_op jit(solution)/shard_map/ppermute | solution.py:185

commit v6 on v5

--- a/solution.py
+++ b/solution.py
@@ -26,12 +26,19 @@
     return lax.ppermute(value, axis, pairs)
 
 
-def update(padded, inverse):
+def update(padded, inverse, cells_last=False):
     centre = padded[:, :, 1:-1, 1:-1]
-    inner = padded[:, :, 1:-1, :-2]
-    outer = padded[:, :, 1:-1, 2:]
-    behind = padded[:, :, :-2, 1:-1]
-    ahead = padded[:, :, 2:, 1:-1]
+    if cells_last:
+        inner = padded[:, :, :-2, 1:-1]
+        outer = padded[:, :, 2:, 1:-1]
+        behind = padded[:, :, 1:-1, :-2]
+        ahead = padded[:, :, 1:-1, 2:]
+        inverse = inverse[:, None]
+    else:
+        inner = padded[:, :, 1:-1, :-2]
+        outer = padded[:, :, 1:-1, 2:]
+        behind = padded[:, :, :-2, 1:-1]
+        ahead = padded[:, :, 2:, 1:-1]
     polar_pad = jnp.concatenate([centre[:, :1], centre, centre[:, -1:]], axis=1)
     polar_sum = polar_pad[:, 2:] + polar_pad[:, :-2]
     radial_vel = centre[1]
@@ -106,21 +113,26 @@
     return wide, wide_shifts
 
 
-def rotate_window(window, offsets, out_len):
+def rotate_window(window, offsets, out_len, axis=2):
     take = SMAX - offsets
     nbits = SMAX.bit_length()
-    spare = (1 << nbits) - 1 + out_len - window.shape[2]
+    spare = (1 << nbits) - 1 + out_len - window.shape[axis]
     if spare > 0:
-        pad = jnp.zeros(window.shape[:2] + (spare,) + window.shape[3:], window.dtype)
-        window = jnp.concatenate([window, pad], axis=2)
+        shape = list(window.shape)
+        shape[axis] = spare
+        pad = jnp.zeros(shape, window.dtype)
+        window = jnp.concatenate([window, pad], axis=axis)
     for bit in range(nbits):
         amount = 1 << bit
-        length = window.shape[2] - amount
+        length = window.shape[axis] - amount
         chosen = take // amount % 2 == 1
+        chosen = chosen[None, None, None, :] if axis == 2 else chosen[None, None, :, None]
         window = jnp.where(
-            chosen[None, None, None, :], window[:, :, amount:], window[:, :, :length]
+            chosen,
+            lax.slice_in_dim(window, amount, amount + length, axis=axis),
+            lax.slice_in_dim(window, 0, length, axis=axis),
         )
-    return window[:, :, :out_len]
+    return lax.slice_in_dim(window, 0, out_len, axis=axis)
 
 
 def relay_seat(lane, source, plane, blocks):
@@ -235,6 +247,7 @@
     if group > 1:
         wide, wide_shifts = regroup(wide, wide_shifts, cells, rows, width, group)
         start_row = start_row + lax.axis_index("azi") % group * (rows // group)
+        wide = jnp.swapaxes(wide, 2, 3)
     span = cells * group
     sub_rows = rows // group
     blocks = (SMAX + span - 1) // span
@@ -242,25 +255,29 @@
         w = width - step
         row_index = start_row - w + jnp.arange(sub_rows + 2 * w, dtype=jnp.int32)
         inside = (row_index >= 0) & (row_index < total_rows)
-        wide = jnp.where(inside[None, None, None, :], wide, 0.0)
         inner_rows = row_index[1:-1]
         radius = 1.0 + (inner_rows.astype(jnp.float32) + 0.5) / jnp.float32(total_rows)
         inverse = 1.0 / radius
-        updated = update(wide, inverse)
         a = w - 1
         if group > 1:
-            head = updated[:, :, blocks * span - SMAX : span]
+            wide = jnp.where(inside[None, None, :, None], wide, 0.0)
+            updated = update(wide, inverse, cells_last=True)
+            head = updated[:, :, :, blocks * span - SMAX : span]
             pieces = [passed_along(head, "azi", group * k) for k in range(1, blocks + 1)]
-            window = jnp.concatenate(pieces[::-1] + [updated], axis=2)
-        else:
-            head = updated[:, :, :span]
-            pieces = rotation_pieces(head, PLANE, blocks)
-            window = jnp.concatenate(pieces[::-1] + [updated], axis=2)
-            window = window[:, :, blocks * span - SMAX :]
+            window = jnp.concatenate(pieces[::-1] + [updated], axis=3)
+            wide_shifts = wide_shifts[:, 1:-1]
+            wide = rotate_window(window, wide_shifts[step], span + 2 * a, axis=3)
+            continue
+        wide = jnp.where(inside[None, None, None, :], wide, 0.0)
+        updated = update(wide, inverse)
+        head = updated[:, :, :span]
+        pieces = rotation_pieces(head, PLANE, blocks)
+        window = jnp.concatenate(pieces[::-1] + [updated], axis=2)
+        window = window[:, :, blocks * span - SMAX :]
         wide_shifts = wide_shifts[:, 1:-1]
         wide = rotate_window(window, wide_shifts[step], span + 2 * a)
     if group > 1:
-        wide = ungroup(wide, cells, group)
+        wide = ungroup(jnp.swapaxes(wide, 2, 3), cells, group)
     return wide
 
 

time: 187 us -> 187 us (level)
  no operation moved by 1% of the time
where the time goes in v6:
time: 187 us
  waiting for transfers between devices  78.3 us (42%)
  starting transfers between devices  73.7 us (39%)
  other arithmetic  26.2 us (14%)
  local copies, waits for them, and re-layouts  7.62 us (4%)
    ppermute x7, waiting for transfers between devices, passed_along(): return lax.ppermute(value, axis, pairs)  69.6 us
    ppermute x6, starting transfers between devices, in_group(): return lax.ppermute(value, 'azi', pairs)  48.5 us
    ppermute x7, starting transfers between devices, passed_along(): return lax.ppermute(value, axis, pairs)  25.2 us
    ppermute x6, waiting for transfers between devices, in_group(): return lax.ppermute(value, 'azi', pairs)  8.65 us
    select_n x22, other arithmetic, rotate_window(): jnp.where(chosen, lax.slice_in_dim(window, amount, amount + length, axis=...  8.56 us
    add x3, other arithmetic, update(): outer + inner - 2.0 * centre  5.48 us
  transfers between devices with their start and end apart: 13, of which 9 were waited for; matrix products, arithmetic and copies ran while one was open for 1% of the time, Pallas kernels for 0%

profile of v6, /device:TPU:72, one launch (start us, length us, event | category | flops | bytes accessed | tf_op | source)
XLA Modules:
  0.0 186.6 jit_solution(14955857379841651479)
XLA Ops:
  0.0 0.7 fusion.106
  0.8 1.9 %collective-permute-start.1 = (f32[5,1,3,128]{3,2,1,0:T(4,128)S(1)}, f32[5,1,3,128]{3,2,1,0:T(4,128)S(1)}, u32[]{:S(2)}, u32[]{:S(2)}) collective-permute-start(f32[5,1,3,128]{3,2,1,0:T(4,128)S(1)} %get-tuple-element.53), channel_id=1, source_target_pairs={{0,127},{1,0},{2,1},{3,2},{4,3},{5,4},{6,5},{7,6},{8,7},{9,8},{10,... | collective-permute-start | bytes 23048 | tf_op jit(solution)/shard_map/ppermute | solution.py:26
  2.7 2.4 %collective-permute-start = (f32[5,1,3,128]{3,2,1,0:T(4,128)S(1)}, f32[5,1,3,128]{3,2,1,0:T(4,128)S(1)}, u32[]{:S(2)}, u32[]{:S(2)}) collective-permute-start(f32[5,1,3,128]{3,2,1,0:T(4,128)S(1)} %get-tuple-element.52), channel_id=1, source_target_pairs={{0,1},{1,2},{2,3},{3,4},{4,5},{5,6},{6,7},{7,8},{8,9},{9,10},{10,1... | collective-permute-start | bytes 23048 | tf_op jit(solution)/shard_map/ppermute | solution.py:26
  5.2 0.6 copy-done.1
  6.7 1.0 collective-permute-done
  7.8 0.2 reshape.1189
  8.1 13.0 %collective-permute-start.3 = (f32[1059]{0:T(1024)S(1)}, f32[1059]{0:T(1024)S(1)}, u32[]{:S(2)}, u32[]{:S(2)}) collective-permute-start(f32[1059]{0:T(1024)S(1)} %pad_maximum_fusion.6), channel_id=1, source_target_pairs={{128,0},{256,128},{384,256},{512,384},{640,512},{768,640},{896,768... | collective-permute-start | bytes 12716 | tf_op jit(solution)/shard_map/ppermute | solution.py:26
  21.1 0.2 reshape.1187
  21.4 1.9 %collective-permute-start.2 = (f32[1059]{0:T(1024)S(1)}, f32[1059]{0:T(1024)S(1)}, u32[]{:S(2)}, u32[]{:S(2)}) collective-permute-start(f32[1059]{0:T(1024)S(1)} %pad_maximum_fusion.5), channel_id=1, source_target_pairs={{0,128},{128,256},{256,384},{384,512},{512,640},{640,768},{768,896... | collective-permute-start | bytes 12716 | tf_op jit(solution)/shard_map/ppermute | solution.py:26
  23.5 3.4 %collective-permute-done.2 = f32[1059]{0:T(1024)S(1)} collective-permute-done((f32[1059]{0:T(1024)S(1)}, f32[1059]{0:T(1024)S(1)}, u32[]{:S(2)}, u32[]{:S(2)}) %collective-permute-start.2) | collective-permute-done | bytes 4268 | tf_op jit(solution)/shard_map/ppermute | solution.py:26
  27.1 0.2 reshape.1192
  27.5 0.2 pad_maximum_fusion.1
  27.9 9.1 %collective-permute-start.6 = (f32[5,1,70,38]{3,2,1,0:T(8,128)S(1)}, f32[5,1,70,38]{3,2,1,0:T(8,128)S(1)}, u32[]{:S(2)}, u32[]{:S(2)}) collective-permute-start(f32[5,1,70,38]{3,2,1,0:T(8,128)S(1)} %get-tuple-element.18), channel_id=1, source_target_pairs={{0,3},{1,0},{2,1},{3,2},{4,7},{5,4},{6,5},{7,6},{8,11},{9,8},{10,9... | collective-permute-start | bytes 159608 | tf_op jit(solution)/shard_map/ppermute | solution.py:197
  37.0 0.2 fusion.107
  37.5 18.6 %collective-permute-start.5 = (f32[5,1,70,38]{3,2,0,1:T(8,128)S(1)}, f32[5,1,70,38]{3,2,0,1:T(8,128)S(1)}, u32[]{:S(2)}, u32[]{:S(2)}) collective-permute-start(f32[5,1,70,38]{3,2,0,1:T(8,128)S(1)} %get-tuple-element.20), channel_id=1, source_target_pairs={{0,2},{1,3},{2,0},{3,1},{4,6},{5,7},{6,4},{7,5},{8,10},{9,11},{10,... | collective-permute-start | bytes 159608 | tf_op jit(solution)/shard_map/ppermute | solution.py:197
  56.1 2.1 %collective-permute-start.4 = (f32[5,1,70,38]{3,2,0,1:T(8,128)S(1)}, f32[5,1,70,38]{3,2,0,1:T(8,128)S(1)}, u32[]{:S(2)}, u32[]{:S(2)}) collective-permute-start(f32[5,1,70,38]{3,2,0,1:T(8,128)S(1)} %get-tuple-element.19), channel_id=1, source_target_pairs={{0,1},{1,2},{2,3},{3,0},{4,5},{5,6},{6,7},{7,4},{8,9},{9,10},{10,1... | collective-permute-start | bytes 159608 | tf_op jit(solution)/shard_map/ppermute | solution.py:197
  58.3 3.3 %collective-permute-done.5 = f32[5,1,70,38]{3,2,0,1:T(8,128)S(1)} collective-permute-done((f32[5,1,70,38]{3,2,0,1:T(8,128)S(1)}, f32[5,1,70,38]{3,2,0,1:T(8,128)S(1)}, u32[]{:S(2)}, u32[]{:S(2)}) %collective-permute-start.5) | collective-permute-done | bytes 53232 | tf_op jit(solution)/shard_map/ppermute | solution.py:197
  61.5 1.8 collective-permute-done.4
  63.6 0.3 slice.632
  64.0 0.3 slice.631
  64.4 0.3 slice.630
  64.8 1.3 fusion.1
  66.2 0.3 broadcast_maximum_fusion.1
  66.5 1.2 subtract_multiply_fusion.1
  67.7 2.6 %subtract_add_fusion = (f32[5,1,36,260]{3,1,2,0:T(1,128)S(1)}, f32[5,1,36,260]{3,1,2,0:T(1,128)S(1)}, f32[5,1,36,260]{3,1,2,0:T(1,128)S(1)}) fusion(f32[5,1,38,262]{3,1,2,0:T(1,128)S(1)} %fusion.1, f32[36]{0:T(128)S(1)} %get-tuple-element.85, f32[36,260]{1,0:T(8,128)S(1)} %get-tuple-element.87, f32[36,260]{1,0:T(8,128)S(1)} %get-tuple-element.88, ...), kind=kLoop, calls=%fused_computation.33 | loop fusion | flops 1170000 | bytes 1647648 | tf_op jit(solution)/shard_map/add | solution.py:56
  70.3 0.2 fusion.18
  70.5 0.5 fusion.4
  71.0 0.5 fusion.11
  71.5 0.2 fusion.9
  71.7 0.3 fusion.6
  72.0 0.4 slice.658
  72.4 2.1 %collective-permute-start.7 = (f32[5,1,36,192]{3,1,2,0:T(1,128)S(1)}, f32[5,1,36,192]{3,1,2,0:T(1,128)S(1)}, u32[]{:S(2)}, u32[]{:S(2)}) collective-permute-start(f32[5,1,36,192]{3,1,2,0:T(1,128)S(1)} %slice.658), channel_id=1, source_target_pairs={{0,4},{1,5},{2,6},{3,7},{4,8},{5,9},{6,10},{7,11},{8,12},{9,13},{1... | collective-permute-start | bytes 414728 | tf_op jit(solution)/shard_map/ppermute | solution.py:26
  74.6 26.9 %collective-permute-done.7 = f32[5,1,36,192]{3,1,2,0:T(1,128)S(1)} collective-permute-done((f32[5,1,36,192]{3,1,2,0:T(1,128)S(1)}, f32[5,1,36,192]{3,1,2,0:T(1,128)S(1)}, u32[]{:S(2)}, u32[]{:S(2)}) %collective-permute-start.7) | collective-permute-done | bytes 138272 | tf_op jit(solution)/shard_map/ppermute | solution.py:26
  101.5 0.8 maximum_maximum_fusion
  102.4 1.1 broadcast_select_fusion
  103.4 0.9 broadcast_select_fusion.1
  104.3 0.9 broadcast_select_fusion.2
  105.2 0.9 broadcast_select_fusion.3
  106.0 0.9 broadcast_select_fusion.4
  106.9 0.9 broadcast_select_fusion.5
  107.8 0.9 broadcast_select_fusion.6
  108.6 0.4 broadcast_select_fusion.9
  109.0 0.3 broadcast_maximum_fusion.3
  109.3 1.1 subtract_multiply_fusion.3
  110.5 2.7 %subtract_add_fusion.1 = (f32[5,1,34,258]{3,1,2,0:T(1,128)S(1)}, f32[5,1,34,258]{3,1,2,0:T(1,128)S(1)}, f32[5,1,34,258]{3,1,2,0:T(1,128)S(1)}) fusion(f32[5,1,36,260]{3,1,2,0:T(1,128)S(1)} %broadcast_select_fusion.9, f32[34]{0:T(128)S(1)} %get-tuple-element.83, f32[34,258]{1,0:T(8,128)S(1)} %bitcast.239, f32[34,258]{1,0:T(8,128)S(1)} %bitcast.240, ...), kind=kLoop, calls=%fused_computation.38 | loop fusion | flops 1096500 | bytes 1544144 | tf_op jit(solution)/shard_map/add | solution.py:56
  113.2 0.2 fusion.35
  113.4 0.5 fusion.21
  113.9 0.5 fusion.28
  114.4 0.2 fusion.26
  114.6 0.2 fusion.23
  114.8 0.4 slice.700
  115.2 1.9 %collective-permute-start.8 = (f32[5,1,34,192]{3,1,2,0:T(1,128)S(1)}, f32[5,1,34,192]{3,1,2,0:T(1,128)S(1)}, u32[]{:S(2)}, u32[]{:S(2)}) collective-permute-start(f32[5,1,34,192]{3,1,2,0:T(1,128)S(1)} %slice.700), channel_id=1, source_target_pairs={{0,4},{1,5},{2,6},{3,7},{4,8},{5,9},{6,10},{7,11},{8,12},{9,13},{1... | collective-permute-start | bytes 391688 | tf_op jit(solution)/shard_map/ppermute | solution.py:26
  117.3 19.3 %collective-permute-done.8 = f32[5,1,34,192]{3,1,2,0:T(1,128)S(1)} collective-permute-done((f32[5,1,34,192]{3,1,2,0:T(1,128)S(1)}, f32[5,1,34,192]{3,1,2,0:T(1,128)S(1)}, u32[]{:S(2)}, u32[]{:S(2)}) %collective-permute-start.8) | collective-permute-done | bytes 130592 | tf_op jit(solution)/shard_map/ppermute | solution.py:26
  136.6 0.8 maximum_maximum_fusion.1
  137.4 0.9 fusion.104
  139.9 0.3 subtract_add_fusion.2
  140.8 1.9 %collective-permute-start.9 = (f32[5,1,32,192]{3,2,1,0:T(8,128)S(1)}, f32[5,1,32,192]{3,2,1,0:T(8,128)S(1)}, u32[]{:S(2)}, u32[]{:S(2)}) collective-permute-start(f32[5,1,32,192]{3,2,1,0:T(8,128)S(1)} %slice.742), channel_id=1, source_target_pairs={{0,4},{1,5},{2,6},{3,7},{4,8},{5,9},{6,10},{7,11},{8,12},{9,13},{1... | collective-permute-start | bytes 368648 | tf_op jit(solution)/shard_map/ppermute | solution.py:26
  142.8 19.0 %collective-permute-done.9 = f32[5,1,32,192]{3,2,1,0:T(8,128)S(1)} collective-permute-done((f32[5,1,32,192]{3,2,1,0:T(8,128)S(1)}, f32[5,1,32,192]{3,2,1,0:T(8,128)S(1)}, u32[]{:S(2)}, u32[]{:S(2)}) %collective-permute-start.9) | collective-permute-done | bytes 122912 | tf_op jit(solution)/shard_map/ppermute | solution.py:26
  163.4 1.9 %collective-permute-start.12 = (f32[5,1,64,32]{2,3,0,1:T(8,128)S(1)}, f32[5,1,64,32]{2,3,0,1:T(8,128)S(1)}, u32[]{:S(2)}, u32[]{:S(2)}) collective-permute-start(f32[5,1,64,32]{2,3,0,1:T(8,128)S(1)} %get-tuple-element.49), channel_id=1, source_target_pairs={{0,3},{1,0},{2,1},{3,2},{4,7},{5,4},{6,5},{7,6},{8,11},{9,8},{10,9... | collective-permute-start | bytes 122888 | tf_op jit(solution)/shard_map/ppermute | solution.py:197
  165.3 14.6 %collective-permute-start.11 = (f32[5,1,64,32]{2,3,0,1:T(8,128)S(1)}, f32[5,1,64,32]{2,3,0,1:T(8,128)S(1)}, u32[]{:S(2)}, u32[]{:S(2)}) collective-permute-start(f32[5,1,64,32]{2,3,0,1:T(8,128)S(1)} %get-tuple-element.50), channel_id=1, source_target_pairs={{0,2},{1,3},{2,0},{3,1},{4,6},{5,7},{6,4},{7,5},{8,10},{9,11},{10,... | collective-permute-start | bytes 122888 | tf_op jit(solution)/shard_map/ppermute | solution.py:197
  179.9 2.1 %collective-permute-start.10 = (f32[5,1,64,32]{2,3,0,1:T(8,128)S(1)}, f32[5,1,64,32]{2,3,0,1:T(8,128)S(1)}, u32[]{:S(2)}, u32[]{:S(2)}) collective-permute-start(f32[5,1,64,32]{2,3,0,1:T(8,128)S(1)} %get-tuple-element.51), channel_id=1, source_target_pairs={{0,1},{1,2},{2,3},{3,0},{4,5},{5,6},{6,7},{7,4},{8,9},{9,10},{10,1... | collective-permute-start | bytes 122888 | tf_op jit(solution)/shard_map/ppermute | solution.py:197
  182.1 0.9 collective-permute-done.11
  183.0 2.7 %collective-permute-done.10 = f32[5,1,64,32]{2,3,0,1:T(8,128)S(1)} collective-permute-done((f32[5,1,64,32]{2,3,0,1:T(8,128)S(1)}, f32[5,1,64,32]{2,3,0,1:T(8,128)S(1)}, u32[]{:S(2)}, u32[]{:S(2)}) %collective-permute-start.10) | collective-permute-done | bytes 40992 | tf_op jit(solution)/shard_map/ppermute | solution.py:197
  185.8 0.8 copy.59
  (81 shorter events, 6.6 us)
Async XLA Ops:
  0.8 5.9 %collective-permute-start.1 = (f32[5,1,3,128]{3,2,1,0:T(4,128)S(1)}, f32[5,1,3,128]{3,2,1,0:T(4,128)S(1)}, u32[]{:S(2)}, u32[]{:S(2)}) collective-permute-start(f32[5,1,3,128]{3,2,1,0:T(4,128)S(1)} %get-tuple-element.53), channel_id=1, source_target_pairs={{0,127},{1,0},{2,1},{3,2},{4,3},{5,4},{6,5},{7,6},{8,7},{9,8},{10,... | collective-permute-start | bytes 23048 | tf_op jit(solution)/shard_map/ppermute | solution.py:26
  2.7 5.0 %collective-permute-start = (f32[5,1,3,128]{3,2,1,0:T(4,128)S(1)}, f32[5,1,3,128]{3,2,1,0:T(4,128)S(1)}, u32[]{:S(2)}, u32[]{:S(2)}) collective-permute-start(f32[5,1,3,128]{3,2,1,0:T(4,128)S(1)} %get-tuple-element.52), channel_id=1, source_target_pairs={{0,1},{1,2},{2,3},{3,4},{4,5},{5,6},{6,7},{7,8},{8,9},{9,10},{10,1... | collective-permute-start | bytes 23048 | tf_op jit(solution)/shard_map/ppermute | solution.py:26
  5.1 0.7 copy-start.1
  5.1 2.6 %copy-start = (f32[5,1,64,128]{3,2,1,0:T(8,128)S(1)}, f32[5,1,64,128]{3,2,1,0:T(8,128)}, u32[]{:S(2)}) copy-start(f32[5,1,64,128]{3,2,1,0:T(8,128)} %param.2) | copy-start | bytes 491524
  8.1 15.2 %collective-permute-start.3 = (f32[1059]{0:T(1024)S(1)}, f32[1059]{0:T(1024)S(1)}, u32[]{:S(2)}, u32[]{:S(2)}) collective-permute-start(f32[1059]{0:T(1024)S(1)} %pad_maximum_fusion.6), channel_id=1, source_target_pairs={{128,0},{256,128},{384,256},{512,384},{640,512},{768,640},{896,768... | collective-permute-start | bytes 12716 | tf_op jit(solution)/shard_map/ppermute | solution.py:26
  21.4 5.5 %collective-permute-start.2 = (f32[1059]{0:T(1024)S(1)}, f32[1059]{0:T(1024)S(1)}, u32[]{:S(2)}, u32[]{:S(2)}) collective-permute-start(f32[1059]{0:T(1024)S(1)} %pad_maximum_fusion.5), channel_id=1, source_target_pairs={{0,128},{128,256},{256,384},{384,512},{512,640},{640,768},{768,896... | collective-permute-start | bytes 12716 | tf_op jit(solution)/shard_map/ppermute | solution.py:26
  27.9 30.4 %collective-permute-start.6 = (f32[5,1,70,38]{3,2,1,0:T(8,128)S(1)}, f32[5,1,70,38]{3,2,1,0:T(8,128)S(1)}, u32[]{:S(2)}, u32[]{:S(2)}) collective-permute-start(f32[5,1,70,38]{3,2,1,0:T(8,128)S(1)} %get-tuple-element.18), channel_id=1, source_target_pairs={{0,3},{1,0},{2,1},{3,2},{4,7},{5,4},{6,5},{7,6},{8,11},{9,8},{10,9... | collective-permute-start | bytes 159608 | tf_op jit(solution)/shard_map/ppermute | solution.py:197
  37.5 24.1 %collective-permute-start.5 = (f32[5,1,70,38]{3,2,0,1:T(8,128)S(1)}, f32[5,1,70,38]{3,2,0,1:T(8,128)S(1)}, u32[]{:S(2)}, u32[]{:S(2)}) collective-permute-start(f32[5,1,70,38]{3,2,0,1:T(8,128)S(1)} %get-tuple-element.20), channel_id=1, source_target_pairs={{0,2},{1,3},{2,0},{3,1},{4,6},{5,7},{6,4},{7,5},{8,10},{9,11},{10,... | collective-permute-start | bytes 159608 | tf_op jit(solution)/shard_map/ppermute | solution.py:197
  56.1 7.3 %collective-permute-start.4 = (f32[5,1,70,38]{3,2,0,1:T(8,128)S(1)}, f32[5,1,70,38]{3,2,0,1:T(8,128)S(1)}, u32[]{:S(2)}, u32[]{:S(2)}) collective-permute-start(f32[5,1,70,38]{3,2,0,1:T(8,128)S(1)} %get-tuple-element.19), channel_id=1, source_target_pairs={{0,1},{1,2},{2,3},{3,0},{4,5},{5,6},{6,7},{7,4},{8,9},{9,10},{10,1... | collective-permute-start | bytes 159608 | tf_op jit(solution)/shard_map/ppermute | solution.py:197
  72.4 29.1 %collective-permute-start.7 = (f32[5,1,36,192]{3,1,2,0:T(1,128)S(1)}, f32[5,1,36,192]{3,1,2,0:T(1,128)S(1)}, u32[]{:S(2)}, u32[]{:S(2)}) collective-permute-start(f32[5,1,36,192]{3,1,2,0:T(1,128)S(1)} %slice.658), channel_id=1, source_target_pairs={{0,4},{1,5},{2,6},{3,7},{4,8},{5,9},{6,10},{7,11},{8,12},{9,13},{1... | collective-permute-start | bytes 414728 | tf_op jit(solution)/shard_map/ppermute | solution.py:26
  115.2 21.4 %collective-permute-start.8 = (f32[5,1,34,192]{3,1,2,0:T(1,128)S(1)}, f32[5,1,34,192]{3,1,2,0:T(1,128)S(1)}, u32[]{:S(2)}, u32[]{:S(2)}) collective-permute-start(f32[5,1,34,192]{3,1,2,0:T(1,128)S(1)} %slice.700), channel_id=1, source_target_pairs={{0,4},{1,5},{2,6},{3,7},{4,8},{5,9},{6,10},{7,11},{8,12},{9,13},{1... | collective-permute-start | bytes 391688 | tf_op jit(solution)/shard_map/ppermute | solution.py:26
  140.8 21.0 %collective-permute-start.9 = (f32[5,1,32,192]{3,2,1,0:T(8,128)S(1)}, f32[5,1,32,192]{3,2,1,0:T(8,128)S(1)}, u32[]{:S(2)}, u32[]{:S(2)}) collective-permute-start(f32[5,1,32,192]{3,2,1,0:T(8,128)S(1)} %slice.742), channel_id=1, source_target_pairs={{0,4},{1,5},{2,6},{3,7},{4,8},{5,9},{6,10},{7,11},{8,12},{9,13},{1... | collective-permute-start | bytes 368648 | tf_op jit(solution)/shard_map/ppermute | solution.py:26
  163.4 18.7 %collective-permute-start.12 = (f32[5,1,64,32]{2,3,0,1:T(8,128)S(1)}, f32[5,1,64,32]{2,3,0,1:T(8,128)S(1)}, u32[]{:S(2)}, u32[]{:S(2)}) collective-permute-start(f32[5,1,64,32]{2,3,0,1:T(8,128)S(1)} %get-tuple-element.49), channel_id=1, source_target_pairs={{0,3},{1,0},{2,1},{3,2},{4,7},{5,4},{6,5},{7,6},{8,11},{9,8},{10,9... | collective-permute-start | bytes 122888 | tf_op jit(solution)/shard_map/ppermute | solution.py:197
  165.3 17.7 %collective-permute-start.11 = (f32[5,1,64,32]{2,3,0,1:T(8,128)S(1)}, f32[5,1,64,32]{2,3,0,1:T(8,128)S(1)}, u32[]{:S(2)}, u32[]{:S(2)}) collective-permute-start(f32[5,1,64,32]{2,3,0,1:T(8,128)S(1)} %get-tuple-element.50), channel_id=1, source_target_pairs={{0,2},{1,3},{2,0},{3,1},{4,6},{5,7},{6,4},{7,5},{8,10},{9,11},{10,... | collective-permute-start | bytes 122888 | tf_op jit(solution)/shard_map/ppermute | solution.py:197
  179.9 5.8 %collective-permute-start.10 = (f32[5,1,64,32]{2,3,0,1:T(8,128)S(1)}, f32[5,1,64,32]{2,3,0,1:T(8,128)S(1)}, u32[]{:S(2)}, u32[]{:S(2)}) collective-permute-start(f32[5,1,64,32]{2,3,0,1:T(8,128)S(1)} %get-tuple-element.51), channel_id=1, source_target_pairs={{0,1},{1,2},{2,3},{3,0},{4,5},{5,6},{6,7},{7,4},{8,9},{9,10},{10,1... | collective-permute-start | bytes 122888 | tf_op jit(solution)/shard_map/ppermute | solution.py:197

commit v7 on v6

--- a/solution.py
+++ b/solution.py
@@ -233,6 +233,36 @@
     return jnp.concatenate(by_source(received, seat, group), axis=3)
 
 
+def group_piece(head, group):
+    count = lax.axis_size("azi")
+    groups = lax.axis_size("rad")
+    plane = PLANE
+    if count % plane or count <= plane or plane < 4 * group:
+        return passed_along(head, "azi", group)
+    pairs = [
+        (a, (a + group) % count)
+        for a in range(count)
+        if a // plane == ((a + group) % count) // plane
+    ]
+    near = lax.ppermute(head, "azi", pairs)
+    half = plane // 2
+    first, second = [], []
+    for g in range(groups):
+        for block in range(count // plane):
+            base = block * plane
+            after = (base + plane) % count
+            for q in range(group):
+                source = plane - group + q
+                lane = (g + 2 * q) % half
+                seat = source if source // 2 == lane else 2 * lane + source % 2
+                first.append((g * count + base + source, g * count + base + seat))
+                second.append((g * count + base + seat, g * count + after + q))
+    relayed = lax.ppermute(head, ("rad", "azi"), first)
+    crossed = lax.ppermute(relayed, ("rad", "azi"), second)
+    position = lax.axis_index("azi") % plane
+    return jnp.where(position < group, crossed, near)
+
+
 def local(fields, shifts):
     cells = fields.shape[2]
     rows = fields.shape[3]
@@ -263,7 +293,7 @@
             wide = jnp.where(inside[None, None, :, None], wide, 0.0)
             updated = update(wide, inverse, cells_last=True)
             head = updated[:, :, :, blocks * span - SMAX : span]
-            pieces = [passed_along(head, "azi", group * k) for k in range(1, blocks + 1)]
+            pieces = [group_piece(head, group)]
             window = jnp.concatenate(pieces[::-1] + [updated], axis=3)
             wide_shifts = wide_shifts[:, 1:-1]
             wide = rotate_window(window, wide_shifts[step], span + 2 * a, axis=3)

time: 187 us -> 207 us (1.11)
  the two profiles are of different devices: /device:TPU:72 before, /device:TPU:64 now
where the time goes in v7:
time: 207 us; the launch traced here: 206 us
  waiting for transfers between devices  92.9 us (45%)
  starting transfers between devices  77.8 us (38%)
  other arithmetic  27.4 us (13%)
  local copies, waits for them, and re-layouts  7.55 us (4%)
    ppermute x3, waiting for transfers between devices, group_piece(): crossed = lax.ppermute(relayed, ('rad', 'azi'), second)  62.1 us
    ppermute x6, starting transfers between devices, in_group(): return lax.ppermute(value, 'azi', pairs)  37.1 us
    ppermute x4, starting transfers between devices, passed_along(): return lax.ppermute(value, axis, pairs)  30.7 us
    ppermute x4, waiting for transfers between devices, passed_along(): return lax.ppermute(value, axis, pairs)  16.3 us
    ppermute x6, waiting for transfers between devices, in_group(): return lax.ppermute(value, 'azi', pairs)  10.1 us
    select_n x22, other arithmetic, rotate_window(): jnp.where(chosen, lax.slice_in_dim(window, amount, amount + length, axis=...  8.56 us
    add x3, other arithmetic, update(): outer + inner - 2.0 * centre  5.48 us
    ppermute x3, waiting for transfers between devices, group_piece(): near = lax.ppermute(head, 'azi', pairs)  4.35 us
  transfers between devices with their start and end apart: 19, of which 12 were waited for; matrix products, arithmetic and copies ran while one was open for 2% of the time, Pallas kernels for 0%

profile of v7, /device:TPU:64, one launch (start us, length us, event | category | flops | bytes accessed | tf_op | source)
XLA Modules:
  0.0 206.5 jit_solution(4616940134461111730)
XLA Ops:
  0.0 0.8 fusion.106
  0.8 23.0 %collective-permute-start.1 = (f32[5,1,3,128]{3,2,1,0:T(4,128)S(1)}, f32[5,1,3,128]{3,2,1,0:T(4,128)S(1)}, u32[]{:S(2)}, u32[]{:S(2)}) collective-permute-start(f32[5,1,3,128]{3,2,1,0:T(4,128)S(1)} %get-tuple-element.53), channel_id=1, source_target_pairs={{0,127},{1,0},{2,1},{3,2},{4,3},{5,4},{6,5},{7,6},{8,7},{9,8},{10,... | collective-permute-start | bytes 23048 | tf_op jit(solution)/shard_map/ppermute | solution.py:26
  23.8 1.9 collective-permute-start
  25.8 0.8 slice_convert_fusion.1
  27.1 14.6 %collective-permute-done = f32[5,1,3,128]{3,2,1,0:T(4,128)S(1)} collective-permute-done((f32[5,1,3,128]{3,2,1,0:T(4,128)S(1)}, f32[5,1,3,128]{3,2,1,0:T(4,128)S(1)}, u32[]{:S(2)}, u32[]{:S(2)}) %collective-permute-start) | collective-permute-done | bytes 7712 | tf_op jit(solution)/shard_map/ppermute | solution.py:26
  42.2 2.5 %collective-permute-start.3 = (f32[1059]{0:T(1024)S(1)}, f32[1059]{0:T(1024)S(1)}, u32[]{:S(2)}, u32[]{:S(2)}) collective-permute-start(f32[1059]{0:T(1024)S(1)} %pad_maximum_fusion.6), channel_id=1, source_target_pairs={{128,0},{256,128},{384,256},{512,384},{640,512},{768,640},{896,768... | collective-permute-start | bytes 12716 | tf_op jit(solution)/shard_map/ppermute | solution.py:26
  44.9 3.4 %collective-permute-start.2 = (f32[1059]{0:T(1024)S(1)}, f32[1059]{0:T(1024)S(1)}, u32[]{:S(2)}, u32[]{:S(2)}) collective-permute-start(f32[1059]{0:T(1024)S(1)} %pad_maximum_fusion.5), channel_id=1, source_target_pairs={{0,128},{128,256},{256,384},{384,512},{512,640},{640,768},{768,896... | collective-permute-start | bytes 12716 | tf_op jit(solution)/shard_map/ppermute | solution.py:26
  48.7 1.7 collective-permute-done.2
  51.0 1.9 collective-permute-start.6
  53.4 1.9 collective-permute-start.5
  55.3 2.4 %collective-permute-start.4 = (f32[5,1,70,38]{3,2,0,1:T(8,128)S(1)}, f32[5,1,70,38]{3,2,0,1:T(8,128)S(1)}, u32[]{:S(2)}, u32[]{:S(2)}) collective-permute-start(f32[5,1,70,38]{3,2,0,1:T(8,128)S(1)} %get-tuple-element.19), channel_id=1, source_target_pairs={{0,1},{1,2},{2,3},{3,0},{4,5},{5,6},{6,7},{7,4},{8,9},{9,10},{10,1... | collective-permute-start | bytes 159608 | tf_op jit(solution)/shard_map/ppermute | solution.py:197
  57.8 4.9 %collective-permute-done.5 = f32[5,1,70,38]{3,2,0,1:T(8,128)S(1)} collective-permute-done((f32[5,1,70,38]{3,2,0,1:T(8,128)S(1)}, f32[5,1,70,38]{3,2,0,1:T(8,128)S(1)}, u32[]{:S(2)}, u32[]{:S(2)}) %collective-permute-start.5) | collective-permute-done | bytes 53232 | tf_op jit(solution)/shard_map/ppermute | solution.py:197
  62.7 1.6 collective-permute-done.4
  64.6 0.3 slice.632
  65.0 0.3 slice.631
  65.4 0.3 slice.630
  65.8 1.3 fusion.1
  67.1 0.3 broadcast_maximum_fusion.1
  67.4 1.2 subtract_multiply_fusion.1
  68.7 2.6 %subtract_add_fusion = (f32[5,1,36,260]{3,1,2,0:T(1,128)S(1)}, f32[5,1,36,260]{3,1,2,0:T(1,128)S(1)}, f32[5,1,36,260]{3,1,2,0:T(1,128)S(1)}) fusion(f32[5,1,38,262]{3,1,2,0:T(1,128)S(1)} %fusion.1, f32[36]{0:T(128)S(1)} %get-tuple-element.85, f32[36,260]{1,0:T(8,128)S(1)} %get-tuple-element.87, f32[36,260]{1,0:T(8,128)S(1)} %get-tuple-element.88, ...), kind=kLoop, calls=%fused_computation.35 | loop fusion | flops 1170000 | bytes 1647648 | tf_op jit(solution)/shard_map/add | solution.py:56
  71.5 0.5 fusion.4
  72.0 0.5 fusion.11
  72.7 0.3 fusion.6
  73.0 0.4 slice.658
  73.4 0.7 collective-permute-start.7
  74.3 0.5 copy-done.1
  74.9 1.3 collective-permute-start.9
  76.2 1.5 collective-permute-start.8
  77.8 1.5 collective-permute-done.9
  79.3 16.8 %collective-permute-done.8 = f32[5,1,36,192]{3,1,2,0:T(1,128)S(1)} collective-permute-done((f32[5,1,36,192]{3,1,2,0:T(1,128)S(1)}, f32[5,1,36,192]{3,1,2,0:T(1,128)S(1)}, u32[]{:S(2)}, u32[]{:S(2)}) %collective-permute-start.8) | collective-permute-done | bytes 138272 | tf_op jit(solution)/shard_map/ppermute | solution.py:261
  96.3 0.8 maximum_maximum_fusion
  97.2 1.1 broadcast_select_fusion
  98.2 0.9 broadcast_select_fusion.1
  99.1 0.9 broadcast_select_fusion.2
  100.0 0.9 broadcast_select_fusion.3
  100.8 0.9 broadcast_select_fusion.4
  101.7 0.9 broadcast_select_fusion.5
  102.6 0.9 broadcast_select_fusion.6
  103.5 0.4 broadcast_select_fusion.9
  103.8 0.3 broadcast_maximum_fusion.3
  104.1 1.1 subtract_multiply_fusion.3
  105.3 2.7 %subtract_add_fusion.1 = (f32[5,1,34,258]{3,1,2,0:T(1,128)S(1)}, f32[5,1,34,258]{3,1,2,0:T(1,128)S(1)}, f32[5,1,34,258]{3,1,2,0:T(1,128)S(1)}) fusion(f32[5,1,36,260]{3,1,2,0:T(1,128)S(1)} %broadcast_select_fusion.9, f32[34]{0:T(128)S(1)} %get-tuple-element.83, f32[34,258]{1,0:T(8,128)S(1)} %bitcast.239, f32[34,258]{1,0:T(8,128)S(1)} %bitcast.240, ...), kind=kLoop, calls=%fused_computation.40 | loop fusion | flops 1096500 | bytes 1544144 | tf_op jit(solution)/shard_map/add | solution.py:56
  108.2 0.5 fusion.21
  108.7 0.5 fusion.28
  109.6 0.4 slice.700
  110.1 0.7 collective-permute-start.10
  110.7 1.3 collective-permute-start.12
  112.1 1.3 collective-permute-start.11
  113.5 1.5 collective-permute-done.12
  115.0 19.4 %collective-permute-done.11 = f32[5,1,34,192]{3,1,2,0:T(1,128)S(1)} collective-permute-done((f32[5,1,34,192]{3,1,2,0:T(1,128)S(1)}, f32[5,1,34,192]{3,1,2,0:T(1,128)S(1)}, u32[]{:S(2)}, u32[]{:S(2)}) %collective-permute-start.11) | collective-permute-done | bytes 130592 | tf_op jit(solution)/shard_map/ppermute | solution.py:261
  134.5 0.8 maximum_maximum_fusion.1
  135.4 0.9 fusion.104
  137.9 0.3 subtract_add_fusion.2
  138.7 0.7 collective-permute-start.13
  139.5 1.3 collective-permute-start.15
  140.8 1.3 collective-permute-start.14
  142.2 1.4 collective-permute-done.15
  143.6 25.9 %collective-permute-done.14 = f32[5,1,32,192]{3,2,1,0:T(8,128)S(1)} collective-permute-done((f32[5,1,32,192]{3,2,1,0:T(8,128)S(1)}, f32[5,1,32,192]{3,2,1,0:T(8,128)S(1)}, u32[]{:S(2)}, u32[]{:S(2)}) %collective-permute-start.14) | collective-permute-done | bytes 122912 | tf_op jit(solution)/shard_map/ppermute | solution.py:261
  171.0 1.9 collective-permute-start.18
  172.9 26.8 %collective-permute-start.17 = (f32[5,1,64,32]{2,3,0,1:T(8,128)S(1)}, f32[5,1,64,32]{2,3,0,1:T(8,128)S(1)}, u32[]{:S(2)}, u32[]{:S(2)}) collective-permute-start(f32[5,1,64,32]{2,3,0,1:T(8,128)S(1)} %get-tuple-element.50), channel_id=1, source_target_pairs={{0,2},{1,3},{2,0},{3,1},{4,6},{5,7},{6,4},{7,5},{8,10},{9,11},{10,... | collective-permute-start | bytes 122888 | tf_op jit(solution)/shard_map/ppermute | solution.py:197
  199.8 2.1 %collective-permute-start.16 = (f32[5,1,64,32]{2,3,0,1:T(8,128)S(1)}, f32[5,1,64,32]{2,3,0,1:T(8,128)S(1)}, u32[]{:S(2)}, u32[]{:S(2)}) collective-permute-start(f32[5,1,64,32]{2,3,0,1:T(8,128)S(1)} %get-tuple-element.51), channel_id=1, source_target_pairs={{0,1},{1,2},{2,3},{3,0},{4,5},{5,6},{6,7},{7,4},{8,9},{9,10},{10,1... | collective-permute-start | bytes 122888 | tf_op jit(solution)/shard_map/ppermute | solution.py:197
  201.9 0.9 collective-permute-done.17
  202.9 2.7 %collective-permute-done.16 = f32[5,1,64,32]{2,3,0,1:T(8,128)S(1)} collective-permute-done((f32[5,1,64,32]{2,3,0,1:T(8,128)S(1)}, f32[5,1,64,32]{2,3,0,1:T(8,128)S(1)}, u32[]{:S(2)}, u32[]{:S(2)}) %collective-permute-start.16) | collective-permute-done | bytes 40992 | tf_op jit(solution)/shard_map/ppermute | solution.py:197
  205.6 0.8 copy.59
  (96 shorter events, 9.1 us)
Async XLA Ops:
  0.0 41.7 %copy-start = (f32[5,1,64,128]{3,2,1,0:T(8,128)S(1)}, f32[5,1,64,128]{3,2,1,0:T(8,128)}, u32[]{:S(2)}) copy-start(f32[5,1,64,128]{3,2,1,0:T(8,128)} %param.2) | copy-start | bytes 491524
  0.8 26.3 %collective-permute-start.1 = (f32[5,1,3,128]{3,2,1,0:T(4,128)S(1)}, f32[5,1,3,128]{3,2,1,0:T(4,128)S(1)}, u32[]{:S(2)}, u32[]{:S(2)}) collective-permute-start(f32[5,1,3,128]{3,2,1,0:T(4,128)S(1)} %get-tuple-element.53), channel_id=1, source_target_pairs={{0,127},{1,0},{2,1},{3,2},{4,3},{5,4},{6,5},{7,6},{8,7},{9,8},{10,... | collective-permute-start | bytes 23048 | tf_op jit(solution)/shard_map/ppermute | solution.py:26
  23.8 17.9 %collective-permute-start = (f32[5,1,3,128]{3,2,1,0:T(4,128)S(1)}, f32[5,1,3,128]{3,2,1,0:T(4,128)S(1)}, u32[]{:S(2)}, u32[]{:S(2)}) collective-permute-start(f32[5,1,3,128]{3,2,1,0:T(4,128)S(1)} %get-tuple-element.52), channel_id=1, source_target_pairs={{0,1},{1,2},{2,3},{3,4},{4,5},{5,6},{6,7},{7,8},{8,9},{9,10},{10,1... | collective-permute-start | bytes 23048 | tf_op jit(solution)/shard_map/ppermute | solution.py:26
  42.2 6.4 %collective-permute-start.3 = (f32[1059]{0:T(1024)S(1)}, f32[1059]{0:T(1024)S(1)}, u32[]{:S(2)}, u32[]{:S(2)}) collective-permute-start(f32[1059]{0:T(1024)S(1)} %pad_maximum_fusion.6), channel_id=1, source_target_pairs={{128,0},{256,128},{384,256},{512,384},{640,512},{768,640},{896,768... | collective-permute-start | bytes 12716 | tf_op jit(solution)/shard_map/ppermute | solution.py:26
  44.9 5.5 %collective-permute-start.2 = (f32[1059]{0:T(1024)S(1)}, f32[1059]{0:T(1024)S(1)}, u32[]{:S(2)}, u32[]{:S(2)}) collective-permute-start(f32[1059]{0:T(1024)S(1)} %pad_maximum_fusion.5), channel_id=1, source_target_pairs={{0,128},{128,256},{256,384},{384,512},{512,640},{640,768},{768,896... | collective-permute-start | bytes 12716 | tf_op jit(solution)/shard_map/ppermute | solution.py:26
  51.0 6.8 %collective-permute-start.6 = (f32[5,1,70,38]{3,2,1,0:T(8,128)S(1)}, f32[5,1,70,38]{3,2,1,0:T(8,128)S(1)}, u32[]{:S(2)}, u32[]{:S(2)}) collective-permute-start(f32[5,1,70,38]{3,2,1,0:T(8,128)S(1)} %get-tuple-element.18), channel_id=1, source_target_pairs={{0,3},{1,0},{2,1},{3,2},{4,7},{5,4},{6,5},{7,6},{8,11},{9,8},{10,9... | collective-permute-start | bytes 159608 | tf_op jit(solution)/shard_map/ppermute | solution.py:197
  53.4 9.3 %collective-permute-start.5 = (f32[5,1,70,38]{3,2,0,1:T(8,128)S(1)}, f32[5,1,70,38]{3,2,0,1:T(8,128)S(1)}, u32[]{:S(2)}, u32[]{:S(2)}) collective-permute-start(f32[5,1,70,38]{3,2,0,1:T(8,128)S(1)} %get-tuple-element.20), channel_id=1, source_target_pairs={{0,2},{1,3},{2,0},{3,1},{4,6},{5,7},{6,4},{7,5},{8,10},{9,11},{10,... | collective-permute-start | bytes 159608 | tf_op jit(solution)/shard_map/ppermute | solution.py:197
  55.3 9.0 %collective-permute-start.4 = (f32[5,1,70,38]{3,2,0,1:T(8,128)S(1)}, f32[5,1,70,38]{3,2,0,1:T(8,128)S(1)}, u32[]{:S(2)}, u32[]{:S(2)}) collective-permute-start(f32[5,1,70,38]{3,2,0,1:T(8,128)S(1)} %get-tuple-element.19), channel_id=1, source_target_pairs={{0,1},{1,2},{2,3},{3,0},{4,5},{5,6},{6,7},{7,4},{8,9},{9,10},{10,1... | collective-permute-start | bytes 159608 | tf_op jit(solution)/shard_map/ppermute | solution.py:197
  73.4 2.8 %collective-permute-start.7 = (f32[5,1,36,192]{3,1,2,0:T(1,128)S(1)}, f32[5,1,36,192]{3,1,2,0:T(1,128)S(1)}, u32[]{:S(2)}, u32[]{:S(2)}) collective-permute-start(f32[5,1,36,192]{3,1,2,0:T(1,128)S(1)} %slice.658), channel_id=1, source_target_pairs={{12,0},{13,5},{14,8},{15,13},{28,16},{29,21},{30,24},{31,29},{44,3... | collective-permute-start | bytes 414728 | tf_op jit(solution)/shard_map/ppermute | solution.py:260
  74.2 0.7 copy-start.1
  74.9 4.4 %collective-permute-start.9 = (f32[5,1,36,192]{3,1,2,0:T(1,128)S(1)}, f32[5,1,36,192]{3,1,2,0:T(1,128)S(1)}, u32[]{:S(2)}, u32[]{:S(2)}) collective-permute-start(f32[5,1,36,192]{3,1,2,0:T(1,128)S(1)} %slice.658), channel_id=1, source_target_pairs={{0,4},{1,5},{2,6},{3,7},{4,8},{5,9},{6,10},{7,11},{8,12},{9,13},{1... | collective-permute-start | bytes 414728 | tf_op jit(solution)/shard_map/ppermute | solution.py:247
  76.2 19.9 %collective-permute-start.8 = (f32[5,1,36,192]{3,1,2,0:T(1,128)S(1)}, f32[5,1,36,192]{3,1,2,0:T(1,128)S(1)}, u32[]{:S(2)}, u32[]{:S(2)}) collective-permute-start(f32[5,1,36,192]{3,1,2,0:T(1,128)S(1)} %collective-permute-done.7), channel_id=1, source_target_pairs={{0,16},{5,17},{8,18},{13,19},{16,32},{21,33},{24,34},{29,35},{32,4... | collective-permute-start | bytes 414728 | tf_op jit(solution)/shard_map/ppermute | solution.py:261
  110.1 2.0 collective-permute-start.10
  110.7 4.2 %collective-permute-start.12 = (f32[5,1,34,192]{3,1,2,0:T(1,128)S(1)}, f32[5,1,34,192]{3,1,2,0:T(1,128)S(1)}, u32[]{:S(2)}, u32[]{:S(2)}) collective-permute-start(f32[5,1,34,192]{3,1,2,0:T(1,128)S(1)} %slice.700), channel_id=1, source_target_pairs={{0,4},{1,5},{2,6},{3,7},{4,8},{5,9},{6,10},{7,11},{8,12},{9,13},{1... | collective-permute-start | bytes 391688 | tf_op jit(solution)/shard_map/ppermute | solution.py:247
  112.1 22.3 %collective-permute-start.11 = (f32[5,1,34,192]{3,1,2,0:T(1,128)S(1)}, f32[5,1,34,192]{3,1,2,0:T(1,128)S(1)}, u32[]{:S(2)}, u32[]{:S(2)}) collective-permute-start(f32[5,1,34,192]{3,1,2,0:T(1,128)S(1)} %collective-permute-done.10), channel_id=1, source_target_pairs={{0,16},{5,17},{8,18},{13,19},{16,32},{21,33},{24,34},{29,35},{32,4... | collective-permute-start | bytes 391688 | tf_op jit(solution)/shard_map/ppermute | solution.py:261
  138.7 2.1 collective-permute-start.13
  139.5 4.1 %collective-permute-start.15 = (f32[5,1,32,192]{3,2,1,0:T(8,128)S(1)}, f32[5,1,32,192]{3,2,1,0:T(8,128)S(1)}, u32[]{:S(2)}, u32[]{:S(2)}) collective-permute-start(f32[5,1,32,192]{3,2,1,0:T(8,128)S(1)} %slice.742), channel_id=1, source_target_pairs={{0,4},{1,5},{2,6},{3,7},{4,8},{5,9},{6,10},{7,11},{8,12},{9,13},{1... | collective-permute-start | bytes 368648 | tf_op jit(solution)/shard_map/ppermute | solution.py:247
  140.8 28.7 %collective-permute-start.14 = (f32[5,1,32,192]{3,2,1,0:T(8,128)S(1)}, f32[5,1,32,192]{3,2,1,0:T(8,128)S(1)}, u32[]{:S(2)}, u32[]{:S(2)}) collective-permute-start(f32[5,1,32,192]{3,2,1,0:T(8,128)S(1)} %collective-permute-done.13), channel_id=1, source_target_pairs={{0,16},{5,17},{8,18},{13,19},{16,32},{21,33},{24,34},{29,35},{32,4... | collective-permute-start | bytes 368648 | tf_op jit(solution)/shard_map/ppermute | solution.py:261
  171.0 30.9 %collective-permute-start.18 = (f32[5,1,64,32]{2,3,0,1:T(8,128)S(1)}, f32[5,1,64,32]{2,3,0,1:T(8,128)S(1)}, u32[]{:S(2)}, u32[]{:S(2)}) collective-permute-start(f32[5,1,64,32]{2,3,0,1:T(8,128)S(1)} %get-tuple-element.49), channel_id=1, source_target_pairs={{0,3},{1,0},{2,1},{3,2},{4,7},{5,4},{6,5},{7,6},{8,11},{9,8},{10,9... | collective-permute-start | bytes 122888 | tf_op jit(solution)/shard_map/ppermute | solution.py:197
  172.9 29.9 %collective-permute-start.17 = (f32[5,1,64,32]{2,3,0,1:T(8,128)S(1)}, f32[5,1,64,32]{2,3,0,1:T(8,128)S(1)}, u32[]{:S(2)}, u32[]{:S(2)}) collective-permute-start(f32[5,1,64,32]{2,3,0,1:T(8,128)S(1)} %get-tuple-element.50), channel_id=1, source_target_pairs={{0,2},{1,3},{2,0},{3,1},{4,6},{5,7},{6,4},{7,5},{8,10},{9,11},{10,... | collective-permute-start | bytes 122888 | tf_op jit(solution)/shard_map/ppermute | solution.py:197
  199.8 5.8 %collective-permute-start.16 = (f32[5,1,64,32]{2,3,0,1:T(8,128)S(1)}, f32[5,1,64,32]{2,3,0,1:T(8,128)S(1)}, u32[]{:S(2)}, u32[]{:S(2)}) collective-permute-start(f32[5,1,64,32]{2,3,0,1:T(8,128)S(1)} %get-tuple-element.51), channel_id=1, source_target_pairs={{0,1},{1,2},{2,3},{3,0},{4,5},{5,6},{6,7},{7,4},{8,9},{9,10},{10,1... | collective-permute-start | bytes 122888 | tf_op jit(solution)/shard_map/ppermute | solution.py:197

commit v8 on v4

--- a/solution.py
+++ b/solution.py
@@ -158,9 +158,12 @@
             if a // plane == ((a + k) % count) // plane
         ]
         near.append(lax.ppermute(head, "azi", pairs))
-    first, second = crossing_relays(groups, count, plane, blocks)
-    relayed = lax.ppermute(head, ("rad", "azi"), first)
-    crossed = lax.ppermute(relayed, ("rad", "azi"), second)
+    pairs = [
+        (base + plane - j, (base + plane) % count + blocks - j)
+        for base in range(0, count, plane)
+        for j in range(1, blocks + 1)
+    ]
+    crossed = lax.ppermute(head, "azi", pairs)
     position = lax.axis_index("azi") % plane
     pieces = []
     for k in range(1, blocks + 1):

time: 167 us -> 186 us (1.11)
  the two profiles are of different devices: /device:TPU:64 before, /device:TPU:128 now
where the time goes in v8:
time: 186 us; the launch traced here: 185 us
  waiting for transfers between devices  109 us (59%)
  starting transfers between devices  61.3 us (33%)
  other arithmetic  10.1 us (5%)
  local copies, waits for them, and re-layouts  3.57 us (2%)
    ppermute x3, waiting for transfers between devices, rotation_pieces(): crossed = lax.ppermute(head, 'azi', pairs)  56.3 us
    ppermute x6, waiting for transfers between devices, rotation_pieces(): far = lax.ppermute(crossed, 'azi', pairs)  49.7 us
    ppermute x4, starting transfers between devices, passed_along(): return lax.ppermute(value, axis, pairs)  29.8 us
    ppermute x9, starting transfers between devices, rotation_pieces(): near.append(lax.ppermute(head, 'azi', pairs))  19.8 us
    ppermute x6, starting transfers between devices, rotation_pieces(): far = lax.ppermute(crossed, 'azi', pairs)  7.72 us
    ppermute x3, starting transfers between devices, rotation_pieces(): crossed = lax.ppermute(head, 'azi', pairs)  3.88 us
  transfers between devices with their start and end apart: 22, of which 9 were waited for; matrix products, arithmetic and copies ran while one was open for 1% of the time, Pallas kernels for 0%

profile of v8, /device:TPU:128, one launch (start us, length us, event | category | flops | bytes accessed | tf_op | source)
XLA Modules:
  0.0 184.9 jit_solution(2750303857319499488)
XLA Ops:
  0.0 0.8 fusion.103
  0.8 1.9 %collective-permute-start = (f32[5,1,3,128]{3,2,1,0:T(4,128)S(1)}, f32[5,1,3,128]{3,2,1,0:T(4,128)S(1)}, u32[]{:S(2)}, u32[]{:S(2)}) collective-permute-start(f32[5,1,3,128]{3,2,1,0:T(4,128)S(1)} %get-tuple-element.46), channel_id=1, source_target_pairs={{0,1},{1,2},{2,3},{3,4},{4,5},{5,6},{6,7},{7,8},{8,9},{9,10},{10,1... | collective-permute-start | bytes 23048 | tf_op jit(solution)/shard_map/ppermute | solution.py:25
  2.7 22.1 %collective-permute-start.1 = (f32[5,1,3,128]{3,2,1,0:T(4,128)S(1)}, f32[5,1,3,128]{3,2,1,0:T(4,128)S(1)}, u32[]{:S(2)}, u32[]{:S(2)}) collective-permute-start(f32[5,1,3,128]{3,2,1,0:T(4,128)S(1)} %get-tuple-element.47), channel_id=1, source_target_pairs={{0,127},{1,0},{2,1},{3,2},{4,3},{5,4},{6,5},{7,6},{8,7},{9,8},{10,... | collective-permute-start | bytes 23048 | tf_op jit(solution)/shard_map/ppermute | solution.py:25
  24.8 0.8 slice_convert_fusion.1
  26.2 0.9 pad_maximum_fusion
  27.1 0.1 fusion.102
  27.3 0.2 reshape.1273
  27.5 3.4 %collective-permute-start.2 = (f32[1059]{0:T(1024)S(1)}, f32[1059]{0:T(1024)S(1)}, u32[]{:S(2)}, u32[]{:S(2)}) collective-permute-start(f32[1059]{0:T(1024)S(1)} %pad_maximum_fusion.1), channel_id=1, source_target_pairs={{0,128},{128,256},{256,384},{384,512},{512,640},{640,768},{768,896... | collective-permute-start | bytes 12716 | tf_op jit(solution)/shard_map/ppermute | solution.py:25
  30.9 0.2 reshape.1275
  31.2 2.5 %collective-permute-start.3 = (f32[1059]{0:T(1024)S(1)}, f32[1059]{0:T(1024)S(1)}, u32[]{:S(2)}, u32[]{:S(2)}) collective-permute-start(f32[1059]{0:T(1024)S(1)} %pad_maximum_fusion.2), channel_id=1, source_target_pairs={{128,0},{256,128},{384,256},{512,384},{640,512},{768,640},{896,768... | collective-permute-start | bytes 12716 | tf_op jit(solution)/shard_map/ppermute | solution.py:25
  33.7 0.2 concatenate.40
  33.9 2.8 %collective-permute-done.3 = f32[1059]{0:T(1024)S(1)} collective-permute-done((f32[1059]{0:T(1024)S(1)}, f32[1059]{0:T(1024)S(1)}, u32[]{:S(2)}, u32[]{:S(2)}) %collective-permute-start.3) | collective-permute-done | bytes 4268 | tf_op jit(solution)/shard_map/ppermute | solution.py:25
  36.7 0.2 concatenate.41
  36.9 0.2 maximum_select_fusion
  37.2 0.1 maximum_bitcast_fusion.3
  37.3 0.2 subtract_multiply_fusion.3
  37.5 0.6 subtract_add_fusion.1
  38.2 0.1 fusion.4
  38.3 0.1 fusion.29
  38.7 1.3 collective-permute-start.4
  40.0 1.3 collective-permute-start.9
  41.3 1.3 collective-permute-start.7
  42.6 1.3 collective-permute-start.5
  44.5 21.5 %collective-permute-done.4 = f32[5,1,64,132]{3,2,1,0:T(8,128)S(1)} collective-permute-done((f32[5,1,64,132]{3,2,1,0:T(8,128)S(1)}, f32[5,1,64,132]{3,2,1,0:T(8,128)S(1)}, u32[]{:S(2)}, u32[]{:S(2)}) %collective-permute-start.4) | collective-permute-done | bytes 168992 | tf_op jit(solution)/shard_map/ppermute | solution.py:166
  66.0 1.3 collective-permute-start.8
  67.3 1.3 collective-permute-start.6
  68.7 19.4 %collective-permute-done.8 = f32[5,1,64,132]{3,2,1,0:T(8,128)S(1)} collective-permute-done((f32[5,1,64,132]{3,2,1,0:T(8,128)S(1)}, f32[5,1,64,132]{3,2,1,0:T(8,128)S(1)}, u32[]{:S(2)}, u32[]{:S(2)}) %collective-permute-start.8) | collective-permute-done | bytes 168992 | tf_op jit(solution)/shard_map/ppermute | solution.py:179
  88.3 0.7 concatenate.43
  89.0 0.2 slice_select_fusion
  89.1 0.2 slice_select_fusion.5
  89.3 0.2 slice_select_fusion.4
  89.5 0.1 slice_select_fusion.7
  89.6 0.1 slice_select_fusion.9
  90.0 0.1 maximum_bitcast_fusion.1
  90.1 0.2 subtract_multiply_fusion.1
  90.3 0.6 subtract_add_fusion
  91.0 0.1 fusion.7
  91.1 0.1 fusion.14
  91.5 1.3 collective-permute-start.10
  92.8 1.3 collective-permute-start.11
  94.2 5.2 %collective-permute-start.15 = (f32[5,1,64,130]{3,2,1,0:T(8,128)S(1)}, f32[5,1,64,130]{3,2,1,0:T(8,128)S(1)}, u32[]{:S(2)}, u32[]{:S(2)}) collective-permute-start(f32[5,1,64,130]{3,2,1,0:T(8,128)S(1)} %slice.677), channel_id=1, source_target_pairs={{0,1},{1,2},{2,3},{3,4},{4,5},{5,6},{6,7},{7,8},{8,9},{9,10},{10,1... | collective-permute-start | bytes 499208 | tf_op jit(solution)/shard_map/ppermute | solution.py:160
  99.3 1.6 collective-permute-start.13
  101.0 20.5 %collective-permute-done.10 = f32[5,1,64,130]{3,2,1,0:T(8,128)S(1)} collective-permute-done((f32[5,1,64,130]{3,2,1,0:T(8,128)S(1)}, f32[5,1,64,130]{3,2,1,0:T(8,128)S(1)}, u32[]{:S(2)}, u32[]{:S(2)}) %collective-permute-start.10) | collective-permute-done | bytes 166432 | tf_op jit(solution)/shard_map/ppermute | solution.py:166
  121.5 1.3 collective-permute-start.14
  122.8 1.3 collective-permute-start.12
  124.2 20.8 %collective-permute-done.14 = f32[5,1,64,130]{3,2,1,0:T(8,128)S(1)} collective-permute-done((f32[5,1,64,130]{3,2,1,0:T(8,128)S(1)}, f32[5,1,64,130]{3,2,1,0:T(8,128)S(1)}, u32[]{:S(2)}, u32[]{:S(2)}) %collective-permute-start.14) | collective-permute-done | bytes 166432 | tf_op jit(solution)/shard_map/ppermute | solution.py:179
  145.2 0.7 concatenate.44
  145.9 0.2 slice_select_fusion.3
  146.1 0.2 slice_select_fusion.2
  146.2 0.2 slice_select_fusion.1
  146.4 0.1 slice_select_fusion.6
  146.6 0.1 slice_select_fusion.8
  147.0 0.1 subtract_multiply_fusion.5
  147.2 0.3 subtract_add_fusion.2
  147.9 1.3 collective-permute-start.16
  149.2 1.3 collective-permute-start.17
  150.6 4.9 %collective-permute-start.19 = (f32[5,1,64,128]{3,2,1,0:T(8,128)S(1)}, f32[5,1,64,128]{3,2,1,0:T(8,128)S(1)}, u32[]{:S(2)}, u32[]{:S(2)}) collective-permute-start(f32[5,1,64,128]{3,2,1,0:T(8,128)S(1)} %get-tuple-element.5), channel_id=1, source_target_pairs={{0,2},{1,3},{2,4},{3,5},{4,6},{5,7},{6,8},{7,9},{8,10},{9,11},{10,... | collective-permute-start | bytes 491528 | tf_op jit(solution)/shard_map/ppermute | solution.py:160
  155.5 1.6 collective-permute-start.21
  157.0 14.3 %collective-permute-done.16 = f32[5,1,64,128]{3,2,1,0:T(8,128)S(1)} collective-permute-done((f32[5,1,64,128]{3,2,1,0:T(8,128)S(1)}, f32[5,1,64,128]{3,2,1,0:T(8,128)S(1)}, u32[]{:S(2)}, u32[]{:S(2)}) %collective-permute-start.16) | collective-permute-done | bytes 163872 | tf_op jit(solution)/shard_map/ppermute | solution.py:166
  171.3 1.3 collective-permute-start.18
  172.6 1.3 collective-permute-start.20
  174.0 3.7 %collective-permute-done.18 = f32[5,1,64,128]{3,2,1,0:T(8,128)S(1)} collective-permute-done((f32[5,1,64,128]{3,2,1,0:T(8,128)S(1)}, f32[5,1,64,128]{3,2,1,0:T(8,128)S(1)}, u32[]{:S(2)}, u32[]{:S(2)}) %collective-permute-start.18) | collective-permute-done | bytes 163872 | tf_op jit(solution)/shard_map/ppermute | solution.py:179
  177.8 5.7 %collective-permute-done.20 = f32[5,1,64,128]{3,2,1,0:T(8,128)S(1)} collective-permute-done((f32[5,1,64,128]{3,2,1,0:T(8,128)S(1)}, f32[5,1,64,128]{3,2,1,0:T(8,128)S(1)}, u32[]{:S(2)}, u32[]{:S(2)}) %collective-permute-start.20) | collective-permute-done | bytes 163872 | tf_op jit(solution)/shard_map/ppermute | solution.py:179
  184.2 0.7 slice_select_fusion.23
  (87 shorter events, 3.9 us)
Async XLA Ops:
  0.0 36.9 %copy-start = (f32[5,1,64,128]{3,2,1,0:T(8,128)S(1)}, f32[5,1,64,128]{3,2,1,0:T(8,128)}, u32[]{:S(2)}) copy-start(f32[5,1,64,128]{3,2,1,0:T(8,128)} %param.2) | copy-start | bytes 491524
  0.8 25.3 %collective-permute-start = (f32[5,1,3,128]{3,2,1,0:T(4,128)S(1)}, f32[5,1,3,128]{3,2,1,0:T(4,128)S(1)}, u32[]{:S(2)}, u32[]{:S(2)}) collective-permute-start(f32[5,1,3,128]{3,2,1,0:T(4,128)S(1)} %get-tuple-element.46), channel_id=1, source_target_pairs={{0,1},{1,2},{2,3},{3,4},{4,5},{5,6},{6,7},{7,8},{8,9},{9,10},{10,1... | collective-permute-start | bytes 23048 | tf_op jit(solution)/shard_map/ppermute | solution.py:25
  2.7 23.5 %collective-permute-start.1 = (f32[5,1,3,128]{3,2,1,0:T(4,128)S(1)}, f32[5,1,3,128]{3,2,1,0:T(4,128)S(1)}, u32[]{:S(2)}, u32[]{:S(2)}) collective-permute-start(f32[5,1,3,128]{3,2,1,0:T(4,128)S(1)} %get-tuple-element.47), channel_id=1, source_target_pairs={{0,127},{1,0},{2,1},{3,2},{4,3},{5,4},{6,5},{7,6},{8,7},{9,8},{10,... | collective-permute-start | bytes 23048 | tf_op jit(solution)/shard_map/ppermute | solution.py:25
  27.5 6.2 %collective-permute-start.2 = (f32[1059]{0:T(1024)S(1)}, f32[1059]{0:T(1024)S(1)}, u32[]{:S(2)}, u32[]{:S(2)}) collective-permute-start(f32[1059]{0:T(1024)S(1)} %pad_maximum_fusion.1), channel_id=1, source_target_pairs={{0,128},{128,256},{256,384},{384,512},{512,640},{640,768},{768,896... | collective-permute-start | bytes 12716 | tf_op jit(solution)/shard_map/ppermute | solution.py:25
  31.2 5.5 %collective-permute-start.3 = (f32[1059]{0:T(1024)S(1)}, f32[1059]{0:T(1024)S(1)}, u32[]{:S(2)}, u32[]{:S(2)}) collective-permute-start(f32[1059]{0:T(1024)S(1)} %pad_maximum_fusion.2), channel_id=1, source_target_pairs={{128,0},{256,128},{384,256},{512,384},{640,512},{768,640},{896,768... | collective-permute-start | bytes 12716 | tf_op jit(solution)/shard_map/ppermute | solution.py:25
  38.1 6.2 %copy-start.1 = (s32[3,128]{1,0:T(4,128)S(1)}, s32[3,128]{1,0:T(4,128)}, u32[]{:S(2)}) copy-start(s32[3,128]{1,0:T(4,128)} %param.3) | copy-start | bytes 4612
  38.7 27.3 %collective-permute-start.4 = (f32[5,1,64,132]{3,2,1,0:T(8,128)S(1)}, f32[5,1,64,132]{3,2,1,0:T(8,128)S(1)}, u32[]{:S(2)}, u32[]{:S(2)}) collective-permute-start(f32[5,1,64,132]{3,2,1,0:T(8,128)S(1)} %slice.635), channel_id=1, source_target_pairs={{15,18},{14,17},{13,16},{31,34},{30,33},{29,32},{47,50},{46,49},{4... | collective-permute-start | bytes 506888 | tf_op jit(solution)/shard_map/ppermute | solution.py:166
  40.0 28.7 %collective-permute-start.9 = (f32[5,1,64,132]{3,2,1,0:T(8,128)S(1)}, f32[5,1,64,132]{3,2,1,0:T(8,128)S(1)}, u32[]{:S(2)}, u32[]{:S(2)}) collective-permute-start(f32[5,1,64,132]{3,2,1,0:T(8,128)S(1)} %slice.635), channel_id=1, source_target_pairs={{0,1},{1,2},{2,3},{3,4},{4,5},{5,6},{6,7},{7,8},{8,9},{9,10},{10,1... | collective-permute-start | bytes 506888 | tf_op jit(solution)/shard_map/ppermute | solution.py:160
  41.3 46.8 %collective-permute-start.7 = (f32[5,1,64,132]{3,2,1,0:T(8,128)S(1)}, f32[5,1,64,132]{3,2,1,0:T(8,128)S(1)}, u32[]{:S(2)}, u32[]{:S(2)}) collective-permute-start(f32[5,1,64,132]{3,2,1,0:T(8,128)S(1)} %slice.635), channel_id=1, source_target_pairs={{0,2},{1,3},{2,4},{3,5},{4,6},{5,7},{6,8},{7,9},{8,10},{9,11},{10,... | collective-permute-start | bytes 506888 | tf_op jit(solution)/shard_map/ppermute | solution.py:160
  42.6 26.0 %collective-permute-start.5 = (f32[5,1,64,132]{3,2,1,0:T(8,128)S(1)}, f32[5,1,64,132]{3,2,1,0:T(8,128)S(1)}, u32[]{:S(2)}, u32[]{:S(2)}) collective-permute-start(f32[5,1,64,132]{3,2,1,0:T(8,128)S(1)} %slice.635), channel_id=1, source_target_pairs={{0,3},{1,4},{2,5},{3,6},{4,7},{5,8},{6,9},{7,10},{8,11},{9,12},{10... | collective-permute-start | bytes 506888 | tf_op jit(solution)/shard_map/ppermute | solution.py:160
  66.0 22.1 %collective-permute-start.8 = (f32[5,1,64,132]{3,2,1,0:T(8,128)S(1)}, f32[5,1,64,132]{3,2,1,0:T(8,128)S(1)}, u32[]{:S(2)}, u32[]{:S(2)}) collective-permute-start(f32[5,1,64,132]{3,2,1,0:T(8,128)S(1)} %collective-permute-done.4), channel_id=1, source_target_pairs={{2,0},{18,16},{34,32},{50,48},{66,64},{82,80},{98,96},{114,112},{1... | collective-permute-start | bytes 506888 | tf_op jit(solution)/shard_map/ppermute | solution.py:179
  67.3 20.8 %collective-permute-start.6 = (f32[5,1,64,132]{3,2,1,0:T(8,128)S(1)}, f32[5,1,64,132]{3,2,1,0:T(8,128)S(1)}, u32[]{:S(2)}, u32[]{:S(2)}) collective-permute-start(f32[5,1,64,132]{3,2,1,0:T(8,128)S(1)} %collective-permute-done.4), channel_id=1, source_target_pairs={{1,0},{2,1},{17,16},{18,17},{33,32},{34,33},{49,48},{50,49},{65,64... | collective-permute-start | bytes 506888 | tf_op jit(solution)/shard_map/ppermute | solution.py:179
  91.5 30.0 %collective-permute-start.10 = (f32[5,1,64,130]{3,2,1,0:T(8,128)S(1)}, f32[5,1,64,130]{3,2,1,0:T(8,128)S(1)}, u32[]{:S(2)}, u32[]{:S(2)}) collective-permute-start(f32[5,1,64,130]{3,2,1,0:T(8,128)S(1)} %slice.677), channel_id=1, source_target_pairs={{15,18},{14,17},{13,16},{31,34},{30,33},{29,32},{47,50},{46,49},{4... | collective-permute-start | bytes 499208 | tf_op jit(solution)/shard_map/ppermute | solution.py:166
  92.8 31.3 %collective-permute-start.11 = (f32[5,1,64,130]{3,2,1,0:T(8,128)S(1)}, f32[5,1,64,130]{3,2,1,0:T(8,128)S(1)}, u32[]{:S(2)}, u32[]{:S(2)}) collective-permute-start(f32[5,1,64,130]{3,2,1,0:T(8,128)S(1)} %slice.677), channel_id=1, source_target_pairs={{0,3},{1,4},{2,5},{3,6},{4,7},{5,8},{6,9},{7,10},{8,11},{9,12},{10... | collective-permute-start | bytes 499208 | tf_op jit(solution)/shard_map/ppermute | solution.py:160
  94.2 30.0 %collective-permute-start.15 = (f32[5,1,64,130]{3,2,1,0:T(8,128)S(1)}, f32[5,1,64,130]{3,2,1,0:T(8,128)S(1)}, u32[]{:S(2)}, u32[]{:S(2)}) collective-permute-start(f32[5,1,64,130]{3,2,1,0:T(8,128)S(1)} %slice.677), channel_id=1, source_target_pairs={{0,1},{1,2},{2,3},{3,4},{4,5},{5,6},{6,7},{7,8},{8,9},{9,10},{10,1... | collective-permute-start | bytes 499208 | tf_op jit(solution)/shard_map/ppermute | solution.py:160
  99.3 45.7 %collective-permute-start.13 = (f32[5,1,64,130]{3,2,1,0:T(8,128)S(1)}, f32[5,1,64,130]{3,2,1,0:T(8,128)S(1)}, u32[]{:S(2)}, u32[]{:S(2)}) collective-permute-start(f32[5,1,64,130]{3,2,1,0:T(8,128)S(1)} %slice.677), channel_id=1, source_target_pairs={{0,2},{1,3},{2,4},{3,5},{4,6},{5,7},{6,8},{7,9},{8,10},{9,11},{10,... | collective-permute-start | bytes 499208 | tf_op jit(solution)/shard_map/ppermute | solution.py:160
  121.5 23.5 %collective-permute-start.14 = (f32[5,1,64,130]{3,2,1,0:T(8,128)S(1)}, f32[5,1,64,130]{3,2,1,0:T(8,128)S(1)}, u32[]{:S(2)}, u32[]{:S(2)}) collective-permute-start(f32[5,1,64,130]{3,2,1,0:T(8,128)S(1)} %collective-permute-done.10), channel_id=1, source_target_pairs={{2,0},{18,16},{34,32},{50,48},{66,64},{82,80},{98,96},{114,112},{1... | collective-permute-start | bytes 499208 | tf_op jit(solution)/shard_map/ppermute | solution.py:179
  122.8 22.3 %collective-permute-start.12 = (f32[5,1,64,130]{3,2,1,0:T(8,128)S(1)}, f32[5,1,64,130]{3,2,1,0:T(8,128)S(1)}, u32[]{:S(2)}, u32[]{:S(2)}) collective-permute-start(f32[5,1,64,130]{3,2,1,0:T(8,128)S(1)} %collective-permute-done.10), channel_id=1, source_target_pairs={{1,0},{2,1},{17,16},{18,17},{33,32},{34,33},{49,48},{50,49},{65,64... | collective-permute-start | bytes 499208 | tf_op jit(solution)/shard_map/ppermute | solution.py:179
  147.9 23.4 %collective-permute-start.16 = (f32[5,1,64,128]{3,2,1,0:T(8,128)S(1)}, f32[5,1,64,128]{3,2,1,0:T(8,128)S(1)}, u32[]{:S(2)}, u32[]{:S(2)}) collective-permute-start(f32[5,1,64,128]{3,2,1,0:T(8,128)S(1)} %get-tuple-element.5), channel_id=1, source_target_pairs={{15,18},{14,17},{13,16},{31,34},{30,33},{29,32},{47,50},{46,49},{4... | collective-permute-start | bytes 491528 | tf_op jit(solution)/shard_map/ppermute | solution.py:166
  149.2 24.7 %collective-permute-start.17 = (f32[5,1,64,128]{3,2,1,0:T(8,128)S(1)}, f32[5,1,64,128]{3,2,1,0:T(8,128)S(1)}, u32[]{:S(2)}, u32[]{:S(2)}) collective-permute-start(f32[5,1,64,128]{3,2,1,0:T(8,128)S(1)} %get-tuple-element.5), channel_id=1, source_target_pairs={{0,3},{1,4},{2,5},{3,6},{4,7},{5,8},{6,9},{7,10},{8,11},{9,12},{10... | collective-permute-start | bytes 491528 | tf_op jit(solution)/shard_map/ppermute | solution.py:160
  150.6 23.4 %collective-permute-start.19 = (f32[5,1,64,128]{3,2,1,0:T(8,128)S(1)}, f32[5,1,64,128]{3,2,1,0:T(8,128)S(1)}, u32[]{:S(2)}, u32[]{:S(2)}) collective-permute-start(f32[5,1,64,128]{3,2,1,0:T(8,128)S(1)} %get-tuple-element.5), channel_id=1, source_target_pairs={{0,2},{1,3},{2,4},{3,5},{4,6},{5,7},{6,8},{7,9},{8,10},{9,11},{10,... | collective-permute-start | bytes 491528 | tf_op jit(solution)/shard_map/ppermute | solution.py:160
  155.5 22.3 %collective-permute-start.21 = (f32[5,1,64,128]{3,2,1,0:T(8,128)S(1)}, f32[5,1,64,128]{3,2,1,0:T(8,128)S(1)}, u32[]{:S(2)}, u32[]{:S(2)}) collective-permute-start(f32[5,1,64,128]{3,2,1,0:T(8,128)S(1)} %get-tuple-element.5), channel_id=1, source_target_pairs={{0,1},{1,2},{2,3},{3,4},{4,5},{5,6},{6,7},{7,8},{8,9},{9,10},{10,1... | collective-permute-start | bytes 491528 | tf_op jit(solution)/shard_map/ppermute | solution.py:160
  171.3 6.4 %collective-permute-start.18 = (f32[5,1,64,128]{3,2,1,0:T(8,128)S(1)}, f32[5,1,64,128]{3,2,1,0:T(8,128)S(1)}, u32[]{:S(2)}, u32[]{:S(2)}) collective-permute-start(f32[5,1,64,128]{3,2,1,0:T(8,128)S(1)} %collective-permute-done.16), channel_id=1, source_target_pairs={{1,0},{2,1},{17,16},{18,17},{33,32},{34,33},{49,48},{50,49},{65,64... | collective-permute-start | bytes 491528 | tf_op jit(solution)/shard_map/ppermute | solution.py:179
  172.6 10.9 %collective-permute-start.20 = (f32[5,1,64,128]{3,2,1,0:T(8,128)S(1)}, f32[5,1,64,128]{3,2,1,0:T(8,128)S(1)}, u32[]{:S(2)}, u32[]{:S(2)}) collective-permute-start(f32[5,1,64,128]{3,2,1,0:T(8,128)S(1)} %collective-permute-done.16), channel_id=1, source_target_pairs={{2,0},{18,16},{34,32},{50,48},{66,64},{82,80},{98,96},{114,112},{1... | collective-permute-start | bytes 491528 | tf_op jit(solution)/shard_map/ppermute | solution.py:179

commit v9 on v4

--- a/solution.py
+++ b/solution.py
@@ -6,6 +6,7 @@
 STEPS = 3
 SMAX = 192
 PLANE = 16
+HALVES = 2
 
 
 courant = 0.2
@@ -130,18 +131,20 @@
     return 2 * lane
 
 
-def crossing_relays(groups, count, plane, blocks):
+def crossing_relays(groups, count, plane, blocks, halves):
     half = plane // 2
-    first, second = [], []
+    first = [[] for _ in range(halves)]
+    second = [[] for _ in range(halves)]
     for g in range(groups):
         for block in range(count // plane):
             base = block * plane
             after = (base + plane) % count
             for j in range(1, blocks + 1):
-                lane = (3 * g + j - 1) % half
-                relay = base + relay_seat(lane, plane - j, plane, blocks)
-                first.append((g * count + base + plane - j, g * count + relay))
-                second.append((g * count + relay, g * count + after + blocks - j))
+                for h in range(halves):
+                    lane = (3 * g + j - 1 + h * half // halves) % half
+                    relay = base + relay_seat(lane, plane - j, plane, blocks)
+                    first[h].append((g * count + base + plane - j, g * count + relay))
+                    second[h].append((g * count + relay, g * count + after + blocks - j))
     return first, second
 
 
@@ -158,9 +161,15 @@
             if a // plane == ((a + k) % count) // plane
         ]
         near.append(lax.ppermute(head, "azi", pairs))
-    first, second = crossing_relays(groups, count, plane, blocks)
-    relayed = lax.ppermute(head, ("rad", "azi"), first)
-    crossed = lax.ppermute(relayed, ("rad", "azi"), second)
+    halves = HALVES if head.shape[2] % HALVES == 0 and plane >= 4 * blocks else 1
+    first, second = crossing_relays(groups, count, plane, blocks, halves)
+    size = head.shape[2] // halves
+    parts = []
+    for h in range(halves):
+        part = head[:, :, h * size : (h + 1) * size]
+        relayed = lax.ppermute(part, ("rad", "azi"), first[h])
+        parts.append(lax.ppermute(relayed, ("rad", "azi"), second[h]))
+    crossed = jnp.concatenate(parts, axis=2)
     position = lax.axis_index("azi") % plane
     pieces = []
     for k in range(1, blocks + 1):

time: 167 us -> 205 us (1.23)
  the two profiles are of different devices: /device:TPU:64 before, /device:TPU:6 now
where the time goes in v9:
time: 205 us; the launch traced here: 204 us
  starting transfers between devices  100 us (49%)
  waiting for transfers between devices  89.2 us (44%)
  other arithmetic  10.1 us (5%)
  local copies, waits for them, and re-layouts  3.69 us (2%)
    ppermute x6, waiting for transfers between devices, rotation_pieces(): parts.append(lax.ppermute(relayed, ('rad', 'azi'), second[h]))  65.7 us
    ppermute x9, starting transfers between devices, rotation_pieces(): near.append(lax.ppermute(head, 'azi', pairs))  52.3 us
    ppermute x4, starting transfers between devices, passed_along(): return lax.ppermute(value, axis, pairs)  28.5 us
    ppermute x6, waiting for transfers between devices, rotation_pieces(): far = lax.ppermute(crossed, 'azi', pairs)  19.4 us
    ppermute x6, starting transfers between devices, rotation_pieces(): far = lax.ppermute(crossed, 'azi', pairs)  7.75 us
    ppermute x6, starting transfers between devices, rotation_pieces(): parts.append(lax.ppermute(relayed, ('rad', 'azi'), second[h]))  7.75 us
  transfers between devices with their start and end apart: 31, of which 9 were waited for; matrix products, arithmetic and copies ran while one was open for 1% of the time, Pallas kernels for 0%

profile of v9, /device:TPU:6, one launch (start us, length us, event | category | flops | bytes accessed | tf_op | source)
XLA Modules:
  0.0 204.4 jit_solution(12895841444729159935)
XLA Ops:
  0.0 0.8 fusion.106
  0.8 1.9 collective-permute-start
  2.7 22.0 %collective-permute-start.1 = (f32[5,1,3,128]{3,2,1,0:T(4,128)S(1)}, f32[5,1,3,128]{3,2,1,0:T(4,128)S(1)}, u32[]{:S(2)}, u32[]{:S(2)}) collective-permute-start(f32[5,1,3,128]{3,2,1,0:T(4,128)S(1)} %get-tuple-element.53), channel_id=1, source_target_pairs={{0,127},{1,0},{2,1},{3,2},{4,3},{5,4},{6,5},{7,6},{8,7},{9,8},{10,... | collective-permute-start | bytes 23048 | tf_op jit(solution)/shard_map/ppermute | solution.py:26
  24.7 0.8 slice_convert_fusion.1
  26.1 0.9 pad_maximum_fusion
  27.1 0.2 reshape.1273
  27.4 3.4 %collective-permute-start.2 = (f32[1059]{0:T(1024)S(1)}, f32[1059]{0:T(1024)S(1)}, u32[]{:S(2)}, u32[]{:S(2)}) collective-permute-start(f32[1059]{0:T(1024)S(1)} %pad_maximum_fusion.1), channel_id=1, source_target_pairs={{0,128},{128,256},{256,384},{384,512},{512,640},{640,768},{768,896... | collective-permute-start | bytes 12716 | tf_op jit(solution)/shard_map/ppermute | solution.py:26
  30.8 0.2 reshape.1275
  31.1 1.3 collective-permute-start.3
  32.4 0.2 concatenate.49
  32.6 4.0 %collective-permute-done.3 = f32[1059]{0:T(1024)S(1)} collective-permute-done((f32[1059]{0:T(1024)S(1)}, f32[1059]{0:T(1024)S(1)}, u32[]{:S(2)}, u32[]{:S(2)}) %collective-permute-start.3) | collective-permute-done | bytes 4268 | tf_op jit(solution)/shard_map/ppermute | solution.py:26
  36.6 0.2 concatenate.50
  36.8 0.2 maximum_select_fusion
  37.2 0.2 subtract_multiply_fusion.3
  37.3 0.6 subtract_add_fusion.1
  38.6 1.3 collective-permute-start.12
  39.9 1.3 collective-permute-start.10
  41.2 1.3 collective-permute-start.8
  42.5 0.7 collective-permute-start.4
  43.2 0.7 collective-permute-start.6
  44.4 1.3 collective-permute-start.5
  45.8 1.3 collective-permute-start.7
  47.0 29.5 %collective-permute-done.5 = f32[5,1,32,132]{3,2,1,0:T(8,128)S(1)} collective-permute-done((f32[5,1,32,132]{3,2,1,0:T(8,128)S(1)}, f32[5,1,32,132]{3,2,1,0:T(8,128)S(1)}, u32[]{:S(2)}, u32[]{:S(2)}) %collective-permute-start.5) | collective-permute-done | bytes 84512 | tf_op jit(solution)/shard_map/ppermute | solution.py:171
  76.6 1.3 collective-permute-start.11
  77.9 1.3 collective-permute-start.9
  79.3 6.3 %collective-permute-done.11 = f32[5,1,64,132]{3,2,1,0:T(8,128)S(1)} collective-permute-done((f32[5,1,64,132]{3,2,1,0:T(8,128)S(1)}, f32[5,1,64,132]{3,2,1,0:T(8,128)S(1)}, u32[]{:S(2)}, u32[]{:S(2)}) %collective-permute-start.11) | collective-permute-done | bytes 168992 | tf_op jit(solution)/shard_map/ppermute | solution.py:185
  85.8 0.7 concatenate.53
  86.5 0.2 slice_select_fusion
  86.6 0.2 slice_select_fusion.5
  86.8 0.2 slice_select_fusion.4
  87.0 0.1 slice_select_fusion.7
  87.6 0.2 subtract_multiply_fusion.1
  87.8 0.6 subtract_add_fusion
  88.6 0.1 fusion.14
  89.0 0.7 collective-permute-start.13
  89.7 0.7 collective-permute-start.15
  90.4 1.3 collective-permute-start.14
  91.8 15.6 %collective-permute-start.21 = (f32[5,1,64,130]{3,2,1,0:T(8,128)S(1)}, f32[5,1,64,130]{3,2,1,0:T(8,128)S(1)}, u32[]{:S(2)}, u32[]{:S(2)}) collective-permute-start(f32[5,1,64,130]{3,2,1,0:T(8,128)S(1)} %slice.709), channel_id=1, source_target_pairs={{0,1},{1,2},{2,3},{3,4},{4,5},{5,6},{6,7},{7,8},{8,9},{9,10},{10,1... | collective-permute-start | bytes 499208 | tf_op jit(solution)/shard_map/ppermute | solution.py:163
  107.4 9.7 %collective-permute-start.19 = (f32[5,1,64,130]{3,2,1,0:T(8,128)S(1)}, f32[5,1,64,130]{3,2,1,0:T(8,128)S(1)}, u32[]{:S(2)}, u32[]{:S(2)}) collective-permute-start(f32[5,1,64,130]{3,2,1,0:T(8,128)S(1)} %slice.709), channel_id=1, source_target_pairs={{0,2},{1,3},{2,4},{3,5},{4,6},{5,7},{6,8},{7,9},{8,10},{9,11},{10,... | collective-permute-start | bytes 499208 | tf_op jit(solution)/shard_map/ppermute | solution.py:163
  117.1 1.5 collective-permute-start.17
  118.6 1.3 collective-permute-start.16
  120.0 19.1 %collective-permute-done.16 = f32[5,1,32,130]{3,2,1,0:T(8,128)S(1)} collective-permute-done((f32[5,1,32,130]{3,2,1,0:T(8,128)S(1)}, f32[5,1,32,130]{3,2,1,0:T(8,128)S(1)}, u32[]{:S(2)}, u32[]{:S(2)}) %collective-permute-start.16) | collective-permute-done | bytes 83232 | tf_op jit(solution)/shard_map/ppermute | solution.py:171
  139.1 1.3 collective-permute-start.20
  140.4 1.3 collective-permute-start.18
  141.7 6.3 %collective-permute-done.20 = f32[5,1,64,130]{3,2,1,0:T(8,128)S(1)} collective-permute-done((f32[5,1,64,130]{3,2,1,0:T(8,128)S(1)}, f32[5,1,64,130]{3,2,1,0:T(8,128)S(1)}, u32[]{:S(2)}, u32[]{:S(2)}) %collective-permute-start.20) | collective-permute-done | bytes 166432 | tf_op jit(solution)/shard_map/ppermute | solution.py:185
  148.2 0.7 concatenate.55
  148.9 0.2 slice_select_fusion.3
  149.1 0.2 slice_select_fusion.2
  149.2 0.2 slice_select_fusion.1
  149.4 0.1 slice_select_fusion.6
  150.2 0.3 subtract_add_fusion.2
  150.9 0.7 collective-permute-start.22
  151.6 0.7 collective-permute-start.24
  152.3 1.3 collective-permute-start.23
  153.6 17.6 %collective-permute-start.26 = (f32[5,1,64,128]{3,2,1,0:T(8,128)S(1)}, f32[5,1,64,128]{3,2,1,0:T(8,128)S(1)}, u32[]{:S(2)}, u32[]{:S(2)}) collective-permute-start(f32[5,1,64,128]{3,2,1,0:T(8,128)S(1)} %get-tuple-element.5), channel_id=1, source_target_pairs={{0,3},{1,4},{2,5},{3,6},{4,7},{5,8},{6,9},{7,10},{8,11},{9,12},{10... | collective-permute-start | bytes 491528 | tf_op jit(solution)/shard_map/ppermute | solution.py:163
  171.2 1.3 collective-permute-start.28
  172.5 2.6 %collective-permute-start.30 = (f32[5,1,64,128]{3,2,1,0:T(8,128)S(1)}, f32[5,1,64,128]{3,2,1,0:T(8,128)S(1)}, u32[]{:S(2)}, u32[]{:S(2)}) collective-permute-start(f32[5,1,64,128]{3,2,1,0:T(8,128)S(1)} %get-tuple-element.5), channel_id=1, source_target_pairs={{0,1},{1,2},{2,3},{3,4},{4,5},{5,6},{6,7},{7,8},{8,9},{9,10},{10,1... | collective-permute-start | bytes 491528 | tf_op jit(solution)/shard_map/ppermute | solution.py:163
  175.2 1.3 collective-permute-start.25
  176.5 17.1 %collective-permute-done.25 = f32[5,1,32,128]{3,2,1,0:T(8,128)S(1)} collective-permute-done((f32[5,1,32,128]{3,2,1,0:T(8,128)S(1)}, f32[5,1,32,128]{3,2,1,0:T(8,128)S(1)}, u32[]{:S(2)}, u32[]{:S(2)}) %collective-permute-start.25) | collective-permute-done | bytes 81952 | tf_op jit(solution)/shard_map/ppermute | solution.py:171
  193.6 1.3 collective-permute-start.27
  194.9 1.3 collective-permute-start.29
  196.2 1.0 collective-permute-done.27
  197.3 5.7 %collective-permute-done.29 = f32[5,1,64,128]{3,2,1,0:T(8,128)S(1)} collective-permute-done((f32[5,1,64,128]{3,2,1,0:T(8,128)S(1)}, f32[5,1,64,128]{3,2,1,0:T(8,128)S(1)}, u32[]{:S(2)}, u32[]{:S(2)}) %collective-permute-start.29) | collective-permute-done | bytes 163872 | tf_op jit(solution)/shard_map/ppermute | solution.py:185
  203.8 0.7 slice_select_fusion.23
  (114 shorter events, 5.1 us)
Async XLA Ops:
  0.0 36.8 %copy-start = (f32[5,1,64,128]{3,2,1,0:T(8,128)S(1)}, f32[5,1,64,128]{3,2,1,0:T(8,128)}, u32[]{:S(2)}) copy-start(f32[5,1,64,128]{3,2,1,0:T(8,128)} %param.2) | copy-start | bytes 491524
  0.8 25.2 %collective-permute-start = (f32[5,1,3,128]{3,2,1,0:T(4,128)S(1)}, f32[5,1,3,128]{3,2,1,0:T(4,128)S(1)}, u32[]{:S(2)}, u32[]{:S(2)}) collective-permute-start(f32[5,1,3,128]{3,2,1,0:T(4,128)S(1)} %get-tuple-element.52), channel_id=1, source_target_pairs={{0,1},{1,2},{2,3},{3,4},{4,5},{5,6},{6,7},{7,8},{8,9},{9,10},{10,1... | collective-permute-start | bytes 23048 | tf_op jit(solution)/shard_map/ppermute | solution.py:26
  2.7 23.3 %collective-permute-start.1 = (f32[5,1,3,128]{3,2,1,0:T(4,128)S(1)}, f32[5,1,3,128]{3,2,1,0:T(4,128)S(1)}, u32[]{:S(2)}, u32[]{:S(2)}) collective-permute-start(f32[5,1,3,128]{3,2,1,0:T(4,128)S(1)} %get-tuple-element.53), channel_id=1, source_target_pairs={{0,127},{1,0},{2,1},{3,2},{4,3},{5,4},{6,5},{7,6},{8,7},{9,8},{10,... | collective-permute-start | bytes 23048 | tf_op jit(solution)/shard_map/ppermute | solution.py:26
  27.4 5.0 %collective-permute-start.2 = (f32[1059]{0:T(1024)S(1)}, f32[1059]{0:T(1024)S(1)}, u32[]{:S(2)}, u32[]{:S(2)}) collective-permute-start(f32[1059]{0:T(1024)S(1)} %pad_maximum_fusion.1), channel_id=1, source_target_pairs={{0,128},{128,256},{256,384},{384,512},{512,640},{640,768},{768,896... | collective-permute-start | bytes 12716 | tf_op jit(solution)/shard_map/ppermute | solution.py:26
  31.1 5.5 %collective-permute-start.3 = (f32[1059]{0:T(1024)S(1)}, f32[1059]{0:T(1024)S(1)}, u32[]{:S(2)}, u32[]{:S(2)}) collective-permute-start(f32[1059]{0:T(1024)S(1)} %pad_maximum_fusion.2), channel_id=1, source_target_pairs={{128,0},{256,128},{384,256},{512,384},{640,512},{768,640},{896,768... | collective-permute-start | bytes 12716 | tf_op jit(solution)/shard_map/ppermute | solution.py:26
  38.0 6.2 %copy-start.1 = (s32[3,128]{1,0:T(4,128)S(1)}, s32[3,128]{1,0:T(4,128)}, u32[]{:S(2)}) copy-start(s32[3,128]{1,0:T(4,128)} %param.3) | copy-start | bytes 4612
  38.6 40.7 %collective-permute-start.12 = (f32[5,1,64,132]{3,2,1,0:T(8,128)S(1)}, f32[5,1,64,132]{3,2,1,0:T(8,128)S(1)}, u32[]{:S(2)}, u32[]{:S(2)}) collective-permute-start(f32[5,1,64,132]{3,2,1,0:T(8,128)S(1)} %slice.665), channel_id=1, source_target_pairs={{0,1},{1,2},{2,3},{3,4},{4,5},{5,6},{6,7},{7,8},{8,9},{9,10},{10,1... | collective-permute-start | bytes 506888 | tf_op jit(solution)/shard_map/ppermute | solution.py:163
  39.9 45.7 %collective-permute-start.10 = (f32[5,1,64,132]{3,2,1,0:T(8,128)S(1)}, f32[5,1,64,132]{3,2,1,0:T(8,128)S(1)}, u32[]{:S(2)}, u32[]{:S(2)}) collective-permute-start(f32[5,1,64,132]{3,2,1,0:T(8,128)S(1)} %slice.665), channel_id=1, source_target_pairs={{0,2},{1,3},{2,4},{3,5},{4,6},{5,7},{6,8},{7,9},{8,10},{9,11},{10,... | collective-permute-start | bytes 506888 | tf_op jit(solution)/shard_map/ppermute | solution.py:163
  41.2 38.0 %collective-permute-start.8 = (f32[5,1,64,132]{3,2,1,0:T(8,128)S(1)}, f32[5,1,64,132]{3,2,1,0:T(8,128)S(1)}, u32[]{:S(2)}, u32[]{:S(2)}) collective-permute-start(f32[5,1,64,132]{3,2,1,0:T(8,128)S(1)} %slice.665), channel_id=1, source_target_pairs={{0,3},{1,4},{2,5},{3,6},{4,7},{5,8},{6,9},{7,10},{8,11},{9,12},{10... | collective-permute-start | bytes 506888 | tf_op jit(solution)/shard_map/ppermute | solution.py:163
  42.5 1.8 collective-permute-start.4
  43.2 2.5 %collective-permute-start.6 = (f32[5,1,32,132]{3,2,1,0:T(8,128)S(1)}, f32[5,1,32,132]{3,2,1,0:T(8,128)S(1)}, u32[]{:S(2)}, u32[]{:S(2)}) collective-permute-start(f32[5,1,32,132]{3,2,1,0:T(8,128)S(1)} %get-tuple-element.39), channel_id=1, source_target_pairs={{15,8},{14,10},{13,13},{31,24},{30,26},{29,29},{47,40},{46,42},{45... | collective-permute-start | bytes 253448 | tf_op jit(solution)/shard_map/ppermute | solution.py:170
  44.4 32.2 %collective-permute-start.5 = (f32[5,1,32,132]{3,2,1,0:T(8,128)S(1)}, f32[5,1,32,132]{3,2,1,0:T(8,128)S(1)}, u32[]{:S(2)}, u32[]{:S(2)}) collective-permute-start(f32[5,1,32,132]{3,2,1,0:T(8,128)S(1)} %collective-permute-done.4), channel_id=1, source_target_pairs={{1,18},{3,17},{4,16},{17,34},{19,33},{20,32},{33,50},{35,49},{36,4... | collective-permute-start | bytes 253448 | tf_op jit(solution)/shard_map/ppermute | solution.py:171
  45.8 30.9 %collective-permute-start.7 = (f32[5,1,32,132]{3,2,1,0:T(8,128)S(1)}, f32[5,1,32,132]{3,2,1,0:T(8,128)S(1)}, u32[]{:S(2)}, u32[]{:S(2)}) collective-permute-start(f32[5,1,32,132]{3,2,1,0:T(8,128)S(1)} %collective-permute-done.6), channel_id=1, source_target_pairs={{8,18},{10,17},{13,16},{24,34},{26,33},{29,32},{40,50},{42,49},{45... | collective-permute-start | bytes 253448 | tf_op jit(solution)/shard_map/ppermute | solution.py:171
  76.6 9.0 %collective-permute-start.11 = (f32[5,1,64,132]{3,2,1,0:T(8,128)S(1)}, f32[5,1,64,132]{3,2,1,0:T(8,128)S(1)}, u32[]{:S(2)}, u32[]{:S(2)}) collective-permute-start(f32[5,1,64,132]{3,2,1,0:T(8,128)S(1)} %constant_dynamic-update-slice_fusion), channel_id=1, source_target_pairs={{2,0},{18,16},{34,32},{50,48},{66,64},{82,80},{98,96},{114,112},{1... | collective-permute-start | bytes 506888 | tf_op jit(solution)/shard_map/ppermute | solution.py:185
  77.9 7.7 %collective-permute-start.9 = (f32[5,1,64,132]{3,2,1,0:T(8,128)S(1)}, f32[5,1,64,132]{3,2,1,0:T(8,128)S(1)}, u32[]{:S(2)}, u32[]{:S(2)}) collective-permute-start(f32[5,1,64,132]{3,2,1,0:T(8,128)S(1)} %constant_dynamic-update-slice_fusion), channel_id=1, source_target_pairs={{1,0},{2,1},{17,16},{18,17},{33,32},{34,33},{49,48},{50,49},{65,64... | collective-permute-start | bytes 506888 | tf_op jit(solution)/shard_map/ppermute | solution.py:185
  89.0 1.4 collective-permute-start.13
  89.7 28.9 %collective-permute-start.15 = (f32[5,1,32,130]{3,2,1,0:T(8,128)S(1)}, f32[5,1,32,130]{3,2,1,0:T(8,128)S(1)}, u32[]{:S(2)}, u32[]{:S(2)}) collective-permute-start(f32[5,1,32,130]{3,2,1,0:T(8,128)S(1)} %get-tuple-element.30), channel_id=1, source_target_pairs={{15,8},{14,10},{13,13},{31,24},{30,26},{29,29},{47,40},{46,42},{45... | collective-permute-start | bytes 249608 | tf_op jit(solution)/shard_map/ppermute | solution.py:170
  90.4 29.5 %collective-permute-start.14 = (f32[5,1,32,130]{3,2,1,0:T(8,128)S(1)}, f32[5,1,32,130]{3,2,1,0:T(8,128)S(1)}, u32[]{:S(2)}, u32[]{:S(2)}) collective-permute-start(f32[5,1,32,130]{3,2,1,0:T(8,128)S(1)} %collective-permute-done.13), channel_id=1, source_target_pairs={{1,18},{3,17},{4,16},{17,34},{19,33},{20,32},{33,50},{35,49},{36,4... | collective-permute-start | bytes 249608 | tf_op jit(solution)/shard_map/ppermute | solution.py:171
  91.8 50.0 %collective-permute-start.21 = (f32[5,1,64,130]{3,2,1,0:T(8,128)S(1)}, f32[5,1,64,130]{3,2,1,0:T(8,128)S(1)}, u32[]{:S(2)}, u32[]{:S(2)}) collective-permute-start(f32[5,1,64,130]{3,2,1,0:T(8,128)S(1)} %slice.709), channel_id=1, source_target_pairs={{0,1},{1,2},{2,3},{3,4},{4,5},{5,6},{6,7},{7,8},{8,9},{9,10},{10,1... | collective-permute-start | bytes 499208 | tf_op jit(solution)/shard_map/ppermute | solution.py:163
  107.4 40.7 %collective-permute-start.19 = (f32[5,1,64,130]{3,2,1,0:T(8,128)S(1)}, f32[5,1,64,130]{3,2,1,0:T(8,128)S(1)}, u32[]{:S(2)}, u32[]{:S(2)}) collective-permute-start(f32[5,1,64,130]{3,2,1,0:T(8,128)S(1)} %slice.709), channel_id=1, source_target_pairs={{0,2},{1,3},{2,4},{3,5},{4,6},{5,7},{6,8},{7,9},{8,10},{9,11},{10,... | collective-permute-start | bytes 499208 | tf_op jit(solution)/shard_map/ppermute | solution.py:163
  117.1 24.6 %collective-permute-start.17 = (f32[5,1,64,130]{3,2,1,0:T(8,128)S(1)}, f32[5,1,64,130]{3,2,1,0:T(8,128)S(1)}, u32[]{:S(2)}, u32[]{:S(2)}) collective-permute-start(f32[5,1,64,130]{3,2,1,0:T(8,128)S(1)} %slice.709), channel_id=1, source_target_pairs={{0,3},{1,4},{2,5},{3,6},{4,7},{5,8},{6,9},{7,10},{8,11},{9,12},{10... | collective-permute-start | bytes 499208 | tf_op jit(solution)/shard_map/ppermute | solution.py:163
  118.6 20.4 %collective-permute-start.16 = (f32[5,1,32,130]{3,2,1,0:T(8,128)S(1)}, f32[5,1,32,130]{3,2,1,0:T(8,128)S(1)}, u32[]{:S(2)}, u32[]{:S(2)}) collective-permute-start(f32[5,1,32,130]{3,2,1,0:T(8,128)S(1)} %collective-permute-done.15), channel_id=1, source_target_pairs={{8,18},{10,17},{13,16},{24,34},{26,33},{29,32},{40,50},{42,49},{45... | collective-permute-start | bytes 249608 | tf_op jit(solution)/shard_map/ppermute | solution.py:171
  139.1 9.0 %collective-permute-start.20 = (f32[5,1,64,130]{3,2,1,0:T(8,128)S(1)}, f32[5,1,64,130]{3,2,1,0:T(8,128)S(1)}, u32[]{:S(2)}, u32[]{:S(2)}) collective-permute-start(f32[5,1,64,130]{3,2,1,0:T(8,128)S(1)} %constant_dynamic-update-slice_fusion.2), channel_id=1, source_target_pairs={{2,0},{18,16},{34,32},{50,48},{66,64},{82,80},{98,96},{114,112},{1... | collective-permute-start | bytes 499208 | tf_op jit(solution)/shard_map/ppermute | solution.py:185
  140.4 7.7 %collective-permute-start.18 = (f32[5,1,64,130]{3,2,1,0:T(8,128)S(1)}, f32[5,1,64,130]{3,2,1,0:T(8,128)S(1)}, u32[]{:S(2)}, u32[]{:S(2)}) collective-permute-start(f32[5,1,64,130]{3,2,1,0:T(8,128)S(1)} %constant_dynamic-update-slice_fusion.2), channel_id=1, source_target_pairs={{1,0},{2,1},{17,16},{18,17},{33,32},{34,33},{49,48},{50,49},{65,64... | collective-permute-start | bytes 499208 | tf_op jit(solution)/shard_map/ppermute | solution.py:185
  150.9 1.4 collective-permute-start.22
  151.6 23.6 %collective-permute-start.24 = (f32[5,1,32,128]{3,2,1,0:T(8,128)S(1)}, f32[5,1,32,128]{3,2,1,0:T(8,128)S(1)}, u32[]{:S(2)}, u32[]{:S(2)}) collective-permute-start(f32[5,1,32,128]{3,2,1,0:T(8,128)S(1)} %get-tuple-element.50), channel_id=1, source_target_pairs={{15,8},{14,10},{13,13},{31,24},{30,26},{29,29},{47,40},{46,42},{45... | collective-permute-start | bytes 245768 | tf_op jit(solution)/shard_map/ppermute | solution.py:170
  152.3 24.2 %collective-permute-start.23 = (f32[5,1,32,128]{3,2,1,0:T(8,128)S(1)}, f32[5,1,32,128]{3,2,1,0:T(8,128)S(1)}, u32[]{:S(2)}, u32[]{:S(2)}) collective-permute-start(f32[5,1,32,128]{3,2,1,0:T(8,128)S(1)} %collective-permute-done.22), channel_id=1, source_target_pairs={{1,18},{3,17},{4,16},{17,34},{19,33},{20,32},{33,50},{35,49},{36,4... | collective-permute-start | bytes 245768 | tf_op jit(solution)/shard_map/ppermute | solution.py:171
  153.6 42.6 %collective-permute-start.26 = (f32[5,1,64,128]{3,2,1,0:T(8,128)S(1)}, f32[5,1,64,128]{3,2,1,0:T(8,128)S(1)}, u32[]{:S(2)}, u32[]{:S(2)}) collective-permute-start(f32[5,1,64,128]{3,2,1,0:T(8,128)S(1)} %get-tuple-element.5), channel_id=1, source_target_pairs={{0,3},{1,4},{2,5},{3,6},{4,7},{5,8},{6,9},{7,10},{8,11},{9,12},{10... | collective-permute-start | bytes 491528 | tf_op jit(solution)/shard_map/ppermute | solution.py:163
  171.2 25.0 %collective-permute-start.28 = (f32[5,1,64,128]{3,2,1,0:T(8,128)S(1)}, f32[5,1,64,128]{3,2,1,0:T(8,128)S(1)}, u32[]{:S(2)}, u32[]{:S(2)}) collective-permute-start(f32[5,1,64,128]{3,2,1,0:T(8,128)S(1)} %get-tuple-element.5), channel_id=1, source_target_pairs={{0,2},{1,3},{2,4},{3,5},{4,6},{5,7},{6,8},{7,9},{8,10},{9,11},{10,... | collective-permute-start | bytes 491528 | tf_op jit(solution)/shard_map/ppermute | solution.py:163
  172.5 24.8 %collective-permute-start.30 = (f32[5,1,64,128]{3,2,1,0:T(8,128)S(1)}, f32[5,1,64,128]{3,2,1,0:T(8,128)S(1)}, u32[]{:S(2)}, u32[]{:S(2)}) collective-permute-start(f32[5,1,64,128]{3,2,1,0:T(8,128)S(1)} %get-tuple-element.5), channel_id=1, source_target_pairs={{0,1},{1,2},{2,3},{3,4},{4,5},{5,6},{6,7},{7,8},{8,9},{9,10},{10,1... | collective-permute-start | bytes 491528 | tf_op jit(solution)/shard_map/ppermute | solution.py:163
  175.2 18.4 %collective-permute-start.25 = (f32[5,1,32,128]{3,2,1,0:T(8,128)S(1)}, f32[5,1,32,128]{3,2,1,0:T(8,128)S(1)}, u32[]{:S(2)}, u32[]{:S(2)}) collective-permute-start(f32[5,1,32,128]{3,2,1,0:T(8,128)S(1)} %collective-permute-done.24), channel_id=1, source_target_pairs={{8,18},{10,17},{13,16},{24,34},{26,33},{29,32},{40,50},{42,49},{45... | collective-permute-start | bytes 245768 | tf_op jit(solution)/shard_map/ppermute | solution.py:171
  193.6 3.7 %collective-permute-start.27 = (f32[5,1,64,128]{3,2,1,0:T(8,128)S(1)}, f32[5,1,64,128]{3,2,1,0:T(8,128)S(1)}, u32[]{:S(2)}, u32[]{:S(2)}) collective-permute-start(f32[5,1,64,128]{3,2,1,0:T(8,128)S(1)} %constant_dynamic-update-slice_fusion.9), channel_id=1, source_target_pairs={{1,0},{2,1},{17,16},{18,17},{33,32},{34,33},{49,48},{50,49},{65,64... | collective-permute-start | bytes 491528 | tf_op jit(solution)/shard_map/ppermute | solution.py:185
  194.9 8.2 %collective-permute-start.29 = (f32[5,1,64,128]{3,2,1,0:T(8,128)S(1)}, f32[5,1,64,128]{3,2,1,0:T(8,128)S(1)}, u32[]{:S(2)}, u32[]{:S(2)}) collective-permute-start(f32[5,1,64,128]{3,2,1,0:T(8,128)S(1)} %constant_dynamic-update-slice_fusion.9), channel_id=1, source_target_pairs={{2,0},{18,16},{34,32},{50,48},{66,64},{82,80},{98,96},{114,112},{1... | collective-permute-start | bytes 491528 | tf_op jit(solution)/shard_map/ppermute | solution.py:185

commit v10 on v4

--- a/solution.py
+++ b/solution.py
@@ -160,6 +160,7 @@
         near.append(lax.ppermute(head, "azi", pairs))
     first, second = crossing_relays(groups, count, plane, blocks)
     relayed = lax.ppermute(head, ("rad", "azi"), first)
+    near, relayed = lax.optimization_barrier((near, relayed))
     crossed = lax.ppermute(relayed, ("rad", "azi"), second)
     position = lax.axis_index("azi") % plane
     pieces = []

time: 167 us -> 207 us (1.24)
  waiting for transfers between devices: 84.7 us -> 124 us
    ppermute x9, waiting for transfers between devices: 0.02 us -> 24.2 us  [rotation_pieces(): near.append(lax.ppermute(head, 'azi', pairs))]
    ppermute x3, waiting for transfers between devices: 62.9 us -> 79.9 us  [rotation_pieces(): crossed = lax.ppermute(relayed, ('rad', 'azi'), second)]
  transfers between devices with their start and end apart: 25 -> 25, of which waited for: 9 -> 15; matrix products, arithmetic and copies ran while one was open for 2% -> 1% of each run, Pallas kernels for 0% -> 0%
where the time goes in v10:
time: 207 us; the launch traced here: 206 us
  waiting for transfers between devices  124 us (60%)
  starting transfers between devices  67.8 us (33%)
  other arithmetic  10.1 us (5%)
  local copies, waits for them, and re-layouts  3.57 us (2%)
    ppermute x3, waiting for transfers between devices, rotation_pieces(): crossed = lax.ppermute(relayed, ('rad', 'azi'), second)  79.9 us
    ppermute x4, starting transfers between devices, passed_along(): return lax.ppermute(value, axis, pairs)  34 us
    ppermute x9, waiting for transfers between devices, rotation_pieces(): near.append(lax.ppermute(head, 'azi', pairs))  24.2 us
    ppermute x9, starting transfers between devices, rotation_pieces(): near.append(lax.ppermute(head, 'azi', pairs))  20.2 us
    ppermute x6, waiting for transfers between devices, rotation_pieces(): far = lax.ppermute(crossed, 'azi', pairs)  18.5 us
    ppermute x6, starting transfers between devices, rotation_pieces(): far = lax.ppermute(crossed, 'azi', pairs)  7.72 us
  transfers between devices with their start and end apart: 25, of which 15 were waited for; matrix products, arithmetic and copies ran while one was open for 1% of the time, Pallas kernels for 0%

profile of v10, /device:TPU:64, one launch (start us, length us, event | category | flops | bytes accessed | tf_op | source)
XLA Modules:
  0.0 206.1 jit_solution(11609696289865137837)
XLA Ops:
  0.0 0.8 fusion.103
  0.8 1.9 collective-permute-start
  2.7 23.0 %collective-permute-start.1 = (f32[5,1,3,128]{3,2,1,0:T(4,128)S(1)}, f32[5,1,3,128]{3,2,1,0:T(4,128)S(1)}, u32[]{:S(2)}, u32[]{:S(2)}) collective-permute-start(f32[5,1,3,128]{3,2,1,0:T(4,128)S(1)} %get-tuple-element.71), channel_id=1, source_target_pairs={{0,127},{1,0},{2,1},{3,2},{4,3},{5,4},{6,5},{7,6},{8,7},{9,8},{10,... | collective-permute-start | bytes 23048 | tf_op jit(solution)/shard_map/ppermute | solution.py:25
  25.7 0.8 slice_convert_fusion.1
  27.1 0.9 pad_maximum_fusion
  28.2 0.2 reshape.1273
  28.4 3.4 %collective-permute-start.2 = (f32[1059]{0:T(1024)S(1)}, f32[1059]{0:T(1024)S(1)}, u32[]{:S(2)}, u32[]{:S(2)}) collective-permute-start(f32[1059]{0:T(1024)S(1)} %pad_maximum_fusion.1), channel_id=1, source_target_pairs={{0,128},{128,256},{256,384},{384,512},{512,640},{640,768},{768,896... | collective-permute-start | bytes 12716 | tf_op jit(solution)/shard_map/ppermute | solution.py:25
  31.8 0.2 reshape.1275
  32.1 5.7 %collective-permute-start.3 = (f32[1059]{0:T(1024)S(1)}, f32[1059]{0:T(1024)S(1)}, u32[]{:S(2)}, u32[]{:S(2)}) collective-permute-start(f32[1059]{0:T(1024)S(1)} %pad_maximum_fusion.2), channel_id=1, source_target_pairs={{128,0},{256,128},{384,256},{512,384},{640,512},{768,640},{896,768... | collective-permute-start | bytes 12716 | tf_op jit(solution)/shard_map/ppermute | solution.py:25
  37.8 0.2 concatenate.40
  38.0 1.1 collective-permute-done.3
  39.1 0.2 concatenate.41
  39.3 0.2 maximum_select_fusion
  39.7 0.2 subtract_multiply_fusion.3
  39.9 0.6 subtract_add_fusion.1
  41.1 1.3 collective-permute-start.4
  42.4 1.3 collective-permute-start.5
  43.7 1.3 collective-permute-start.6
  45.0 0.7 collective-permute-start.7
  46.2 2.0 collective-permute-done.5
  48.3 3.5 %collective-permute-done.6 = f32[5,1,64,132]{3,2,1,0:T(8,128)S(1)} collective-permute-done((f32[5,1,64,132]{3,2,1,0:T(8,128)S(1)}, f32[5,1,64,132]{3,2,1,0:T(8,128)S(1)}, u32[]{:S(2)}, u32[]{:S(2)}) %collective-permute-start.6) | collective-permute-done | bytes 168992 | tf_op jit(solution)/shard_map/ppermute | solution.py:160
  51.8 1.3 collective-permute-start.8
  53.1 31.1 %collective-permute-done.8 = f32[5,1,64,132]{3,2,1,0:T(8,128)S(1)} collective-permute-done((f32[5,1,64,132]{3,2,1,0:T(8,128)S(1)}, f32[5,1,64,132]{3,2,1,0:T(8,128)S(1)}, u32[]{:S(2)}, u32[]{:S(2)}) %collective-permute-start.8) | collective-permute-done | bytes 168992 | tf_op jit(solution)/shard_map/ppermute | solution.py:164
  84.2 1.3 collective-permute-start.10
  85.5 1.3 collective-permute-start.9
  86.9 6.3 %collective-permute-done.10 = f32[5,1,64,132]{3,2,1,0:T(8,128)S(1)} collective-permute-done((f32[5,1,64,132]{3,2,1,0:T(8,128)S(1)}, f32[5,1,64,132]{3,2,1,0:T(8,128)S(1)}, u32[]{:S(2)}, u32[]{:S(2)}) %collective-permute-start.10) | collective-permute-done | bytes 168992 | tf_op jit(solution)/shard_map/ppermute | solution.py:177
  93.3 0.7 concatenate.43
  94.0 0.2 slice_select_fusion
  94.2 0.2 slice_select_fusion.5
  94.4 0.2 slice_select_fusion.4
  94.6 0.1 slice_select_fusion.7
  95.2 0.2 subtract_multiply_fusion.1
  95.4 0.6 subtract_add_fusion
  96.2 0.1 fusion.14
  96.6 5.2 %collective-permute-start.11 = (f32[5,1,64,130]{3,2,1,0:T(8,128)S(1)}, f32[5,1,64,130]{3,2,1,0:T(8,128)S(1)}, u32[]{:S(2)}, u32[]{:S(2)}) collective-permute-start(f32[5,1,64,130]{3,2,1,0:T(8,128)S(1)} %slice.677), channel_id=1, source_target_pairs={{0,1},{1,2},{2,3},{3,4},{4,5},{5,6},{6,7},{7,8},{8,9},{9,10},{10,1... | collective-permute-start | bytes 499208 | tf_op jit(solution)/shard_map/ppermute | solution.py:160
  101.8 1.6 collective-permute-start.12
  103.4 1.3 collective-permute-start.13
  104.7 0.7 collective-permute-start.14
  105.5 6.1 %collective-permute-done.12 = f32[5,1,64,130]{3,2,1,0:T(8,128)S(1)} collective-permute-done((f32[5,1,64,130]{3,2,1,0:T(8,128)S(1)}, f32[5,1,64,130]{3,2,1,0:T(8,128)S(1)}, u32[]{:S(2)}, u32[]{:S(2)}) %collective-permute-start.12) | collective-permute-done | bytes 166432 | tf_op jit(solution)/shard_map/ppermute | solution.py:160
  111.5 7.0 %collective-permute-done.13 = f32[5,1,64,130]{3,2,1,0:T(8,128)S(1)} collective-permute-done((f32[5,1,64,130]{3,2,1,0:T(8,128)S(1)}, f32[5,1,64,130]{3,2,1,0:T(8,128)S(1)}, u32[]{:S(2)}, u32[]{:S(2)}) %collective-permute-start.13) | collective-permute-done | bytes 166432 | tf_op jit(solution)/shard_map/ppermute | solution.py:160
  118.6 1.3 collective-permute-start.15
  119.9 26.5 %collective-permute-done.15 = f32[5,1,64,130]{3,2,1,0:T(8,128)S(1)} collective-permute-done((f32[5,1,64,130]{3,2,1,0:T(8,128)S(1)}, f32[5,1,64,130]{3,2,1,0:T(8,128)S(1)}, u32[]{:S(2)}, u32[]{:S(2)}) %collective-permute-start.15) | collective-permute-done | bytes 166432 | tf_op jit(solution)/shard_map/ppermute | solution.py:164
  146.4 1.3 collective-permute-start.17
  147.7 1.3 collective-permute-start.16
  149.0 6.3 %collective-permute-done.17 = f32[5,1,64,130]{3,2,1,0:T(8,128)S(1)} collective-permute-done((f32[5,1,64,130]{3,2,1,0:T(8,128)S(1)}, f32[5,1,64,130]{3,2,1,0:T(8,128)S(1)}, u32[]{:S(2)}, u32[]{:S(2)}) %collective-permute-start.17) | collective-permute-done | bytes 166432 | tf_op jit(solution)/shard_map/ppermute | solution.py:177
  155.5 0.7 concatenate.44
  156.2 0.2 slice_select_fusion.3
  156.4 0.2 slice_select_fusion.2
  156.5 0.2 slice_select_fusion.1
  156.7 0.1 slice_select_fusion.6
  157.5 0.3 subtract_add_fusion.2
  158.2 5.2 %collective-permute-start.18 = (f32[5,1,64,128]{3,2,1,0:T(8,128)S(1)}, f32[5,1,64,128]{3,2,1,0:T(8,128)S(1)}, u32[]{:S(2)}, u32[]{:S(2)}) collective-permute-start(f32[5,1,64,128]{3,2,1,0:T(8,128)S(1)} %get-tuple-element.29), channel_id=1, source_target_pairs={{0,1},{1,2},{2,3},{3,4},{4,5},{5,6},{6,7},{7,8},{8,9},{9,10},{10,1... | collective-permute-start | bytes 491528 | tf_op jit(solution)/shard_map/ppermute | solution.py:160
  163.4 1.6 collective-permute-start.19
  165.0 1.3 collective-permute-start.20
  166.3 0.7 collective-permute-start.21
  167.0 2.6 %collective-permute-done.19 = f32[5,1,64,128]{3,2,1,0:T(8,128)S(1)} collective-permute-done((f32[5,1,64,128]{3,2,1,0:T(8,128)S(1)}, f32[5,1,64,128]{3,2,1,0:T(8,128)S(1)}, u32[]{:S(2)}, u32[]{:S(2)}) %collective-permute-start.19) | collective-permute-done | bytes 163872 | tf_op jit(solution)/shard_map/ppermute | solution.py:160
  169.7 2.9 %collective-permute-done.20 = f32[5,1,64,128]{3,2,1,0:T(8,128)S(1)} collective-permute-done((f32[5,1,64,128]{3,2,1,0:T(8,128)S(1)}, f32[5,1,64,128]{3,2,1,0:T(8,128)S(1)}, u32[]{:S(2)}, u32[]{:S(2)}) %collective-permute-start.20) | collective-permute-done | bytes 163872 | tf_op jit(solution)/shard_map/ppermute | solution.py:160
  172.5 1.3 collective-permute-start.22
  173.9 22.3 %collective-permute-done.22 = f32[5,1,64,128]{3,2,1,0:T(8,128)S(1)} collective-permute-done((f32[5,1,64,128]{3,2,1,0:T(8,128)S(1)}, f32[5,1,64,128]{3,2,1,0:T(8,128)S(1)}, u32[]{:S(2)}, u32[]{:S(2)}) %collective-permute-start.22) | collective-permute-done | bytes 163872 | tf_op jit(solution)/shard_map/ppermute | solution.py:164
  196.2 1.3 collective-permute-start.23
  197.5 1.3 collective-permute-start.24
  198.8 0.7 collective-permute-done.23
  199.5 5.2 %collective-permute-done.24 = f32[5,1,64,128]{3,2,1,0:T(8,128)S(1)} collective-permute-done((f32[5,1,64,128]{3,2,1,0:T(8,128)S(1)}, f32[5,1,64,128]{3,2,1,0:T(8,128)S(1)}, u32[]{:S(2)}, u32[]{:S(2)}) %collective-permute-start.24) | collective-permute-done | bytes 163872 | tf_op jit(solution)/shard_map/ppermute | solution.py:177
  205.4 0.7 slice_select_fusion.23
  (93 shorter events, 4.9 us)
Async XLA Ops:
  0.0 39.3 %copy-start = (f32[5,1,64,128]{3,2,1,0:T(8,128)S(1)}, f32[5,1,64,128]{3,2,1,0:T(8,128)}, u32[]{:S(2)}) copy-start(f32[5,1,64,128]{3,2,1,0:T(8,128)} %param.2) | copy-start | bytes 491524
  0.8 26.2 %collective-permute-start = (f32[5,1,3,128]{3,2,1,0:T(4,128)S(1)}, f32[5,1,3,128]{3,2,1,0:T(4,128)S(1)}, u32[]{:S(2)}, u32[]{:S(2)}) collective-permute-start(f32[5,1,3,128]{3,2,1,0:T(4,128)S(1)} %get-tuple-element.70), channel_id=1, source_target_pairs={{0,1},{1,2},{2,3},{3,4},{4,5},{5,6},{6,7},{7,8},{8,9},{9,10},{10,1... | collective-permute-start | bytes 23048 | tf_op jit(solution)/shard_map/ppermute | solution.py:25
  2.7 24.4 %collective-permute-start.1 = (f32[5,1,3,128]{3,2,1,0:T(4,128)S(1)}, f32[5,1,3,128]{3,2,1,0:T(4,128)S(1)}, u32[]{:S(2)}, u32[]{:S(2)}) collective-permute-start(f32[5,1,3,128]{3,2,1,0:T(4,128)S(1)} %get-tuple-element.71), channel_id=1, source_target_pairs={{0,127},{1,0},{2,1},{3,2},{4,3},{5,4},{6,5},{7,6},{8,7},{9,8},{10,... | collective-permute-start | bytes 23048 | tf_op jit(solution)/shard_map/ppermute | solution.py:25
  28.4 9.4 %collective-permute-start.2 = (f32[1059]{0:T(1024)S(1)}, f32[1059]{0:T(1024)S(1)}, u32[]{:S(2)}, u32[]{:S(2)}) collective-permute-start(f32[1059]{0:T(1024)S(1)} %pad_maximum_fusion.1), channel_id=1, source_target_pairs={{0,128},{128,256},{256,384},{384,512},{512,640},{640,768},{768,896... | collective-permute-start | bytes 12716 | tf_op jit(solution)/shard_map/ppermute | solution.py:25
  32.1 7.0 %collective-permute-start.3 = (f32[1059]{0:T(1024)S(1)}, f32[1059]{0:T(1024)S(1)}, u32[]{:S(2)}, u32[]{:S(2)}) collective-permute-start(f32[1059]{0:T(1024)S(1)} %pad_maximum_fusion.2), channel_id=1, source_target_pairs={{128,0},{256,128},{384,256},{512,384},{640,512},{768,640},{896,768... | collective-permute-start | bytes 12716 | tf_op jit(solution)/shard_map/ppermute | solution.py:25
  40.5 5.6 %copy-start.1 = (s32[3,128]{1,0:T(4,128)S(1)}, s32[3,128]{1,0:T(4,128)}, u32[]{:S(2)}) copy-start(s32[3,128]{1,0:T(4,128)} %param.3) | copy-start | bytes 4612
  41.1 5.1 %collective-permute-start.4 = (f32[5,1,64,132]{3,2,1,0:T(8,128)S(1)}, f32[5,1,64,132]{3,2,1,0:T(8,128)S(1)}, u32[]{:S(2)}, u32[]{:S(2)}) collective-permute-start(f32[5,1,64,132]{3,2,1,0:T(8,128)S(1)} %slice.635), channel_id=1, source_target_pairs={{0,1},{1,2},{2,3},{3,4},{4,5},{5,6},{6,7},{7,8},{8,9},{9,10},{10,1... | collective-permute-start | bytes 506888 | tf_op jit(solution)/shard_map/ppermute | solution.py:160
  42.4 5.9 %collective-permute-start.5 = (f32[5,1,64,132]{3,2,1,0:T(8,128)S(1)}, f32[5,1,64,132]{3,2,1,0:T(8,128)S(1)}, u32[]{:S(2)}, u32[]{:S(2)}) collective-permute-start(f32[5,1,64,132]{3,2,1,0:T(8,128)S(1)} %slice.635), channel_id=1, source_target_pairs={{0,2},{1,3},{2,4},{3,5},{4,6},{5,7},{6,8},{7,9},{8,10},{9,11},{10,... | collective-permute-start | bytes 506888 | tf_op jit(solution)/shard_map/ppermute | solution.py:160
  43.7 8.1 %collective-permute-start.6 = (f32[5,1,64,132]{3,2,1,0:T(8,128)S(1)}, f32[5,1,64,132]{3,2,1,0:T(8,128)S(1)}, u32[]{:S(2)}, u32[]{:S(2)}) collective-permute-start(f32[5,1,64,132]{3,2,1,0:T(8,128)S(1)} %slice.635), channel_id=1, source_target_pairs={{0,3},{1,4},{2,5},{3,6},{4,7},{5,8},{6,9},{7,10},{8,11},{9,12},{10... | collective-permute-start | bytes 506888 | tf_op jit(solution)/shard_map/ppermute | solution.py:160
  45.0 6.8 %collective-permute-start.7 = (f32[5,1,64,132]{3,2,1,0:T(8,128)S(1)}, f32[5,1,64,132]{3,2,1,0:T(8,128)S(1)}, u32[]{:S(2)}, u32[]{:S(2)}) collective-permute-start(f32[5,1,64,132]{3,2,1,0:T(8,128)S(1)} %slice.635), channel_id=1, source_target_pairs={{15,1},{14,3},{13,4},{31,17},{30,19},{29,20},{47,33},{46,35},{45,3... | collective-permute-start | bytes 506888 | tf_op jit(solution)/shard_map/ppermute | solution.py:162
  51.8 32.4 %collective-permute-start.8 = (f32[5,1,64,132]{3,2,1,0:T(8,128)S(1)}, f32[5,1,64,132]{3,2,1,0:T(8,128)S(1)}, u32[]{:S(2)}, u32[]{:S(2)}) collective-permute-start(f32[5,1,64,132]{3,2,1,0:T(8,128)S(1)} %collective-permute-done.7), channel_id=1, source_target_pairs={{1,18},{3,17},{4,16},{17,34},{19,33},{20,32},{33,50},{35,49},{36,4... | collective-permute-start | bytes 506888 | tf_op jit(solution)/shard_map/ppermute | solution.py:164
  84.2 9.0 %collective-permute-start.10 = (f32[5,1,64,132]{3,2,1,0:T(8,128)S(1)}, f32[5,1,64,132]{3,2,1,0:T(8,128)S(1)}, u32[]{:S(2)}, u32[]{:S(2)}) collective-permute-start(f32[5,1,64,132]{3,2,1,0:T(8,128)S(1)} %collective-permute-done.8), channel_id=1, source_target_pairs={{2,0},{18,16},{34,32},{50,48},{66,64},{82,80},{98,96},{114,112},{1... | collective-permute-start | bytes 506888 | tf_op jit(solution)/shard_map/ppermute | solution.py:177
  85.5 7.7 %collective-permute-start.9 = (f32[5,1,64,132]{3,2,1,0:T(8,128)S(1)}, f32[5,1,64,132]{3,2,1,0:T(8,128)S(1)}, u32[]{:S(2)}, u32[]{:S(2)}) collective-permute-start(f32[5,1,64,132]{3,2,1,0:T(8,128)S(1)} %collective-permute-done.8), channel_id=1, source_target_pairs={{1,0},{2,1},{17,16},{18,17},{33,32},{34,33},{49,48},{50,49},{65,64... | collective-permute-start | bytes 506888 | tf_op jit(solution)/shard_map/ppermute | solution.py:177
  96.6 8.9 %collective-permute-start.11 = (f32[5,1,64,130]{3,2,1,0:T(8,128)S(1)}, f32[5,1,64,130]{3,2,1,0:T(8,128)S(1)}, u32[]{:S(2)}, u32[]{:S(2)}) collective-permute-start(f32[5,1,64,130]{3,2,1,0:T(8,128)S(1)} %slice.677), channel_id=1, source_target_pairs={{0,1},{1,2},{2,3},{3,4},{4,5},{5,6},{6,7},{7,8},{8,9},{9,10},{10,1... | collective-permute-start | bytes 499208 | tf_op jit(solution)/shard_map/ppermute | solution.py:160
  101.8 9.8 %collective-permute-start.12 = (f32[5,1,64,130]{3,2,1,0:T(8,128)S(1)}, f32[5,1,64,130]{3,2,1,0:T(8,128)S(1)}, u32[]{:S(2)}, u32[]{:S(2)}) collective-permute-start(f32[5,1,64,130]{3,2,1,0:T(8,128)S(1)} %slice.677), channel_id=1, source_target_pairs={{0,2},{1,3},{2,4},{3,5},{4,6},{5,7},{6,8},{7,9},{8,10},{9,11},{10,... | collective-permute-start | bytes 499208 | tf_op jit(solution)/shard_map/ppermute | solution.py:160
  103.4 15.2 %collective-permute-start.13 = (f32[5,1,64,130]{3,2,1,0:T(8,128)S(1)}, f32[5,1,64,130]{3,2,1,0:T(8,128)S(1)}, u32[]{:S(2)}, u32[]{:S(2)}) collective-permute-start(f32[5,1,64,130]{3,2,1,0:T(8,128)S(1)} %slice.677), channel_id=1, source_target_pairs={{0,3},{1,4},{2,5},{3,6},{4,7},{5,8},{6,9},{7,10},{8,11},{9,12},{10... | collective-permute-start | bytes 499208 | tf_op jit(solution)/shard_map/ppermute | solution.py:160
  104.7 13.8 %collective-permute-start.14 = (f32[5,1,64,130]{3,2,1,0:T(8,128)S(1)}, f32[5,1,64,130]{3,2,1,0:T(8,128)S(1)}, u32[]{:S(2)}, u32[]{:S(2)}) collective-permute-start(f32[5,1,64,130]{3,2,1,0:T(8,128)S(1)} %slice.677), channel_id=1, source_target_pairs={{15,1},{14,3},{13,4},{31,17},{30,19},{29,20},{47,33},{46,35},{45,3... | collective-permute-start | bytes 499208 | tf_op jit(solution)/shard_map/ppermute | solution.py:162
  118.6 27.8 %collective-permute-start.15 = (f32[5,1,64,130]{3,2,1,0:T(8,128)S(1)}, f32[5,1,64,130]{3,2,1,0:T(8,128)S(1)}, u32[]{:S(2)}, u32[]{:S(2)}) collective-permute-start(f32[5,1,64,130]{3,2,1,0:T(8,128)S(1)} %collective-permute-done.14), channel_id=1, source_target_pairs={{1,18},{3,17},{4,16},{17,34},{19,33},{20,32},{33,50},{35,49},{36,4... | collective-permute-start | bytes 499208 | tf_op jit(solution)/shard_map/ppermute | solution.py:164
  146.4 9.0 %collective-permute-start.17 = (f32[5,1,64,130]{3,2,1,0:T(8,128)S(1)}, f32[5,1,64,130]{3,2,1,0:T(8,128)S(1)}, u32[]{:S(2)}, u32[]{:S(2)}) collective-permute-start(f32[5,1,64,130]{3,2,1,0:T(8,128)S(1)} %collective-permute-done.15), channel_id=1, source_target_pairs={{2,0},{18,16},{34,32},{50,48},{66,64},{82,80},{98,96},{114,112},{1... | collective-permute-start | bytes 499208 | tf_op jit(solution)/shard_map/ppermute | solution.py:177
  147.7 7.7 %collective-permute-start.16 = (f32[5,1,64,130]{3,2,1,0:T(8,128)S(1)}, f32[5,1,64,130]{3,2,1,0:T(8,128)S(1)}, u32[]{:S(2)}, u32[]{:S(2)}) collective-permute-start(f32[5,1,64,130]{3,2,1,0:T(8,128)S(1)} %collective-permute-done.15), channel_id=1, source_target_pairs={{1,0},{2,1},{17,16},{18,17},{33,32},{34,33},{49,48},{50,49},{65,64... | collective-permute-start | bytes 499208 | tf_op jit(solution)/shard_map/ppermute | solution.py:177
  158.2 8.8 %collective-permute-start.18 = (f32[5,1,64,128]{3,2,1,0:T(8,128)S(1)}, f32[5,1,64,128]{3,2,1,0:T(8,128)S(1)}, u32[]{:S(2)}, u32[]{:S(2)}) collective-permute-start(f32[5,1,64,128]{3,2,1,0:T(8,128)S(1)} %get-tuple-element.29), channel_id=1, source_target_pairs={{0,1},{1,2},{2,3},{3,4},{4,5},{5,6},{6,7},{7,8},{8,9},{9,10},{10,1... | collective-permute-start | bytes 491528 | tf_op jit(solution)/shard_map/ppermute | solution.py:160
  163.4 6.3 %collective-permute-start.19 = (f32[5,1,64,128]{3,2,1,0:T(8,128)S(1)}, f32[5,1,64,128]{3,2,1,0:T(8,128)S(1)}, u32[]{:S(2)}, u32[]{:S(2)}) collective-permute-start(f32[5,1,64,128]{3,2,1,0:T(8,128)S(1)} %get-tuple-element.29), channel_id=1, source_target_pairs={{0,2},{1,3},{2,4},{3,5},{4,6},{5,7},{6,8},{7,9},{8,10},{9,11},{10,... | collective-permute-start | bytes 491528 | tf_op jit(solution)/shard_map/ppermute | solution.py:160
  165.0 7.5 %collective-permute-start.20 = (f32[5,1,64,128]{3,2,1,0:T(8,128)S(1)}, f32[5,1,64,128]{3,2,1,0:T(8,128)S(1)}, u32[]{:S(2)}, u32[]{:S(2)}) collective-permute-start(f32[5,1,64,128]{3,2,1,0:T(8,128)S(1)} %get-tuple-element.29), channel_id=1, source_target_pairs={{0,3},{1,4},{2,5},{3,6},{4,7},{5,8},{6,9},{7,10},{8,11},{9,12},{10... | collective-permute-start | bytes 491528 | tf_op jit(solution)/shard_map/ppermute | solution.py:160
  166.3 6.2 %collective-permute-start.21 = (f32[5,1,64,128]{3,2,1,0:T(8,128)S(1)}, f32[5,1,64,128]{3,2,1,0:T(8,128)S(1)}, u32[]{:S(2)}, u32[]{:S(2)}) collective-permute-start(f32[5,1,64,128]{3,2,1,0:T(8,128)S(1)} %get-tuple-element.29), channel_id=1, source_target_pairs={{15,1},{14,3},{13,4},{31,17},{30,19},{29,20},{47,33},{46,35},{45,3... | collective-permute-start | bytes 491528 | tf_op jit(solution)/shard_map/ppermute | solution.py:162
  172.5 23.7 %collective-permute-start.22 = (f32[5,1,64,128]{3,2,1,0:T(8,128)S(1)}, f32[5,1,64,128]{3,2,1,0:T(8,128)S(1)}, u32[]{:S(2)}, u32[]{:S(2)}) collective-permute-start(f32[5,1,64,128]{3,2,1,0:T(8,128)S(1)} %collective-permute-done.21), channel_id=1, source_target_pairs={{1,18},{3,17},{4,16},{17,34},{19,33},{20,32},{33,50},{35,49},{36,4... | collective-permute-start | bytes 491528 | tf_op jit(solution)/shard_map/ppermute | solution.py:164
  196.2 3.3 %collective-permute-start.23 = (f32[5,1,64,128]{3,2,1,0:T(8,128)S(1)}, f32[5,1,64,128]{3,2,1,0:T(8,128)S(1)}, u32[]{:S(2)}, u32[]{:S(2)}) collective-permute-start(f32[5,1,64,128]{3,2,1,0:T(8,128)S(1)} %collective-permute-done.22), channel_id=1, source_target_pairs={{1,0},{2,1},{17,16},{18,17},{33,32},{34,33},{49,48},{50,49},{65,64... | collective-permute-start | bytes 491528 | tf_op jit(solution)/shard_map/ppermute | solution.py:177
  197.5 7.2 %collective-permute-start.24 = (f32[5,1,64,128]{3,2,1,0:T(8,128)S(1)}, f32[5,1,64,128]{3,2,1,0:T(8,128)S(1)}, u32[]{:S(2)}, u32[]{:S(2)}) collective-permute-start(f32[5,1,64,128]{3,2,1,0:T(8,128)S(1)} %collective-permute-done.22), channel_id=1, source_target_pairs={{2,0},{18,16},{34,32},{50,48},{66,64},{82,80},{98,96},{114,112},{1... | collective-permute-start | bytes 491528 | tf_op jit(solution)/shard_map/ppermute | solution.py:177

commit v11 on v4

--- a/solution.py
+++ b/solution.py
@@ -150,6 +150,10 @@
     groups = lax.axis_size("rad")
     if count % plane or count <= plane or plane < 2 * blocks:
         return [passed_along(head, "azi", k) for k in range(1, blocks + 1)]
+    first, second = crossing_relays(groups, count, plane, blocks)
+    relayed = lax.ppermute(head, ("rad", "azi"), first)
+    crossed = lax.ppermute(relayed, ("rad", "azi"), second)
+    later, _ = lax.optimization_barrier((head, relayed))
     near = []
     for k in range(1, blocks + 1):
         pairs = [
@@ -157,10 +161,7 @@
             for a in range(count)
             if a // plane == ((a + k) % count) // plane
         ]
-        near.append(lax.ppermute(head, "azi", pairs))
-    first, second = crossing_relays(groups, count, plane, blocks)
-    relayed = lax.ppermute(head, ("rad", "azi"), first)
-    crossed = lax.ppermute(relayed, ("rad", "azi"), second)
+        near.append(lax.ppermute(later, "azi", pairs))
     position = lax.axis_index("azi") % plane
     pieces = []
     for k in range(1, blocks + 1):

time: 167 us -> 174 us (1.042)
  the two profiles are of different devices: /device:TPU:64 before, /device:TPU:6 now
where the time goes in v11:
time: 174 us; the launch traced here: 172 us
  starting transfers between devices  119 us (68%)
  waiting for transfers between devices  38.3 us (22%)
  other arithmetic  10.1 us (6%)
  local copies, waits for them, and re-layouts  3.56 us (2%)
    ppermute x9, starting transfers between devices, rotation_pieces(): near.append(lax.ppermute(later, 'azi', pairs))  77.1 us
    ppermute x4, starting transfers between devices, passed_along(): return lax.ppermute(value, axis, pairs)  28.5 us
    ppermute x6, waiting for transfers between devices, rotation_pieces(): far = lax.ppermute(crossed, 'azi', pairs)  23.6 us
    ppermute x3, waiting for transfers between devices, rotation_pieces(): crossed = lax.ppermute(relayed, ('rad', 'azi'), second)  10.5 us
    ppermute x6, starting transfers between devices, rotation_pieces(): far = lax.ppermute(crossed, 'azi', pairs)  7.74 us
    ppermute x4, waiting for transfers between devices, passed_along(): return lax.ppermute(value, axis, pairs)  4.09 us
    ppermute x3, starting transfers between devices, rotation_pieces(): crossed = lax.ppermute(relayed, ('rad', 'azi'), second)  3.88 us
  transfers between devices with their start and end apart: 25, of which 7 were waited for; matrix products, arithmetic and copies ran while one was open for 1% of the time, Pallas kernels for 0%

profile of v11, /device:TPU:6, one launch (start us, length us, event | category | flops | bytes accessed | tf_op | source)
XLA Modules:
  0.0 172.2 jit_solution(13207893869754080504)
XLA Ops:
  0.0 0.8 fusion.103
  0.8 1.9 %collective-permute-start = (f32[5,1,3,128]{3,2,1,0:T(4,128)S(1)}, f32[5,1,3,128]{3,2,1,0:T(4,128)S(1)}, u32[]{:S(2)}, u32[]{:S(2)}) collective-permute-start(f32[5,1,3,128]{3,2,1,0:T(4,128)S(1)} %get-tuple-element.52), channel_id=1, source_target_pairs={{0,1},{1,2},{2,3},{3,4},{4,5},{5,6},{6,7},{7,8},{8,9},{9,10},{10,1... | collective-permute-start | bytes 23048 | tf_op jit(solution)/shard_map/ppermute | solution.py:25
  2.7 22.0 %collective-permute-start.1 = (f32[5,1,3,128]{3,2,1,0:T(4,128)S(1)}, f32[5,1,3,128]{3,2,1,0:T(4,128)S(1)}, u32[]{:S(2)}, u32[]{:S(2)}) collective-permute-start(f32[5,1,3,128]{3,2,1,0:T(4,128)S(1)} %get-tuple-element.53), channel_id=1, source_target_pairs={{0,127},{1,0},{2,1},{3,2},{4,3},{5,4},{6,5},{7,6},{8,7},{9,8},{10,... | collective-permute-start | bytes 23048 | tf_op jit(solution)/shard_map/ppermute | solution.py:25
  24.7 0.8 slice_convert_fusion.1
  26.1 0.9 pad_maximum_fusion
  27.1 0.2 reshape.1273
  27.4 3.4 %collective-permute-start.2 = (f32[1059]{0:T(1024)S(1)}, f32[1059]{0:T(1024)S(1)}, u32[]{:S(2)}, u32[]{:S(2)}) collective-permute-start(f32[1059]{0:T(1024)S(1)} %pad_maximum_fusion.1), channel_id=1, source_target_pairs={{0,128},{128,256},{256,384},{384,512},{512,640},{640,768},{768,896... | collective-permute-start | bytes 12716 | tf_op jit(solution)/shard_map/ppermute | solution.py:25
  30.8 0.2 reshape.1275
  31.1 1.3 collective-permute-start.3
  32.4 0.2 concatenate.40
  32.6 4.0 %collective-permute-done.3 = f32[1059]{0:T(1024)S(1)} collective-permute-done((f32[1059]{0:T(1024)S(1)}, f32[1059]{0:T(1024)S(1)}, u32[]{:S(2)}, u32[]{:S(2)}) %collective-permute-start.3) | collective-permute-done | bytes 4268 | tf_op jit(solution)/shard_map/ppermute | solution.py:25
  36.6 0.2 concatenate.41
  36.8 0.2 maximum_select_fusion
  37.1 0.1 maximum_bitcast_fusion.3
  37.2 0.2 subtract_multiply_fusion.3
  37.8 0.6 subtract_add_fusion.1
  38.5 0.1 fusion.4
  38.6 0.1 fusion.29
  39.0 0.7 collective-permute-start.4
  39.7 7.9 %collective-permute-start.6 = (f32[5,1,64,132]{3,2,1,0:T(8,128)S(1)}, f32[5,1,64,132]{3,2,1,0:T(8,128)S(1)}, u32[]{:S(2)}, u32[]{:S(2)}) collective-permute-start(f32[5,1,64,132]{3,2,1,0:T(8,128)S(1)} %slice.635), channel_id=1, source_target_pairs={{0,3},{1,4},{2,5},{3,6},{4,7},{5,8},{6,9},{7,10},{8,11},{9,12},{10... | collective-permute-start | bytes 506888 | tf_op jit(solution)/shard_map/ppermute | solution.py:164
  47.6 1.3 collective-permute-start.5
  48.9 12.0 %collective-permute-start.10 = (f32[5,1,64,132]{3,2,1,0:T(8,128)S(1)}, f32[5,1,64,132]{3,2,1,0:T(8,128)S(1)}, u32[]{:S(2)}, u32[]{:S(2)}) collective-permute-start(f32[5,1,64,132]{3,2,1,0:T(8,128)S(1)} %slice.635), channel_id=1, source_target_pairs={{0,1},{1,2},{2,3},{3,4},{4,5},{5,6},{6,7},{7,8},{8,9},{9,10},{10,1... | collective-permute-start | bytes 506888 | tf_op jit(solution)/shard_map/ppermute | solution.py:164
  61.0 9.2 %collective-permute-start.8 = (f32[5,1,64,132]{3,2,1,0:T(8,128)S(1)}, f32[5,1,64,132]{3,2,1,0:T(8,128)S(1)}, u32[]{:S(2)}, u32[]{:S(2)}) collective-permute-start(f32[5,1,64,132]{3,2,1,0:T(8,128)S(1)} %slice.635), channel_id=1, source_target_pairs={{0,2},{1,3},{2,4},{3,5},{4,6},{5,7},{6,8},{7,9},{8,10},{9,11},{10,... | collective-permute-start | bytes 506888 | tf_op jit(solution)/shard_map/ppermute | solution.py:164
  70.2 1.3 collective-permute-start.9
  71.5 1.3 collective-permute-start.7
  72.9 6.3 %collective-permute-done.9 = f32[5,1,64,132]{3,2,1,0:T(8,128)S(1)} collective-permute-done((f32[5,1,64,132]{3,2,1,0:T(8,128)S(1)}, f32[5,1,64,132]{3,2,1,0:T(8,128)S(1)}, u32[]{:S(2)}, u32[]{:S(2)}) %collective-permute-start.9) | collective-permute-done | bytes 168992 | tf_op jit(solution)/shard_map/ppermute | solution.py:177
  79.3 0.7 concatenate.43
  80.0 0.2 slice_select_fusion
  80.2 0.2 slice_select_fusion.5
  80.4 0.2 slice_select_fusion.4
  80.6 0.1 slice_select_fusion.7
  80.7 0.1 slice_select_fusion.9
  81.1 0.1 maximum_bitcast_fusion.1
  81.2 0.2 subtract_multiply_fusion.1
  81.4 0.6 subtract_add_fusion
  82.1 0.1 fusion.7
  82.2 0.1 fusion.14
  82.6 0.7 collective-permute-start.11
  83.3 16.5 %collective-permute-start.13 = (f32[5,1,64,130]{3,2,1,0:T(8,128)S(1)}, f32[5,1,64,130]{3,2,1,0:T(8,128)S(1)}, u32[]{:S(2)}, u32[]{:S(2)}) collective-permute-start(f32[5,1,64,130]{3,2,1,0:T(8,128)S(1)} %slice.677), channel_id=1, source_target_pairs={{0,3},{1,4},{2,5},{3,6},{4,7},{5,8},{6,9},{7,10},{8,11},{9,12},{10... | collective-permute-start | bytes 499208 | tf_op jit(solution)/shard_map/ppermute | solution.py:164
  99.8 1.3 collective-permute-start.12
  101.2 2.7 %collective-permute-start.17 = (f32[5,1,64,130]{3,2,1,0:T(8,128)S(1)}, f32[5,1,64,130]{3,2,1,0:T(8,128)S(1)}, u32[]{:S(2)}, u32[]{:S(2)}) collective-permute-start(f32[5,1,64,130]{3,2,1,0:T(8,128)S(1)} %slice.677), channel_id=1, source_target_pairs={{0,1},{1,2},{2,3},{3,4},{4,5},{5,6},{6,7},{7,8},{8,9},{9,10},{10,1... | collective-permute-start | bytes 499208 | tf_op jit(solution)/shard_map/ppermute | solution.py:164
  103.9 7.6 %collective-permute-start.15 = (f32[5,1,64,130]{3,2,1,0:T(8,128)S(1)}, f32[5,1,64,130]{3,2,1,0:T(8,128)S(1)}, u32[]{:S(2)}, u32[]{:S(2)}) collective-permute-start(f32[5,1,64,130]{3,2,1,0:T(8,128)S(1)} %slice.677), channel_id=1, source_target_pairs={{0,2},{1,3},{2,4},{3,5},{4,6},{5,7},{6,8},{7,9},{8,10},{9,11},{10,... | collective-permute-start | bytes 499208 | tf_op jit(solution)/shard_map/ppermute | solution.py:164
  111.5 10.5 %collective-permute-done.12 = f32[5,1,64,130]{3,2,1,0:T(8,128)S(1)} collective-permute-done((f32[5,1,64,130]{3,2,1,0:T(8,128)S(1)}, f32[5,1,64,130]{3,2,1,0:T(8,128)S(1)}, u32[]{:S(2)}, u32[]{:S(2)}) %collective-permute-start.12) | collective-permute-done | bytes 166432 | tf_op jit(solution)/shard_map/ppermute | solution.py:155
  122.0 1.3 collective-permute-start.16
  123.3 1.3 collective-permute-start.14
  124.7 6.3 %collective-permute-done.16 = f32[5,1,64,130]{3,2,1,0:T(8,128)S(1)} collective-permute-done((f32[5,1,64,130]{3,2,1,0:T(8,128)S(1)}, f32[5,1,64,130]{3,2,1,0:T(8,128)S(1)}, u32[]{:S(2)}, u32[]{:S(2)}) %collective-permute-start.16) | collective-permute-done | bytes 166432 | tf_op jit(solution)/shard_map/ppermute | solution.py:177
  131.1 0.7 concatenate.44
  131.8 0.2 slice_select_fusion.3
  132.0 0.2 slice_select_fusion.2
  132.2 0.2 slice_select_fusion.1
  132.4 0.1 slice_select_fusion.6
  132.5 0.1 slice_select_fusion.8
  133.0 0.1 subtract_multiply_fusion.5
  133.1 0.3 subtract_add_fusion.2
  133.9 0.7 collective-permute-start.18
  134.6 3.5 %collective-permute-start.20 = (f32[5,1,64,128]{3,2,1,0:T(8,128)S(1)}, f32[5,1,64,128]{3,2,1,0:T(8,128)S(1)}, u32[]{:S(2)}, u32[]{:S(2)}) collective-permute-start(f32[5,1,64,128]{3,2,1,0:T(8,128)S(1)} %get-tuple-element.10), channel_id=1, source_target_pairs={{0,3},{1,4},{2,5},{3,6},{4,7},{5,8},{6,9},{7,10},{8,11},{9,12},{10... | collective-permute-start | bytes 491528 | tf_op jit(solution)/shard_map/ppermute | solution.py:164
  138.1 1.3 collective-permute-start.19
  139.4 2.7 %collective-permute-start.22 = (f32[5,1,64,128]{3,2,1,0:T(8,128)S(1)}, f32[5,1,64,128]{3,2,1,0:T(8,128)S(1)}, u32[]{:S(2)}, u32[]{:S(2)}) collective-permute-start(f32[5,1,64,128]{3,2,1,0:T(8,128)S(1)} %get-tuple-element.10), channel_id=1, source_target_pairs={{0,2},{1,3},{2,4},{3,5},{4,6},{5,7},{6,8},{7,9},{8,10},{9,11},{10,... | collective-permute-start | bytes 491528 | tf_op jit(solution)/shard_map/ppermute | solution.py:164
  142.1 15.0 %collective-permute-start.24 = (f32[5,1,64,128]{3,2,1,0:T(8,128)S(1)}, f32[5,1,64,128]{3,2,1,0:T(8,128)S(1)}, u32[]{:S(2)}, u32[]{:S(2)}) collective-permute-start(f32[5,1,64,128]{3,2,1,0:T(8,128)S(1)} %get-tuple-element.10), channel_id=1, source_target_pairs={{0,1},{1,2},{2,3},{3,4},{4,5},{5,6},{6,7},{7,8},{8,9},{9,10},{10,1... | collective-permute-start | bytes 491528 | tf_op jit(solution)/shard_map/ppermute | solution.py:164
  157.1 1.3 collective-permute-start.21
  158.4 1.3 collective-permute-start.23
  159.7 5.3 %collective-permute-done.21 = f32[5,1,64,128]{3,2,1,0:T(8,128)S(1)} collective-permute-done((f32[5,1,64,128]{3,2,1,0:T(8,128)S(1)}, f32[5,1,64,128]{3,2,1,0:T(8,128)S(1)}, u32[]{:S(2)}, u32[]{:S(2)}) %collective-permute-start.21) | collective-permute-done | bytes 163872 | tf_op jit(solution)/shard_map/ppermute | solution.py:177
  165.1 5.7 %collective-permute-done.23 = f32[5,1,64,128]{3,2,1,0:T(8,128)S(1)} collective-permute-done((f32[5,1,64,128]{3,2,1,0:T(8,128)S(1)}, f32[5,1,64,128]{3,2,1,0:T(8,128)S(1)}, u32[]{:S(2)}, u32[]{:S(2)}) %collective-permute-start.23) | collective-permute-done | bytes 163872 | tf_op jit(solution)/shard_map/ppermute | solution.py:177
  171.5 0.7 slice_select_fusion.23
  (93 shorter events, 4.0 us)
Async XLA Ops:
  0.0 36.8 %copy-start = (f32[5,1,64,128]{3,2,1,0:T(8,128)S(1)}, f32[5,1,64,128]{3,2,1,0:T(8,128)}, u32[]{:S(2)}) copy-start(f32[5,1,64,128]{3,2,1,0:T(8,128)} %param.2) | copy-start | bytes 491524
  0.8 25.2 %collective-permute-start = (f32[5,1,3,128]{3,2,1,0:T(4,128)S(1)}, f32[5,1,3,128]{3,2,1,0:T(4,128)S(1)}, u32[]{:S(2)}, u32[]{:S(2)}) collective-permute-start(f32[5,1,3,128]{3,2,1,0:T(4,128)S(1)} %get-tuple-element.52), channel_id=1, source_target_pairs={{0,1},{1,2},{2,3},{3,4},{4,5},{5,6},{6,7},{7,8},{8,9},{9,10},{10,1... | collective-permute-start | bytes 23048 | tf_op jit(solution)/shard_map/ppermute | solution.py:25
  2.7 23.3 %collective-permute-start.1 = (f32[5,1,3,128]{3,2,1,0:T(4,128)S(1)}, f32[5,1,3,128]{3,2,1,0:T(4,128)S(1)}, u32[]{:S(2)}, u32[]{:S(2)}) collective-permute-start(f32[5,1,3,128]{3,2,1,0:T(4,128)S(1)} %get-tuple-element.53), channel_id=1, source_target_pairs={{0,127},{1,0},{2,1},{3,2},{4,3},{5,4},{6,5},{7,6},{8,7},{9,8},{10,... | collective-permute-start | bytes 23048 | tf_op jit(solution)/shard_map/ppermute | solution.py:25
  27.1 10.6 %copy-start.1 = (s32[3,128]{1,0:T(4,128)S(1)}, s32[3,128]{1,0:T(4,128)}, u32[]{:S(2)}) copy-start(s32[3,128]{1,0:T(4,128)} %param.3) | copy-start | bytes 4612
  27.4 5.0 %collective-permute-start.2 = (f32[1059]{0:T(1024)S(1)}, f32[1059]{0:T(1024)S(1)}, u32[]{:S(2)}, u32[]{:S(2)}) collective-permute-start(f32[1059]{0:T(1024)S(1)} %pad_maximum_fusion.1), channel_id=1, source_target_pairs={{0,128},{128,256},{256,384},{384,512},{512,640},{640,768},{768,896... | collective-permute-start | bytes 12716 | tf_op jit(solution)/shard_map/ppermute | solution.py:25
  31.1 5.5 %collective-permute-start.3 = (f32[1059]{0:T(1024)S(1)}, f32[1059]{0:T(1024)S(1)}, u32[]{:S(2)}, u32[]{:S(2)}) collective-permute-start(f32[1059]{0:T(1024)S(1)} %pad_maximum_fusion.2), channel_id=1, source_target_pairs={{128,0},{256,128},{384,256},{512,384},{640,512},{768,640},{896,768... | collective-permute-start | bytes 12716 | tf_op jit(solution)/shard_map/ppermute | solution.py:25
  39.0 0.7 collective-permute-start.4
  39.7 33.1 %collective-permute-start.6 = (f32[5,1,64,132]{3,2,1,0:T(8,128)S(1)}, f32[5,1,64,132]{3,2,1,0:T(8,128)S(1)}, u32[]{:S(2)}, u32[]{:S(2)}) collective-permute-start(f32[5,1,64,132]{3,2,1,0:T(8,128)S(1)} %slice.635), channel_id=1, source_target_pairs={{0,3},{1,4},{2,5},{3,6},{4,7},{5,8},{6,9},{7,10},{8,11},{9,12},{10... | collective-permute-start | bytes 506888 | tf_op jit(solution)/shard_map/ppermute | solution.py:164
  47.6 22.6 %collective-permute-start.5 = (f32[5,1,64,132]{3,2,1,0:T(8,128)S(1)}, f32[5,1,64,132]{3,2,1,0:T(8,128)S(1)}, u32[]{:S(2)}, u32[]{:S(2)}) collective-permute-start(f32[5,1,64,132]{3,2,1,0:T(8,128)S(1)} %collective-permute-done.4), channel_id=1, source_target_pairs={{1,18},{3,17},{4,16},{17,34},{19,33},{20,32},{33,50},{35,49},{36,4... | collective-permute-start | bytes 506888 | tf_op jit(solution)/shard_map/ppermute | solution.py:155
  48.9 23.9 %collective-permute-start.10 = (f32[5,1,64,132]{3,2,1,0:T(8,128)S(1)}, f32[5,1,64,132]{3,2,1,0:T(8,128)S(1)}, u32[]{:S(2)}, u32[]{:S(2)}) collective-permute-start(f32[5,1,64,132]{3,2,1,0:T(8,128)S(1)} %slice.635), channel_id=1, source_target_pairs={{0,1},{1,2},{2,3},{3,4},{4,5},{5,6},{6,7},{7,8},{8,9},{9,10},{10,1... | collective-permute-start | bytes 506888 | tf_op jit(solution)/shard_map/ppermute | solution.py:164
  61.0 18.3 %collective-permute-start.8 = (f32[5,1,64,132]{3,2,1,0:T(8,128)S(1)}, f32[5,1,64,132]{3,2,1,0:T(8,128)S(1)}, u32[]{:S(2)}, u32[]{:S(2)}) collective-permute-start(f32[5,1,64,132]{3,2,1,0:T(8,128)S(1)} %slice.635), channel_id=1, source_target_pairs={{0,2},{1,3},{2,4},{3,5},{4,6},{5,7},{6,8},{7,9},{8,10},{9,11},{10,... | collective-permute-start | bytes 506888 | tf_op jit(solution)/shard_map/ppermute | solution.py:164
  70.2 9.0 %collective-permute-start.9 = (f32[5,1,64,132]{3,2,1,0:T(8,128)S(1)}, f32[5,1,64,132]{3,2,1,0:T(8,128)S(1)}, u32[]{:S(2)}, u32[]{:S(2)}) collective-permute-start(f32[5,1,64,132]{3,2,1,0:T(8,128)S(1)} %collective-permute-done.5), channel_id=1, source_target_pairs={{2,0},{18,16},{34,32},{50,48},{66,64},{82,80},{98,96},{114,112},{1... | collective-permute-start | bytes 506888 | tf_op jit(solution)/shard_map/ppermute | solution.py:177
  71.5 7.7 %collective-permute-start.7 = (f32[5,1,64,132]{3,2,1,0:T(8,128)S(1)}, f32[5,1,64,132]{3,2,1,0:T(8,128)S(1)}, u32[]{:S(2)}, u32[]{:S(2)}) collective-permute-start(f32[5,1,64,132]{3,2,1,0:T(8,128)S(1)} %collective-permute-done.5), channel_id=1, source_target_pairs={{1,0},{2,1},{17,16},{18,17},{33,32},{34,33},{49,48},{50,49},{65,64... | collective-permute-start | bytes 506888 | tf_op jit(solution)/shard_map/ppermute | solution.py:177
  82.6 0.7 collective-permute-start.11
  83.3 41.3 %collective-permute-start.13 = (f32[5,1,64,130]{3,2,1,0:T(8,128)S(1)}, f32[5,1,64,130]{3,2,1,0:T(8,128)S(1)}, u32[]{:S(2)}, u32[]{:S(2)}) collective-permute-start(f32[5,1,64,130]{3,2,1,0:T(8,128)S(1)} %slice.677), channel_id=1, source_target_pairs={{0,3},{1,4},{2,5},{3,6},{4,7},{5,8},{6,9},{7,10},{8,11},{9,12},{10... | collective-permute-start | bytes 499208 | tf_op jit(solution)/shard_map/ppermute | solution.py:164
  99.8 22.2 %collective-permute-start.12 = (f32[5,1,64,130]{3,2,1,0:T(8,128)S(1)}, f32[5,1,64,130]{3,2,1,0:T(8,128)S(1)}, u32[]{:S(2)}, u32[]{:S(2)}) collective-permute-start(f32[5,1,64,130]{3,2,1,0:T(8,128)S(1)} %collective-permute-done.11), channel_id=1, source_target_pairs={{1,18},{3,17},{4,16},{17,34},{19,33},{20,32},{33,50},{35,49},{36,4... | collective-permute-start | bytes 499208 | tf_op jit(solution)/shard_map/ppermute | solution.py:155
  101.2 23.5 %collective-permute-start.17 = (f32[5,1,64,130]{3,2,1,0:T(8,128)S(1)}, f32[5,1,64,130]{3,2,1,0:T(8,128)S(1)}, u32[]{:S(2)}, u32[]{:S(2)}) collective-permute-start(f32[5,1,64,130]{3,2,1,0:T(8,128)S(1)} %slice.677), channel_id=1, source_target_pairs={{0,1},{1,2},{2,3},{3,4},{4,5},{5,6},{6,7},{7,8},{8,9},{9,10},{10,1... | collective-permute-start | bytes 499208 | tf_op jit(solution)/shard_map/ppermute | solution.py:164
  103.9 27.1 %collective-permute-start.15 = (f32[5,1,64,130]{3,2,1,0:T(8,128)S(1)}, f32[5,1,64,130]{3,2,1,0:T(8,128)S(1)}, u32[]{:S(2)}, u32[]{:S(2)}) collective-permute-start(f32[5,1,64,130]{3,2,1,0:T(8,128)S(1)} %slice.677), channel_id=1, source_target_pairs={{0,2},{1,3},{2,4},{3,5},{4,6},{5,7},{6,8},{7,9},{8,10},{9,11},{10,... | collective-permute-start | bytes 499208 | tf_op jit(solution)/shard_map/ppermute | solution.py:164
  122.0 9.0 %collective-permute-start.16 = (f32[5,1,64,130]{3,2,1,0:T(8,128)S(1)}, f32[5,1,64,130]{3,2,1,0:T(8,128)S(1)}, u32[]{:S(2)}, u32[]{:S(2)}) collective-permute-start(f32[5,1,64,130]{3,2,1,0:T(8,128)S(1)} %collective-permute-done.12), channel_id=1, source_target_pairs={{2,0},{18,16},{34,32},{50,48},{66,64},{82,80},{98,96},{114,112},{1... | collective-permute-start | bytes 499208 | tf_op jit(solution)/shard_map/ppermute | solution.py:177
  123.3 7.7 %collective-permute-start.14 = (f32[5,1,64,130]{3,2,1,0:T(8,128)S(1)}, f32[5,1,64,130]{3,2,1,0:T(8,128)S(1)}, u32[]{:S(2)}, u32[]{:S(2)}) collective-permute-start(f32[5,1,64,130]{3,2,1,0:T(8,128)S(1)} %collective-permute-done.12), channel_id=1, source_target_pairs={{1,0},{2,1},{17,16},{18,17},{33,32},{34,33},{49,48},{50,49},{65,64... | collective-permute-start | bytes 499208 | tf_op jit(solution)/shard_map/ppermute | solution.py:177
  133.9 0.7 collective-permute-start.18
  134.6 25.1 %collective-permute-start.20 = (f32[5,1,64,128]{3,2,1,0:T(8,128)S(1)}, f32[5,1,64,128]{3,2,1,0:T(8,128)S(1)}, u32[]{:S(2)}, u32[]{:S(2)}) collective-permute-start(f32[5,1,64,128]{3,2,1,0:T(8,128)S(1)} %get-tuple-element.10), channel_id=1, source_target_pairs={{0,3},{1,4},{2,5},{3,6},{4,7},{5,8},{6,9},{7,10},{8,11},{9,12},{10... | collective-permute-start | bytes 491528 | tf_op jit(solution)/shard_map/ppermute | solution.py:164
  138.1 19.0 %collective-permute-start.19 = (f32[5,1,64,128]{3,2,1,0:T(8,128)S(1)}, f32[5,1,64,128]{3,2,1,0:T(8,128)S(1)}, u32[]{:S(2)}, u32[]{:S(2)}) collective-permute-start(f32[5,1,64,128]{3,2,1,0:T(8,128)S(1)} %collective-permute-done.18), channel_id=1, source_target_pairs={{1,18},{3,17},{4,16},{17,34},{19,33},{20,32},{33,50},{35,49},{36,4... | collective-permute-start | bytes 491528 | tf_op jit(solution)/shard_map/ppermute | solution.py:155
  139.4 20.3 %collective-permute-start.22 = (f32[5,1,64,128]{3,2,1,0:T(8,128)S(1)}, f32[5,1,64,128]{3,2,1,0:T(8,128)S(1)}, u32[]{:S(2)}, u32[]{:S(2)}) collective-permute-start(f32[5,1,64,128]{3,2,1,0:T(8,128)S(1)} %get-tuple-element.10), channel_id=1, source_target_pairs={{0,2},{1,3},{2,4},{3,5},{4,6},{5,7},{6,8},{7,9},{8,10},{9,11},{10,... | collective-permute-start | bytes 491528 | tf_op jit(solution)/shard_map/ppermute | solution.py:164
  142.1 23.0 %collective-permute-start.24 = (f32[5,1,64,128]{3,2,1,0:T(8,128)S(1)}, f32[5,1,64,128]{3,2,1,0:T(8,128)S(1)}, u32[]{:S(2)}, u32[]{:S(2)}) collective-permute-start(f32[5,1,64,128]{3,2,1,0:T(8,128)S(1)} %get-tuple-element.10), channel_id=1, source_target_pairs={{0,1},{1,2},{2,3},{3,4},{4,5},{5,6},{6,7},{7,8},{8,9},{9,10},{10,1... | collective-permute-start | bytes 491528 | tf_op jit(solution)/shard_map/ppermute | solution.py:164
  157.1 8.0 %collective-permute-start.21 = (f32[5,1,64,128]{3,2,1,0:T(8,128)S(1)}, f32[5,1,64,128]{3,2,1,0:T(8,128)S(1)}, u32[]{:S(2)}, u32[]{:S(2)}) collective-permute-start(f32[5,1,64,128]{3,2,1,0:T(8,128)S(1)} %collective-permute-done.19), channel_id=1, source_target_pairs={{1,0},{2,1},{17,16},{18,17},{33,32},{34,33},{49,48},{50,49},{65,64... | collective-permute-start | bytes 491528 | tf_op jit(solution)/shard_map/ppermute | solution.py:177
  158.4 12.4 %collective-permute-start.23 = (f32[5,1,64,128]{3,2,1,0:T(8,128)S(1)}, f32[5,1,64,128]{3,2,1,0:T(8,128)S(1)}, u32[]{:S(2)}, u32[]{:S(2)}) collective-permute-start(f32[5,1,64,128]{3,2,1,0:T(8,128)S(1)} %collective-permute-done.19), channel_id=1, source_target_pairs={{2,0},{18,16},{34,32},{50,48},{66,64},{82,80},{98,96},{114,112},{1... | collective-permute-start | bytes 491528 | tf_op jit(solution)/shard_map/ppermute | solution.py:177

commit v12 on v4

--- a/solution.py
+++ b/solution.py
@@ -161,11 +161,19 @@
     first, second = crossing_relays(groups, count, plane, blocks)
     relayed = lax.ppermute(head, ("rad", "azi"), first)
     crossed = lax.ppermute(relayed, ("rad", "azi"), second)
+    direct = [
+        (a, b - (blocks - 1))
+        for a, b in second
+        if (b % plane) == blocks - 1
+    ]
+    first_seat = lax.ppermute(relayed, ("rad", "azi"), direct)
     position = lax.axis_index("azi") % plane
     pieces = []
     for k in range(1, blocks + 1):
         if k == blocks:
             far = crossed
+        elif k == 1 and blocks > 1:
+            far = first_seat
         else:
             t = blocks - k
             pairs = [

time: 167 us -> 165 us (0.988)
  the two profiles are of different devices: /device:TPU:64 before, /device:TPU:6 now
where the time goes in v12:
time: 165 us; the launch traced here: 162 us
  starting transfers between devices  85.2 us (52%)
  waiting for transfers between devices  61.9 us (38%)
  other arithmetic  10.1 us (6%)
  local copies, waits for them, and re-layouts  3.57 us (2%)
    ppermute x9, starting transfers between devices, rotation_pieces(): near.append(lax.ppermute(head, 'azi', pairs))  43 us
    ppermute x4, starting transfers between devices, passed_along(): return lax.ppermute(value, axis, pairs)  28.5 us
    ppermute x3, waiting for transfers between devices, rotation_pieces(): crossed = lax.ppermute(relayed, ('rad', 'azi'), second)  23.9 us
    ppermute x3, waiting for transfers between devices, rotation_pieces(): first_seat = lax.ppermute(relayed, ('rad', 'azi'), direct)  19.8 us
    ppermute x3, waiting for transfers between devices, rotation_pieces(): far = lax.ppermute(crossed, 'azi', pairs)  14 us
    ppermute x4, waiting for transfers between devices, passed_along(): return lax.ppermute(value, axis, pairs)  4.09 us
    ppermute x3, starting transfers between devices, rotation_pieces(): crossed = lax.ppermute(relayed, ('rad', 'azi'), second)  3.88 us
    ppermute x3, starting transfers between devices, rotation_pieces(): first_seat = lax.ppermute(relayed, ('rad', 'azi'), direct)  3.88 us
  transfers between devices with their start and end apart: 25, of which 9 were waited for; matrix products, arithmetic and copies ran while one was open for 2% of the time, Pallas kernels for 0%

profile of v12, /device:TPU:6, one launch (start us, length us, event | category | flops | bytes accessed | tf_op | source)
XLA Modules:
  0.0 161.7 jit_solution(6489600133381758327)
XLA Ops:
  0.0 0.8 fusion.103
  0.8 1.9 %collective-permute-start = (f32[5,1,3,128]{3,2,1,0:T(4,128)S(1)}, f32[5,1,3,128]{3,2,1,0:T(4,128)S(1)}, u32[]{:S(2)}, u32[]{:S(2)}) collective-permute-start(f32[5,1,3,128]{3,2,1,0:T(4,128)S(1)} %get-tuple-element.46), channel_id=1, source_target_pairs={{0,1},{1,2},{2,3},{3,4},{4,5},{5,6},{6,7},{7,8},{8,9},{9,10},{10,1... | collective-permute-start | bytes 23048 | tf_op jit(solution)/shard_map/ppermute | solution.py:25
  2.7 22.0 %collective-permute-start.1 = (f32[5,1,3,128]{3,2,1,0:T(4,128)S(1)}, f32[5,1,3,128]{3,2,1,0:T(4,128)S(1)}, u32[]{:S(2)}, u32[]{:S(2)}) collective-permute-start(f32[5,1,3,128]{3,2,1,0:T(4,128)S(1)} %get-tuple-element.47), channel_id=1, source_target_pairs={{0,127},{1,0},{2,1},{3,2},{4,3},{5,4},{6,5},{7,6},{8,7},{9,8},{10,... | collective-permute-start | bytes 23048 | tf_op jit(solution)/shard_map/ppermute | solution.py:25
  24.7 0.8 slice_convert_fusion.1
  26.1 0.9 pad_maximum_fusion
  27.1 0.2 reshape.1273
  27.4 3.4 %collective-permute-start.2 = (f32[1059]{0:T(1024)S(1)}, f32[1059]{0:T(1024)S(1)}, u32[]{:S(2)}, u32[]{:S(2)}) collective-permute-start(f32[1059]{0:T(1024)S(1)} %pad_maximum_fusion.1), channel_id=1, source_target_pairs={{0,128},{128,256},{256,384},{384,512},{512,640},{640,768},{768,896... | collective-permute-start | bytes 12716 | tf_op jit(solution)/shard_map/ppermute | solution.py:25
  30.8 0.2 reshape.1275
  31.1 1.3 collective-permute-start.3
  32.4 0.2 concatenate.40
  32.6 4.0 %collective-permute-done.3 = f32[1059]{0:T(1024)S(1)} collective-permute-done((f32[1059]{0:T(1024)S(1)}, f32[1059]{0:T(1024)S(1)}, u32[]{:S(2)}, u32[]{:S(2)}) %collective-permute-start.3) | collective-permute-done | bytes 4268 | tf_op jit(solution)/shard_map/ppermute | solution.py:25
  36.6 0.2 concatenate.41
  36.8 0.2 maximum_select_fusion
  37.2 0.2 subtract_multiply_fusion.3
  37.3 0.6 subtract_add_fusion.1
  38.0 0.1 fusion.4
  38.2 0.1 fusion.29
  38.6 0.7 collective-permute-start.4
  39.2 1.3 collective-permute-start.10
  40.6 1.3 collective-permute-start.8
  41.9 1.3 collective-permute-start.6
  43.7 1.3 collective-permute-start.5
  45.0 1.3 collective-permute-start.9
  46.4 18.6 %collective-permute-done.5 = f32[5,1,64,132]{3,2,1,0:T(8,128)S(1)} collective-permute-done((f32[5,1,64,132]{3,2,1,0:T(8,128)S(1)}, f32[5,1,64,132]{3,2,1,0:T(8,128)S(1)}, u32[]{:S(2)}, u32[]{:S(2)}) %collective-permute-start.5) | collective-permute-done | bytes 168992 | tf_op jit(solution)/shard_map/ppermute | solution.py:163
  65.0 1.3 collective-permute-start.7
  66.3 1.4 collective-permute-done.9
  67.8 8.9 %collective-permute-done.7 = f32[5,1,64,132]{3,2,1,0:T(8,128)S(1)} collective-permute-done((f32[5,1,64,132]{3,2,1,0:T(8,128)S(1)}, f32[5,1,64,132]{3,2,1,0:T(8,128)S(1)}, u32[]{:S(2)}, u32[]{:S(2)}) %collective-permute-start.7) | collective-permute-done | bytes 168992 | tf_op jit(solution)/shard_map/ppermute | solution.py:184
  76.7 0.7 concatenate.43
  77.4 0.2 slice_select_fusion
  77.6 0.2 slice_select_fusion.5
  77.8 0.2 slice_select_fusion.4
  77.9 0.1 slice_select_fusion.7
  78.1 0.1 slice_select_fusion.9
  78.6 0.2 subtract_multiply_fusion.1
  78.7 0.6 subtract_add_fusion
  79.4 0.1 fusion.7
  79.6 0.1 fusion.14
  79.9 0.7 collective-permute-start.11
  80.7 1.3 collective-permute-start.13
  82.0 1.3 collective-permute-start.12
  83.3 14.9 %collective-permute-start.17 = (f32[5,1,64,130]{3,2,1,0:T(8,128)S(1)}, f32[5,1,64,130]{3,2,1,0:T(8,128)S(1)}, u32[]{:S(2)}, u32[]{:S(2)}) collective-permute-start(f32[5,1,64,130]{3,2,1,0:T(8,128)S(1)} %slice.677), channel_id=1, source_target_pairs={{0,1},{1,2},{2,3},{3,4},{4,5},{5,6},{6,7},{7,8},{8,9},{9,10},{10,1... | collective-permute-start | bytes 499208 | tf_op jit(solution)/shard_map/ppermute | solution.py:160
  98.2 9.1 %collective-permute-start.15 = (f32[5,1,64,130]{3,2,1,0:T(8,128)S(1)}, f32[5,1,64,130]{3,2,1,0:T(8,128)S(1)}, u32[]{:S(2)}, u32[]{:S(2)}) collective-permute-start(f32[5,1,64,130]{3,2,1,0:T(8,128)S(1)} %slice.677), channel_id=1, source_target_pairs={{0,2},{1,3},{2,4},{3,5},{4,6},{5,7},{6,8},{7,9},{8,10},{9,11},{10,... | collective-permute-start | bytes 499208 | tf_op jit(solution)/shard_map/ppermute | solution.py:160
  107.3 1.3 collective-permute-start.16
  108.6 1.3 collective-permute-start.14
  110.0 15.3 %collective-permute-done.16 = f32[5,1,64,130]{3,2,1,0:T(8,128)S(1)} collective-permute-done((f32[5,1,64,130]{3,2,1,0:T(8,128)S(1)}, f32[5,1,64,130]{3,2,1,0:T(8,128)S(1)}, u32[]{:S(2)}, u32[]{:S(2)}) %collective-permute-start.16) | collective-permute-done | bytes 166432 | tf_op jit(solution)/shard_map/ppermute | solution.py:169
  125.5 0.7 concatenate.44
  126.2 0.2 slice_select_fusion.3
  126.4 0.2 slice_select_fusion.2
  126.5 0.2 slice_select_fusion.1
  126.7 0.1 slice_select_fusion.6
  126.9 0.1 slice_select_fusion.8
  127.3 0.1 subtract_multiply_fusion.5
  127.4 0.3 subtract_add_fusion.2
  128.2 0.7 collective-permute-start.18
  128.9 1.3 collective-permute-start.20
  130.2 1.3 collective-permute-start.19
  131.5 1.3 collective-permute-start.22
  132.9 11.2 %collective-permute-start.24 = (f32[5,1,64,128]{3,2,1,0:T(8,128)S(1)}, f32[5,1,64,128]{3,2,1,0:T(8,128)S(1)}, u32[]{:S(2)}, u32[]{:S(2)}) collective-permute-start(f32[5,1,64,128]{3,2,1,0:T(8,128)S(1)} %get-tuple-element.5), channel_id=1, source_target_pairs={{0,1},{1,2},{2,3},{3,4},{4,5},{5,6},{6,7},{7,8},{8,9},{9,10},{10,1... | collective-permute-start | bytes 491528 | tf_op jit(solution)/shard_map/ppermute | solution.py:160
  144.0 1.3 collective-permute-start.23
  145.3 5.3 %collective-permute-done.19 = f32[5,1,64,128]{3,2,1,0:T(8,128)S(1)} collective-permute-done((f32[5,1,64,128]{3,2,1,0:T(8,128)S(1)}, f32[5,1,64,128]{3,2,1,0:T(8,128)S(1)}, u32[]{:S(2)}, u32[]{:S(2)}) %collective-permute-start.19) | collective-permute-done | bytes 163872 | tf_op jit(solution)/shard_map/ppermute | solution.py:163
  150.7 1.3 collective-permute-start.21
  152.0 5.2 %collective-permute-done.21 = f32[5,1,64,128]{3,2,1,0:T(8,128)S(1)} collective-permute-done((f32[5,1,64,128]{3,2,1,0:T(8,128)S(1)}, f32[5,1,64,128]{3,2,1,0:T(8,128)S(1)}, u32[]{:S(2)}, u32[]{:S(2)}) %collective-permute-start.21) | collective-permute-done | bytes 163872 | tf_op jit(solution)/shard_map/ppermute | solution.py:184
  157.2 3.1 %collective-permute-done.23 = f32[5,1,64,128]{3,2,1,0:T(8,128)S(1)} collective-permute-done((f32[5,1,64,128]{3,2,1,0:T(8,128)S(1)}, f32[5,1,64,128]{3,2,1,0:T(8,128)S(1)}, u32[]{:S(2)}, u32[]{:S(2)}) %collective-permute-start.23) | collective-permute-done | bytes 163872 | tf_op jit(solution)/shard_map/ppermute | solution.py:169
  161.0 0.7 slice_select_fusion.23
  (93 shorter events, 4.2 us)
Async XLA Ops:
  0.0 36.8 %copy-start = (f32[5,1,64,128]{3,2,1,0:T(8,128)S(1)}, f32[5,1,64,128]{3,2,1,0:T(8,128)}, u32[]{:S(2)}) copy-start(f32[5,1,64,128]{3,2,1,0:T(8,128)} %param.2) | copy-start | bytes 491524
  0.8 25.2 %collective-permute-start = (f32[5,1,3,128]{3,2,1,0:T(4,128)S(1)}, f32[5,1,3,128]{3,2,1,0:T(4,128)S(1)}, u32[]{:S(2)}, u32[]{:S(2)}) collective-permute-start(f32[5,1,3,128]{3,2,1,0:T(4,128)S(1)} %get-tuple-element.46), channel_id=1, source_target_pairs={{0,1},{1,2},{2,3},{3,4},{4,5},{5,6},{6,7},{7,8},{8,9},{9,10},{10,1... | collective-permute-start | bytes 23048 | tf_op jit(solution)/shard_map/ppermute | solution.py:25
  2.7 23.3 %collective-permute-start.1 = (f32[5,1,3,128]{3,2,1,0:T(4,128)S(1)}, f32[5,1,3,128]{3,2,1,0:T(4,128)S(1)}, u32[]{:S(2)}, u32[]{:S(2)}) collective-permute-start(f32[5,1,3,128]{3,2,1,0:T(4,128)S(1)} %get-tuple-element.47), channel_id=1, source_target_pairs={{0,127},{1,0},{2,1},{3,2},{4,3},{5,4},{6,5},{7,6},{8,7},{9,8},{10,... | collective-permute-start | bytes 23048 | tf_op jit(solution)/shard_map/ppermute | solution.py:25
  27.4 5.0 %collective-permute-start.2 = (f32[1059]{0:T(1024)S(1)}, f32[1059]{0:T(1024)S(1)}, u32[]{:S(2)}, u32[]{:S(2)}) collective-permute-start(f32[1059]{0:T(1024)S(1)} %pad_maximum_fusion.1), channel_id=1, source_target_pairs={{0,128},{128,256},{256,384},{384,512},{512,640},{640,768},{768,896... | collective-permute-start | bytes 12716 | tf_op jit(solution)/shard_map/ppermute | solution.py:25
  31.1 5.5 %collective-permute-start.3 = (f32[1059]{0:T(1024)S(1)}, f32[1059]{0:T(1024)S(1)}, u32[]{:S(2)}, u32[]{:S(2)}) collective-permute-start(f32[1059]{0:T(1024)S(1)} %pad_maximum_fusion.2), channel_id=1, source_target_pairs={{128,0},{256,128},{384,256},{512,384},{640,512},{768,640},{896,768... | collective-permute-start | bytes 12716 | tf_op jit(solution)/shard_map/ppermute | solution.py:25
  37.9 5.6 %copy-start.1 = (s32[3,128]{1,0:T(4,128)S(1)}, s32[3,128]{1,0:T(4,128)}, u32[]{:S(2)}) copy-start(s32[3,128]{1,0:T(4,128)} %param.3) | copy-start | bytes 4612
  38.6 5.1 %collective-permute-start.4 = (f32[5,1,64,132]{3,2,1,0:T(8,128)S(1)}, f32[5,1,64,132]{3,2,1,0:T(8,128)S(1)}, u32[]{:S(2)}, u32[]{:S(2)}) collective-permute-start(f32[5,1,64,132]{3,2,1,0:T(8,128)S(1)} %slice.635), channel_id=1, source_target_pairs={{15,1},{14,3},{13,4},{31,17},{30,19},{29,20},{47,33},{46,35},{45,3... | collective-permute-start | bytes 506888 | tf_op jit(solution)/shard_map/ppermute | solution.py:162
  39.2 27.1 %collective-permute-start.10 = (f32[5,1,64,132]{3,2,1,0:T(8,128)S(1)}, f32[5,1,64,132]{3,2,1,0:T(8,128)S(1)}, u32[]{:S(2)}, u32[]{:S(2)}) collective-permute-start(f32[5,1,64,132]{3,2,1,0:T(8,128)S(1)} %slice.635), channel_id=1, source_target_pairs={{0,1},{1,2},{2,3},{3,4},{4,5},{5,6},{6,7},{7,8},{8,9},{9,10},{10,1... | collective-permute-start | bytes 506888 | tf_op jit(solution)/shard_map/ppermute | solution.py:160
  40.6 27.2 %collective-permute-start.8 = (f32[5,1,64,132]{3,2,1,0:T(8,128)S(1)}, f32[5,1,64,132]{3,2,1,0:T(8,128)S(1)}, u32[]{:S(2)}, u32[]{:S(2)}) collective-permute-start(f32[5,1,64,132]{3,2,1,0:T(8,128)S(1)} %slice.635), channel_id=1, source_target_pairs={{0,2},{1,3},{2,4},{3,5},{4,6},{5,7},{6,8},{7,9},{8,10},{9,11},{10,... | collective-permute-start | bytes 506888 | tf_op jit(solution)/shard_map/ppermute | solution.py:160
  41.9 24.4 %collective-permute-start.6 = (f32[5,1,64,132]{3,2,1,0:T(8,128)S(1)}, f32[5,1,64,132]{3,2,1,0:T(8,128)S(1)}, u32[]{:S(2)}, u32[]{:S(2)}) collective-permute-start(f32[5,1,64,132]{3,2,1,0:T(8,128)S(1)} %slice.635), channel_id=1, source_target_pairs={{0,3},{1,4},{2,5},{3,6},{4,7},{5,8},{6,9},{7,10},{8,11},{9,12},{10... | collective-permute-start | bytes 506888 | tf_op jit(solution)/shard_map/ppermute | solution.py:160
  43.7 21.2 %collective-permute-start.5 = (f32[5,1,64,132]{3,2,1,0:T(8,128)S(1)}, f32[5,1,64,132]{3,2,1,0:T(8,128)S(1)}, u32[]{:S(2)}, u32[]{:S(2)}) collective-permute-start(f32[5,1,64,132]{3,2,1,0:T(8,128)S(1)} %collective-permute-done.4), channel_id=1, source_target_pairs={{1,18},{3,17},{4,16},{17,34},{19,33},{20,32},{33,50},{35,49},{36,4... | collective-permute-start | bytes 506888 | tf_op jit(solution)/shard_map/ppermute | solution.py:163
  45.0 22.6 %collective-permute-start.9 = (f32[5,1,64,132]{3,2,1,0:T(8,128)S(1)}, f32[5,1,64,132]{3,2,1,0:T(8,128)S(1)}, u32[]{:S(2)}, u32[]{:S(2)}) collective-permute-start(f32[5,1,64,132]{3,2,1,0:T(8,128)S(1)} %collective-permute-done.4), channel_id=1, source_target_pairs={{1,16},{17,32},{33,48},{49,64},{65,80},{81,96},{97,112},{113,0},{1... | collective-permute-start | bytes 506888 | tf_op jit(solution)/shard_map/ppermute | solution.py:169
  65.0 11.7 %collective-permute-start.7 = (f32[5,1,64,132]{3,2,1,0:T(8,128)S(1)}, f32[5,1,64,132]{3,2,1,0:T(8,128)S(1)}, u32[]{:S(2)}, u32[]{:S(2)}) collective-permute-start(f32[5,1,64,132]{3,2,1,0:T(8,128)S(1)} %collective-permute-done.5), channel_id=1, source_target_pairs={{1,0},{2,1},{17,16},{18,17},{33,32},{34,33},{49,48},{50,49},{65,64... | collective-permute-start | bytes 506888 | tf_op jit(solution)/shard_map/ppermute | solution.py:184
  79.9 2.0 %collective-permute-start.11 = (f32[5,1,64,130]{3,2,1,0:T(8,128)S(1)}, f32[5,1,64,130]{3,2,1,0:T(8,128)S(1)}, u32[]{:S(2)}, u32[]{:S(2)}) collective-permute-start(f32[5,1,64,130]{3,2,1,0:T(8,128)S(1)} %slice.677), channel_id=1, source_target_pairs={{15,1},{14,3},{13,4},{31,17},{30,19},{29,20},{47,33},{46,35},{45,3... | collective-permute-start | bytes 499208 | tf_op jit(solution)/shard_map/ppermute | solution.py:162
  80.7 29.3 %collective-permute-start.13 = (f32[5,1,64,130]{3,2,1,0:T(8,128)S(1)}, f32[5,1,64,130]{3,2,1,0:T(8,128)S(1)}, u32[]{:S(2)}, u32[]{:S(2)}) collective-permute-start(f32[5,1,64,130]{3,2,1,0:T(8,128)S(1)} %slice.677), channel_id=1, source_target_pairs={{0,3},{1,4},{2,5},{3,6},{4,7},{5,8},{6,9},{7,10},{8,11},{9,12},{10... | collective-permute-start | bytes 499208 | tf_op jit(solution)/shard_map/ppermute | solution.py:160
  82.0 26.6 %collective-permute-start.12 = (f32[5,1,64,130]{3,2,1,0:T(8,128)S(1)}, f32[5,1,64,130]{3,2,1,0:T(8,128)S(1)}, u32[]{:S(2)}, u32[]{:S(2)}) collective-permute-start(f32[5,1,64,130]{3,2,1,0:T(8,128)S(1)} %collective-permute-done.11), channel_id=1, source_target_pairs={{1,18},{3,17},{4,16},{17,34},{19,33},{20,32},{33,50},{35,49},{36,4... | collective-permute-start | bytes 499208 | tf_op jit(solution)/shard_map/ppermute | solution.py:163
  83.3 26.7 %collective-permute-start.17 = (f32[5,1,64,130]{3,2,1,0:T(8,128)S(1)}, f32[5,1,64,130]{3,2,1,0:T(8,128)S(1)}, u32[]{:S(2)}, u32[]{:S(2)}) collective-permute-start(f32[5,1,64,130]{3,2,1,0:T(8,128)S(1)} %slice.677), channel_id=1, source_target_pairs={{0,1},{1,2},{2,3},{3,4},{4,5},{5,6},{6,7},{7,8},{8,9},{9,10},{10,1... | collective-permute-start | bytes 499208 | tf_op jit(solution)/shard_map/ppermute | solution.py:160
  98.2 27.1 %collective-permute-start.15 = (f32[5,1,64,130]{3,2,1,0:T(8,128)S(1)}, f32[5,1,64,130]{3,2,1,0:T(8,128)S(1)}, u32[]{:S(2)}, u32[]{:S(2)}) collective-permute-start(f32[5,1,64,130]{3,2,1,0:T(8,128)S(1)} %slice.677), channel_id=1, source_target_pairs={{0,2},{1,3},{2,4},{3,5},{4,6},{5,7},{6,8},{7,9},{8,10},{9,11},{10,... | collective-permute-start | bytes 499208 | tf_op jit(solution)/shard_map/ppermute | solution.py:160
  107.3 18.0 %collective-permute-start.16 = (f32[5,1,64,130]{3,2,1,0:T(8,128)S(1)}, f32[5,1,64,130]{3,2,1,0:T(8,128)S(1)}, u32[]{:S(2)}, u32[]{:S(2)}) collective-permute-start(f32[5,1,64,130]{3,2,1,0:T(8,128)S(1)} %collective-permute-done.11), channel_id=1, source_target_pairs={{1,16},{17,32},{33,48},{49,64},{65,80},{81,96},{97,112},{113,0},{1... | collective-permute-start | bytes 499208 | tf_op jit(solution)/shard_map/ppermute | solution.py:169
  108.6 16.8 %collective-permute-start.14 = (f32[5,1,64,130]{3,2,1,0:T(8,128)S(1)}, f32[5,1,64,130]{3,2,1,0:T(8,128)S(1)}, u32[]{:S(2)}, u32[]{:S(2)}) collective-permute-start(f32[5,1,64,130]{3,2,1,0:T(8,128)S(1)} %collective-permute-done.12), channel_id=1, source_target_pairs={{1,0},{2,1},{17,16},{18,17},{33,32},{34,33},{49,48},{50,49},{65,64... | collective-permute-start | bytes 499208 | tf_op jit(solution)/shard_map/ppermute | solution.py:184
  128.2 2.0 %collective-permute-start.18 = (f32[5,1,64,128]{3,2,1,0:T(8,128)S(1)}, f32[5,1,64,128]{3,2,1,0:T(8,128)S(1)}, u32[]{:S(2)}, u32[]{:S(2)}) collective-permute-start(f32[5,1,64,128]{3,2,1,0:T(8,128)S(1)} %get-tuple-element.5), channel_id=1, source_target_pairs={{15,1},{14,3},{13,4},{31,17},{30,19},{29,20},{47,33},{46,35},{45,3... | collective-permute-start | bytes 491528 | tf_op jit(solution)/shard_map/ppermute | solution.py:162
  128.9 23.1 %collective-permute-start.20 = (f32[5,1,64,128]{3,2,1,0:T(8,128)S(1)}, f32[5,1,64,128]{3,2,1,0:T(8,128)S(1)}, u32[]{:S(2)}, u32[]{:S(2)}) collective-permute-start(f32[5,1,64,128]{3,2,1,0:T(8,128)S(1)} %get-tuple-element.5), channel_id=1, source_target_pairs={{0,3},{1,4},{2,5},{3,6},{4,7},{5,8},{6,9},{7,10},{8,11},{9,12},{10... | collective-permute-start | bytes 491528 | tf_op jit(solution)/shard_map/ppermute | solution.py:160
  130.2 20.5 %collective-permute-start.19 = (f32[5,1,64,128]{3,2,1,0:T(8,128)S(1)}, f32[5,1,64,128]{3,2,1,0:T(8,128)S(1)}, u32[]{:S(2)}, u32[]{:S(2)}) collective-permute-start(f32[5,1,64,128]{3,2,1,0:T(8,128)S(1)} %collective-permute-done.18), channel_id=1, source_target_pairs={{1,18},{3,17},{4,16},{17,34},{19,33},{20,32},{33,50},{35,49},{36,4... | collective-permute-start | bytes 491528 | tf_op jit(solution)/shard_map/ppermute | solution.py:163
  131.5 20.5 %collective-permute-start.22 = (f32[5,1,64,128]{3,2,1,0:T(8,128)S(1)}, f32[5,1,64,128]{3,2,1,0:T(8,128)S(1)}, u32[]{:S(2)}, u32[]{:S(2)}) collective-permute-start(f32[5,1,64,128]{3,2,1,0:T(8,128)S(1)} %get-tuple-element.5), channel_id=1, source_target_pairs={{0,2},{1,3},{2,4},{3,5},{4,6},{5,7},{6,8},{7,9},{8,10},{9,11},{10,... | collective-permute-start | bytes 491528 | tf_op jit(solution)/shard_map/ppermute | solution.py:160
  132.9 24.3 %collective-permute-start.24 = (f32[5,1,64,128]{3,2,1,0:T(8,128)S(1)}, f32[5,1,64,128]{3,2,1,0:T(8,128)S(1)}, u32[]{:S(2)}, u32[]{:S(2)}) collective-permute-start(f32[5,1,64,128]{3,2,1,0:T(8,128)S(1)} %get-tuple-element.5), channel_id=1, source_target_pairs={{0,1},{1,2},{2,3},{3,4},{4,5},{5,6},{6,7},{7,8},{8,9},{9,10},{10,1... | collective-permute-start | bytes 491528 | tf_op jit(solution)/shard_map/ppermute | solution.py:160
  144.0 16.3 %collective-permute-start.23 = (f32[5,1,64,128]{3,2,1,0:T(8,128)S(1)}, f32[5,1,64,128]{3,2,1,0:T(8,128)S(1)}, u32[]{:S(2)}, u32[]{:S(2)}) collective-permute-start(f32[5,1,64,128]{3,2,1,0:T(8,128)S(1)} %collective-permute-done.18), channel_id=1, source_target_pairs={{1,16},{17,32},{33,48},{49,64},{65,80},{81,96},{97,112},{113,0},{1... | collective-permute-start | bytes 491528 | tf_op jit(solution)/shard_map/ppermute | solution.py:169
  150.7 6.5 %collective-permute-start.21 = (f32[5,1,64,128]{3,2,1,0:T(8,128)S(1)}, f32[5,1,64,128]{3,2,1,0:T(8,128)S(1)}, u32[]{:S(2)}, u32[]{:S(2)}) collective-permute-start(f32[5,1,64,128]{3,2,1,0:T(8,128)S(1)} %collective-permute-done.19), channel_id=1, source_target_pairs={{1,0},{2,1},{17,16},{18,17},{33,32},{34,33},{49,48},{50,49},{65,64... | collective-permute-start | bytes 491528 | tf_op jit(solution)/shard_map/ppermute | solution.py:184

commit v13 on v12

--- a/solution.py
+++ b/solution.py
@@ -168,6 +168,12 @@
     ]
     first_seat = lax.ppermute(relayed, ("rad", "azi"), direct)
     position = lax.axis_index("azi") % plane
+    if blocks == 3:
+        swap = [(b + s, b + 1 - s) for b in range(0, count, plane) for s in (0, 1)]
+        given = jnp.where(position == 0, first_seat, crossed)
+        swapped = lax.ppermute(given, "azi", swap)
+        fars = [first_seat, swapped, crossed]
+        return [jnp.where(position < k, fars[k - 1], near[k - 1]) for k in (1, 2, 3)]
     pieces = []
     for k in range(1, blocks + 1):
         if k == blocks:

time: 165 us -> 165 us (level)
  the two profiles are of different devices: /device:TPU:6 before, /device:TPU:136 now
where the time goes in v13:
time: 165 us; the launch traced here: 164 us
  waiting for transfers between devices  105 us (64%)
  starting transfers between devices  44.6 us (27%)
  other arithmetic  10.2 us (6%)
  local copies, waits for them, and re-layouts  3.56 us (2%)
    ppermute x3, waiting for transfers between devices, rotation_pieces(): crossed = lax.ppermute(relayed, ('rad', 'azi'), second)  53.7 us
    ppermute x9, waiting for transfers between devices, rotation_pieces(): near.append(lax.ppermute(head, 'azi', pairs))  45.9 us
    ppermute x9, starting transfers between devices, rotation_pieces(): near.append(lax.ppermute(head, 'azi', pairs))  22.9 us
    ppermute x4, starting transfers between devices, passed_along(): return lax.ppermute(value, axis, pairs)  11.7 us
    ppermute x4, waiting for transfers between devices, passed_along(): return lax.ppermute(value, axis, pairs)  5.03 us
    ppermute x3, starting transfers between devices, rotation_pieces(): crossed = lax.ppermute(relayed, ('rad', 'azi'), second)  3.87 us
  transfers between devices with their start and end apart: 25, of which 9 were waited for; matrix products, arithmetic and copies ran while one was open for 2% of the time, Pallas kernels for 0%

profile of v13, /device:TPU:136, one launch (start us, length us, event | category | flops | bytes accessed | tf_op | source)
XLA Modules:
  0.0 164.0 jit_solution(5009076515939531023)
XLA Ops:
  0.0 0.8 fusion.103
  0.8 1.9 %collective-permute-start = (f32[5,1,3,128]{3,2,1,0:T(4,128)S(1)}, f32[5,1,3,128]{3,2,1,0:T(4,128)S(1)}, u32[]{:S(2)}, u32[]{:S(2)}) collective-permute-start(f32[5,1,3,128]{3,2,1,0:T(4,128)S(1)} %get-tuple-element.54), channel_id=1, source_target_pairs={{0,1},{1,2},{2,3},{3,4},{4,5},{5,6},{6,7},{7,8},{8,9},{9,10},{10,1... | collective-permute-start | bytes 23048 | tf_op jit(solution)/shard_map/ppermute | solution.py:25
  2.7 3.6 %collective-permute-start.1 = (f32[5,1,3,128]{3,2,1,0:T(4,128)S(1)}, f32[5,1,3,128]{3,2,1,0:T(4,128)S(1)}, u32[]{:S(2)}, u32[]{:S(2)}) collective-permute-start(f32[5,1,3,128]{3,2,1,0:T(4,128)S(1)} %get-tuple-element.55), channel_id=1, source_target_pairs={{0,127},{1,0},{2,1},{3,2},{4,3},{5,4},{6,5},{7,6},{8,7},{9,8},{10,... | collective-permute-start | bytes 23048 | tf_op jit(solution)/shard_map/ppermute | solution.py:25
  6.4 0.8 slice_convert_fusion.1
  7.7 0.9 pad_maximum_fusion
  8.8 0.2 reshape.1273
  9.1 4.3 %collective-permute-start.2 = (f32[1059]{0:T(1024)S(1)}, f32[1059]{0:T(1024)S(1)}, u32[]{:S(2)}, u32[]{:S(2)}) collective-permute-start(f32[1059]{0:T(1024)S(1)} %pad_maximum_fusion.1), channel_id=1, source_target_pairs={{0,128},{128,256},{256,384},{384,512},{512,640},{640,768},{768,896... | collective-permute-start | bytes 12716 | tf_op jit(solution)/shard_map/ppermute | solution.py:25
  13.4 0.2 reshape.1275
  13.6 1.9 %collective-permute-start.3 = (f32[1059]{0:T(1024)S(1)}, f32[1059]{0:T(1024)S(1)}, u32[]{:S(2)}, u32[]{:S(2)}) collective-permute-start(f32[1059]{0:T(1024)S(1)} %pad_maximum_fusion.2), channel_id=1, source_target_pairs={{128,0},{256,128},{384,256},{512,384},{640,512},{768,640},{896,768... | collective-permute-start | bytes 12716 | tf_op jit(solution)/shard_map/ppermute | solution.py:25
  15.6 0.2 concatenate.40
  15.8 4.9 %collective-permute-done.3 = f32[1059]{0:T(1024)S(1)} collective-permute-done((f32[1059]{0:T(1024)S(1)}, f32[1059]{0:T(1024)S(1)}, u32[]{:S(2)}, u32[]{:S(2)}) %collective-permute-start.3) | collective-permute-done | bytes 4268 | tf_op jit(solution)/shard_map/ppermute | solution.py:25
  20.7 0.2 concatenate.41
  21.0 0.2 maximum_select_fusion
  21.3 0.2 subtract_multiply_fusion.3
  21.5 0.6 subtract_add_fusion.1
  22.2 0.1 fusion.4
  22.3 0.1 fusion.29
  22.7 0.7 collective-permute-start.4
  23.4 2.4 %collective-permute-start.10 = (f32[5,1,64,132]{3,2,1,0:T(8,128)S(1)}, f32[5,1,64,132]{3,2,1,0:T(8,128)S(1)}, u32[]{:S(2)}, u32[]{:S(2)}) collective-permute-start(f32[5,1,64,132]{3,2,1,0:T(8,128)S(1)} %slice.635), channel_id=1, source_target_pairs={{0,1},{1,2},{2,3},{3,4},{4,5},{5,6},{6,7},{7,8},{8,9},{9,10},{10,1... | collective-permute-start | bytes 506888 | tf_op jit(solution)/shard_map/ppermute | solution.py:160
  25.8 4.7 %collective-permute-start.6 = (f32[5,1,64,132]{3,2,1,0:T(8,128)S(1)}, f32[5,1,64,132]{3,2,1,0:T(8,128)S(1)}, u32[]{:S(2)}, u32[]{:S(2)}) collective-permute-start(f32[5,1,64,132]{3,2,1,0:T(8,128)S(1)} %slice.635), channel_id=1, source_target_pairs={{0,3},{1,4},{2,5},{3,6},{4,7},{5,8},{6,9},{7,10},{8,11},{9,12},{10... | collective-permute-start | bytes 506888 | tf_op jit(solution)/shard_map/ppermute | solution.py:160
  30.6 5.4 %collective-permute-start.9 = (f32[5,1,64,132]{3,2,1,0:T(8,128)S(1)}, f32[5,1,64,132]{3,2,1,0:T(8,128)S(1)}, u32[]{:S(2)}, u32[]{:S(2)}) collective-permute-start(f32[5,1,64,132]{3,2,1,0:T(8,128)S(1)} %slice.635), channel_id=1, source_target_pairs={{0,2},{1,3},{2,4},{3,5},{4,6},{5,7},{6,8},{7,9},{8,10},{9,11},{10,... | collective-permute-start | bytes 506888 | tf_op jit(solution)/shard_map/ppermute | solution.py:160
  36.4 1.3 collective-permute-start.5
  37.7 0.7 collective-permute-start.7
  38.4 3.0 %collective-permute-done.6 = f32[5,1,64,132]{3,2,1,0:T(8,128)S(1)} collective-permute-done((f32[5,1,64,132]{3,2,1,0:T(8,128)S(1)}, f32[5,1,64,132]{3,2,1,0:T(8,128)S(1)}, u32[]{:S(2)}, u32[]{:S(2)}) %collective-permute-start.6) | collective-permute-done | bytes 168992 | tf_op jit(solution)/shard_map/ppermute | solution.py:160
  41.5 27.1 %collective-permute-done.5 = f32[5,1,64,132]{3,2,1,0:T(8,128)S(1)} collective-permute-done((f32[5,1,64,132]{3,2,1,0:T(8,128)S(1)}, f32[5,1,64,132]{3,2,1,0:T(8,128)S(1)}, u32[]{:S(2)}, u32[]{:S(2)}) %collective-permute-start.5) | collective-permute-done | bytes 168992 | tf_op jit(solution)/shard_map/ppermute | solution.py:163
  68.6 0.1 broadcast_select_fusion.3
  68.7 0.7 collective-permute-start.8
  69.5 0.7 concatenate.43
  70.2 0.2 slice_select_fusion
  70.4 0.2 slice_select_fusion.5
  70.6 0.2 slice_select_fusion.4
  70.8 0.1 slice_select_fusion.7
  70.9 0.1 slice_select_fusion.9
  71.4 0.2 subtract_multiply_fusion.1
  71.6 0.6 subtract_add_fusion
  72.3 0.1 fusion.7
  72.4 0.1 fusion.14
  72.8 0.7 collective-permute-start.11
  73.5 1.3 collective-permute-start.13
  74.9 1.9 %collective-permute-start.17 = (f32[5,1,64,130]{3,2,1,0:T(8,128)S(1)}, f32[5,1,64,130]{3,2,1,0:T(8,128)S(1)}, u32[]{:S(2)}, u32[]{:S(2)}) collective-permute-start(f32[5,1,64,130]{3,2,1,0:T(8,128)S(1)} %slice.677), channel_id=1, source_target_pairs={{0,1},{1,2},{2,3},{3,4},{4,5},{5,6},{6,7},{7,8},{8,9},{9,10},{10,1... | collective-permute-start | bytes 499208 | tf_op jit(solution)/shard_map/ppermute | solution.py:160
  76.8 1.3 collective-permute-start.12
  78.1 0.7 collective-permute-start.14
  78.8 1.9 %collective-permute-start.16 = (f32[5,1,64,130]{3,2,1,0:T(8,128)S(1)}, f32[5,1,64,130]{3,2,1,0:T(8,128)S(1)}, u32[]{:S(2)}, u32[]{:S(2)}) collective-permute-start(f32[5,1,64,130]{3,2,1,0:T(8,128)S(1)} %slice.677), channel_id=1, source_target_pairs={{0,2},{1,3},{2,4},{3,5},{4,6},{5,7},{6,8},{7,9},{8,10},{9,11},{10,... | collective-permute-start | bytes 499208 | tf_op jit(solution)/shard_map/ppermute | solution.py:160
  80.7 0.2 collective-permute-done.13
  81.0 22.0 %collective-permute-done.17 = f32[5,1,64,130]{3,2,1,0:T(8,128)S(1)} collective-permute-done((f32[5,1,64,130]{3,2,1,0:T(8,128)S(1)}, f32[5,1,64,130]{3,2,1,0:T(8,128)S(1)}, u32[]{:S(2)}, u32[]{:S(2)}) %collective-permute-start.17) | collective-permute-done | bytes 166432 | tf_op jit(solution)/shard_map/ppermute | solution.py:160
  103.0 1.2 collective-permute-done.12
  104.2 0.7 collective-permute-start.15
  105.1 0.7 concatenate.44
  105.8 0.2 slice_select_fusion.3
  105.9 0.2 slice_select_fusion.2
  106.1 0.2 slice_select_fusion.1
  106.3 0.1 slice_select_fusion.6
  106.9 0.1 subtract_multiply_fusion.5
  107.0 0.3 subtract_add_fusion.2
  107.8 0.7 collective-permute-start.18
  108.5 1.3 collective-permute-start.20
  109.8 1.3 collective-permute-start.19
  111.1 0.7 collective-permute-start.21
  111.8 1.9 %collective-permute-start.23 = (f32[5,1,64,128]{3,2,1,0:T(8,128)S(1)}, f32[5,1,64,128]{3,2,1,0:T(8,128)S(1)}, u32[]{:S(2)}, u32[]{:S(2)}) collective-permute-start(f32[5,1,64,128]{3,2,1,0:T(8,128)S(1)} %get-tuple-element.5), channel_id=1, source_target_pairs={{0,2},{1,3},{2,4},{3,5},{4,6},{5,7},{6,8},{7,9},{8,10},{9,11},{10,... | collective-permute-start | bytes 491528 | tf_op jit(solution)/shard_map/ppermute | solution.py:160
  113.7 25.5 %collective-permute-done.19 = f32[5,1,64,128]{3,2,1,0:T(8,128)S(1)} collective-permute-done((f32[5,1,64,128]{3,2,1,0:T(8,128)S(1)}, f32[5,1,64,128]{3,2,1,0:T(8,128)S(1)}, u32[]{:S(2)}, u32[]{:S(2)}) %collective-permute-start.19) | collective-permute-done | bytes 163872 | tf_op jit(solution)/shard_map/ppermute | solution.py:163
  139.2 0.7 collective-permute-start.22
  139.9 1.9 %collective-permute-start.24 = (f32[5,1,64,128]{3,2,1,0:T(8,128)S(1)}, f32[5,1,64,128]{3,2,1,0:T(8,128)S(1)}, u32[]{:S(2)}, u32[]{:S(2)}) collective-permute-start(f32[5,1,64,128]{3,2,1,0:T(8,128)S(1)} %get-tuple-element.5), channel_id=1, source_target_pairs={{0,1},{1,2},{2,3},{3,4},{4,5},{5,6},{6,7},{7,8},{8,9},{9,10},{10,1... | collective-permute-start | bytes 491528 | tf_op jit(solution)/shard_map/ppermute | solution.py:160
  141.9 20.7 %collective-permute-done.24 = f32[5,1,64,128]{3,2,1,0:T(8,128)S(1)} collective-permute-done((f32[5,1,64,128]{3,2,1,0:T(8,128)S(1)}, f32[5,1,64,128]{3,2,1,0:T(8,128)S(1)}, u32[]{:S(2)}, u32[]{:S(2)}) %collective-permute-start.24) | collective-permute-done | bytes 163872 | tf_op jit(solution)/shard_map/ppermute | solution.py:160
  163.3 0.7 slice_select_fusion.23
  (91 shorter events, 4.3 us)
Async XLA Ops:
  0.0 20.9 %copy-start = (f32[5,1,64,128]{3,2,1,0:T(8,128)S(1)}, f32[5,1,64,128]{3,2,1,0:T(8,128)}, u32[]{:S(2)}) copy-start(f32[5,1,64,128]{3,2,1,0:T(8,128)} %param.2) | copy-start | bytes 491524
  0.8 6.8 %collective-permute-start = (f32[5,1,3,128]{3,2,1,0:T(4,128)S(1)}, f32[5,1,3,128]{3,2,1,0:T(4,128)S(1)}, u32[]{:S(2)}, u32[]{:S(2)}) collective-permute-start(f32[5,1,3,128]{3,2,1,0:T(4,128)S(1)} %get-tuple-element.54), channel_id=1, source_target_pairs={{0,1},{1,2},{2,3},{3,4},{4,5},{5,6},{6,7},{7,8},{8,9},{9,10},{10,1... | collective-permute-start | bytes 23048 | tf_op jit(solution)/shard_map/ppermute | solution.py:25
  2.7 5.0 %collective-permute-start.1 = (f32[5,1,3,128]{3,2,1,0:T(4,128)S(1)}, f32[5,1,3,128]{3,2,1,0:T(4,128)S(1)}, u32[]{:S(2)}, u32[]{:S(2)}) collective-permute-start(f32[5,1,3,128]{3,2,1,0:T(4,128)S(1)} %get-tuple-element.55), channel_id=1, source_target_pairs={{0,127},{1,0},{2,1},{3,2},{4,3},{5,4},{6,5},{7,6},{8,7},{9,8},{10,... | collective-permute-start | bytes 23048 | tf_op jit(solution)/shard_map/ppermute | solution.py:25
  9.1 6.5 %collective-permute-start.2 = (f32[1059]{0:T(1024)S(1)}, f32[1059]{0:T(1024)S(1)}, u32[]{:S(2)}, u32[]{:S(2)}) collective-permute-start(f32[1059]{0:T(1024)S(1)} %pad_maximum_fusion.1), channel_id=1, source_target_pairs={{0,128},{128,256},{256,384},{384,512},{512,640},{640,768},{768,896... | collective-permute-start | bytes 12716 | tf_op jit(solution)/shard_map/ppermute | solution.py:25
  13.6 7.1 %collective-permute-start.3 = (f32[1059]{0:T(1024)S(1)}, f32[1059]{0:T(1024)S(1)}, u32[]{:S(2)}, u32[]{:S(2)}) collective-permute-start(f32[1059]{0:T(1024)S(1)} %pad_maximum_fusion.2), channel_id=1, source_target_pairs={{128,0},{256,128},{384,256},{512,384},{640,512},{768,640},{896,768... | collective-permute-start | bytes 12716 | tf_op jit(solution)/shard_map/ppermute | solution.py:25
  22.1 14.2 %copy-start.1 = (s32[3,128]{1,0:T(4,128)S(1)}, s32[3,128]{1,0:T(4,128)}, u32[]{:S(2)}) copy-start(s32[3,128]{1,0:T(4,128)} %param.3) | copy-start | bytes 4612
  22.7 13.7 %collective-permute-start.4 = (f32[5,1,64,132]{3,2,1,0:T(8,128)S(1)}, f32[5,1,64,132]{3,2,1,0:T(8,128)S(1)}, u32[]{:S(2)}, u32[]{:S(2)}) collective-permute-start(f32[5,1,64,132]{3,2,1,0:T(8,128)S(1)} %slice.635), channel_id=1, source_target_pairs={{15,1},{14,3},{13,4},{31,17},{30,19},{29,20},{47,33},{46,35},{45,3... | collective-permute-start | bytes 506888 | tf_op jit(solution)/shard_map/ppermute | solution.py:162
  23.4 15.0 %collective-permute-start.10 = (f32[5,1,64,132]{3,2,1,0:T(8,128)S(1)}, f32[5,1,64,132]{3,2,1,0:T(8,128)S(1)}, u32[]{:S(2)}, u32[]{:S(2)}) collective-permute-start(f32[5,1,64,132]{3,2,1,0:T(8,128)S(1)} %slice.635), channel_id=1, source_target_pairs={{0,1},{1,2},{2,3},{3,4},{4,5},{5,6},{6,7},{7,8},{8,9},{9,10},{10,1... | collective-permute-start | bytes 506888 | tf_op jit(solution)/shard_map/ppermute | solution.py:160
  25.8 15.6 %collective-permute-start.6 = (f32[5,1,64,132]{3,2,1,0:T(8,128)S(1)}, f32[5,1,64,132]{3,2,1,0:T(8,128)S(1)}, u32[]{:S(2)}, u32[]{:S(2)}) collective-permute-start(f32[5,1,64,132]{3,2,1,0:T(8,128)S(1)} %slice.635), channel_id=1, source_target_pairs={{0,3},{1,4},{2,5},{3,6},{4,7},{5,8},{6,9},{7,10},{8,11},{9,12},{10... | collective-permute-start | bytes 506888 | tf_op jit(solution)/shard_map/ppermute | solution.py:160
  30.6 38.9 %collective-permute-start.9 = (f32[5,1,64,132]{3,2,1,0:T(8,128)S(1)}, f32[5,1,64,132]{3,2,1,0:T(8,128)S(1)}, u32[]{:S(2)}, u32[]{:S(2)}) collective-permute-start(f32[5,1,64,132]{3,2,1,0:T(8,128)S(1)} %slice.635), channel_id=1, source_target_pairs={{0,2},{1,3},{2,4},{3,5},{4,6},{5,7},{6,8},{7,9},{8,10},{9,11},{10,... | collective-permute-start | bytes 506888 | tf_op jit(solution)/shard_map/ppermute | solution.py:160
  36.4 32.2 %collective-permute-start.5 = (f32[5,1,64,132]{3,2,1,0:T(8,128)S(1)}, f32[5,1,64,132]{3,2,1,0:T(8,128)S(1)}, u32[]{:S(2)}, u32[]{:S(2)}) collective-permute-start(f32[5,1,64,132]{3,2,1,0:T(8,128)S(1)} %collective-permute-done.4), channel_id=1, source_target_pairs={{1,18},{3,17},{4,16},{17,34},{19,33},{20,32},{33,50},{35,49},{36,4... | collective-permute-start | bytes 506888 | tf_op jit(solution)/shard_map/ppermute | solution.py:163
  37.7 30.9 %collective-permute-start.7 = (f32[5,1,64,132]{3,2,1,0:T(8,128)S(1)}, f32[5,1,64,132]{3,2,1,0:T(8,128)S(1)}, u32[]{:S(2)}, u32[]{:S(2)}) collective-permute-start(f32[5,1,64,132]{3,2,1,0:T(8,128)S(1)} %collective-permute-done.4), channel_id=1, source_target_pairs={{1,16},{17,32},{33,48},{49,64},{65,80},{81,96},{97,112},{113,0},{1... | collective-permute-start | bytes 506888 | tf_op jit(solution)/shard_map/ppermute | solution.py:169
  68.7 0.7 collective-permute-start.8
  72.8 4.0 %collective-permute-start.11 = (f32[5,1,64,130]{3,2,1,0:T(8,128)S(1)}, f32[5,1,64,130]{3,2,1,0:T(8,128)S(1)}, u32[]{:S(2)}, u32[]{:S(2)}) collective-permute-start(f32[5,1,64,130]{3,2,1,0:T(8,128)S(1)} %slice.677), channel_id=1, source_target_pairs={{15,1},{14,3},{13,4},{31,17},{30,19},{29,20},{47,33},{46,35},{45,3... | collective-permute-start | bytes 499208 | tf_op jit(solution)/shard_map/ppermute | solution.py:162
  73.5 7.4 %collective-permute-start.13 = (f32[5,1,64,130]{3,2,1,0:T(8,128)S(1)}, f32[5,1,64,130]{3,2,1,0:T(8,128)S(1)}, u32[]{:S(2)}, u32[]{:S(2)}) collective-permute-start(f32[5,1,64,130]{3,2,1,0:T(8,128)S(1)} %slice.677), channel_id=1, source_target_pairs={{0,3},{1,4},{2,5},{3,6},{4,7},{5,8},{6,9},{7,10},{8,11},{9,12},{10... | collective-permute-start | bytes 499208 | tf_op jit(solution)/shard_map/ppermute | solution.py:160
  74.9 28.1 %collective-permute-start.17 = (f32[5,1,64,130]{3,2,1,0:T(8,128)S(1)}, f32[5,1,64,130]{3,2,1,0:T(8,128)S(1)}, u32[]{:S(2)}, u32[]{:S(2)}) collective-permute-start(f32[5,1,64,130]{3,2,1,0:T(8,128)S(1)} %slice.677), channel_id=1, source_target_pairs={{0,1},{1,2},{2,3},{3,4},{4,5},{5,6},{6,7},{7,8},{8,9},{9,10},{10,1... | collective-permute-start | bytes 499208 | tf_op jit(solution)/shard_map/ppermute | solution.py:160
  76.8 27.3 %collective-permute-start.12 = (f32[5,1,64,130]{3,2,1,0:T(8,128)S(1)}, f32[5,1,64,130]{3,2,1,0:T(8,128)S(1)}, u32[]{:S(2)}, u32[]{:S(2)}) collective-permute-start(f32[5,1,64,130]{3,2,1,0:T(8,128)S(1)} %collective-permute-done.11), channel_id=1, source_target_pairs={{1,18},{3,17},{4,16},{17,34},{19,33},{20,32},{33,50},{35,49},{36,4... | collective-permute-start | bytes 499208 | tf_op jit(solution)/shard_map/ppermute | solution.py:163
  78.1 26.0 %collective-permute-start.14 = (f32[5,1,64,130]{3,2,1,0:T(8,128)S(1)}, f32[5,1,64,130]{3,2,1,0:T(8,128)S(1)}, u32[]{:S(2)}, u32[]{:S(2)}) collective-permute-start(f32[5,1,64,130]{3,2,1,0:T(8,128)S(1)} %collective-permute-done.11), channel_id=1, source_target_pairs={{1,16},{17,32},{33,48},{49,64},{65,80},{81,96},{97,112},{113,0},{1... | collective-permute-start | bytes 499208 | tf_op jit(solution)/shard_map/ppermute | solution.py:169
  78.8 26.1 %collective-permute-start.16 = (f32[5,1,64,130]{3,2,1,0:T(8,128)S(1)}, f32[5,1,64,130]{3,2,1,0:T(8,128)S(1)}, u32[]{:S(2)}, u32[]{:S(2)}) collective-permute-start(f32[5,1,64,130]{3,2,1,0:T(8,128)S(1)} %slice.677), channel_id=1, source_target_pairs={{0,2},{1,3},{2,4},{3,5},{4,6},{5,7},{6,8},{7,9},{8,10},{9,11},{10,... | collective-permute-start | bytes 499208 | tf_op jit(solution)/shard_map/ppermute | solution.py:160
  104.2 0.7 collective-permute-start.15
  107.8 2.0 %collective-permute-start.18 = (f32[5,1,64,128]{3,2,1,0:T(8,128)S(1)}, f32[5,1,64,128]{3,2,1,0:T(8,128)S(1)}, u32[]{:S(2)}, u32[]{:S(2)}) collective-permute-start(f32[5,1,64,128]{3,2,1,0:T(8,128)S(1)} %get-tuple-element.5), channel_id=1, source_target_pairs={{15,1},{14,3},{13,4},{31,17},{30,19},{29,20},{47,33},{46,35},{45,3... | collective-permute-start | bytes 491528 | tf_op jit(solution)/shard_map/ppermute | solution.py:162
  108.5 5.2 %collective-permute-start.20 = (f32[5,1,64,128]{3,2,1,0:T(8,128)S(1)}, f32[5,1,64,128]{3,2,1,0:T(8,128)S(1)}, u32[]{:S(2)}, u32[]{:S(2)}) collective-permute-start(f32[5,1,64,128]{3,2,1,0:T(8,128)S(1)} %get-tuple-element.5), channel_id=1, source_target_pairs={{0,3},{1,4},{2,5},{3,6},{4,7},{5,8},{6,9},{7,10},{8,11},{9,12},{10... | collective-permute-start | bytes 491528 | tf_op jit(solution)/shard_map/ppermute | solution.py:160
  109.8 29.4 %collective-permute-start.19 = (f32[5,1,64,128]{3,2,1,0:T(8,128)S(1)}, f32[5,1,64,128]{3,2,1,0:T(8,128)S(1)}, u32[]{:S(2)}, u32[]{:S(2)}) collective-permute-start(f32[5,1,64,128]{3,2,1,0:T(8,128)S(1)} %collective-permute-done.18), channel_id=1, source_target_pairs={{1,18},{3,17},{4,16},{17,34},{19,33},{20,32},{33,50},{35,49},{36,4... | collective-permute-start | bytes 491528 | tf_op jit(solution)/shard_map/ppermute | solution.py:163
  111.1 28.1 %collective-permute-start.21 = (f32[5,1,64,128]{3,2,1,0:T(8,128)S(1)}, f32[5,1,64,128]{3,2,1,0:T(8,128)S(1)}, u32[]{:S(2)}, u32[]{:S(2)}) collective-permute-start(f32[5,1,64,128]{3,2,1,0:T(8,128)S(1)} %collective-permute-done.18), channel_id=1, source_target_pairs={{1,16},{17,32},{33,48},{49,64},{65,80},{81,96},{97,112},{113,0},{1... | collective-permute-start | bytes 491528 | tf_op jit(solution)/shard_map/ppermute | solution.py:169
  111.8 30.1 %collective-permute-start.23 = (f32[5,1,64,128]{3,2,1,0:T(8,128)S(1)}, f32[5,1,64,128]{3,2,1,0:T(8,128)S(1)}, u32[]{:S(2)}, u32[]{:S(2)}) collective-permute-start(f32[5,1,64,128]{3,2,1,0:T(8,128)S(1)} %get-tuple-element.5), channel_id=1, source_target_pairs={{0,2},{1,3},{2,4},{3,5},{4,6},{5,7},{6,8},{7,9},{8,10},{9,11},{10,... | collective-permute-start | bytes 491528 | tf_op jit(solution)/shard_map/ppermute | solution.py:160
  139.2 2.7 %collective-permute-start.22 = (f32[5,1,64,128]{3,2,1,0:T(8,128)S(1)}, f32[5,1,64,128]{3,2,1,0:T(8,128)S(1)}, u32[]{:S(2)}, u32[]{:S(2)}) collective-permute-start(f32[5,1,64,128]{3,2,1,0:T(8,128)S(1)} %get-tuple-element.52), channel_id=1, source_target_pairs={{0,1},{1,0},{16,17},{17,16},{32,33},{33,32},{48,49},{49,48},{64,65... | collective-permute-start | bytes 491528 | tf_op jit(solution)/shard_map/ppermute | solution.py:174
  139.9 22.6 %collective-permute-start.24 = (f32[5,1,64,128]{3,2,1,0:T(8,128)S(1)}, f32[5,1,64,128]{3,2,1,0:T(8,128)S(1)}, u32[]{:S(2)}, u32[]{:S(2)}) collective-permute-start(f32[5,1,64,128]{3,2,1,0:T(8,128)S(1)} %get-tuple-element.5), channel_id=1, source_target_pairs={{0,1},{1,2},{2,3},{3,4},{4,5},{5,6},{6,7},{7,8},{8,9},{9,10},{10,1... | collective-permute-start | bytes 491528 | tf_op jit(solution)/shard_map/ppermute | solution.py:160

commit v14 on v12

--- a/solution.py
+++ b/solution.py
@@ -125,7 +125,7 @@
 def relay_seat(lane, source, plane, blocks):
     if source // 2 == lane:
         return source
-    if 2 * lane + 1 < plane - blocks and 2 * lane < blocks:
+    if 2 < 2 * lane + 1 < plane - blocks and 2 * lane < blocks:
         return 2 * lane + 1
     return 2 * lane
 

time: 165 us -> 180 us (1.091)
  the two profiles are of different devices: /device:TPU:6 before, /device:TPU:134 now
where the time goes in v14:
time: 180 us
  starting transfers between devices  86.6 us (48%)
  waiting for transfers between devices  78.5 us (44%)
  other arithmetic  10.1 us (6%)
  local copies, waits for them, and re-layouts  3.57 us (2%)
    ppermute x3, waiting for transfers between devices, rotation_pieces(): first_seat = lax.ppermute(relayed, ('rad', 'azi'), direct)  36.4 us
    ppermute x3, starting transfers between devices, rotation_pieces(): crossed = lax.ppermute(relayed, ('rad', 'azi'), second)  35.3 us
    ppermute x4, starting transfers between devices, passed_along(): return lax.ppermute(value, axis, pairs)  27.9 us
    ppermute x3, waiting for transfers between devices, rotation_pieces(): relayed = lax.ppermute(head, ('rad', 'azi'), first)  18.7 us
    ppermute x3, waiting for transfers between devices, rotation_pieces(): crossed = lax.ppermute(relayed, ('rad', 'azi'), second)  18.4 us
    ppermute x9, starting transfers between devices, rotation_pieces(): near.append(lax.ppermute(head, 'azi', pairs))  11.8 us
    ppermute x3, starting transfers between devices, rotation_pieces(): first_seat = lax.ppermute(relayed, ('rad', 'azi'), direct)  3.88 us
    ppermute x3, starting transfers between devices, rotation_pieces(): relayed = lax.ppermute(head, ('rad', 'azi'), first)  3.88 us
  transfers between devices with their start and end apart: 25, of which 11 were waited for; matrix products, arithmetic and copies ran while one was open for 1% of the time, Pallas kernels for 0%

profile of v14, /device:TPU:134, one launch (start us, length us, event | category | flops | bytes accessed | tf_op | source)
XLA Modules:
  0.0 179.7 jit_solution(3317872253712722597)
XLA Ops:
  0.0 0.8 fusion.103
  0.8 1.9 %collective-permute-start = (f32[5,1,3,128]{3,2,1,0:T(4,128)S(1)}, f32[5,1,3,128]{3,2,1,0:T(4,128)S(1)}, u32[]{:S(2)}, u32[]{:S(2)}) collective-permute-start(f32[5,1,3,128]{3,2,1,0:T(4,128)S(1)} %get-tuple-element.46), channel_id=1, source_target_pairs={{0,1},{1,2},{2,3},{3,4},{4,5},{5,6},{6,7},{7,8},{8,9},{9,10},{10,1... | collective-permute-start | bytes 23048 | tf_op jit(solution)/shard_map/ppermute | solution.py:25
  2.7 20.2 %collective-permute-start.1 = (f32[5,1,3,128]{3,2,1,0:T(4,128)S(1)}, f32[5,1,3,128]{3,2,1,0:T(4,128)S(1)}, u32[]{:S(2)}, u32[]{:S(2)}) collective-permute-start(f32[5,1,3,128]{3,2,1,0:T(4,128)S(1)} %get-tuple-element.47), channel_id=1, source_target_pairs={{0,127},{1,0},{2,1},{3,2},{4,3},{5,4},{6,5},{7,6},{8,7},{9,8},{10,... | collective-permute-start | bytes 23048 | tf_op jit(solution)/shard_map/ppermute | solution.py:25
  22.9 0.8 slice_convert_fusion.1
  24.3 0.9 pad_maximum_fusion
  25.3 0.2 reshape.1273
  25.6 3.4 %collective-permute-start.2 = (f32[1059]{0:T(1024)S(1)}, f32[1059]{0:T(1024)S(1)}, u32[]{:S(2)}, u32[]{:S(2)}) collective-permute-start(f32[1059]{0:T(1024)S(1)} %pad_maximum_fusion.1), channel_id=1, source_target_pairs={{0,128},{128,256},{256,384},{384,512},{512,640},{640,768},{768,896... | collective-permute-start | bytes 12716 | tf_op jit(solution)/shard_map/ppermute | solution.py:25
  29.0 0.2 reshape.1275
  29.3 2.5 %collective-permute-start.3 = (f32[1059]{0:T(1024)S(1)}, f32[1059]{0:T(1024)S(1)}, u32[]{:S(2)}, u32[]{:S(2)}) collective-permute-start(f32[1059]{0:T(1024)S(1)} %pad_maximum_fusion.2), channel_id=1, source_target_pairs={{128,0},{256,128},{384,256},{512,384},{640,512},{768,640},{896,768... | collective-permute-start | bytes 12716 | tf_op jit(solution)/shard_map/ppermute | solution.py:25
  31.8 0.2 concatenate.40
  32.0 2.8 %collective-permute-done.3 = f32[1059]{0:T(1024)S(1)} collective-permute-done((f32[1059]{0:T(1024)S(1)}, f32[1059]{0:T(1024)S(1)}, u32[]{:S(2)}, u32[]{:S(2)}) %collective-permute-start.3) | collective-permute-done | bytes 4268 | tf_op jit(solution)/shard_map/ppermute | solution.py:25
  34.8 0.2 concatenate.41
  35.0 0.2 maximum_select_fusion
  35.4 0.2 subtract_multiply_fusion.3
  35.6 0.6 subtract_add_fusion.1
  36.3 0.1 fusion.4
  36.4 0.1 fusion.29
  36.8 1.3 collective-permute-start.4
  38.1 1.3 collective-permute-start.10
  39.4 1.3 collective-permute-start.8
  40.7 1.3 collective-permute-start.6
  42.5 4.7 %collective-permute-done.4 = f32[5,1,64,132]{3,2,1,0:T(8,128)S(1)} collective-permute-done((f32[5,1,64,132]{3,2,1,0:T(8,128)S(1)}, f32[5,1,64,132]{3,2,1,0:T(8,128)S(1)}, u32[]{:S(2)}, u32[]{:S(2)}) %collective-permute-start.4) | collective-permute-done | bytes 168992 | tf_op jit(solution)/shard_map/ppermute | solution.py:162
  47.3 11.8 %collective-permute-start.5 = (f32[5,1,64,132]{3,2,1,0:T(8,128)S(1)}, f32[5,1,64,132]{3,2,1,0:T(8,128)S(1)}, u32[]{:S(2)}, u32[]{:S(2)}) collective-permute-start(f32[5,1,64,132]{3,2,1,0:T(8,128)S(1)} %collective-permute-done.4), channel_id=1, source_target_pairs={{0,18},{3,17},{4,16},{16,34},{19,33},{20,32},{32,50},{35,49},{36,4... | collective-permute-start | bytes 506888 | tf_op jit(solution)/shard_map/ppermute | solution.py:163
  59.2 1.3 collective-permute-start.9
  60.5 6.7 %collective-permute-done.5 = f32[5,1,64,132]{3,2,1,0:T(8,128)S(1)} collective-permute-done((f32[5,1,64,132]{3,2,1,0:T(8,128)S(1)}, f32[5,1,64,132]{3,2,1,0:T(8,128)S(1)}, u32[]{:S(2)}, u32[]{:S(2)}) %collective-permute-start.5) | collective-permute-done | bytes 168992 | tf_op jit(solution)/shard_map/ppermute | solution.py:163
  67.1 1.3 collective-permute-start.7
  68.5 14.0 %collective-permute-done.9 = f32[5,1,64,132]{3,2,1,0:T(8,128)S(1)} collective-permute-done((f32[5,1,64,132]{3,2,1,0:T(8,128)S(1)}, f32[5,1,64,132]{3,2,1,0:T(8,128)S(1)}, u32[]{:S(2)}, u32[]{:S(2)}) %collective-permute-start.9) | collective-permute-done | bytes 168992 | tf_op jit(solution)/shard_map/ppermute | solution.py:169
  82.7 0.7 concatenate.43
  83.4 0.2 slice_select_fusion
  83.5 0.2 slice_select_fusion.5
  83.7 0.2 slice_select_fusion.4
  83.9 0.1 slice_select_fusion.7
  84.5 0.2 subtract_multiply_fusion.1
  84.7 0.6 subtract_add_fusion
  85.4 0.1 fusion.7
  85.5 0.1 fusion.14
  85.9 1.3 collective-permute-start.11
  87.2 1.3 collective-permute-start.13
  88.6 7.9 %collective-permute-done.11 = f32[5,1,64,130]{3,2,1,0:T(8,128)S(1)} collective-permute-done((f32[5,1,64,130]{3,2,1,0:T(8,128)S(1)}, f32[5,1,64,130]{3,2,1,0:T(8,128)S(1)}, u32[]{:S(2)}, u32[]{:S(2)}) %collective-permute-start.11) | collective-permute-done | bytes 166432 | tf_op jit(solution)/shard_map/ppermute | solution.py:162
  96.4 2.9 %collective-permute-start.12 = (f32[5,1,64,130]{3,2,1,0:T(8,128)S(1)}, f32[5,1,64,130]{3,2,1,0:T(8,128)S(1)}, u32[]{:S(2)}, u32[]{:S(2)}) collective-permute-start(f32[5,1,64,130]{3,2,1,0:T(8,128)S(1)} %collective-permute-done.11), channel_id=1, source_target_pairs={{0,18},{3,17},{4,16},{16,34},{19,33},{20,32},{32,50},{35,49},{36,4... | collective-permute-start | bytes 499208 | tf_op jit(solution)/shard_map/ppermute | solution.py:163
  99.4 1.3 collective-permute-start.17
  100.7 1.3 collective-permute-start.15
  102.0 1.3 collective-permute-start.16
  103.3 11.8 %collective-permute-done.12 = f32[5,1,64,130]{3,2,1,0:T(8,128)S(1)} collective-permute-done((f32[5,1,64,130]{3,2,1,0:T(8,128)S(1)}, f32[5,1,64,130]{3,2,1,0:T(8,128)S(1)}, u32[]{:S(2)}, u32[]{:S(2)}) %collective-permute-start.12) | collective-permute-done | bytes 166432 | tf_op jit(solution)/shard_map/ppermute | solution.py:163
  115.1 1.3 collective-permute-start.14
  116.5 7.1 %collective-permute-done.16 = f32[5,1,64,130]{3,2,1,0:T(8,128)S(1)} collective-permute-done((f32[5,1,64,130]{3,2,1,0:T(8,128)S(1)}, f32[5,1,64,130]{3,2,1,0:T(8,128)S(1)}, u32[]{:S(2)}, u32[]{:S(2)}) %collective-permute-start.16) | collective-permute-done | bytes 166432 | tf_op jit(solution)/shard_map/ppermute | solution.py:169
  123.8 0.7 concatenate.44
  124.5 0.2 slice_select_fusion.3
  124.6 0.2 slice_select_fusion.2
  124.8 0.2 slice_select_fusion.1
  125.0 0.1 slice_select_fusion.6
  125.6 0.1 subtract_multiply_fusion.5
  125.7 0.3 subtract_add_fusion.2
  126.5 1.3 collective-permute-start.18
  127.8 1.3 collective-permute-start.20
  129.1 6.1 %collective-permute-done.18 = f32[5,1,64,128]{3,2,1,0:T(8,128)S(1)} collective-permute-done((f32[5,1,64,128]{3,2,1,0:T(8,128)S(1)}, f32[5,1,64,128]{3,2,1,0:T(8,128)S(1)}, u32[]{:S(2)}, u32[]{:S(2)}) %collective-permute-start.18) | collective-permute-done | bytes 163872 | tf_op jit(solution)/shard_map/ppermute | solution.py:162
  135.2 20.6 %collective-permute-start.19 = (f32[5,1,64,128]{3,2,1,0:T(8,128)S(1)}, f32[5,1,64,128]{3,2,1,0:T(8,128)S(1)}, u32[]{:S(2)}, u32[]{:S(2)}) collective-permute-start(f32[5,1,64,128]{3,2,1,0:T(8,128)S(1)} %collective-permute-done.18), channel_id=1, source_target_pairs={{0,18},{3,17},{4,16},{16,34},{19,33},{20,32},{32,50},{35,49},{36,4... | collective-permute-start | bytes 491528 | tf_op jit(solution)/shard_map/ppermute | solution.py:163
  155.9 1.3 collective-permute-start.22
  157.2 1.3 collective-permute-start.24
  158.5 1.3 collective-permute-start.23
  159.8 1.3 collective-permute-start.21
  161.1 1.9 %collective-permute-done.21 = f32[5,1,64,128]{3,2,1,0:T(8,128)S(1)} collective-permute-done((f32[5,1,64,128]{3,2,1,0:T(8,128)S(1)}, f32[5,1,64,128]{3,2,1,0:T(8,128)S(1)}, u32[]{:S(2)}, u32[]{:S(2)}) %collective-permute-start.21) | collective-permute-done | bytes 163872 | tf_op jit(solution)/shard_map/ppermute | solution.py:184
  163.1 15.2 %collective-permute-done.23 = f32[5,1,64,128]{3,2,1,0:T(8,128)S(1)} collective-permute-done((f32[5,1,64,128]{3,2,1,0:T(8,128)S(1)}, f32[5,1,64,128]{3,2,1,0:T(8,128)S(1)}, u32[]{:S(2)}, u32[]{:S(2)}) %collective-permute-start.23) | collective-permute-done | bytes 163872 | tf_op jit(solution)/shard_map/ppermute | solution.py:169
  179.0 0.7 slice_select_fusion.23
  (93 shorter events, 4.5 us)
Async XLA Ops:
  0.0 35.0 %copy-start = (f32[5,1,64,128]{3,2,1,0:T(8,128)S(1)}, f32[5,1,64,128]{3,2,1,0:T(8,128)}, u32[]{:S(2)}) copy-start(f32[5,1,64,128]{3,2,1,0:T(8,128)} %param.2) | copy-start | bytes 491524
  0.8 23.4 %collective-permute-start = (f32[5,1,3,128]{3,2,1,0:T(4,128)S(1)}, f32[5,1,3,128]{3,2,1,0:T(4,128)S(1)}, u32[]{:S(2)}, u32[]{:S(2)}) collective-permute-start(f32[5,1,3,128]{3,2,1,0:T(4,128)S(1)} %get-tuple-element.46), channel_id=1, source_target_pairs={{0,1},{1,2},{2,3},{3,4},{4,5},{5,6},{6,7},{7,8},{8,9},{9,10},{10,1... | collective-permute-start | bytes 23048 | tf_op jit(solution)/shard_map/ppermute | solution.py:25
  2.7 21.5 %collective-permute-start.1 = (f32[5,1,3,128]{3,2,1,0:T(4,128)S(1)}, f32[5,1,3,128]{3,2,1,0:T(4,128)S(1)}, u32[]{:S(2)}, u32[]{:S(2)}) collective-permute-start(f32[5,1,3,128]{3,2,1,0:T(4,128)S(1)} %get-tuple-element.47), channel_id=1, source_target_pairs={{0,127},{1,0},{2,1},{3,2},{4,3},{5,4},{6,5},{7,6},{8,7},{9,8},{10,... | collective-permute-start | bytes 23048 | tf_op jit(solution)/shard_map/ppermute | solution.py:25
  25.6 6.2 %collective-permute-start.2 = (f32[1059]{0:T(1024)S(1)}, f32[1059]{0:T(1024)S(1)}, u32[]{:S(2)}, u32[]{:S(2)}) collective-permute-start(f32[1059]{0:T(1024)S(1)} %pad_maximum_fusion.1), channel_id=1, source_target_pairs={{0,128},{128,256},{256,384},{384,512},{512,640},{640,768},{768,896... | collective-permute-start | bytes 12716 | tf_op jit(solution)/shard_map/ppermute | solution.py:25
  29.3 5.5 %collective-permute-start.3 = (f32[1059]{0:T(1024)S(1)}, f32[1059]{0:T(1024)S(1)}, u32[]{:S(2)}, u32[]{:S(2)}) collective-permute-start(f32[1059]{0:T(1024)S(1)} %pad_maximum_fusion.2), channel_id=1, source_target_pairs={{128,0},{256,128},{384,256},{512,384},{640,512},{768,640},{896,768... | collective-permute-start | bytes 12716 | tf_op jit(solution)/shard_map/ppermute | solution.py:25
  36.1 6.2 %copy-start.1 = (s32[3,128]{1,0:T(4,128)S(1)}, s32[3,128]{1,0:T(4,128)}, u32[]{:S(2)}) copy-start(s32[3,128]{1,0:T(4,128)} %param.3) | copy-start | bytes 4612
  36.8 10.5 %collective-permute-start.4 = (f32[5,1,64,132]{3,2,1,0:T(8,128)S(1)}, f32[5,1,64,132]{3,2,1,0:T(8,128)S(1)}, u32[]{:S(2)}, u32[]{:S(2)}) collective-permute-start(f32[5,1,64,132]{3,2,1,0:T(8,128)S(1)} %slice.635), channel_id=1, source_target_pairs={{15,0},{14,3},{13,4},{31,16},{30,19},{29,20},{47,32},{46,35},{45,3... | collective-permute-start | bytes 506888 | tf_op jit(solution)/shard_map/ppermute | solution.py:162
  38.1 30.4 %collective-permute-start.10 = (f32[5,1,64,132]{3,2,1,0:T(8,128)S(1)}, f32[5,1,64,132]{3,2,1,0:T(8,128)S(1)}, u32[]{:S(2)}, u32[]{:S(2)}) collective-permute-start(f32[5,1,64,132]{3,2,1,0:T(8,128)S(1)} %slice.635), channel_id=1, source_target_pairs={{0,1},{1,2},{2,3},{3,4},{4,5},{5,6},{6,7},{7,8},{8,9},{9,10},{10,1... | collective-permute-start | bytes 506888 | tf_op jit(solution)/shard_map/ppermute | solution.py:160
  39.4 43.2 %collective-permute-start.8 = (f32[5,1,64,132]{3,2,1,0:T(8,128)S(1)}, f32[5,1,64,132]{3,2,1,0:T(8,128)S(1)}, u32[]{:S(2)}, u32[]{:S(2)}) collective-permute-start(f32[5,1,64,132]{3,2,1,0:T(8,128)S(1)} %slice.635), channel_id=1, source_target_pairs={{0,2},{1,3},{2,4},{3,5},{4,6},{5,7},{6,8},{7,9},{8,10},{9,11},{10,... | collective-permute-start | bytes 506888 | tf_op jit(solution)/shard_map/ppermute | solution.py:160
  40.7 27.7 %collective-permute-start.6 = (f32[5,1,64,132]{3,2,1,0:T(8,128)S(1)}, f32[5,1,64,132]{3,2,1,0:T(8,128)S(1)}, u32[]{:S(2)}, u32[]{:S(2)}) collective-permute-start(f32[5,1,64,132]{3,2,1,0:T(8,128)S(1)} %slice.635), channel_id=1, source_target_pairs={{0,3},{1,4},{2,5},{3,6},{4,7},{5,8},{6,9},{7,10},{8,11},{9,12},{10... | collective-permute-start | bytes 506888 | tf_op jit(solution)/shard_map/ppermute | solution.py:160
  47.3 19.8 %collective-permute-start.5 = (f32[5,1,64,132]{3,2,1,0:T(8,128)S(1)}, f32[5,1,64,132]{3,2,1,0:T(8,128)S(1)}, u32[]{:S(2)}, u32[]{:S(2)}) collective-permute-start(f32[5,1,64,132]{3,2,1,0:T(8,128)S(1)} %collective-permute-done.4), channel_id=1, source_target_pairs={{0,18},{3,17},{4,16},{16,34},{19,33},{20,32},{32,50},{35,49},{36,4... | collective-permute-start | bytes 506888 | tf_op jit(solution)/shard_map/ppermute | solution.py:163
  59.2 23.4 %collective-permute-start.9 = (f32[5,1,64,132]{3,2,1,0:T(8,128)S(1)}, f32[5,1,64,132]{3,2,1,0:T(8,128)S(1)}, u32[]{:S(2)}, u32[]{:S(2)}) collective-permute-start(f32[5,1,64,132]{3,2,1,0:T(8,128)S(1)} %collective-permute-done.4), channel_id=1, source_target_pairs={{0,16},{16,32},{32,48},{48,64},{64,80},{80,96},{96,112},{112,0},{1... | collective-permute-start | bytes 506888 | tf_op jit(solution)/shard_map/ppermute | solution.py:169
  67.1 15.5 %collective-permute-start.7 = (f32[5,1,64,132]{3,2,1,0:T(8,128)S(1)}, f32[5,1,64,132]{3,2,1,0:T(8,128)S(1)}, u32[]{:S(2)}, u32[]{:S(2)}) collective-permute-start(f32[5,1,64,132]{3,2,1,0:T(8,128)S(1)} %collective-permute-done.5), channel_id=1, source_target_pairs={{1,0},{2,1},{17,16},{18,17},{33,32},{34,33},{49,48},{50,49},{65,64... | collective-permute-start | bytes 506888 | tf_op jit(solution)/shard_map/ppermute | solution.py:184
  85.9 10.5 %collective-permute-start.11 = (f32[5,1,64,130]{3,2,1,0:T(8,128)S(1)}, f32[5,1,64,130]{3,2,1,0:T(8,128)S(1)}, u32[]{:S(2)}, u32[]{:S(2)}) collective-permute-start(f32[5,1,64,130]{3,2,1,0:T(8,128)S(1)} %slice.677), channel_id=1, source_target_pairs={{15,0},{14,3},{13,4},{31,16},{30,19},{29,20},{47,32},{46,35},{45,3... | collective-permute-start | bytes 499208 | tf_op jit(solution)/shard_map/ppermute | solution.py:162
  87.2 29.1 %collective-permute-start.13 = (f32[5,1,64,130]{3,2,1,0:T(8,128)S(1)}, f32[5,1,64,130]{3,2,1,0:T(8,128)S(1)}, u32[]{:S(2)}, u32[]{:S(2)}) collective-permute-start(f32[5,1,64,130]{3,2,1,0:T(8,128)S(1)} %slice.677), channel_id=1, source_target_pairs={{0,3},{1,4},{2,5},{3,6},{4,7},{5,8},{6,9},{7,10},{8,11},{9,12},{10... | collective-permute-start | bytes 499208 | tf_op jit(solution)/shard_map/ppermute | solution.py:160
  96.4 18.7 %collective-permute-start.12 = (f32[5,1,64,130]{3,2,1,0:T(8,128)S(1)}, f32[5,1,64,130]{3,2,1,0:T(8,128)S(1)}, u32[]{:S(2)}, u32[]{:S(2)}) collective-permute-start(f32[5,1,64,130]{3,2,1,0:T(8,128)S(1)} %collective-permute-done.11), channel_id=1, source_target_pairs={{0,18},{3,17},{4,16},{16,34},{19,33},{20,32},{32,50},{35,49},{36,4... | collective-permute-start | bytes 499208 | tf_op jit(solution)/shard_map/ppermute | solution.py:163
  99.4 17.1 %collective-permute-start.17 = (f32[5,1,64,130]{3,2,1,0:T(8,128)S(1)}, f32[5,1,64,130]{3,2,1,0:T(8,128)S(1)}, u32[]{:S(2)}, u32[]{:S(2)}) collective-permute-start(f32[5,1,64,130]{3,2,1,0:T(8,128)S(1)} %slice.677), channel_id=1, source_target_pairs={{0,1},{1,2},{2,3},{3,4},{4,5},{5,6},{6,7},{7,8},{8,9},{9,10},{10,1... | collective-permute-start | bytes 499208 | tf_op jit(solution)/shard_map/ppermute | solution.py:160
  100.7 23.0 %collective-permute-start.15 = (f32[5,1,64,130]{3,2,1,0:T(8,128)S(1)}, f32[5,1,64,130]{3,2,1,0:T(8,128)S(1)}, u32[]{:S(2)}, u32[]{:S(2)}) collective-permute-start(f32[5,1,64,130]{3,2,1,0:T(8,128)S(1)} %slice.677), channel_id=1, source_target_pairs={{0,2},{1,3},{2,4},{3,5},{4,6},{5,7},{6,8},{7,9},{8,10},{9,11},{10,... | collective-permute-start | bytes 499208 | tf_op jit(solution)/shard_map/ppermute | solution.py:160
  102.0 21.6 %collective-permute-start.16 = (f32[5,1,64,130]{3,2,1,0:T(8,128)S(1)}, f32[5,1,64,130]{3,2,1,0:T(8,128)S(1)}, u32[]{:S(2)}, u32[]{:S(2)}) collective-permute-start(f32[5,1,64,130]{3,2,1,0:T(8,128)S(1)} %collective-permute-done.11), channel_id=1, source_target_pairs={{0,16},{16,32},{32,48},{48,64},{64,80},{80,96},{96,112},{112,0},{1... | collective-permute-start | bytes 499208 | tf_op jit(solution)/shard_map/ppermute | solution.py:169
  115.1 8.6 %collective-permute-start.14 = (f32[5,1,64,130]{3,2,1,0:T(8,128)S(1)}, f32[5,1,64,130]{3,2,1,0:T(8,128)S(1)}, u32[]{:S(2)}, u32[]{:S(2)}) collective-permute-start(f32[5,1,64,130]{3,2,1,0:T(8,128)S(1)} %collective-permute-done.12), channel_id=1, source_target_pairs={{1,0},{2,1},{17,16},{18,17},{33,32},{34,33},{49,48},{50,49},{65,64... | collective-permute-start | bytes 499208 | tf_op jit(solution)/shard_map/ppermute | solution.py:184
  126.5 8.7 %collective-permute-start.18 = (f32[5,1,64,128]{3,2,1,0:T(8,128)S(1)}, f32[5,1,64,128]{3,2,1,0:T(8,128)S(1)}, u32[]{:S(2)}, u32[]{:S(2)}) collective-permute-start(f32[5,1,64,128]{3,2,1,0:T(8,128)S(1)} %get-tuple-element.5), channel_id=1, source_target_pairs={{15,0},{14,3},{13,4},{31,16},{30,19},{29,20},{47,32},{46,35},{45,3... | collective-permute-start | bytes 491528 | tf_op jit(solution)/shard_map/ppermute | solution.py:162
  127.8 33.3 %collective-permute-start.20 = (f32[5,1,64,128]{3,2,1,0:T(8,128)S(1)}, f32[5,1,64,128]{3,2,1,0:T(8,128)S(1)}, u32[]{:S(2)}, u32[]{:S(2)}) collective-permute-start(f32[5,1,64,128]{3,2,1,0:T(8,128)S(1)} %get-tuple-element.5), channel_id=1, source_target_pairs={{0,3},{1,4},{2,5},{3,6},{4,7},{5,8},{6,9},{7,10},{8,11},{9,12},{10... | collective-permute-start | bytes 491528 | tf_op jit(solution)/shard_map/ppermute | solution.py:160
  135.2 24.6 %collective-permute-start.19 = (f32[5,1,64,128]{3,2,1,0:T(8,128)S(1)}, f32[5,1,64,128]{3,2,1,0:T(8,128)S(1)}, u32[]{:S(2)}, u32[]{:S(2)}) collective-permute-start(f32[5,1,64,128]{3,2,1,0:T(8,128)S(1)} %collective-permute-done.18), channel_id=1, source_target_pairs={{0,18},{3,17},{4,16},{16,34},{19,33},{20,32},{32,50},{35,49},{36,4... | collective-permute-start | bytes 491528 | tf_op jit(solution)/shard_map/ppermute | solution.py:163
  155.9 5.3 %collective-permute-start.22 = (f32[5,1,64,128]{3,2,1,0:T(8,128)S(1)}, f32[5,1,64,128]{3,2,1,0:T(8,128)S(1)}, u32[]{:S(2)}, u32[]{:S(2)}) collective-permute-start(f32[5,1,64,128]{3,2,1,0:T(8,128)S(1)} %get-tuple-element.5), channel_id=1, source_target_pairs={{0,2},{1,3},{2,4},{3,5},{4,6},{5,7},{6,8},{7,9},{8,10},{9,11},{10,... | collective-permute-start | bytes 491528 | tf_op jit(solution)/shard_map/ppermute | solution.py:160
  157.2 5.9 %collective-permute-start.24 = (f32[5,1,64,128]{3,2,1,0:T(8,128)S(1)}, f32[5,1,64,128]{3,2,1,0:T(8,128)S(1)}, u32[]{:S(2)}, u32[]{:S(2)}) collective-permute-start(f32[5,1,64,128]{3,2,1,0:T(8,128)S(1)} %get-tuple-element.5), channel_id=1, source_target_pairs={{0,1},{1,2},{2,3},{3,4},{4,5},{5,6},{6,7},{7,8},{8,9},{9,10},{10,1... | collective-permute-start | bytes 491528 | tf_op jit(solution)/shard_map/ppermute | solution.py:160
  158.5 19.8 %collective-permute-start.23 = (f32[5,1,64,128]{3,2,1,0:T(8,128)S(1)}, f32[5,1,64,128]{3,2,1,0:T(8,128)S(1)}, u32[]{:S(2)}, u32[]{:S(2)}) collective-permute-start(f32[5,1,64,128]{3,2,1,0:T(8,128)S(1)} %collective-permute-done.18), channel_id=1, source_target_pairs={{0,16},{16,32},{32,48},{48,64},{64,80},{80,96},{96,112},{112,0},{1... | collective-permute-start | bytes 491528 | tf_op jit(solution)/shard_map/ppermute | solution.py:169
  159.8 3.3 %collective-permute-start.21 = (f32[5,1,64,128]{3,2,1,0:T(8,128)S(1)}, f32[5,1,64,128]{3,2,1,0:T(8,128)S(1)}, u32[]{:S(2)}, u32[]{:S(2)}) collective-permute-start(f32[5,1,64,128]{3,2,1,0:T(8,128)S(1)} %collective-permute-done.19), channel_id=1, source_target_pairs={{1,0},{2,1},{17,16},{18,17},{33,32},{34,33},{49,48},{50,49},{65,64... | collective-permute-start | bytes 491528 | tf_op jit(solution)/shard_map/ppermute | solution.py:184

commit v15 on v12

--- a/solution.py
+++ b/solution.py
@@ -168,6 +168,14 @@
     ]
     first_seat = lax.ppermute(relayed, ("rad", "azi"), direct)
     position = lax.axis_index("azi") % plane
+    if blocks == 3:
+        second_block = [(a, b - 1) for a, b in second if (b % plane) == 1]
+        second_seat = lax.ppermute(relayed, ("rad", "azi"), second_block)
+        pairs = [(base + 2, base + 1) for base in range(0, count, plane)]
+        passed = lax.ppermute(crossed, "azi", pairs)
+        middle = jnp.where(position == 0, second_seat, passed)
+        fars = [first_seat, middle, crossed]
+        return [jnp.where(position < k, fars[k - 1], near[k - 1]) for k in (1, 2, 3)]
     pieces = []
     for k in range(1, blocks + 1):
         if k == blocks:

time: 165 us -> 172 us (1.042)
  the two profiles are of different devices: /device:TPU:6 before, /device:TPU:128 now
where the time goes in v15:
time: 172 us; the launch traced here: 171 us
  starting transfers between devices  80.7 us (47%)
  waiting for transfers between devices  75.8 us (44%)
  other arithmetic  10.2 us (6%)
  local copies, waits for them, and re-layouts  3.57 us (2%)
    ppermute x9, starting transfers between devices, rotation_pieces(): near.append(lax.ppermute(head, 'azi', pairs))  35.3 us
    ppermute x3, waiting for transfers between devices, rotation_pieces(): first_seat = lax.ppermute(relayed, ('rad', 'azi'), direct)  33.5 us
    ppermute x4, starting transfers between devices, passed_along(): return lax.ppermute(value, axis, pairs)  29.8 us
    ppermute x3, waiting for transfers between devices, rotation_pieces(): crossed = lax.ppermute(relayed, ('rad', 'azi'), second)  18.5 us
    ppermute x3, waiting for transfers between devices, rotation_pieces(): second_seat = lax.ppermute(relayed, ('rad', 'azi'), second_block)  17.2 us
    ppermute x3, starting transfers between devices, rotation_pieces(): crossed = lax.ppermute(relayed, ('rad', 'azi'), second)  3.88 us
    ppermute x3, starting transfers between devices, rotation_pieces(): first_seat = lax.ppermute(relayed, ('rad', 'azi'), direct)  3.88 us
    ppermute x3, starting transfers between devices, rotation_pieces(): second_seat = lax.ppermute(relayed, ('rad', 'azi'), second_block)  3.86 us
  transfers between devices with their start and end apart: 28, of which 12 were waited for; matrix products, arithmetic and copies ran while one was open for 2% of the time, Pallas kernels for 0%

profile of v15, /device:TPU:128, one launch (start us, length us, event | category | flops | bytes accessed | tf_op | source)
XLA Modules:
  0.0 171.2 jit_solution(13999425741511363397)
XLA Ops:
  0.0 0.8 fusion.103
  0.8 1.9 %collective-permute-start = (f32[5,1,3,128]{3,2,1,0:T(4,128)S(1)}, f32[5,1,3,128]{3,2,1,0:T(4,128)S(1)}, u32[]{:S(2)}, u32[]{:S(2)}) collective-permute-start(f32[5,1,3,128]{3,2,1,0:T(4,128)S(1)} %get-tuple-element.46), channel_id=1, source_target_pairs={{0,1},{1,2},{2,3},{3,4},{4,5},{5,6},{6,7},{7,8},{8,9},{9,10},{10,1... | collective-permute-start | bytes 23048 | tf_op jit(solution)/shard_map/ppermute | solution.py:25
  2.7 22.1 %collective-permute-start.1 = (f32[5,1,3,128]{3,2,1,0:T(4,128)S(1)}, f32[5,1,3,128]{3,2,1,0:T(4,128)S(1)}, u32[]{:S(2)}, u32[]{:S(2)}) collective-permute-start(f32[5,1,3,128]{3,2,1,0:T(4,128)S(1)} %get-tuple-element.47), channel_id=1, source_target_pairs={{0,127},{1,0},{2,1},{3,2},{4,3},{5,4},{6,5},{7,6},{8,7},{9,8},{10,... | collective-permute-start | bytes 23048 | tf_op jit(solution)/shard_map/ppermute | solution.py:25
  24.8 0.8 slice_convert_fusion.1
  26.2 0.9 pad_maximum_fusion
  27.3 0.2 reshape.1273
  27.5 3.4 %collective-permute-start.2 = (f32[1059]{0:T(1024)S(1)}, f32[1059]{0:T(1024)S(1)}, u32[]{:S(2)}, u32[]{:S(2)}) collective-permute-start(f32[1059]{0:T(1024)S(1)} %pad_maximum_fusion.1), channel_id=1, source_target_pairs={{0,128},{128,256},{256,384},{384,512},{512,640},{640,768},{768,896... | collective-permute-start | bytes 12716 | tf_op jit(solution)/shard_map/ppermute | solution.py:25
  30.9 0.2 reshape.1275
  31.2 2.5 %collective-permute-start.3 = (f32[1059]{0:T(1024)S(1)}, f32[1059]{0:T(1024)S(1)}, u32[]{:S(2)}, u32[]{:S(2)}) collective-permute-start(f32[1059]{0:T(1024)S(1)} %pad_maximum_fusion.2), channel_id=1, source_target_pairs={{128,0},{256,128},{384,256},{512,384},{640,512},{768,640},{896,768... | collective-permute-start | bytes 12716 | tf_op jit(solution)/shard_map/ppermute | solution.py:25
  33.7 0.2 concatenate.40
  33.9 2.8 %collective-permute-done.3 = f32[1059]{0:T(1024)S(1)} collective-permute-done((f32[1059]{0:T(1024)S(1)}, f32[1059]{0:T(1024)S(1)}, u32[]{:S(2)}, u32[]{:S(2)}) %collective-permute-start.3) | collective-permute-done | bytes 4268 | tf_op jit(solution)/shard_map/ppermute | solution.py:25
  36.7 0.2 concatenate.41
  36.9 0.2 maximum_select_fusion
  37.3 0.2 subtract_multiply_fusion.3
  37.5 0.6 subtract_add_fusion.1
  38.7 0.7 collective-permute-start.4
  39.4 1.3 collective-permute-start.11
  40.7 1.3 collective-permute-start.9
  42.0 1.3 collective-permute-start.6
  43.8 1.3 collective-permute-start.5
  45.2 1.3 collective-permute-start.10
  46.5 3.6 %collective-permute-done.6 = f32[5,1,64,132]{3,2,1,0:T(8,128)S(1)} collective-permute-done((f32[5,1,64,132]{3,2,1,0:T(8,128)S(1)}, f32[5,1,64,132]{3,2,1,0:T(8,128)S(1)}, u32[]{:S(2)}, u32[]{:S(2)}) %collective-permute-start.6) | collective-permute-done | bytes 168992 | tf_op jit(solution)/shard_map/ppermute | solution.py:160
  50.1 1.3 collective-permute-start.7
  51.4 13.3 %collective-permute-done.5 = f32[5,1,64,132]{3,2,1,0:T(8,128)S(1)} collective-permute-done((f32[5,1,64,132]{3,2,1,0:T(8,128)S(1)}, f32[5,1,64,132]{3,2,1,0:T(8,128)S(1)}, u32[]{:S(2)}, u32[]{:S(2)}) %collective-permute-start.5) | collective-permute-done | bytes 168992 | tf_op jit(solution)/shard_map/ppermute | solution.py:163
  64.7 0.7 collective-permute-start.8
  65.4 10.0 %collective-permute-done.10 = f32[5,1,64,132]{3,2,1,0:T(8,128)S(1)} collective-permute-done((f32[5,1,64,132]{3,2,1,0:T(8,128)S(1)}, f32[5,1,64,132]{3,2,1,0:T(8,128)S(1)}, u32[]{:S(2)}, u32[]{:S(2)}) %collective-permute-start.10) | collective-permute-done | bytes 168992 | tf_op jit(solution)/shard_map/ppermute | solution.py:169
  75.5 3.9 %collective-permute-done.7 = f32[5,1,64,132]{3,2,1,0:T(8,128)S(1)} collective-permute-done((f32[5,1,64,132]{3,2,1,0:T(8,128)S(1)}, f32[5,1,64,132]{3,2,1,0:T(8,128)S(1)}, u32[]{:S(2)}, u32[]{:S(2)}) %collective-permute-start.7) | collective-permute-done | bytes 168992 | tf_op jit(solution)/shard_map/ppermute | solution.py:173
  79.5 0.7 concatenate.43
  80.2 0.2 slice_select_fusion
  80.4 0.2 slice_select_fusion.5
  80.5 0.2 slice_select_fusion.4
  80.7 0.1 slice_select_fusion.7
  81.4 0.2 subtract_multiply_fusion.1
  81.5 0.6 subtract_add_fusion
  82.4 0.1 fusion.14
  82.7 0.7 collective-permute-start.12
  83.5 1.3 collective-permute-start.14
  84.8 1.3 collective-permute-start.13
  86.1 17.6 %collective-permute-start.19 = (f32[5,1,64,130]{3,2,1,0:T(8,128)S(1)}, f32[5,1,64,130]{3,2,1,0:T(8,128)S(1)}, u32[]{:S(2)}, u32[]{:S(2)}) collective-permute-start(f32[5,1,64,130]{3,2,1,0:T(8,128)S(1)} %slice.677), channel_id=1, source_target_pairs={{0,1},{1,2},{2,3},{3,4},{4,5},{5,6},{6,7},{7,8},{8,9},{9,10},{10,1... | collective-permute-start | bytes 499208 | tf_op jit(solution)/shard_map/ppermute | solution.py:160
  103.8 1.3 collective-permute-start.17
  105.1 1.3 collective-permute-start.18
  106.4 1.3 collective-permute-start.15
  107.7 1.5 collective-permute-done.13
  109.2 0.7 collective-permute-start.16
  109.9 21.3 %collective-permute-done.18 = f32[5,1,64,130]{3,2,1,0:T(8,128)S(1)} collective-permute-done((f32[5,1,64,130]{3,2,1,0:T(8,128)S(1)}, f32[5,1,64,130]{3,2,1,0:T(8,128)S(1)}, u32[]{:S(2)}, u32[]{:S(2)}) %collective-permute-start.18) | collective-permute-done | bytes 166432 | tf_op jit(solution)/shard_map/ppermute | solution.py:169
  131.3 0.2 collective-permute-done.15
  131.6 0.7 concatenate.44
  132.4 0.2 slice_select_fusion.3
  132.5 0.2 slice_select_fusion.2
  132.7 0.2 slice_select_fusion.1
  132.9 0.1 slice_select_fusion.6
  133.6 0.3 subtract_add_fusion.2
  134.4 0.7 collective-permute-start.20
  135.0 1.3 collective-permute-start.22
  136.4 1.3 collective-permute-start.21
  137.7 1.3 collective-permute-start.25
  139.0 8.5 %collective-permute-start.27 = (f32[5,1,64,128]{3,2,1,0:T(8,128)S(1)}, f32[5,1,64,128]{3,2,1,0:T(8,128)S(1)}, u32[]{:S(2)}, u32[]{:S(2)}) collective-permute-start(f32[5,1,64,128]{3,2,1,0:T(8,128)S(1)} %get-tuple-element.5), channel_id=1, source_target_pairs={{0,1},{1,2},{2,3},{3,4},{4,5},{5,6},{6,7},{7,8},{8,9},{9,10},{10,1... | collective-permute-start | bytes 491528 | tf_op jit(solution)/shard_map/ppermute | solution.py:160
  147.5 1.3 collective-permute-start.23
  148.8 1.3 collective-permute-start.26
  150.1 3.7 %collective-permute-done.21 = f32[5,1,64,128]{3,2,1,0:T(8,128)S(1)} collective-permute-done((f32[5,1,64,128]{3,2,1,0:T(8,128)S(1)}, f32[5,1,64,128]{3,2,1,0:T(8,128)S(1)}, u32[]{:S(2)}, u32[]{:S(2)}) %collective-permute-start.21) | collective-permute-done | bytes 163872 | tf_op jit(solution)/shard_map/ppermute | solution.py:163
  153.8 0.7 collective-permute-start.24
  154.5 13.1 %collective-permute-done.23 = f32[5,1,64,128]{3,2,1,0:T(8,128)S(1)} collective-permute-done((f32[5,1,64,128]{3,2,1,0:T(8,128)S(1)}, f32[5,1,64,128]{3,2,1,0:T(8,128)S(1)}, u32[]{:S(2)}, u32[]{:S(2)}) %collective-permute-start.23) | collective-permute-done | bytes 163872 | tf_op jit(solution)/shard_map/ppermute | solution.py:173
  167.7 2.2 %collective-permute-done.26 = f32[5,1,64,128]{3,2,1,0:T(8,128)S(1)} collective-permute-done((f32[5,1,64,128]{3,2,1,0:T(8,128)S(1)}, f32[5,1,64,128]{3,2,1,0:T(8,128)S(1)}, u32[]{:S(2)}, u32[]{:S(2)}) %collective-permute-start.26) | collective-permute-done | bytes 163872 | tf_op jit(solution)/shard_map/ppermute | solution.py:169
  170.5 0.7 slice_select_fusion.23
  (99 shorter events, 5.0 us)
Async XLA Ops:
  0.0 36.9 %copy-start = (f32[5,1,64,128]{3,2,1,0:T(8,128)S(1)}, f32[5,1,64,128]{3,2,1,0:T(8,128)}, u32[]{:S(2)}) copy-start(f32[5,1,64,128]{3,2,1,0:T(8,128)} %param.2) | copy-start | bytes 491524
  0.8 25.3 %collective-permute-start = (f32[5,1,3,128]{3,2,1,0:T(4,128)S(1)}, f32[5,1,3,128]{3,2,1,0:T(4,128)S(1)}, u32[]{:S(2)}, u32[]{:S(2)}) collective-permute-start(f32[5,1,3,128]{3,2,1,0:T(4,128)S(1)} %get-tuple-element.46), channel_id=1, source_target_pairs={{0,1},{1,2},{2,3},{3,4},{4,5},{5,6},{6,7},{7,8},{8,9},{9,10},{10,1... | collective-permute-start | bytes 23048 | tf_op jit(solution)/shard_map/ppermute | solution.py:25
  2.7 23.5 %collective-permute-start.1 = (f32[5,1,3,128]{3,2,1,0:T(4,128)S(1)}, f32[5,1,3,128]{3,2,1,0:T(4,128)S(1)}, u32[]{:S(2)}, u32[]{:S(2)}) collective-permute-start(f32[5,1,3,128]{3,2,1,0:T(4,128)S(1)} %get-tuple-element.47), channel_id=1, source_target_pairs={{0,127},{1,0},{2,1},{3,2},{4,3},{5,4},{6,5},{7,6},{8,7},{9,8},{10,... | collective-permute-start | bytes 23048 | tf_op jit(solution)/shard_map/ppermute | solution.py:25
  27.5 6.2 %collective-permute-start.2 = (f32[1059]{0:T(1024)S(1)}, f32[1059]{0:T(1024)S(1)}, u32[]{:S(2)}, u32[]{:S(2)}) collective-permute-start(f32[1059]{0:T(1024)S(1)} %pad_maximum_fusion.1), channel_id=1, source_target_pairs={{0,128},{128,256},{256,384},{384,512},{512,640},{640,768},{768,896... | collective-permute-start | bytes 12716 | tf_op jit(solution)/shard_map/ppermute | solution.py:25
  31.2 5.5 %collective-permute-start.3 = (f32[1059]{0:T(1024)S(1)}, f32[1059]{0:T(1024)S(1)}, u32[]{:S(2)}, u32[]{:S(2)}) collective-permute-start(f32[1059]{0:T(1024)S(1)} %pad_maximum_fusion.2), channel_id=1, source_target_pairs={{128,0},{256,128},{384,256},{512,384},{640,512},{768,640},{896,768... | collective-permute-start | bytes 12716 | tf_op jit(solution)/shard_map/ppermute | solution.py:25
  38.1 5.6 %copy-start.1 = (s32[3,128]{1,0:T(4,128)S(1)}, s32[3,128]{1,0:T(4,128)}, u32[]{:S(2)}) copy-start(s32[3,128]{1,0:T(4,128)} %param.3) | copy-start | bytes 4612
  38.7 5.1 %collective-permute-start.4 = (f32[5,1,64,132]{3,2,1,0:T(8,128)S(1)}, f32[5,1,64,132]{3,2,1,0:T(8,128)S(1)}, u32[]{:S(2)}, u32[]{:S(2)}) collective-permute-start(f32[5,1,64,132]{3,2,1,0:T(8,128)S(1)} %slice.635), channel_id=1, source_target_pairs={{15,1},{14,3},{13,4},{31,17},{30,19},{29,20},{47,33},{46,35},{45,3... | collective-permute-start | bytes 506888 | tf_op jit(solution)/shard_map/ppermute | solution.py:162
  39.4 26.0 %collective-permute-start.11 = (f32[5,1,64,132]{3,2,1,0:T(8,128)S(1)}, f32[5,1,64,132]{3,2,1,0:T(8,128)S(1)}, u32[]{:S(2)}, u32[]{:S(2)}) collective-permute-start(f32[5,1,64,132]{3,2,1,0:T(8,128)S(1)} %slice.635), channel_id=1, source_target_pairs={{0,1},{1,2},{2,3},{3,4},{4,5},{5,6},{6,7},{7,8},{8,9},{9,10},{10,1... | collective-permute-start | bytes 506888 | tf_op jit(solution)/shard_map/ppermute | solution.py:160
  40.7 34.8 %collective-permute-start.9 = (f32[5,1,64,132]{3,2,1,0:T(8,128)S(1)}, f32[5,1,64,132]{3,2,1,0:T(8,128)S(1)}, u32[]{:S(2)}, u32[]{:S(2)}) collective-permute-start(f32[5,1,64,132]{3,2,1,0:T(8,128)S(1)} %slice.635), channel_id=1, source_target_pairs={{0,2},{1,3},{2,4},{3,5},{4,6},{5,7},{6,8},{7,9},{8,10},{9,11},{10,... | collective-permute-start | bytes 506888 | tf_op jit(solution)/shard_map/ppermute | solution.py:160
  42.0 8.1 %collective-permute-start.6 = (f32[5,1,64,132]{3,2,1,0:T(8,128)S(1)}, f32[5,1,64,132]{3,2,1,0:T(8,128)S(1)}, u32[]{:S(2)}, u32[]{:S(2)}) collective-permute-start(f32[5,1,64,132]{3,2,1,0:T(8,128)S(1)} %slice.635), channel_id=1, source_target_pairs={{0,3},{1,4},{2,5},{3,6},{4,7},{5,8},{6,9},{7,10},{8,11},{9,12},{10... | collective-permute-start | bytes 506888 | tf_op jit(solution)/shard_map/ppermute | solution.py:160
  43.8 20.8 %collective-permute-start.5 = (f32[5,1,64,132]{3,2,1,0:T(8,128)S(1)}, f32[5,1,64,132]{3,2,1,0:T(8,128)S(1)}, u32[]{:S(2)}, u32[]{:S(2)}) collective-permute-start(f32[5,1,64,132]{3,2,1,0:T(8,128)S(1)} %collective-permute-done.4), channel_id=1, source_target_pairs={{1,18},{3,17},{4,16},{17,34},{19,33},{20,32},{33,50},{35,49},{36,4... | collective-permute-start | bytes 506888 | tf_op jit(solution)/shard_map/ppermute | solution.py:163
  45.2 30.3 %collective-permute-start.10 = (f32[5,1,64,132]{3,2,1,0:T(8,128)S(1)}, f32[5,1,64,132]{3,2,1,0:T(8,128)S(1)}, u32[]{:S(2)}, u32[]{:S(2)}) collective-permute-start(f32[5,1,64,132]{3,2,1,0:T(8,128)S(1)} %collective-permute-done.4), channel_id=1, source_target_pairs={{1,16},{17,32},{33,48},{49,64},{65,80},{81,96},{97,112},{113,0},{1... | collective-permute-start | bytes 506888 | tf_op jit(solution)/shard_map/ppermute | solution.py:169
  50.1 29.3 %collective-permute-start.7 = (f32[5,1,64,132]{3,2,1,0:T(8,128)S(1)}, f32[5,1,64,132]{3,2,1,0:T(8,128)S(1)}, u32[]{:S(2)}, u32[]{:S(2)}) collective-permute-start(f32[5,1,64,132]{3,2,1,0:T(8,128)S(1)} %collective-permute-done.4), channel_id=1, source_target_pairs={{3,16},{19,32},{35,48},{51,64},{67,80},{83,96},{99,112},{115,0},{1... | collective-permute-start | bytes 506888 | tf_op jit(solution)/shard_map/ppermute | solution.py:173
  64.7 14.7 %collective-permute-start.8 = (f32[5,1,64,132]{3,2,1,0:T(8,128)S(1)}, f32[5,1,64,132]{3,2,1,0:T(8,128)S(1)}, u32[]{:S(2)}, u32[]{:S(2)}) collective-permute-start(f32[5,1,64,132]{3,2,1,0:T(8,128)S(1)} %collective-permute-done.5), channel_id=1, source_target_pairs={{2,1},{18,17},{34,33},{50,49},{66,65},{82,81},{98,97},{114,113},{1... | collective-permute-start | bytes 506888 | tf_op jit(solution)/shard_map/ppermute | solution.py:175
  82.7 2.0 %collective-permute-start.12 = (f32[5,1,64,130]{3,2,1,0:T(8,128)S(1)}, f32[5,1,64,130]{3,2,1,0:T(8,128)S(1)}, u32[]{:S(2)}, u32[]{:S(2)}) collective-permute-start(f32[5,1,64,130]{3,2,1,0:T(8,128)S(1)} %slice.677), channel_id=1, source_target_pairs={{15,1},{14,3},{13,4},{31,17},{30,19},{29,20},{47,33},{46,35},{45,3... | collective-permute-start | bytes 499208 | tf_op jit(solution)/shard_map/ppermute | solution.py:162
  83.5 22.9 %collective-permute-start.14 = (f32[5,1,64,130]{3,2,1,0:T(8,128)S(1)}, f32[5,1,64,130]{3,2,1,0:T(8,128)S(1)}, u32[]{:S(2)}, u32[]{:S(2)}) collective-permute-start(f32[5,1,64,130]{3,2,1,0:T(8,128)S(1)} %slice.677), channel_id=1, source_target_pairs={{0,3},{1,4},{2,5},{3,6},{4,7},{5,8},{6,9},{7,10},{8,11},{9,12},{10... | collective-permute-start | bytes 499208 | tf_op jit(solution)/shard_map/ppermute | solution.py:160
  84.8 24.4 %collective-permute-start.13 = (f32[5,1,64,130]{3,2,1,0:T(8,128)S(1)}, f32[5,1,64,130]{3,2,1,0:T(8,128)S(1)}, u32[]{:S(2)}, u32[]{:S(2)}) collective-permute-start(f32[5,1,64,130]{3,2,1,0:T(8,128)S(1)} %collective-permute-done.12), channel_id=1, source_target_pairs={{1,18},{3,17},{4,16},{17,34},{19,33},{20,32},{33,50},{35,49},{36,4... | collective-permute-start | bytes 499208 | tf_op jit(solution)/shard_map/ppermute | solution.py:163
  86.1 23.8 %collective-permute-start.19 = (f32[5,1,64,130]{3,2,1,0:T(8,128)S(1)}, f32[5,1,64,130]{3,2,1,0:T(8,128)S(1)}, u32[]{:S(2)}, u32[]{:S(2)}) collective-permute-start(f32[5,1,64,130]{3,2,1,0:T(8,128)S(1)} %slice.677), channel_id=1, source_target_pairs={{0,1},{1,2},{2,3},{3,4},{4,5},{5,6},{6,7},{7,8},{8,9},{9,10},{10,1... | collective-permute-start | bytes 499208 | tf_op jit(solution)/shard_map/ppermute | solution.py:160
  103.8 27.6 %collective-permute-start.17 = (f32[5,1,64,130]{3,2,1,0:T(8,128)S(1)}, f32[5,1,64,130]{3,2,1,0:T(8,128)S(1)}, u32[]{:S(2)}, u32[]{:S(2)}) collective-permute-start(f32[5,1,64,130]{3,2,1,0:T(8,128)S(1)} %slice.677), channel_id=1, source_target_pairs={{0,2},{1,3},{2,4},{3,5},{4,6},{5,7},{6,8},{7,9},{8,10},{9,11},{10,... | collective-permute-start | bytes 499208 | tf_op jit(solution)/shard_map/ppermute | solution.py:160
  105.1 26.2 %collective-permute-start.18 = (f32[5,1,64,130]{3,2,1,0:T(8,128)S(1)}, f32[5,1,64,130]{3,2,1,0:T(8,128)S(1)}, u32[]{:S(2)}, u32[]{:S(2)}) collective-permute-start(f32[5,1,64,130]{3,2,1,0:T(8,128)S(1)} %collective-permute-done.12), channel_id=1, source_target_pairs={{1,16},{17,32},{33,48},{49,64},{65,80},{81,96},{97,112},{113,0},{1... | collective-permute-start | bytes 499208 | tf_op jit(solution)/shard_map/ppermute | solution.py:169
  106.4 25.2 %collective-permute-start.15 = (f32[5,1,64,130]{3,2,1,0:T(8,128)S(1)}, f32[5,1,64,130]{3,2,1,0:T(8,128)S(1)}, u32[]{:S(2)}, u32[]{:S(2)}) collective-permute-start(f32[5,1,64,130]{3,2,1,0:T(8,128)S(1)} %collective-permute-done.12), channel_id=1, source_target_pairs={{3,16},{19,32},{35,48},{51,64},{67,80},{83,96},{99,112},{115,0},{1... | collective-permute-start | bytes 499208 | tf_op jit(solution)/shard_map/ppermute | solution.py:173
  109.2 22.3 %collective-permute-start.16 = (f32[5,1,64,130]{3,2,1,0:T(8,128)S(1)}, f32[5,1,64,130]{3,2,1,0:T(8,128)S(1)}, u32[]{:S(2)}, u32[]{:S(2)}) collective-permute-start(f32[5,1,64,130]{3,2,1,0:T(8,128)S(1)} %collective-permute-done.13), channel_id=1, source_target_pairs={{2,1},{18,17},{34,33},{50,49},{66,65},{82,81},{98,97},{114,113},{1... | collective-permute-start | bytes 499208 | tf_op jit(solution)/shard_map/ppermute | solution.py:175
  134.4 2.0 %collective-permute-start.20 = (f32[5,1,64,128]{3,2,1,0:T(8,128)S(1)}, f32[5,1,64,128]{3,2,1,0:T(8,128)S(1)}, u32[]{:S(2)}, u32[]{:S(2)}) collective-permute-start(f32[5,1,64,128]{3,2,1,0:T(8,128)S(1)} %get-tuple-element.5), channel_id=1, source_target_pairs={{15,1},{14,3},{13,4},{31,17},{30,19},{29,20},{47,33},{46,35},{45,3... | collective-permute-start | bytes 491528 | tf_op jit(solution)/shard_map/ppermute | solution.py:162
  135.0 13.8 %collective-permute-start.22 = (f32[5,1,64,128]{3,2,1,0:T(8,128)S(1)}, f32[5,1,64,128]{3,2,1,0:T(8,128)S(1)}, u32[]{:S(2)}, u32[]{:S(2)}) collective-permute-start(f32[5,1,64,128]{3,2,1,0:T(8,128)S(1)} %get-tuple-element.5), channel_id=1, source_target_pairs={{0,3},{1,4},{2,5},{3,6},{4,7},{5,8},{6,9},{7,10},{8,11},{9,12},{10... | collective-permute-start | bytes 491528 | tf_op jit(solution)/shard_map/ppermute | solution.py:160
  136.4 17.5 %collective-permute-start.21 = (f32[5,1,64,128]{3,2,1,0:T(8,128)S(1)}, f32[5,1,64,128]{3,2,1,0:T(8,128)S(1)}, u32[]{:S(2)}, u32[]{:S(2)}) collective-permute-start(f32[5,1,64,128]{3,2,1,0:T(8,128)S(1)} %collective-permute-done.20), channel_id=1, source_target_pairs={{1,18},{3,17},{4,16},{17,34},{19,33},{20,32},{33,50},{35,49},{36,4... | collective-permute-start | bytes 491528 | tf_op jit(solution)/shard_map/ppermute | solution.py:163
  137.7 16.8 %collective-permute-start.25 = (f32[5,1,64,128]{3,2,1,0:T(8,128)S(1)}, f32[5,1,64,128]{3,2,1,0:T(8,128)S(1)}, u32[]{:S(2)}, u32[]{:S(2)}) collective-permute-start(f32[5,1,64,128]{3,2,1,0:T(8,128)S(1)} %get-tuple-element.5), channel_id=1, source_target_pairs={{0,2},{1,3},{2,4},{3,5},{4,6},{5,7},{6,8},{7,9},{8,10},{9,11},{10,... | collective-permute-start | bytes 491528 | tf_op jit(solution)/shard_map/ppermute | solution.py:160
  139.0 28.7 %collective-permute-start.27 = (f32[5,1,64,128]{3,2,1,0:T(8,128)S(1)}, f32[5,1,64,128]{3,2,1,0:T(8,128)S(1)}, u32[]{:S(2)}, u32[]{:S(2)}) collective-permute-start(f32[5,1,64,128]{3,2,1,0:T(8,128)S(1)} %get-tuple-element.5), channel_id=1, source_target_pairs={{0,1},{1,2},{2,3},{3,4},{4,5},{5,6},{6,7},{7,8},{8,9},{9,10},{10,1... | collective-permute-start | bytes 491528 | tf_op jit(solution)/shard_map/ppermute | solution.py:160
  147.5 20.1 %collective-permute-start.23 = (f32[5,1,64,128]{3,2,1,0:T(8,128)S(1)}, f32[5,1,64,128]{3,2,1,0:T(8,128)S(1)}, u32[]{:S(2)}, u32[]{:S(2)}) collective-permute-start(f32[5,1,64,128]{3,2,1,0:T(8,128)S(1)} %collective-permute-done.20), channel_id=1, source_target_pairs={{3,16},{19,32},{35,48},{51,64},{67,80},{83,96},{99,112},{115,0},{1... | collective-permute-start | bytes 491528 | tf_op jit(solution)/shard_map/ppermute | solution.py:173
  148.8 21.0 %collective-permute-start.26 = (f32[5,1,64,128]{3,2,1,0:T(8,128)S(1)}, f32[5,1,64,128]{3,2,1,0:T(8,128)S(1)}, u32[]{:S(2)}, u32[]{:S(2)}) collective-permute-start(f32[5,1,64,128]{3,2,1,0:T(8,128)S(1)} %collective-permute-done.20), channel_id=1, source_target_pairs={{1,16},{17,32},{33,48},{49,64},{65,80},{81,96},{97,112},{113,0},{1... | collective-permute-start | bytes 491528 | tf_op jit(solution)/shard_map/ppermute | solution.py:169
  153.8 13.8 %collective-permute-start.24 = (f32[5,1,64,128]{3,2,1,0:T(8,128)S(1)}, f32[5,1,64,128]{3,2,1,0:T(8,128)S(1)}, u32[]{:S(2)}, u32[]{:S(2)}) collective-permute-start(f32[5,1,64,128]{3,2,1,0:T(8,128)S(1)} %collective-permute-done.21), channel_id=1, source_target_pairs={{2,1},{18,17},{34,33},{50,49},{66,65},{82,81},{98,97},{114,113},{1... | collective-permute-start | bytes 491528 | tf_op jit(solution)/shard_map/ppermute | solution.py:175

commit v16 on v12

--- a/solution.py
+++ b/solution.py
@@ -138,7 +138,7 @@
             base = block * plane
             after = (base + plane) % count
             for j in range(1, blocks + 1):
-                lane = (3 * g + j - 1) % half
+                lane = (3 * g + j + 3) % half
                 relay = base + relay_seat(lane, plane - j, plane, blocks)
                 first.append((g * count + base + plane - j, g * count + relay))
                 second.append((g * count + relay, g * count + after + blocks - j))

time: 165 us -> 159 us (0.964)
  the two profiles are of different devices: /device:TPU:6 before, /device:TPU:261 now
where the time goes in v16:
time: 159 us; the launch traced here: 158 us
  starting transfers between devices  81.3 us (51%)
  waiting for transfers between devices  62.3 us (39%)
  other arithmetic  10.1 us (6%)
  local copies, waits for them, and re-layouts  3.57 us (2%)
    ppermute x9, starting transfers between devices, rotation_pieces(): near.append(lax.ppermute(head, 'azi', pairs))  30.5 us
    ppermute x3, waiting for transfers between devices, rotation_pieces(): relayed = lax.ppermute(head, ('rad', 'azi'), first)  25.9 us
    ppermute x3, starting transfers between devices, rotation_pieces(): first_seat = lax.ppermute(relayed, ('rad', 'azi'), direct)  23.3 us
    ppermute x3, waiting for transfers between devices, rotation_pieces(): far = lax.ppermute(crossed, 'azi', pairs)  15.3 us
    ppermute x3, waiting for transfers between devices, rotation_pieces(): crossed = lax.ppermute(relayed, ('rad', 'azi'), second)  15 us
    ppermute x4, starting transfers between devices, passed_along(): return lax.ppermute(value, axis, pairs)  12.1 us
    ppermute x3, starting transfers between devices, rotation_pieces(): far = lax.ppermute(crossed, 'azi', pairs)  5.75 us
    ppermute x3, starting transfers between devices, rotation_pieces(): crossed = lax.ppermute(relayed, ('rad', 'azi'), second)  5.73 us
  transfers between devices with their start and end apart: 25, of which 10 were waited for; matrix products, arithmetic and copies ran while one was open for 2% of the time, Pallas kernels for 0%

profile of v16, /device:TPU:261, one launch (start us, length us, event | category | flops | bytes accessed | tf_op | source)
XLA Modules:
  0.0 158.3 jit_solution(5684021399431177643)
XLA Ops:
  0.0 0.8 fusion.103
  0.8 3.8 %collective-permute-start = (f32[5,1,3,128]{3,2,1,0:T(4,128)S(1)}, f32[5,1,3,128]{3,2,1,0:T(4,128)S(1)}, u32[]{:S(2)}, u32[]{:S(2)}) collective-permute-start(f32[5,1,3,128]{3,2,1,0:T(4,128)S(1)} %get-tuple-element.46), channel_id=1, source_target_pairs={{0,1},{1,2},{2,3},{3,4},{4,5},{5,6},{6,7},{7,8},{8,9},{9,10},{10,1... | collective-permute-start | bytes 23048 | tf_op jit(solution)/shard_map/ppermute | solution.py:25
  4.6 1.9 %collective-permute-start.1 = (f32[5,1,3,128]{3,2,1,0:T(4,128)S(1)}, f32[5,1,3,128]{3,2,1,0:T(4,128)S(1)}, u32[]{:S(2)}, u32[]{:S(2)}) collective-permute-start(f32[5,1,3,128]{3,2,1,0:T(4,128)S(1)} %get-tuple-element.47), channel_id=1, source_target_pairs={{0,127},{1,0},{2,1},{3,2},{4,3},{5,4},{6,5},{7,6},{8,7},{9,8},{10,... | collective-permute-start | bytes 23048 | tf_op jit(solution)/shard_map/ppermute | solution.py:25
  6.5 0.8 slice_convert_fusion.1
  7.8 1.8 %collective-permute-done.1 = f32[5,1,3,128]{3,2,1,0:T(4,128)S(1)} collective-permute-done((f32[5,1,3,128]{3,2,1,0:T(4,128)S(1)}, f32[5,1,3,128]{3,2,1,0:T(4,128)S(1)}, u32[]{:S(2)}, u32[]{:S(2)}) %collective-permute-start.1) | collective-permute-done | bytes 7712 | tf_op jit(solution)/shard_map/ppermute | solution.py:25
  9.6 0.9 pad_maximum_fusion
  10.6 0.2 reshape.1273
  10.9 4.0 %collective-permute-start.2 = (f32[1059]{0:T(1024)S(1)}, f32[1059]{0:T(1024)S(1)}, u32[]{:S(2)}, u32[]{:S(2)}) collective-permute-start(f32[1059]{0:T(1024)S(1)} %pad_maximum_fusion.1), channel_id=1, source_target_pairs={{0,128},{128,256},{256,384},{384,512},{512,640},{640,768},{768,896... | collective-permute-start | bytes 12716 | tf_op jit(solution)/shard_map/ppermute | solution.py:25
  14.9 0.2 reshape.1275
  15.2 2.5 %collective-permute-start.3 = (f32[1059]{0:T(1024)S(1)}, f32[1059]{0:T(1024)S(1)}, u32[]{:S(2)}, u32[]{:S(2)}) collective-permute-start(f32[1059]{0:T(1024)S(1)} %pad_maximum_fusion.2), channel_id=1, source_target_pairs={{128,0},{256,128},{384,256},{512,384},{640,512},{768,640},{896,768... | collective-permute-start | bytes 12716 | tf_op jit(solution)/shard_map/ppermute | solution.py:25
  17.7 0.2 concatenate.40
  17.9 2.3 %collective-permute-done.3 = f32[1059]{0:T(1024)S(1)} collective-permute-done((f32[1059]{0:T(1024)S(1)}, f32[1059]{0:T(1024)S(1)}, u32[]{:S(2)}, u32[]{:S(2)}) %collective-permute-start.3) | collective-permute-done | bytes 4268 | tf_op jit(solution)/shard_map/ppermute | solution.py:25
  20.2 0.2 concatenate.41
  20.4 0.2 maximum_select_fusion
  20.8 0.2 subtract_multiply_fusion.3
  21.0 0.6 subtract_add_fusion.1
  21.7 0.1 fusion.4
  21.8 0.1 fusion.29
  22.2 1.3 collective-permute-start.4
  23.5 2.5 %collective-permute-start.10 = (f32[5,1,64,132]{3,2,1,0:T(8,128)S(1)}, f32[5,1,64,132]{3,2,1,0:T(8,128)S(1)}, u32[]{:S(2)}, u32[]{:S(2)}) collective-permute-start(f32[5,1,64,132]{3,2,1,0:T(8,128)S(1)} %slice.635), channel_id=1, source_target_pairs={{0,1},{1,2},{2,3},{3,4},{4,5},{5,6},{6,7},{7,8},{8,9},{9,10},{10,1... | collective-permute-start | bytes 506888 | tf_op jit(solution)/shard_map/ppermute | solution.py:160
  26.0 3.8 %collective-permute-start.8 = (f32[5,1,64,132]{3,2,1,0:T(8,128)S(1)}, f32[5,1,64,132]{3,2,1,0:T(8,128)S(1)}, u32[]{:S(2)}, u32[]{:S(2)}) collective-permute-start(f32[5,1,64,132]{3,2,1,0:T(8,128)S(1)} %slice.635), channel_id=1, source_target_pairs={{0,2},{1,3},{2,4},{3,5},{4,6},{5,7},{6,8},{7,9},{8,10},{9,11},{10,... | collective-permute-start | bytes 506888 | tf_op jit(solution)/shard_map/ppermute | solution.py:160
  29.8 5.5 %collective-permute-start.6 = (f32[5,1,64,132]{3,2,1,0:T(8,128)S(1)}, f32[5,1,64,132]{3,2,1,0:T(8,128)S(1)}, u32[]{:S(2)}, u32[]{:S(2)}) collective-permute-start(f32[5,1,64,132]{3,2,1,0:T(8,128)S(1)} %slice.635), channel_id=1, source_target_pairs={{0,3},{1,4},{2,5},{3,6},{4,7},{5,8},{6,9},{7,10},{8,11},{9,12},{10... | collective-permute-start | bytes 506888 | tf_op jit(solution)/shard_map/ppermute | solution.py:160
  35.8 14.8 %collective-permute-done.4 = f32[5,1,64,132]{3,2,1,0:T(8,128)S(1)} collective-permute-done((f32[5,1,64,132]{3,2,1,0:T(8,128)S(1)}, f32[5,1,64,132]{3,2,1,0:T(8,128)S(1)}, u32[]{:S(2)}, u32[]{:S(2)}) %collective-permute-start.4) | collective-permute-done | bytes 168992 | tf_op jit(solution)/shard_map/ppermute | solution.py:162
  50.7 1.9 %collective-permute-start.5 = (f32[5,1,64,132]{3,2,1,0:T(8,128)S(1)}, f32[5,1,64,132]{3,2,1,0:T(8,128)S(1)}, u32[]{:S(2)}, u32[]{:S(2)}) collective-permute-start(f32[5,1,64,132]{3,2,1,0:T(8,128)S(1)} %collective-permute-done.4), channel_id=1, source_target_pairs={{8,18},{10,17},{13,16},{24,34},{26,33},{29,32},{40,50},{42,49},{45... | collective-permute-start | bytes 506888 | tf_op jit(solution)/shard_map/ppermute | solution.py:163
  52.6 1.3 collective-permute-start.9
  53.9 15.0 %collective-permute-done.5 = f32[5,1,64,132]{3,2,1,0:T(8,128)S(1)} collective-permute-done((f32[5,1,64,132]{3,2,1,0:T(8,128)S(1)}, f32[5,1,64,132]{3,2,1,0:T(8,128)S(1)}, u32[]{:S(2)}, u32[]{:S(2)}) %collective-permute-start.5) | collective-permute-done | bytes 168992 | tf_op jit(solution)/shard_map/ppermute | solution.py:163
  69.0 1.9 %collective-permute-start.7 = (f32[5,1,64,132]{3,2,1,0:T(8,128)S(1)}, f32[5,1,64,132]{3,2,1,0:T(8,128)S(1)}, u32[]{:S(2)}, u32[]{:S(2)}) collective-permute-start(f32[5,1,64,132]{3,2,1,0:T(8,128)S(1)} %collective-permute-done.5), channel_id=1, source_target_pairs={{1,0},{2,1},{17,16},{18,17},{33,32},{34,33},{49,48},{50,49},{65,64... | collective-permute-start | bytes 506888 | tf_op jit(solution)/shard_map/ppermute | solution.py:184
  71.0 6.3 %collective-permute-done.7 = f32[5,1,64,132]{3,2,1,0:T(8,128)S(1)} collective-permute-done((f32[5,1,64,132]{3,2,1,0:T(8,128)S(1)}, f32[5,1,64,132]{3,2,1,0:T(8,128)S(1)}, u32[]{:S(2)}, u32[]{:S(2)}) %collective-permute-start.7) | collective-permute-done | bytes 168992 | tf_op jit(solution)/shard_map/ppermute | solution.py:184
  77.4 0.7 concatenate.43
  78.1 0.2 slice_select_fusion
  78.3 0.2 slice_select_fusion.5
  78.5 0.2 slice_select_fusion.4
  78.7 0.1 slice_select_fusion.7
  79.3 0.2 subtract_multiply_fusion.1
  79.5 0.6 subtract_add_fusion
  80.2 0.1 fusion.7
  80.3 0.1 fusion.14
  80.7 1.3 collective-permute-start.11
  82.0 1.3 collective-permute-start.13
  83.3 6.4 %collective-permute-done.11 = f32[5,1,64,130]{3,2,1,0:T(8,128)S(1)} collective-permute-done((f32[5,1,64,130]{3,2,1,0:T(8,128)S(1)}, f32[5,1,64,130]{3,2,1,0:T(8,128)S(1)}, u32[]{:S(2)}, u32[]{:S(2)}) %collective-permute-start.11) | collective-permute-done | bytes 166432 | tf_op jit(solution)/shard_map/ppermute | solution.py:162
  89.7 1.9 %collective-permute-start.12 = (f32[5,1,64,130]{3,2,1,0:T(8,128)S(1)}, f32[5,1,64,130]{3,2,1,0:T(8,128)S(1)}, u32[]{:S(2)}, u32[]{:S(2)}) collective-permute-start(f32[5,1,64,130]{3,2,1,0:T(8,128)S(1)} %collective-permute-done.11), channel_id=1, source_target_pairs={{8,18},{10,17},{13,16},{24,34},{26,33},{29,32},{40,50},{42,49},{45... | collective-permute-start | bytes 499208 | tf_op jit(solution)/shard_map/ppermute | solution.py:163
  91.7 1.9 %collective-permute-start.17 = (f32[5,1,64,130]{3,2,1,0:T(8,128)S(1)}, f32[5,1,64,130]{3,2,1,0:T(8,128)S(1)}, u32[]{:S(2)}, u32[]{:S(2)}) collective-permute-start(f32[5,1,64,130]{3,2,1,0:T(8,128)S(1)} %slice.677), channel_id=1, source_target_pairs={{0,1},{1,2},{2,3},{3,4},{4,5},{5,6},{6,7},{7,8},{8,9},{9,10},{10,1... | collective-permute-start | bytes 499208 | tf_op jit(solution)/shard_map/ppermute | solution.py:160
  93.6 5.8 %collective-permute-start.15 = (f32[5,1,64,130]{3,2,1,0:T(8,128)S(1)}, f32[5,1,64,130]{3,2,1,0:T(8,128)S(1)}, u32[]{:S(2)}, u32[]{:S(2)}) collective-permute-start(f32[5,1,64,130]{3,2,1,0:T(8,128)S(1)} %slice.677), channel_id=1, source_target_pairs={{0,2},{1,3},{2,4},{3,5},{4,6},{5,7},{6,8},{7,9},{8,10},{9,11},{10,... | collective-permute-start | bytes 499208 | tf_op jit(solution)/shard_map/ppermute | solution.py:160
  99.4 10.8 %collective-permute-start.16 = (f32[5,1,64,130]{3,2,1,0:T(8,128)S(1)}, f32[5,1,64,130]{3,2,1,0:T(8,128)S(1)}, u32[]{:S(2)}, u32[]{:S(2)}) collective-permute-start(f32[5,1,64,130]{3,2,1,0:T(8,128)S(1)} %collective-permute-done.11), channel_id=1, source_target_pairs={{8,16},{24,32},{40,48},{56,64},{72,80},{88,96},{104,112},{120,0},{... | collective-permute-start | bytes 499208 | tf_op jit(solution)/shard_map/ppermute | solution.py:169
  110.3 1.9 %collective-permute-start.14 = (f32[5,1,64,130]{3,2,1,0:T(8,128)S(1)}, f32[5,1,64,130]{3,2,1,0:T(8,128)S(1)}, u32[]{:S(2)}, u32[]{:S(2)}) collective-permute-start(f32[5,1,64,130]{3,2,1,0:T(8,128)S(1)} %collective-permute-done.12), channel_id=1, source_target_pairs={{1,0},{2,1},{17,16},{18,17},{33,32},{34,33},{49,48},{50,49},{65,64... | collective-permute-start | bytes 499208 | tf_op jit(solution)/shard_map/ppermute | solution.py:184
  112.3 2.0 %collective-permute-done.16 = f32[5,1,64,130]{3,2,1,0:T(8,128)S(1)} collective-permute-done((f32[5,1,64,130]{3,2,1,0:T(8,128)S(1)}, f32[5,1,64,130]{3,2,1,0:T(8,128)S(1)}, u32[]{:S(2)}, u32[]{:S(2)}) %collective-permute-start.16) | collective-permute-done | bytes 166432 | tf_op jit(solution)/shard_map/ppermute | solution.py:169
  114.3 4.4 %collective-permute-done.14 = f32[5,1,64,130]{3,2,1,0:T(8,128)S(1)} collective-permute-done((f32[5,1,64,130]{3,2,1,0:T(8,128)S(1)}, f32[5,1,64,130]{3,2,1,0:T(8,128)S(1)}, u32[]{:S(2)}, u32[]{:S(2)}) %collective-permute-start.14) | collective-permute-done | bytes 166432 | tf_op jit(solution)/shard_map/ppermute | solution.py:184
  118.8 0.7 concatenate.44
  119.5 0.2 slice_select_fusion.3
  119.6 0.2 slice_select_fusion.2
  119.8 0.2 slice_select_fusion.1
  120.0 0.1 slice_select_fusion.6
  120.6 0.1 subtract_multiply_fusion.5
  120.7 0.3 subtract_add_fusion.2
  121.5 1.3 collective-permute-start.18
  122.8 1.3 collective-permute-start.20
  124.1 4.7 %collective-permute-done.18 = f32[5,1,64,128]{3,2,1,0:T(8,128)S(1)} collective-permute-done((f32[5,1,64,128]{3,2,1,0:T(8,128)S(1)}, f32[5,1,64,128]{3,2,1,0:T(8,128)S(1)}, u32[]{:S(2)}, u32[]{:S(2)}) %collective-permute-start.18) | collective-permute-done | bytes 163872 | tf_op jit(solution)/shard_map/ppermute | solution.py:162
  128.8 1.9 %collective-permute-start.19 = (f32[5,1,64,128]{3,2,1,0:T(8,128)S(1)}, f32[5,1,64,128]{3,2,1,0:T(8,128)S(1)}, u32[]{:S(2)}, u32[]{:S(2)}) collective-permute-start(f32[5,1,64,128]{3,2,1,0:T(8,128)S(1)} %collective-permute-done.18), channel_id=1, source_target_pairs={{8,18},{10,17},{13,16},{24,34},{26,33},{29,32},{40,50},{42,49},{45... | collective-permute-start | bytes 491528 | tf_op jit(solution)/shard_map/ppermute | solution.py:163
  130.7 6.0 %collective-permute-start.22 = (f32[5,1,64,128]{3,2,1,0:T(8,128)S(1)}, f32[5,1,64,128]{3,2,1,0:T(8,128)S(1)}, u32[]{:S(2)}, u32[]{:S(2)}) collective-permute-start(f32[5,1,64,128]{3,2,1,0:T(8,128)S(1)} %get-tuple-element.5), channel_id=1, source_target_pairs={{0,2},{1,3},{2,4},{3,5},{4,6},{5,7},{6,8},{7,9},{8,10},{9,11},{10,... | collective-permute-start | bytes 491528 | tf_op jit(solution)/shard_map/ppermute | solution.py:160
  136.7 2.4 %collective-permute-start.24 = (f32[5,1,64,128]{3,2,1,0:T(8,128)S(1)}, f32[5,1,64,128]{3,2,1,0:T(8,128)S(1)}, u32[]{:S(2)}, u32[]{:S(2)}) collective-permute-start(f32[5,1,64,128]{3,2,1,0:T(8,128)S(1)} %get-tuple-element.5), channel_id=1, source_target_pairs={{0,1},{1,2},{2,3},{3,4},{4,5},{5,6},{6,7},{7,8},{8,9},{9,10},{10,1... | collective-permute-start | bytes 491528 | tf_op jit(solution)/shard_map/ppermute | solution.py:160
  139.0 11.2 %collective-permute-start.23 = (f32[5,1,64,128]{3,2,1,0:T(8,128)S(1)}, f32[5,1,64,128]{3,2,1,0:T(8,128)S(1)}, u32[]{:S(2)}, u32[]{:S(2)}) collective-permute-start(f32[5,1,64,128]{3,2,1,0:T(8,128)S(1)} %collective-permute-done.18), channel_id=1, source_target_pairs={{8,16},{24,32},{40,48},{56,64},{72,80},{88,96},{104,112},{120,0},{... | collective-permute-start | bytes 491528 | tf_op jit(solution)/shard_map/ppermute | solution.py:169
  150.2 1.9 %collective-permute-start.21 = (f32[5,1,64,128]{3,2,1,0:T(8,128)S(1)}, f32[5,1,64,128]{3,2,1,0:T(8,128)S(1)}, u32[]{:S(2)}, u32[]{:S(2)}) collective-permute-start(f32[5,1,64,128]{3,2,1,0:T(8,128)S(1)} %collective-permute-done.19), channel_id=1, source_target_pairs={{1,0},{2,1},{17,16},{18,17},{33,32},{34,33},{49,48},{50,49},{65,64... | collective-permute-start | bytes 491528 | tf_op jit(solution)/shard_map/ppermute | solution.py:184
  152.2 4.7 %collective-permute-done.21 = f32[5,1,64,128]{3,2,1,0:T(8,128)S(1)} collective-permute-done((f32[5,1,64,128]{3,2,1,0:T(8,128)S(1)}, f32[5,1,64,128]{3,2,1,0:T(8,128)S(1)}, u32[]{:S(2)}, u32[]{:S(2)}) %collective-permute-start.21) | collective-permute-done | bytes 163872 | tf_op jit(solution)/shard_map/ppermute | solution.py:184
  157.6 0.7 slice_select_fusion.23
  (93 shorter events, 4.4 us)
Async XLA Ops:
  0.0 20.4 %copy-start = (f32[5,1,64,128]{3,2,1,0:T(8,128)S(1)}, f32[5,1,64,128]{3,2,1,0:T(8,128)}, u32[]{:S(2)}) copy-start(f32[5,1,64,128]{3,2,1,0:T(8,128)} %param.2) | copy-start | bytes 491524
  0.8 7.0 %collective-permute-start = (f32[5,1,3,128]{3,2,1,0:T(4,128)S(1)}, f32[5,1,3,128]{3,2,1,0:T(4,128)S(1)}, u32[]{:S(2)}, u32[]{:S(2)}) collective-permute-start(f32[5,1,3,128]{3,2,1,0:T(4,128)S(1)} %get-tuple-element.46), channel_id=1, source_target_pairs={{0,1},{1,2},{2,3},{3,4},{4,5},{5,6},{6,7},{7,8},{8,9},{9,10},{10,1... | collective-permute-start | bytes 23048 | tf_op jit(solution)/shard_map/ppermute | solution.py:25
  4.6 5.0 %collective-permute-start.1 = (f32[5,1,3,128]{3,2,1,0:T(4,128)S(1)}, f32[5,1,3,128]{3,2,1,0:T(4,128)S(1)}, u32[]{:S(2)}, u32[]{:S(2)}) collective-permute-start(f32[5,1,3,128]{3,2,1,0:T(4,128)S(1)} %get-tuple-element.47), channel_id=1, source_target_pairs={{0,127},{1,0},{2,1},{3,2},{4,3},{5,4},{6,5},{7,6},{8,7},{9,8},{10,... | collective-permute-start | bytes 23048 | tf_op jit(solution)/shard_map/ppermute | solution.py:25
  10.9 6.8 %collective-permute-start.2 = (f32[1059]{0:T(1024)S(1)}, f32[1059]{0:T(1024)S(1)}, u32[]{:S(2)}, u32[]{:S(2)}) collective-permute-start(f32[1059]{0:T(1024)S(1)} %pad_maximum_fusion.1), channel_id=1, source_target_pairs={{0,128},{128,256},{256,384},{384,512},{512,640},{640,768},{768,896... | collective-permute-start | bytes 12716 | tf_op jit(solution)/shard_map/ppermute | solution.py:25
  15.2 5.0 %collective-permute-start.3 = (f32[1059]{0:T(1024)S(1)}, f32[1059]{0:T(1024)S(1)}, u32[]{:S(2)}, u32[]{:S(2)}) collective-permute-start(f32[1059]{0:T(1024)S(1)} %pad_maximum_fusion.2), channel_id=1, source_target_pairs={{128,0},{256,128},{384,256},{512,384},{640,512},{768,640},{896,768... | collective-permute-start | bytes 12716 | tf_op jit(solution)/shard_map/ppermute | solution.py:25
  21.5 14.1 %copy-start.1 = (s32[3,128]{1,0:T(4,128)S(1)}, s32[3,128]{1,0:T(4,128)}, u32[]{:S(2)}) copy-start(s32[3,128]{1,0:T(4,128)} %param.3) | copy-start | bytes 4612
  22.2 28.5 %collective-permute-start.4 = (f32[5,1,64,132]{3,2,1,0:T(8,128)S(1)}, f32[5,1,64,132]{3,2,1,0:T(8,128)S(1)}, u32[]{:S(2)}, u32[]{:S(2)}) collective-permute-start(f32[5,1,64,132]{3,2,1,0:T(8,128)S(1)} %slice.635), channel_id=1, source_target_pairs={{15,8},{14,10},{13,13},{31,24},{30,26},{29,29},{47,40},{46,42},{45... | collective-permute-start | bytes 506888 | tf_op jit(solution)/shard_map/ppermute | solution.py:162
  23.5 47.5 %collective-permute-start.10 = (f32[5,1,64,132]{3,2,1,0:T(8,128)S(1)}, f32[5,1,64,132]{3,2,1,0:T(8,128)S(1)}, u32[]{:S(2)}, u32[]{:S(2)}) collective-permute-start(f32[5,1,64,132]{3,2,1,0:T(8,128)S(1)} %slice.635), channel_id=1, source_target_pairs={{0,1},{1,2},{2,3},{3,4},{4,5},{5,6},{6,7},{7,8},{8,9},{9,10},{10,1... | collective-permute-start | bytes 506888 | tf_op jit(solution)/shard_map/ppermute | solution.py:160
  26.0 45.1 %collective-permute-start.8 = (f32[5,1,64,132]{3,2,1,0:T(8,128)S(1)}, f32[5,1,64,132]{3,2,1,0:T(8,128)S(1)}, u32[]{:S(2)}, u32[]{:S(2)}) collective-permute-start(f32[5,1,64,132]{3,2,1,0:T(8,128)S(1)} %slice.635), channel_id=1, source_target_pairs={{0,2},{1,3},{2,4},{3,5},{4,6},{5,7},{6,8},{7,9},{8,10},{9,11},{10,... | collective-permute-start | bytes 506888 | tf_op jit(solution)/shard_map/ppermute | solution.py:160
  29.8 41.1 %collective-permute-start.6 = (f32[5,1,64,132]{3,2,1,0:T(8,128)S(1)}, f32[5,1,64,132]{3,2,1,0:T(8,128)S(1)}, u32[]{:S(2)}, u32[]{:S(2)}) collective-permute-start(f32[5,1,64,132]{3,2,1,0:T(8,128)S(1)} %slice.635), channel_id=1, source_target_pairs={{0,3},{1,4},{2,5},{3,6},{4,7},{5,8},{6,9},{7,10},{8,11},{9,12},{10... | collective-permute-start | bytes 506888 | tf_op jit(solution)/shard_map/ppermute | solution.py:160
  50.7 18.3 %collective-permute-start.5 = (f32[5,1,64,132]{3,2,1,0:T(8,128)S(1)}, f32[5,1,64,132]{3,2,1,0:T(8,128)S(1)}, u32[]{:S(2)}, u32[]{:S(2)}) collective-permute-start(f32[5,1,64,132]{3,2,1,0:T(8,128)S(1)} %collective-permute-done.4), channel_id=1, source_target_pairs={{8,18},{10,17},{13,16},{24,34},{26,33},{29,32},{40,50},{42,49},{45... | collective-permute-start | bytes 506888 | tf_op jit(solution)/shard_map/ppermute | solution.py:163
  52.6 18.4 %collective-permute-start.9 = (f32[5,1,64,132]{3,2,1,0:T(8,128)S(1)}, f32[5,1,64,132]{3,2,1,0:T(8,128)S(1)}, u32[]{:S(2)}, u32[]{:S(2)}) collective-permute-start(f32[5,1,64,132]{3,2,1,0:T(8,128)S(1)} %collective-permute-done.4), channel_id=1, source_target_pairs={{8,16},{24,32},{40,48},{56,64},{72,80},{88,96},{104,112},{120,0},{... | collective-permute-start | bytes 506888 | tf_op jit(solution)/shard_map/ppermute | solution.py:169
  69.0 8.4 %collective-permute-start.7 = (f32[5,1,64,132]{3,2,1,0:T(8,128)S(1)}, f32[5,1,64,132]{3,2,1,0:T(8,128)S(1)}, u32[]{:S(2)}, u32[]{:S(2)}) collective-permute-start(f32[5,1,64,132]{3,2,1,0:T(8,128)S(1)} %collective-permute-done.5), channel_id=1, source_target_pairs={{1,0},{2,1},{17,16},{18,17},{33,32},{34,33},{49,48},{50,49},{65,64... | collective-permute-start | bytes 506888 | tf_op jit(solution)/shard_map/ppermute | solution.py:184
  80.7 9.0 %collective-permute-start.11 = (f32[5,1,64,130]{3,2,1,0:T(8,128)S(1)}, f32[5,1,64,130]{3,2,1,0:T(8,128)S(1)}, u32[]{:S(2)}, u32[]{:S(2)}) collective-permute-start(f32[5,1,64,130]{3,2,1,0:T(8,128)S(1)} %slice.677), channel_id=1, source_target_pairs={{15,8},{14,10},{13,13},{31,24},{30,26},{29,29},{47,40},{46,42},{45... | collective-permute-start | bytes 499208 | tf_op jit(solution)/shard_map/ppermute | solution.py:162
  82.0 30.2 %collective-permute-start.13 = (f32[5,1,64,130]{3,2,1,0:T(8,128)S(1)}, f32[5,1,64,130]{3,2,1,0:T(8,128)S(1)}, u32[]{:S(2)}, u32[]{:S(2)}) collective-permute-start(f32[5,1,64,130]{3,2,1,0:T(8,128)S(1)} %slice.677), channel_id=1, source_target_pairs={{0,3},{1,4},{2,5},{3,6},{4,7},{5,8},{6,9},{7,10},{8,11},{9,12},{10... | collective-permute-start | bytes 499208 | tf_op jit(solution)/shard_map/ppermute | solution.py:160
  89.7 20.6 %collective-permute-start.12 = (f32[5,1,64,130]{3,2,1,0:T(8,128)S(1)}, f32[5,1,64,130]{3,2,1,0:T(8,128)S(1)}, u32[]{:S(2)}, u32[]{:S(2)}) collective-permute-start(f32[5,1,64,130]{3,2,1,0:T(8,128)S(1)} %collective-permute-done.11), channel_id=1, source_target_pairs={{8,18},{10,17},{13,16},{24,34},{26,33},{29,32},{40,50},{42,49},{45... | collective-permute-start | bytes 499208 | tf_op jit(solution)/shard_map/ppermute | solution.py:163
  91.7 20.6 %collective-permute-start.17 = (f32[5,1,64,130]{3,2,1,0:T(8,128)S(1)}, f32[5,1,64,130]{3,2,1,0:T(8,128)S(1)}, u32[]{:S(2)}, u32[]{:S(2)}) collective-permute-start(f32[5,1,64,130]{3,2,1,0:T(8,128)S(1)} %slice.677), channel_id=1, source_target_pairs={{0,1},{1,2},{2,3},{3,4},{4,5},{5,6},{6,7},{7,8},{8,9},{9,10},{10,1... | collective-permute-start | bytes 499208 | tf_op jit(solution)/shard_map/ppermute | solution.py:160
  93.6 20.7 %collective-permute-start.15 = (f32[5,1,64,130]{3,2,1,0:T(8,128)S(1)}, f32[5,1,64,130]{3,2,1,0:T(8,128)S(1)}, u32[]{:S(2)}, u32[]{:S(2)}) collective-permute-start(f32[5,1,64,130]{3,2,1,0:T(8,128)S(1)} %slice.677), channel_id=1, source_target_pairs={{0,2},{1,3},{2,4},{3,5},{4,6},{5,7},{6,8},{7,9},{8,10},{9,11},{10,... | collective-permute-start | bytes 499208 | tf_op jit(solution)/shard_map/ppermute | solution.py:160
  99.4 14.8 %collective-permute-start.16 = (f32[5,1,64,130]{3,2,1,0:T(8,128)S(1)}, f32[5,1,64,130]{3,2,1,0:T(8,128)S(1)}, u32[]{:S(2)}, u32[]{:S(2)}) collective-permute-start(f32[5,1,64,130]{3,2,1,0:T(8,128)S(1)} %collective-permute-done.11), channel_id=1, source_target_pairs={{8,16},{24,32},{40,48},{56,64},{72,80},{88,96},{104,112},{120,0},{... | collective-permute-start | bytes 499208 | tf_op jit(solution)/shard_map/ppermute | solution.py:169
  110.3 8.4 %collective-permute-start.14 = (f32[5,1,64,130]{3,2,1,0:T(8,128)S(1)}, f32[5,1,64,130]{3,2,1,0:T(8,128)S(1)}, u32[]{:S(2)}, u32[]{:S(2)}) collective-permute-start(f32[5,1,64,130]{3,2,1,0:T(8,128)S(1)} %collective-permute-done.12), channel_id=1, source_target_pairs={{1,0},{2,1},{17,16},{18,17},{33,32},{34,33},{49,48},{50,49},{65,64... | collective-permute-start | bytes 499208 | tf_op jit(solution)/shard_map/ppermute | solution.py:184
  121.5 7.3 %collective-permute-start.18 = (f32[5,1,64,128]{3,2,1,0:T(8,128)S(1)}, f32[5,1,64,128]{3,2,1,0:T(8,128)S(1)}, u32[]{:S(2)}, u32[]{:S(2)}) collective-permute-start(f32[5,1,64,128]{3,2,1,0:T(8,128)S(1)} %get-tuple-element.5), channel_id=1, source_target_pairs={{15,8},{14,10},{13,13},{31,24},{30,26},{29,29},{47,40},{46,42},{45... | collective-permute-start | bytes 491528 | tf_op jit(solution)/shard_map/ppermute | solution.py:162
  122.8 29.4 %collective-permute-start.20 = (f32[5,1,64,128]{3,2,1,0:T(8,128)S(1)}, f32[5,1,64,128]{3,2,1,0:T(8,128)S(1)}, u32[]{:S(2)}, u32[]{:S(2)}) collective-permute-start(f32[5,1,64,128]{3,2,1,0:T(8,128)S(1)} %get-tuple-element.5), channel_id=1, source_target_pairs={{0,3},{1,4},{2,5},{3,6},{4,7},{5,8},{6,9},{7,10},{8,11},{9,12},{10... | collective-permute-start | bytes 491528 | tf_op jit(solution)/shard_map/ppermute | solution.py:160
  128.8 21.5 %collective-permute-start.19 = (f32[5,1,64,128]{3,2,1,0:T(8,128)S(1)}, f32[5,1,64,128]{3,2,1,0:T(8,128)S(1)}, u32[]{:S(2)}, u32[]{:S(2)}) collective-permute-start(f32[5,1,64,128]{3,2,1,0:T(8,128)S(1)} %collective-permute-done.18), channel_id=1, source_target_pairs={{8,18},{10,17},{13,16},{24,34},{26,33},{29,32},{40,50},{42,49},{45... | collective-permute-start | bytes 491528 | tf_op jit(solution)/shard_map/ppermute | solution.py:163
  130.7 21.5 %collective-permute-start.22 = (f32[5,1,64,128]{3,2,1,0:T(8,128)S(1)}, f32[5,1,64,128]{3,2,1,0:T(8,128)S(1)}, u32[]{:S(2)}, u32[]{:S(2)}) collective-permute-start(f32[5,1,64,128]{3,2,1,0:T(8,128)S(1)} %get-tuple-element.5), channel_id=1, source_target_pairs={{0,2},{1,3},{2,4},{3,5},{4,6},{5,7},{6,8},{7,9},{8,10},{9,11},{10,... | collective-permute-start | bytes 491528 | tf_op jit(solution)/shard_map/ppermute | solution.py:160
  136.7 20.2 %collective-permute-start.24 = (f32[5,1,64,128]{3,2,1,0:T(8,128)S(1)}, f32[5,1,64,128]{3,2,1,0:T(8,128)S(1)}, u32[]{:S(2)}, u32[]{:S(2)}) collective-permute-start(f32[5,1,64,128]{3,2,1,0:T(8,128)S(1)} %get-tuple-element.5), channel_id=1, source_target_pairs={{0,1},{1,2},{2,3},{3,4},{4,5},{5,6},{6,7},{7,8},{8,9},{9,10},{10,1... | collective-permute-start | bytes 491528 | tf_op jit(solution)/shard_map/ppermute | solution.py:160
  139.0 17.9 %collective-permute-start.23 = (f32[5,1,64,128]{3,2,1,0:T(8,128)S(1)}, f32[5,1,64,128]{3,2,1,0:T(8,128)S(1)}, u32[]{:S(2)}, u32[]{:S(2)}) collective-permute-start(f32[5,1,64,128]{3,2,1,0:T(8,128)S(1)} %collective-permute-done.18), channel_id=1, source_target_pairs={{8,16},{24,32},{40,48},{56,64},{72,80},{88,96},{104,112},{120,0},{... | collective-permute-start | bytes 491528 | tf_op jit(solution)/shard_map/ppermute | solution.py:169
  150.2 6.6 %collective-permute-start.21 = (f32[5,1,64,128]{3,2,1,0:T(8,128)S(1)}, f32[5,1,64,128]{3,2,1,0:T(8,128)S(1)}, u32[]{:S(2)}, u32[]{:S(2)}) collective-permute-start(f32[5,1,64,128]{3,2,1,0:T(8,128)S(1)} %collective-permute-done.19), channel_id=1, source_target_pairs={{1,0},{2,1},{17,16},{18,17},{33,32},{34,33},{49,48},{50,49},{65,64... | collective-permute-start | bytes 491528 | tf_op jit(solution)/shard_map/ppermute | solution.py:184

commit v17 on v16

--- a/solution.py
+++ b/solution.py
@@ -138,7 +138,7 @@
             base = block * plane
             after = (base + plane) % count
             for j in range(1, blocks + 1):
-                lane = (3 * g + j + 3) % half
+                lane = (3 * g + j + 1) % half
                 relay = base + relay_seat(lane, plane - j, plane, blocks)
                 first.append((g * count + base + plane - j, g * count + relay))
                 second.append((g * count + relay, g * count + after + blocks - j))

time: 159 us -> 163 us (1.025)
  the two profiles are of different devices: /device:TPU:261 before, /device:TPU:133 now
where the time goes in v17:
time: 163 us; the launch traced here: 162 us
  starting transfers between devices  79.9 us (49%)
  waiting for transfers between devices  67.7 us (42%)
  other arithmetic  10.1 us (6%)
  local copies, waits for them, and re-layouts  3.57 us (2%)
    ppermute x3, waiting for transfers between devices, rotation_pieces(): relayed = lax.ppermute(head, ('rad', 'azi'), first)  27.7 us
    ppermute x9, starting transfers between devices, rotation_pieces(): near.append(lax.ppermute(head, 'azi', pairs))  27.6 us
    ppermute x3, starting transfers between devices, rotation_pieces(): first_seat = lax.ppermute(relayed, ('rad', 'azi'), direct)  25.4 us
    ppermute x3, waiting for transfers between devices, rotation_pieces(): crossed = lax.ppermute(relayed, ('rad', 'azi'), second)  16.5 us
    ppermute x3, waiting for transfers between devices, rotation_pieces(): far = lax.ppermute(crossed, 'azi', pairs)  15.3 us
    ppermute x4, starting transfers between devices, passed_along(): return lax.ppermute(value, axis, pairs)  11.6 us
    ppermute x4, waiting for transfers between devices, passed_along(): return lax.ppermute(value, axis, pairs)  6.16 us
    ppermute x3, starting transfers between devices, rotation_pieces(): far = lax.ppermute(crossed, 'azi', pairs)  5.75 us
  transfers between devices with their start and end apart: 25, of which 10 were waited for; matrix products, arithmetic and copies ran while one was open for 2% of the time, Pallas kernels for 0%

profile of v17, /device:TPU:133, one launch (start us, length us, event | category | flops | bytes accessed | tf_op | source)
XLA Modules:
  0.0 162.2 jit_solution(16099870039197925769)
XLA Ops:
  0.0 0.8 fusion.103
  0.8 3.8 %collective-permute-start = (f32[5,1,3,128]{3,2,1,0:T(4,128)S(1)}, f32[5,1,3,128]{3,2,1,0:T(4,128)S(1)}, u32[]{:S(2)}, u32[]{:S(2)}) collective-permute-start(f32[5,1,3,128]{3,2,1,0:T(4,128)S(1)} %get-tuple-element.46), channel_id=1, source_target_pairs={{0,1},{1,2},{2,3},{3,4},{4,5},{5,6},{6,7},{7,8},{8,9},{9,10},{10,1... | collective-permute-start | bytes 23048 | tf_op jit(solution)/shard_map/ppermute | solution.py:25
  4.6 1.9 %collective-permute-start.1 = (f32[5,1,3,128]{3,2,1,0:T(4,128)S(1)}, f32[5,1,3,128]{3,2,1,0:T(4,128)S(1)}, u32[]{:S(2)}, u32[]{:S(2)}) collective-permute-start(f32[5,1,3,128]{3,2,1,0:T(4,128)S(1)} %get-tuple-element.47), channel_id=1, source_target_pairs={{0,127},{1,0},{2,1},{3,2},{4,3},{5,4},{6,5},{7,6},{8,7},{9,8},{10,... | collective-permute-start | bytes 23048 | tf_op jit(solution)/shard_map/ppermute | solution.py:25
  6.5 0.8 slice_convert_fusion.1
  7.8 1.8 %collective-permute-done.1 = f32[5,1,3,128]{3,2,1,0:T(4,128)S(1)} collective-permute-done((f32[5,1,3,128]{3,2,1,0:T(4,128)S(1)}, f32[5,1,3,128]{3,2,1,0:T(4,128)S(1)}, u32[]{:S(2)}, u32[]{:S(2)}) %collective-permute-start.1) | collective-permute-done | bytes 7712 | tf_op jit(solution)/shard_map/ppermute | solution.py:25
  9.6 0.9 pad_maximum_fusion
  10.6 0.2 reshape.1273
  10.9 4.0 %collective-permute-start.2 = (f32[1059]{0:T(1024)S(1)}, f32[1059]{0:T(1024)S(1)}, u32[]{:S(2)}, u32[]{:S(2)}) collective-permute-start(f32[1059]{0:T(1024)S(1)} %pad_maximum_fusion.1), channel_id=1, source_target_pairs={{0,128},{128,256},{256,384},{384,512},{512,640},{640,768},{768,896... | collective-permute-start | bytes 12716 | tf_op jit(solution)/shard_map/ppermute | solution.py:25
  14.9 0.2 reshape.1275
  15.2 1.9 %collective-permute-start.3 = (f32[1059]{0:T(1024)S(1)}, f32[1059]{0:T(1024)S(1)}, u32[]{:S(2)}, u32[]{:S(2)}) collective-permute-start(f32[1059]{0:T(1024)S(1)} %pad_maximum_fusion.2), channel_id=1, source_target_pairs={{128,0},{256,128},{384,256},{512,384},{640,512},{768,640},{896,768... | collective-permute-start | bytes 12716 | tf_op jit(solution)/shard_map/ppermute | solution.py:25
  17.1 0.2 concatenate.40
  17.3 4.4 %collective-permute-done.3 = f32[1059]{0:T(1024)S(1)} collective-permute-done((f32[1059]{0:T(1024)S(1)}, f32[1059]{0:T(1024)S(1)}, u32[]{:S(2)}, u32[]{:S(2)}) %collective-permute-start.3) | collective-permute-done | bytes 4268 | tf_op jit(solution)/shard_map/ppermute | solution.py:25
  21.7 0.2 concatenate.41
  21.9 0.2 maximum_select_fusion
  22.3 0.2 subtract_multiply_fusion.3
  22.5 0.6 subtract_add_fusion.1
  23.2 0.1 fusion.4
  23.3 0.1 fusion.29
  23.7 1.3 collective-permute-start.4
  25.0 2.2 %collective-permute-start.10 = (f32[5,1,64,132]{3,2,1,0:T(8,128)S(1)}, f32[5,1,64,132]{3,2,1,0:T(8,128)S(1)}, u32[]{:S(2)}, u32[]{:S(2)}) collective-permute-start(f32[5,1,64,132]{3,2,1,0:T(8,128)S(1)} %slice.635), channel_id=1, source_target_pairs={{0,1},{1,2},{2,3},{3,4},{4,5},{5,6},{6,7},{7,8},{8,9},{9,10},{10,1... | collective-permute-start | bytes 506888 | tf_op jit(solution)/shard_map/ppermute | solution.py:160
  27.2 3.8 %collective-permute-start.8 = (f32[5,1,64,132]{3,2,1,0:T(8,128)S(1)}, f32[5,1,64,132]{3,2,1,0:T(8,128)S(1)}, u32[]{:S(2)}, u32[]{:S(2)}) collective-permute-start(f32[5,1,64,132]{3,2,1,0:T(8,128)S(1)} %slice.635), channel_id=1, source_target_pairs={{0,2},{1,3},{2,4},{3,5},{4,6},{5,7},{6,8},{7,9},{8,10},{9,11},{10,... | collective-permute-start | bytes 506888 | tf_op jit(solution)/shard_map/ppermute | solution.py:160
  31.0 5.5 %collective-permute-start.6 = (f32[5,1,64,132]{3,2,1,0:T(8,128)S(1)}, f32[5,1,64,132]{3,2,1,0:T(8,128)S(1)}, u32[]{:S(2)}, u32[]{:S(2)}) collective-permute-start(f32[5,1,64,132]{3,2,1,0:T(8,128)S(1)} %slice.635), channel_id=1, source_target_pairs={{0,3},{1,4},{2,5},{3,6},{4,7},{5,8},{6,9},{7,10},{8,11},{9,12},{10... | collective-permute-start | bytes 506888 | tf_op jit(solution)/shard_map/ppermute | solution.py:160
  37.0 16.6 %collective-permute-done.4 = f32[5,1,64,132]{3,2,1,0:T(8,128)S(1)} collective-permute-done((f32[5,1,64,132]{3,2,1,0:T(8,128)S(1)}, f32[5,1,64,132]{3,2,1,0:T(8,128)S(1)}, u32[]{:S(2)}, u32[]{:S(2)}) %collective-permute-start.4) | collective-permute-done | bytes 168992 | tf_op jit(solution)/shard_map/ppermute | solution.py:162
  53.7 1.9 %collective-permute-start.5 = (f32[5,1,64,132]{3,2,1,0:T(8,128)S(1)}, f32[5,1,64,132]{3,2,1,0:T(8,128)S(1)}, u32[]{:S(2)}, u32[]{:S(2)}) collective-permute-start(f32[5,1,64,132]{3,2,1,0:T(8,128)S(1)} %collective-permute-done.4), channel_id=1, source_target_pairs={{4,18},{6,17},{8,16},{20,34},{22,33},{24,32},{36,50},{38,49},{40,4... | collective-permute-start | bytes 506888 | tf_op jit(solution)/shard_map/ppermute | solution.py:163
  55.6 1.3 collective-permute-start.9
  56.9 16.5 %collective-permute-done.5 = f32[5,1,64,132]{3,2,1,0:T(8,128)S(1)} collective-permute-done((f32[5,1,64,132]{3,2,1,0:T(8,128)S(1)}, f32[5,1,64,132]{3,2,1,0:T(8,128)S(1)}, u32[]{:S(2)}, u32[]{:S(2)}) %collective-permute-start.5) | collective-permute-done | bytes 168992 | tf_op jit(solution)/shard_map/ppermute | solution.py:163
  73.4 1.9 %collective-permute-start.7 = (f32[5,1,64,132]{3,2,1,0:T(8,128)S(1)}, f32[5,1,64,132]{3,2,1,0:T(8,128)S(1)}, u32[]{:S(2)}, u32[]{:S(2)}) collective-permute-start(f32[5,1,64,132]{3,2,1,0:T(8,128)S(1)} %collective-permute-done.5), channel_id=1, source_target_pairs={{1,0},{2,1},{17,16},{18,17},{33,32},{34,33},{49,48},{50,49},{65,64... | collective-permute-start | bytes 506888 | tf_op jit(solution)/shard_map/ppermute | solution.py:184
  75.5 6.3 %collective-permute-done.7 = f32[5,1,64,132]{3,2,1,0:T(8,128)S(1)} collective-permute-done((f32[5,1,64,132]{3,2,1,0:T(8,128)S(1)}, f32[5,1,64,132]{3,2,1,0:T(8,128)S(1)}, u32[]{:S(2)}, u32[]{:S(2)}) %collective-permute-start.7) | collective-permute-done | bytes 168992 | tf_op jit(solution)/shard_map/ppermute | solution.py:184
  81.9 0.7 concatenate.43
  82.6 0.2 slice_select_fusion
  82.8 0.2 slice_select_fusion.5
  83.0 0.2 slice_select_fusion.4
  83.1 0.1 slice_select_fusion.7
  83.8 0.2 subtract_multiply_fusion.1
  84.0 0.6 subtract_add_fusion
  84.6 0.1 fusion.7
  84.8 0.1 fusion.14
  85.2 1.3 collective-permute-start.11
  86.5 1.3 collective-permute-start.13
  87.8 6.4 %collective-permute-done.11 = f32[5,1,64,130]{3,2,1,0:T(8,128)S(1)} collective-permute-done((f32[5,1,64,130]{3,2,1,0:T(8,128)S(1)}, f32[5,1,64,130]{3,2,1,0:T(8,128)S(1)}, u32[]{:S(2)}, u32[]{:S(2)}) %collective-permute-start.11) | collective-permute-done | bytes 166432 | tf_op jit(solution)/shard_map/ppermute | solution.py:162
  94.2 1.9 %collective-permute-start.12 = (f32[5,1,64,130]{3,2,1,0:T(8,128)S(1)}, f32[5,1,64,130]{3,2,1,0:T(8,128)S(1)}, u32[]{:S(2)}, u32[]{:S(2)}) collective-permute-start(f32[5,1,64,130]{3,2,1,0:T(8,128)S(1)} %collective-permute-done.11), channel_id=1, source_target_pairs={{4,18},{6,17},{8,16},{20,34},{22,33},{24,32},{36,50},{38,49},{40,4... | collective-permute-start | bytes 499208 | tf_op jit(solution)/shard_map/ppermute | solution.py:163
  96.1 1.9 %collective-permute-start.17 = (f32[5,1,64,130]{3,2,1,0:T(8,128)S(1)}, f32[5,1,64,130]{3,2,1,0:T(8,128)S(1)}, u32[]{:S(2)}, u32[]{:S(2)}) collective-permute-start(f32[5,1,64,130]{3,2,1,0:T(8,128)S(1)} %slice.677), channel_id=1, source_target_pairs={{0,1},{1,2},{2,3},{3,4},{4,5},{5,6},{6,7},{7,8},{8,9},{9,10},{10,1... | collective-permute-start | bytes 499208 | tf_op jit(solution)/shard_map/ppermute | solution.py:160
  98.1 3.2 %collective-permute-start.15 = (f32[5,1,64,130]{3,2,1,0:T(8,128)S(1)}, f32[5,1,64,130]{3,2,1,0:T(8,128)S(1)}, u32[]{:S(2)}, u32[]{:S(2)}) collective-permute-start(f32[5,1,64,130]{3,2,1,0:T(8,128)S(1)} %slice.677), channel_id=1, source_target_pairs={{0,2},{1,3},{2,4},{3,5},{4,6},{5,7},{6,8},{7,9},{8,10},{9,11},{10,... | collective-permute-start | bytes 499208 | tf_op jit(solution)/shard_map/ppermute | solution.py:160
  101.3 13.7 %collective-permute-start.16 = (f32[5,1,64,130]{3,2,1,0:T(8,128)S(1)}, f32[5,1,64,130]{3,2,1,0:T(8,128)S(1)}, u32[]{:S(2)}, u32[]{:S(2)}) collective-permute-start(f32[5,1,64,130]{3,2,1,0:T(8,128)S(1)} %collective-permute-done.11), channel_id=1, source_target_pairs={{4,16},{20,32},{36,48},{52,64},{68,80},{84,96},{100,112},{116,0},{... | collective-permute-start | bytes 499208 | tf_op jit(solution)/shard_map/ppermute | solution.py:169
  115.0 1.9 %collective-permute-start.14 = (f32[5,1,64,130]{3,2,1,0:T(8,128)S(1)}, f32[5,1,64,130]{3,2,1,0:T(8,128)S(1)}, u32[]{:S(2)}, u32[]{:S(2)}) collective-permute-start(f32[5,1,64,130]{3,2,1,0:T(8,128)S(1)} %collective-permute-done.12), channel_id=1, source_target_pairs={{1,0},{2,1},{17,16},{18,17},{33,32},{34,33},{49,48},{50,49},{65,64... | collective-permute-start | bytes 499208 | tf_op jit(solution)/shard_map/ppermute | solution.py:184
  117.0 2.0 %collective-permute-done.16 = f32[5,1,64,130]{3,2,1,0:T(8,128)S(1)} collective-permute-done((f32[5,1,64,130]{3,2,1,0:T(8,128)S(1)}, f32[5,1,64,130]{3,2,1,0:T(8,128)S(1)}, u32[]{:S(2)}, u32[]{:S(2)}) %collective-permute-start.16) | collective-permute-done | bytes 166432 | tf_op jit(solution)/shard_map/ppermute | solution.py:169
  119.0 4.4 %collective-permute-done.14 = f32[5,1,64,130]{3,2,1,0:T(8,128)S(1)} collective-permute-done((f32[5,1,64,130]{3,2,1,0:T(8,128)S(1)}, f32[5,1,64,130]{3,2,1,0:T(8,128)S(1)}, u32[]{:S(2)}, u32[]{:S(2)}) %collective-permute-start.14) | collective-permute-done | bytes 166432 | tf_op jit(solution)/shard_map/ppermute | solution.py:184
  123.5 0.7 concatenate.44
  124.2 0.2 slice_select_fusion.3
  124.3 0.2 slice_select_fusion.2
  124.5 0.2 slice_select_fusion.1
  124.7 0.1 slice_select_fusion.6
  125.3 0.1 subtract_multiply_fusion.5
  125.4 0.3 subtract_add_fusion.2
  126.2 1.3 collective-permute-start.18
  127.5 1.3 collective-permute-start.20
  128.8 4.7 %collective-permute-done.18 = f32[5,1,64,128]{3,2,1,0:T(8,128)S(1)} collective-permute-done((f32[5,1,64,128]{3,2,1,0:T(8,128)S(1)}, f32[5,1,64,128]{3,2,1,0:T(8,128)S(1)}, u32[]{:S(2)}, u32[]{:S(2)}) %collective-permute-start.18) | collective-permute-done | bytes 163872 | tf_op jit(solution)/shard_map/ppermute | solution.py:162
  133.5 1.9 %collective-permute-start.19 = (f32[5,1,64,128]{3,2,1,0:T(8,128)S(1)}, f32[5,1,64,128]{3,2,1,0:T(8,128)S(1)}, u32[]{:S(2)}, u32[]{:S(2)}) collective-permute-start(f32[5,1,64,128]{3,2,1,0:T(8,128)S(1)} %collective-permute-done.18), channel_id=1, source_target_pairs={{4,18},{6,17},{8,16},{20,34},{22,33},{24,32},{36,50},{38,49},{40,4... | collective-permute-start | bytes 491528 | tf_op jit(solution)/shard_map/ppermute | solution.py:163
  135.4 5.9 %collective-permute-start.22 = (f32[5,1,64,128]{3,2,1,0:T(8,128)S(1)}, f32[5,1,64,128]{3,2,1,0:T(8,128)S(1)}, u32[]{:S(2)}, u32[]{:S(2)}) collective-permute-start(f32[5,1,64,128]{3,2,1,0:T(8,128)S(1)} %get-tuple-element.5), channel_id=1, source_target_pairs={{0,2},{1,3},{2,4},{3,5},{4,6},{5,7},{6,8},{7,9},{8,10},{9,11},{10,... | collective-permute-start | bytes 491528 | tf_op jit(solution)/shard_map/ppermute | solution.py:160
  141.3 2.4 %collective-permute-start.24 = (f32[5,1,64,128]{3,2,1,0:T(8,128)S(1)}, f32[5,1,64,128]{3,2,1,0:T(8,128)S(1)}, u32[]{:S(2)}, u32[]{:S(2)}) collective-permute-start(f32[5,1,64,128]{3,2,1,0:T(8,128)S(1)} %get-tuple-element.5), channel_id=1, source_target_pairs={{0,1},{1,2},{2,3},{3,4},{4,5},{5,6},{6,7},{7,8},{8,9},{9,10},{10,1... | collective-permute-start | bytes 491528 | tf_op jit(solution)/shard_map/ppermute | solution.py:160
  143.7 10.4 %collective-permute-start.23 = (f32[5,1,64,128]{3,2,1,0:T(8,128)S(1)}, f32[5,1,64,128]{3,2,1,0:T(8,128)S(1)}, u32[]{:S(2)}, u32[]{:S(2)}) collective-permute-start(f32[5,1,64,128]{3,2,1,0:T(8,128)S(1)} %collective-permute-done.18), channel_id=1, source_target_pairs={{4,16},{20,32},{36,48},{52,64},{68,80},{84,96},{100,112},{116,0},{... | collective-permute-start | bytes 491528 | tf_op jit(solution)/shard_map/ppermute | solution.py:169
  154.2 1.9 %collective-permute-start.21 = (f32[5,1,64,128]{3,2,1,0:T(8,128)S(1)}, f32[5,1,64,128]{3,2,1,0:T(8,128)S(1)}, u32[]{:S(2)}, u32[]{:S(2)}) collective-permute-start(f32[5,1,64,128]{3,2,1,0:T(8,128)S(1)} %collective-permute-done.19), channel_id=1, source_target_pairs={{1,0},{2,1},{17,16},{18,17},{33,32},{34,33},{49,48},{50,49},{65,64... | collective-permute-start | bytes 491528 | tf_op jit(solution)/shard_map/ppermute | solution.py:184
  156.2 4.7 %collective-permute-done.21 = f32[5,1,64,128]{3,2,1,0:T(8,128)S(1)} collective-permute-done((f32[5,1,64,128]{3,2,1,0:T(8,128)S(1)}, f32[5,1,64,128]{3,2,1,0:T(8,128)S(1)}, u32[]{:S(2)}, u32[]{:S(2)}) %collective-permute-start.21) | collective-permute-done | bytes 163872 | tf_op jit(solution)/shard_map/ppermute | solution.py:184
  161.6 0.7 slice_select_fusion.23
  (93 shorter events, 4.4 us)
Async XLA Ops:
  0.0 21.9 %copy-start = (f32[5,1,64,128]{3,2,1,0:T(8,128)S(1)}, f32[5,1,64,128]{3,2,1,0:T(8,128)}, u32[]{:S(2)}) copy-start(f32[5,1,64,128]{3,2,1,0:T(8,128)} %param.2) | copy-start | bytes 491524
  0.8 7.0 %collective-permute-start = (f32[5,1,3,128]{3,2,1,0:T(4,128)S(1)}, f32[5,1,3,128]{3,2,1,0:T(4,128)S(1)}, u32[]{:S(2)}, u32[]{:S(2)}) collective-permute-start(f32[5,1,3,128]{3,2,1,0:T(4,128)S(1)} %get-tuple-element.46), channel_id=1, source_target_pairs={{0,1},{1,2},{2,3},{3,4},{4,5},{5,6},{6,7},{7,8},{8,9},{9,10},{10,1... | collective-permute-start | bytes 23048 | tf_op jit(solution)/shard_map/ppermute | solution.py:25
  4.6 5.0 %collective-permute-start.1 = (f32[5,1,3,128]{3,2,1,0:T(4,128)S(1)}, f32[5,1,3,128]{3,2,1,0:T(4,128)S(1)}, u32[]{:S(2)}, u32[]{:S(2)}) collective-permute-start(f32[5,1,3,128]{3,2,1,0:T(4,128)S(1)} %get-tuple-element.47), channel_id=1, source_target_pairs={{0,127},{1,0},{2,1},{3,2},{4,3},{5,4},{6,5},{7,6},{8,7},{9,8},{10,... | collective-permute-start | bytes 23048 | tf_op jit(solution)/shard_map/ppermute | solution.py:25
  10.9 6.2 %collective-permute-start.2 = (f32[1059]{0:T(1024)S(1)}, f32[1059]{0:T(1024)S(1)}, u32[]{:S(2)}, u32[]{:S(2)}) collective-permute-start(f32[1059]{0:T(1024)S(1)} %pad_maximum_fusion.1), channel_id=1, source_target_pairs={{0,128},{128,256},{256,384},{384,512},{512,640},{640,768},{768,896... | collective-permute-start | bytes 12716 | tf_op jit(solution)/shard_map/ppermute | solution.py:25
  15.2 6.5 %collective-permute-start.3 = (f32[1059]{0:T(1024)S(1)}, f32[1059]{0:T(1024)S(1)}, u32[]{:S(2)}, u32[]{:S(2)}) collective-permute-start(f32[1059]{0:T(1024)S(1)} %pad_maximum_fusion.2), channel_id=1, source_target_pairs={{128,0},{256,128},{384,256},{512,384},{640,512},{768,640},{896,768... | collective-permute-start | bytes 12716 | tf_op jit(solution)/shard_map/ppermute | solution.py:25
  23.0 13.8 %copy-start.1 = (s32[3,128]{1,0:T(4,128)S(1)}, s32[3,128]{1,0:T(4,128)}, u32[]{:S(2)}) copy-start(s32[3,128]{1,0:T(4,128)} %param.3) | copy-start | bytes 4612
  23.7 30.0 %collective-permute-start.4 = (f32[5,1,64,132]{3,2,1,0:T(8,128)S(1)}, f32[5,1,64,132]{3,2,1,0:T(8,128)S(1)}, u32[]{:S(2)}, u32[]{:S(2)}) collective-permute-start(f32[5,1,64,132]{3,2,1,0:T(8,128)S(1)} %slice.635), channel_id=1, source_target_pairs={{15,4},{14,6},{13,8},{31,20},{30,22},{29,24},{47,36},{46,38},{45,4... | collective-permute-start | bytes 506888 | tf_op jit(solution)/shard_map/ppermute | solution.py:162
  25.0 50.5 %collective-permute-start.10 = (f32[5,1,64,132]{3,2,1,0:T(8,128)S(1)}, f32[5,1,64,132]{3,2,1,0:T(8,128)S(1)}, u32[]{:S(2)}, u32[]{:S(2)}) collective-permute-start(f32[5,1,64,132]{3,2,1,0:T(8,128)S(1)} %slice.635), channel_id=1, source_target_pairs={{0,1},{1,2},{2,3},{3,4},{4,5},{5,6},{6,7},{7,8},{8,9},{9,10},{10,1... | collective-permute-start | bytes 506888 | tf_op jit(solution)/shard_map/ppermute | solution.py:160
  27.2 48.3 %collective-permute-start.8 = (f32[5,1,64,132]{3,2,1,0:T(8,128)S(1)}, f32[5,1,64,132]{3,2,1,0:T(8,128)S(1)}, u32[]{:S(2)}, u32[]{:S(2)}) collective-permute-start(f32[5,1,64,132]{3,2,1,0:T(8,128)S(1)} %slice.635), channel_id=1, source_target_pairs={{0,2},{1,3},{2,4},{3,5},{4,6},{5,7},{6,8},{7,9},{8,10},{9,11},{10,... | collective-permute-start | bytes 506888 | tf_op jit(solution)/shard_map/ppermute | solution.py:160
  31.0 44.4 %collective-permute-start.6 = (f32[5,1,64,132]{3,2,1,0:T(8,128)S(1)}, f32[5,1,64,132]{3,2,1,0:T(8,128)S(1)}, u32[]{:S(2)}, u32[]{:S(2)}) collective-permute-start(f32[5,1,64,132]{3,2,1,0:T(8,128)S(1)} %slice.635), channel_id=1, source_target_pairs={{0,3},{1,4},{2,5},{3,6},{4,7},{5,8},{6,9},{7,10},{8,11},{9,12},{10... | collective-permute-start | bytes 506888 | tf_op jit(solution)/shard_map/ppermute | solution.py:160
  53.7 19.8 %collective-permute-start.5 = (f32[5,1,64,132]{3,2,1,0:T(8,128)S(1)}, f32[5,1,64,132]{3,2,1,0:T(8,128)S(1)}, u32[]{:S(2)}, u32[]{:S(2)}) collective-permute-start(f32[5,1,64,132]{3,2,1,0:T(8,128)S(1)} %collective-permute-done.4), channel_id=1, source_target_pairs={{4,18},{6,17},{8,16},{20,34},{22,33},{24,32},{36,50},{38,49},{40,4... | collective-permute-start | bytes 506888 | tf_op jit(solution)/shard_map/ppermute | solution.py:163
  55.6 19.8 %collective-permute-start.9 = (f32[5,1,64,132]{3,2,1,0:T(8,128)S(1)}, f32[5,1,64,132]{3,2,1,0:T(8,128)S(1)}, u32[]{:S(2)}, u32[]{:S(2)}) collective-permute-start(f32[5,1,64,132]{3,2,1,0:T(8,128)S(1)} %collective-permute-done.4), channel_id=1, source_target_pairs={{4,16},{20,32},{36,48},{52,64},{68,80},{84,96},{100,112},{116,0},{... | collective-permute-start | bytes 506888 | tf_op jit(solution)/shard_map/ppermute | solution.py:169
  73.4 8.4 %collective-permute-start.7 = (f32[5,1,64,132]{3,2,1,0:T(8,128)S(1)}, f32[5,1,64,132]{3,2,1,0:T(8,128)S(1)}, u32[]{:S(2)}, u32[]{:S(2)}) collective-permute-start(f32[5,1,64,132]{3,2,1,0:T(8,128)S(1)} %collective-permute-done.5), channel_id=1, source_target_pairs={{1,0},{2,1},{17,16},{18,17},{33,32},{34,33},{49,48},{50,49},{65,64... | collective-permute-start | bytes 506888 | tf_op jit(solution)/shard_map/ppermute | solution.py:184
  85.2 9.0 %collective-permute-start.11 = (f32[5,1,64,130]{3,2,1,0:T(8,128)S(1)}, f32[5,1,64,130]{3,2,1,0:T(8,128)S(1)}, u32[]{:S(2)}, u32[]{:S(2)}) collective-permute-start(f32[5,1,64,130]{3,2,1,0:T(8,128)S(1)} %slice.677), channel_id=1, source_target_pairs={{15,4},{14,6},{13,8},{31,20},{30,22},{29,24},{47,36},{46,38},{45,4... | collective-permute-start | bytes 499208 | tf_op jit(solution)/shard_map/ppermute | solution.py:162
  86.5 30.4 %collective-permute-start.13 = (f32[5,1,64,130]{3,2,1,0:T(8,128)S(1)}, f32[5,1,64,130]{3,2,1,0:T(8,128)S(1)}, u32[]{:S(2)}, u32[]{:S(2)}) collective-permute-start(f32[5,1,64,130]{3,2,1,0:T(8,128)S(1)} %slice.677), channel_id=1, source_target_pairs={{0,3},{1,4},{2,5},{3,6},{4,7},{5,8},{6,9},{7,10},{8,11},{9,12},{10... | collective-permute-start | bytes 499208 | tf_op jit(solution)/shard_map/ppermute | solution.py:160
  94.2 20.8 %collective-permute-start.12 = (f32[5,1,64,130]{3,2,1,0:T(8,128)S(1)}, f32[5,1,64,130]{3,2,1,0:T(8,128)S(1)}, u32[]{:S(2)}, u32[]{:S(2)}) collective-permute-start(f32[5,1,64,130]{3,2,1,0:T(8,128)S(1)} %collective-permute-done.11), channel_id=1, source_target_pairs={{4,18},{6,17},{8,16},{20,34},{22,33},{24,32},{36,50},{38,49},{40,4... | collective-permute-start | bytes 499208 | tf_op jit(solution)/shard_map/ppermute | solution.py:163
  96.1 20.8 %collective-permute-start.17 = (f32[5,1,64,130]{3,2,1,0:T(8,128)S(1)}, f32[5,1,64,130]{3,2,1,0:T(8,128)S(1)}, u32[]{:S(2)}, u32[]{:S(2)}) collective-permute-start(f32[5,1,64,130]{3,2,1,0:T(8,128)S(1)} %slice.677), channel_id=1, source_target_pairs={{0,1},{1,2},{2,3},{3,4},{4,5},{5,6},{6,7},{7,8},{8,9},{9,10},{10,1... | collective-permute-start | bytes 499208 | tf_op jit(solution)/shard_map/ppermute | solution.py:160
  98.1 20.9 %collective-permute-start.15 = (f32[5,1,64,130]{3,2,1,0:T(8,128)S(1)}, f32[5,1,64,130]{3,2,1,0:T(8,128)S(1)}, u32[]{:S(2)}, u32[]{:S(2)}) collective-permute-start(f32[5,1,64,130]{3,2,1,0:T(8,128)S(1)} %slice.677), channel_id=1, source_target_pairs={{0,2},{1,3},{2,4},{3,5},{4,6},{5,7},{6,8},{7,9},{8,10},{9,11},{10,... | collective-permute-start | bytes 499208 | tf_op jit(solution)/shard_map/ppermute | solution.py:160
  101.3 17.7 %collective-permute-start.16 = (f32[5,1,64,130]{3,2,1,0:T(8,128)S(1)}, f32[5,1,64,130]{3,2,1,0:T(8,128)S(1)}, u32[]{:S(2)}, u32[]{:S(2)}) collective-permute-start(f32[5,1,64,130]{3,2,1,0:T(8,128)S(1)} %collective-permute-done.11), channel_id=1, source_target_pairs={{4,16},{20,32},{36,48},{52,64},{68,80},{84,96},{100,112},{116,0},{... | collective-permute-start | bytes 499208 | tf_op jit(solution)/shard_map/ppermute | solution.py:169
  115.0 8.4 %collective-permute-start.14 = (f32[5,1,64,130]{3,2,1,0:T(8,128)S(1)}, f32[5,1,64,130]{3,2,1,0:T(8,128)S(1)}, u32[]{:S(2)}, u32[]{:S(2)}) collective-permute-start(f32[5,1,64,130]{3,2,1,0:T(8,128)S(1)} %collective-permute-done.12), channel_id=1, source_target_pairs={{1,0},{2,1},{17,16},{18,17},{33,32},{34,33},{49,48},{50,49},{65,64... | collective-permute-start | bytes 499208 | tf_op jit(solution)/shard_map/ppermute | solution.py:184
  126.2 7.3 %collective-permute-start.18 = (f32[5,1,64,128]{3,2,1,0:T(8,128)S(1)}, f32[5,1,64,128]{3,2,1,0:T(8,128)S(1)}, u32[]{:S(2)}, u32[]{:S(2)}) collective-permute-start(f32[5,1,64,128]{3,2,1,0:T(8,128)S(1)} %get-tuple-element.5), channel_id=1, source_target_pairs={{15,4},{14,6},{13,8},{31,20},{30,22},{29,24},{47,36},{46,38},{45,4... | collective-permute-start | bytes 491528 | tf_op jit(solution)/shard_map/ppermute | solution.py:162
  127.5 28.6 %collective-permute-start.20 = (f32[5,1,64,128]{3,2,1,0:T(8,128)S(1)}, f32[5,1,64,128]{3,2,1,0:T(8,128)S(1)}, u32[]{:S(2)}, u32[]{:S(2)}) collective-permute-start(f32[5,1,64,128]{3,2,1,0:T(8,128)S(1)} %get-tuple-element.5), channel_id=1, source_target_pairs={{0,3},{1,4},{2,5},{3,6},{4,7},{5,8},{6,9},{7,10},{8,11},{9,12},{10... | collective-permute-start | bytes 491528 | tf_op jit(solution)/shard_map/ppermute | solution.py:160
  133.5 20.7 %collective-permute-start.19 = (f32[5,1,64,128]{3,2,1,0:T(8,128)S(1)}, f32[5,1,64,128]{3,2,1,0:T(8,128)S(1)}, u32[]{:S(2)}, u32[]{:S(2)}) collective-permute-start(f32[5,1,64,128]{3,2,1,0:T(8,128)S(1)} %collective-permute-done.18), channel_id=1, source_target_pairs={{4,18},{6,17},{8,16},{20,34},{22,33},{24,32},{36,50},{38,49},{40,4... | collective-permute-start | bytes 491528 | tf_op jit(solution)/shard_map/ppermute | solution.py:163
  135.4 20.7 %collective-permute-start.22 = (f32[5,1,64,128]{3,2,1,0:T(8,128)S(1)}, f32[5,1,64,128]{3,2,1,0:T(8,128)S(1)}, u32[]{:S(2)}, u32[]{:S(2)}) collective-permute-start(f32[5,1,64,128]{3,2,1,0:T(8,128)S(1)} %get-tuple-element.5), channel_id=1, source_target_pairs={{0,2},{1,3},{2,4},{3,5},{4,6},{5,7},{6,8},{7,9},{8,10},{9,11},{10,... | collective-permute-start | bytes 491528 | tf_op jit(solution)/shard_map/ppermute | solution.py:160
  141.3 19.5 %collective-permute-start.24 = (f32[5,1,64,128]{3,2,1,0:T(8,128)S(1)}, f32[5,1,64,128]{3,2,1,0:T(8,128)S(1)}, u32[]{:S(2)}, u32[]{:S(2)}) collective-permute-start(f32[5,1,64,128]{3,2,1,0:T(8,128)S(1)} %get-tuple-element.5), channel_id=1, source_target_pairs={{0,1},{1,2},{2,3},{3,4},{4,5},{5,6},{6,7},{7,8},{8,9},{9,10},{10,1... | collective-permute-start | bytes 491528 | tf_op jit(solution)/shard_map/ppermute | solution.py:160
  143.7 17.1 %collective-permute-start.23 = (f32[5,1,64,128]{3,2,1,0:T(8,128)S(1)}, f32[5,1,64,128]{3,2,1,0:T(8,128)S(1)}, u32[]{:S(2)}, u32[]{:S(2)}) collective-permute-start(f32[5,1,64,128]{3,2,1,0:T(8,128)S(1)} %collective-permute-done.18), channel_id=1, source_target_pairs={{4,16},{20,32},{36,48},{52,64},{68,80},{84,96},{100,112},{116,0},{... | collective-permute-start | bytes 491528 | tf_op jit(solution)/shard_map/ppermute | solution.py:169
  154.2 6.6 %collective-permute-start.21 = (f32[5,1,64,128]{3,2,1,0:T(8,128)S(1)}, f32[5,1,64,128]{3,2,1,0:T(8,128)S(1)}, u32[]{:S(2)}, u32[]{:S(2)}) collective-permute-start(f32[5,1,64,128]{3,2,1,0:T(8,128)S(1)} %collective-permute-done.19), channel_id=1, source_target_pairs={{1,0},{2,1},{17,16},{18,17},{33,32},{34,33},{49,48},{50,49},{65,64... | collective-permute-start | bytes 491528 | tf_op jit(solution)/shard_map/ppermute | solution.py:184
